TPU v7x, 32 devices: a whole 2x2x4 slice. The times are simulated.
32 devices in a mesh: groups: 2 (over y), tm: 4 (over z), comp: 2 (over core), panel: 2 (over x).
Axes of the slice: x: 2, y: 2, z: 4, core: 2. Of those that a mesh axis runs over, the one named last changes fastest.
Arguments:
- orbit_angles: float32 [2, 8192], P(None, ('groups', 'tm')), parts along dimension 1, may hold values from -3.15 to 3.15, as said below
- gap_mask: int32 [8192], P(('groups', 'tm')), parts along dimension 0, may hold values 0 or 1
- column_index: int32 [2, 512], P(None, 'panel'), may hold values from -280 to 280, as said below
- lat_coeffs: bfloat16 [2, 640, 512], P('comp', None, 'panel'), may hold values from -6 to 6
- psd_table: int32 [2, 2049], P('comp'), may hold values from 1024 to 32752, as said below
Outputs:
- normals: float32 [1024, 512], P(('groups', 'tm'), 'panel'), parts along dimension 0
There are 2 independent parts, one for each index of `groups`. A program takes and returns all parts, laid end to end along the dimension named above; an argument that names none is the same for every part. Nothing has to cross between parts.
Inputs may be any that keep to these rules, and one draw needn't show every extreme that they name: orbit_angles holds colatitude in its first row and longitude in its second. `column_index`: the first row holds each unknown's degree, the second its order; a degree is at least 2 and at least the order's magnitude; a negative order stands for the sine term in longitude. `psd_table`: entry g of a component's row is its noise power at frequency g (and 4096 - g), times 8192.
All inputs are finite; a program needn't handle non-finite values. No bound on the sum of `gap_mask` on one device may be relied on, other than what follows from the above.
Results may differ from a plain program's by a relative error of at most 0.0016.
Values may be sent and summed in bfloat16 or wider, within the bound.
No kernel may reach another device: no remote copies, remote signals or barrier semaphores. Data moves between devices by JAX's collectives and lax.ppermute only.
A program may use at most 64 MiB of HBM per device.

v0:
```python
import math

import jax
import jax.numpy as jnp
from jax import lax
from jax.sharding import PartitionSpec as P

SPLIT = 64


def synthesize(angles, keep_rows, column_index, coeffs):
    terms_lat = coeffs.shape[0] // 2
    colatitude = angles[0]
    longit = angles[1]
    wavenumbers = jnp.arange(terms_lat, dtype=jnp.float32)
    phases = colatitude[:, None] * wavenumbers[None, :]
    basis_rows = jnp.concatenate([jnp.cos(phases), jnp.sin(phases)], axis=1).astype(jnp.bfloat16)
    degree = column_index[0]
    orders = column_index[1]
    levels = jnp.arange(2 * terms_lat, dtype=jnp.int32) % terms_lat
    allowed = levels[:, None] <= degree[None, :]
    masked = jnp.where(allowed, coeffs, jnp.zeros_like(coeffs))
    latitude = jnp.dot(basis_rows, masked, preferred_element_type=jnp.float32)
    lon_phase = longit[:, None] * jnp.abs(orders).astype(jnp.float32)[None, :]
    lon_wave = jnp.where(orders[None, :] >= 0, jnp.cos(lon_phase), jnp.sin(lon_phase))
    norm_scale = 1.0 / jnp.sqrt(degree.astype(jnp.float32) + 1.0)
    return latitude * lon_wave * (keep_rows[:, None] * norm_scale[None, :])


def phase_tables(row_index, col_index, length):
    product = row_index[:, None] * col_index[None, :] % length
    angle_grid = product.astype(jnp.float32) * (2.0 * math.pi / length)
    return (jnp.cos(angle_grid), jnp.sin(angle_grid))


def dft_tables(length):
    indices = jnp.arange(length, dtype=jnp.int32)
    return phase_tables(indices, indices, length)


def rotate(real_part, imag_part, outer_index, inner_index, length):
    index_grid = outer_index[:, None] * inner_index[None, :] % length
    angle_grid = index_grid.astype(jnp.float32) * (2.0 * math.pi / length)
    cosine = jnp.cos(angle_grid)[:, :, None]
    sine_grid = jnp.sin(angle_grid)[:, :, None]
    return (real_part * cosine + imag_part * sine_grid, imag_part * cosine - real_part * sine_grid)


def precise_dot(left_side, right_side):
    return jnp.dot(
        left_side, right_side, precision=lax.Precision.HIGHEST, preferred_element_type=jnp.float32
    )


def transform(cos_table, sin_table, real_part, imag_part):
    new_real = precise_dot(cos_table, real_part) + precise_dot(sin_table, imag_part)
    new_imag = precise_dot(cos_table, imag_part) - precise_dot(sin_table, real_part)
    return (new_real, new_imag)


def four_step(real_in, imag_in, samples):
    length = real_in.shape[0]
    columns = real_in.shape[1]
    outer_count = SPLIT
    inner_count = length // SPLIT
    real_part = real_in.reshape(outer_count, inner_count * columns)
    imag_part = imag_in.reshape(outer_count, inner_count * columns)
    cos_outer, sin_outer = dft_tables(outer_count)
    real_part, imag_part = transform(cos_outer, sin_outer, real_part, imag_part)
    real_part = real_part.reshape(outer_count, inner_count, columns)
    imag_part = imag_part.reshape(outer_count, inner_count, columns)
    real_part, imag_part = rotate(
        real_part,
        imag_part,
        jnp.arange(outer_count, dtype=jnp.int32),
        jnp.arange(inner_count, dtype=jnp.int32),
        length,
    )
    real_part = jnp.transpose(real_part, (1, 0, 2)).reshape(inner_count, outer_count * columns)
    imag_part = jnp.transpose(imag_part, (1, 0, 2)).reshape(inner_count, outer_count * columns)
    cos_inner, sin_inner = dft_tables(inner_count)
    real_part, imag_part = transform(cos_inner, sin_inner, real_part, imag_part)
    return (
        real_part.reshape(length, columns) / samples,
        imag_part.reshape(length, columns) / samples,
    )


def local_transform(received, samples):
    real_part, imag_part = four_step(received[0, 0], received[1, 0], samples)
    return (real_part.astype(jnp.bfloat16), imag_part.astype(jnp.bfloat16))


def noise_weighted(spectra, psd_row, frequency, samples):
    folded = jnp.minimum(frequency, samples - frequency)
    inverse_psd = 8192.0 / jnp.take(psd_row, folded).astype(jnp.float32)
    return (spectra.astype(jnp.float32) * inverse_psd[None, :, None]).astype(jnp.bfloat16)


def settle(partial_value, sum_dim):
    summed = lax.psum_scatter(partial_value, "tm", scatter_dimension=sum_dim, tiled=True)
    return lax.psum(summed, "comp")


def body(orbit_angles, gap_mask, column_index, lat_coeffs, psd_table):
    devices_tm = lax.axis_size("tm")
    epochs = orbit_angles.shape[1]
    block_len = epochs // devices_tm
    samples = epochs * devices_tm
    columns = lat_coeffs.shape[2]
    coeffs = lat_coeffs[0]
    keep_rows = gap_mask.astype(jnp.float32)
    packed = jnp.concatenate([orbit_angles, keep_rows[None]], axis=0)[:, None, :]
    received = lax.all_to_all(packed, "tm", split_axis=2, concat_axis=1, tiled=True)
    flat_orbit = received.reshape(3, devices_tm * block_len)
    spread = synthesize(flat_orbit[0:2], flat_orbit[2], column_index, coeffs).reshape(
        devices_tm, block_len, columns
    )
    position = lax.axis_index("tm")
    local_epoch = position * block_len + jnp.arange(block_len, dtype=jnp.int32)
    cos_outer, sin_outer = dft_tables(devices_tm)
    flat_design = spread.reshape(devices_tm, block_len * columns)
    real_part = precise_dot(cos_outer, flat_design).reshape(devices_tm, block_len, columns)
    imag_part = -precise_dot(sin_outer, flat_design).reshape(devices_tm, block_len, columns)
    real_part, imag_part = rotate(
        real_part, imag_part, jnp.arange(devices_tm, dtype=jnp.int32), local_epoch, samples
    )
    twisted = jnp.stack([real_part, imag_part])
    spec_real, spec_imag = local_transform(
        lax.all_to_all(twisted, "tm", split_axis=1, concat_axis=2, tiled=True), samples
    )
    spectra = jnp.stack([spec_real, spec_imag])
    psd_row = psd_table[0]
    contract = (((0, 1), (0, 1)), ((), ()))
    frequency = position + devices_tm * jnp.arange(epochs, dtype=jnp.int32)
    weighted = noise_weighted(spectra, psd_row, frequency, samples)
    partial_value = lax.dot_general(
        lax.all_gather(spectra, "panel", axis=2, tiled=True),
        weighted,
        contract,
        preferred_element_type=jnp.float32,
    )
    return settle(partial_value, 0)


def solution(mesh):
    return jax.shard_map(
        body,
        mesh=mesh,
        in_specs=(
            P(None, ("groups", "tm")),
            P(("groups", "tm")),
            P(None, "panel"),
            P("comp", None, "panel"),
            P("comp", None),
        ),
        out_specs=P(("groups", "tm"), "panel"),
        check_vma=False,
    )
```

profile of v0, /device:TPU:0, one launch (start us, length us, event | category | flops | bytes accessed | tf_op | source)
XLA Modules:
  0.0 205.0 jit_solution(10367188866137886708)
XLA Ops:
  8.8 2.0 reduce.9
  11.8 6.4 %all-to-all-start = ((f32[4,1,768]{2,1,0:T(1,128)}), f32[4,1,768]{2,1,0:T(1,128)S(1)}, u32[]{:S(2)}, u32[]{:S(2)}) async-start(f32[4,1,768]{2,1,0:T(1,128)} %reshape.246), calls=%async_computation | async-start | bytes 24576 | tf_op jit(solution)/shard_map/all_to_all | solution.py:114
  18.7 5.2 %all-to-all-done = f32[4,1,768]{2,1,0:T(1,128)S(1)} async-done(((f32[4,1,768]{2,1,0:T(1,128)}), f32[4,1,768]{2,1,0:T(1,128)S(1)}, u32[]{:S(2)}, u32[]{:S(2)}) %all-to-all-start) | async-done | bytes 12320 | tf_op jit(solution)/shard_map/all_to_all | solution.py:114
  25.3 10.4 %slice_reduce_fusion.1 = (f32[1024]{0:T(1024)S(1)}, f32[1024]{0:T(1024)S(1)}, f32[1024]{0:T(1024)S(1)}) fusion(f32[3,1,1024]{0,1,2:T(1,128)S(1)} %bitcast.77), kind=kLoop, calls=%fused_computation.36 | loop fusion | bytes 24576 | tf_op jit(solution)/shard_map/slice | solution.py:14
  35.7 6.5 %cosine_convert_fusion = (bf16[1024,320]{1,0:T(8,128)(2,1)S(1)}, bf16[1024,320]{1,0:T(8,128)(2,1)S(1)}) fusion(f32[1024]{0:T(1024)S(1)} %get-tuple-element.7), kind=kLoop, calls=%fused_computation.12 | loop fusion | flops 983040 | bytes 1314816 | tf_op jit(solution)/shard_map/convert
  42.3 4.4 %fusion.4 = f32[1024,256]{1,0:T(8,128)S(1)} fusion(bf16[1024,320]{1,0:T(8,128)(2,1)S(1)} %get-tuple-element.15, bf16[1024,320]{1,0:T(8,128)(2,1)S(1)} %get-tuple-element.14, f32[256]{0:T(256)S(1)} %bitcast.85, f32[1024]{0:T(1024)S(1)} %get-tuple-element.6, f32[256]{0:T(256)S(1)} %bitcast.87, f32[1024]{0:T(1024)S(1)} %get-tuple-element.5, ...), kind=kOutput, calls=%fused_computation.18 | convolution fusion | flops 339804160 | bytes 2701056 | tf_op jit(solution)/shard_map/dot_general | solution.py:23
  47.2 1.9 convolution_negate_fusion
  49.2 2.8 %add_bitcast_fusion = (f32[1,4,256,256]{3,1,2,0:T(4,128)S(1)}, f32[1,4,256,256]{3,1,2,0:T(4,128)S(1)}) fusion(f32[4,256,256]{2,0,1:T(4,128)S(1)} %convolution_negate_fusion, f32[4,256]{0,1:T(8,128)S(1)} %copy.48, f32[4,256]{0,1:T(8,128)S(1)} %copy.47, f32[256,256,4]{1,2,0:T(4,128)S(1)} %bitcast.72), kind=kOutput, calls=%fused_computation.33 | convolution fusion | flops 14156000 | bytes 4202496 | tf_op jit(solution)/shard_map/dot_general | solution.py:50
  52.4 1.7 copy.49
  54.2 3.6 %all-to-all-start.1 = ((f32[2,4,256,256]{3,2,0,1:T(8,128)}), f32[2,4,256,256]{3,2,0,1:T(8,128)S(1)}, u32[]{:S(2)}, u32[]{:S(2)}) async-start(f32[2,4,256,256]{3,2,0,1:T(8,128)} %copy.49), calls=%async_computation.1 | async-start | bytes 4194304 | tf_op jit(solution)/shard_map/all_to_all | solution.py:130
  58.1 46.7 %all-to-all-done.1 = f32[2,4,256,256]{3,2,0,1:T(8,128)S(1)} async-done(((f32[2,4,256,256]{3,2,0,1:T(8,128)}), f32[2,4,256,256]{3,2,0,1:T(8,128)S(1)}, u32[]{:S(2)}, u32[]{:S(2)}) %all-to-all-start.1) | async-done | bytes 2097184 | tf_op jit(solution)/shard_map/all_to_all | solution.py:130
  104.8 1.1 fusion.115
  106.1 1.2 fusion.26
  107.3 1.4 reshape_squeeze.7
  108.7 1.2 fusion.24
  109.9 1.2 convolution_add_fusion.1
  111.1 1.2 convolution_subtract_fusion.1
  118.3 1.1 fusion.3
  121.2 6.2 %gather_fusion = s32[1024]{0:T(1024)S(1)} fusion(s32[2049]{0:T(1024)S(1)} %reduce.4, s32[1024]{0:T(1024)S(1)} %broadcast_clamp_fusion), kind=kCustom, calls=%fused_computation | custom fusion | bytes 12288 | tf_op jit(solution)/shard_map/jit(_take)/gather | solution.py:96
  127.3 26.1 %all-gather.2.cloned.1.call-done = bf16[2,1024,512]{1,2,0:T(8,128)(2,1)} async-done(((bf16[2,1024,256]{1,2,0:T(8,128)(2,1)}), bf16[2,1024,512]{1,2,0:T(8,128)(2,1)}) %all-gather.2.cloned.1.call-update) | async-done | bytes 2097168 | tf_op jit(solution)/shard_map/all_gather | solution.py:138
  153.4 3.1 %convolution_bitcast_fusion = f32[512,256]{1,0:T(8,128)} fusion(bf16[2,1024,512]{1,2,0:T(8,128)(2,1)} %all-gather.2.cloned.1.call-done, f32[1024]{0:T(1024)S(1)} %convert_divide_fusion, bf16[1,1024,256]{1,2,0:T(8,128)(2,1)S(1)} %copy.55, bf16[1,1024,256]{1,2,0:T(8,128)(2,1)S(1)} %copy-done.1), kind=kOutput, calls=%fused_computation.22 | convolution fusion | flops 538968064 | bytes 3674112 | tf_op jit(solution)/shard_map/dot_general | solution.py:137
  156.6 21.8 %reduce-scatter.2.cloned.1.call-done = f32[128,256]{1,0:T(8,128)} async-done(((f32[512,256]{1,0:T(8,128)}), f32[128,256]{1,0:T(8,128)}) %reduce-scatter.2.cloned.1.call-update) | async-done | bytes 131088 | tf_op jit(solution)/shard_map/reduce_scatter | solution.py:101
  178.4 18.5 %all-reduce.2.cloned.1.call-done = f32[128,256]{1,0:T(8,128)} async-done(((f32[128,256]{1,0:T(8,128)}), f32[128,256]{1,0:T(8,128)}) %all-reduce.2.cloned.1.call-update) | async-done | bytes 131088 | tf_op jit(solution)/shard_map/psum | solution.py:102
  196.9 1.6 copy.67
  (48 shorter events, 14.2 us)
Async XLA Ops:
  6.5 114.5 %copy-start = (s32[1,2049]{1,0:T(1,128)S(1)}, s32[1,2049]{1,0:T(1,128)}, u32[]{:S(2)}) copy-start(s32[1,2049]{1,0:T(1,128)} %param.9) | copy-start | bytes 24592
  6.5 11.7 %copy-start.2 = (s32[2,256]{1,0:T(2,128)S(1)}, s32[2,256]{1,0:T(2,128)}, u32[]{:S(2)}) copy-start(s32[2,256]{1,0:T(2,128)} %param.7) | copy-start | bytes 6148
  11.8 30.5 %copy-start.3 = (bf16[1,640,256]{2,1,0:T(8,128)(2,1)S(1)}, bf16[1,640,256]{2,1,0:T(8,128)(2,1)}, u32[]{:S(2)}) copy-start(bf16[1,640,256]{2,1,0:T(8,128)(2,1)} %param.8) | copy-start | bytes 983044
  11.8 12.1 %all-to-all-start = ((f32[4,1,768]{2,1,0:T(1,128)}), f32[4,1,768]{2,1,0:T(1,128)S(1)}, u32[]{:S(2)}, u32[]{:S(2)}) async-start(f32[4,1,768]{2,1,0:T(1,128)} %reshape.246), calls=%async_computation | async-start | bytes 24576 | tf_op jit(solution)/shard_map/all_to_all | solution.py:114
  54.2 50.6 %all-to-all-start.1 = ((f32[2,4,256,256]{3,2,0,1:T(8,128)}), f32[2,4,256,256]{3,2,0,1:T(8,128)S(1)}, u32[]{:S(2)}, u32[]{:S(2)}) async-start(f32[2,4,256,256]{3,2,0,1:T(8,128)} %copy.49), calls=%async_computation.1 | async-start | bytes 4194304 | tf_op jit(solution)/shard_map/all_to_all | solution.py:130
  57.8 95.6 %all-gather.2.cloned.1.call-start = ((), (), s32[]{:S(2)}) async-start(), calls=%async_computation.3 | async-start | bytes 3145728 | tf_op jit(solution)/shard_map/all_gather | solution.py:138
  118.3 1.6 copy-start.1
  121.0 57.4 %reduce-scatter.2.cloned.1.call-start = ((), (), s32[]{:S(2)}) async-start(), calls=%async_computation.4 | async-start | bytes 655360 | tf_op jit(solution)/shard_map/reduce_scatter | solution.py:101
  156.6 40.3 %all-reduce.2.cloned.1.call-start = ((), (), s32[]{:S(2)}) async-start(), calls=%async_computation.5 | async-start | bytes 262144 | tf_op jit(solution)/shard_map/psum | solution.py:102
Sparse Core Ops, SparseCore 0:
  121.1 32.2 all-gather.1
  156.7 21.6 reduce-scatter.1
  180.7 16.1 all-reduce.1
where the time goes:
time: 205 us
  waiting for transfers between devices  118 us (58%)
  local copies, waits for them, and re-layouts  28.8 us (14%)
  matrix products  21.3 us (10%)
  between operations  13.4 us (7%)
  other arithmetic  12.8 us (6%)
  starting transfers between devices  10.4 us (5%)
    all_to_all x1, waiting for transfers between devices, body(): lax.all_to_all(twisted, 'tm', split_axis=1, concat_axis=2, tiled=True)  46.7 us
    all_gather x1, waiting for transfers between devices, body(): lax.all_gather(spectra, 'panel', axis=2, tiled=True)  26.1 us
    reduce_scatter x1, waiting for transfers between devices, settle(): lax.psum_scatter(partial_value, 'tm', scatter_dimension=sum_dim, tiled=True)  21.8 us
    psum x1, waiting for transfers between devices, settle(): return lax.psum(summed, 'comp')  18.5 us
    dot_general x10, matrix products, precise_dot(): jnp.dot(left_side, right_side, precision=lax.Precision.HIGHEST, preferred...  13.8 us
    slice x1, local copies, waits for them, and re-layouts, synthesize(): longit = angles[1]  10.4 us
    another operation x1, other arithmetic  6.55 us
    all_to_all x1, starting transfers between devices, body(): lax.all_to_all(packed, 'tm', split_axis=2, concat_axis=1, tiled=True)  6.45 us
  transfers between devices with their start and end apart: 5, of which 5 were waited for; matrix products, arithmetic and copies ran while one was open for 3% of the time, Pallas kernels for 0%

commit v1 on v0

--- a/solution.py
+++ b/solution.py
@@ -91,28 +91,45 @@
     return (real_part.astype(jnp.bfloat16), imag_part.astype(jnp.bfloat16))
 
 
-def noise_weighted(spectra, psd_row, frequency, samples):
-    folded = jnp.minimum(frequency, samples - frequency)
-    inverse_psd = 8192.0 / jnp.take(psd_row, folded).astype(jnp.float32)
-    return (spectra.astype(jnp.float32) * inverse_psd[None, :, None]).astype(jnp.bfloat16)
+def inverse_weights(psd_row, position, devices_tm, epochs, samples):
+    half = samples // 2
+    mirrored = jnp.concatenate([psd_row[: half + 1], psd_row[1:half][::-1]])
+    picked = lax.dynamic_slice_in_dim(mirrored.reshape(epochs, devices_tm), position, 1, axis=1)
+    return 8192.0 / picked[:, 0].astype(jnp.float32)
 
 
-def settle(partial_value, sum_dim):
-    summed = lax.psum_scatter(partial_value, "tm", scatter_dimension=sum_dim, tiled=True)
-    return lax.psum(summed, "comp")
+def panel_spectra(spectra):
+    panels = lax.axis_size("panel")
+    blocks = [spectra]
+    for shift in range(1, panels):
+        pairs = [(src, (src + shift) % panels) for src in range(panels)]
+        blocks.append(lax.ppermute(spectra, "panel", pairs))
+    return blocks
+
+
+def comp_sum(value):
+    comps = lax.axis_size("comp")
+    if comps == 1:
+        return value
+    if comps != 2:
+        return lax.psum(value, "comp")
+    other = lax.ppermute(value, "comp", [(0, 1), (1, 0)])
+    return value + other
 
 
 def body(orbit_angles, gap_mask, column_index, lat_coeffs, psd_table):
     devices_tm = lax.axis_size("tm")
+    panels = lax.axis_size("panel")
     epochs = orbit_angles.shape[1]
     block_len = epochs // devices_tm
     samples = epochs * devices_tm
     columns = lat_coeffs.shape[2]
     coeffs = lat_coeffs[0]
     keep_rows = gap_mask.astype(jnp.float32)
-    packed = jnp.concatenate([orbit_angles, keep_rows[None]], axis=0)[:, None, :]
-    received = lax.all_to_all(packed, "tm", split_axis=2, concat_axis=1, tiled=True)
-    flat_orbit = received.reshape(3, devices_tm * block_len)
+    packed = jnp.concatenate([orbit_angles, keep_rows[None]], axis=0)
+    packed = packed.reshape(3, devices_tm, block_len).transpose(1, 0, 2)
+    received = lax.all_to_all(packed, "tm", 0, 0, tiled=True)
+    flat_orbit = received.transpose(1, 0, 2).reshape(3, devices_tm * block_len)
     spread = synthesize(flat_orbit[0:2], flat_orbit[2], column_index, coeffs).reshape(
         devices_tm, block_len, columns
     )
@@ -125,22 +142,27 @@
     real_part, imag_part = rotate(
         real_part, imag_part, jnp.arange(devices_tm, dtype=jnp.int32), local_epoch, samples
     )
-    twisted = jnp.stack([real_part, imag_part])
-    spec_real, spec_imag = local_transform(
-        lax.all_to_all(twisted, "tm", split_axis=1, concat_axis=2, tiled=True), samples
+    twisted = jnp.stack([real_part, imag_part], axis=1)
+    gathered = lax.all_to_all(twisted, "tm", 0, 0, tiled=True)
+    gathered = gathered.transpose(1, 0, 2, 3).reshape(2, devices_tm * block_len, columns)
+    real_part, imag_part = four_step(gathered[0], gathered[1], samples)
+    spectra = jnp.stack([real_part.astype(jnp.bfloat16), imag_part.astype(jnp.bfloat16)])
+    inverse_psd = inverse_weights(psd_table[0], position, devices_tm, epochs, samples)
+    weighted = (spectra.astype(jnp.float32) * inverse_psd[None, :, None]).astype(jnp.bfloat16)
+    contract = (((0, 1), (0, 1)), ((), ()))
+    products = [
+        lax.dot_general(block, weighted, contract, preferred_element_type=jnp.float32)
+        for block in panel_spectra(spectra)
+    ]
+    by_shift = jnp.stack(products)
+    panel = lax.axis_index("panel")
+    order = (panel - jnp.arange(panels, dtype=jnp.int32)) % panels
+    partial_value = jnp.take(by_shift, order, axis=0).reshape(panels * columns, columns)
+    rows = partial_value.shape[0] // devices_tm
+    pieces = lax.all_to_all(
+        partial_value.reshape(devices_tm, rows, columns), "tm", 0, 0, tiled=True
     )
-    spectra = jnp.stack([spec_real, spec_imag])
-    psd_row = psd_table[0]
-    contract = (((0, 1), (0, 1)), ((), ()))
-    frequency = position + devices_tm * jnp.arange(epochs, dtype=jnp.int32)
-    weighted = noise_weighted(spectra, psd_row, frequency, samples)
-    partial_value = lax.dot_general(
-        lax.all_gather(spectra, "panel", axis=2, tiled=True),
-        weighted,
-        contract,
-        preferred_element_type=jnp.float32,
-    )
-    return settle(partial_value, 0)
+    return comp_sum(jnp.sum(pieces, axis=0))
 
 
 def solution(mesh):

time: 205 us -> 144 us (0.70)
  waiting for transfers between devices: 118 us -> 71.9 us
  local copies, waits for them, and re-layouts: 28.8 us -> 9.72 us
  blocking collectives: 0 us -> 15.5 us
  between operations: 13.4 us -> 0.33 us
    all_gather x1 -> x0, waiting for transfers between devices: 26.1 us -> none  [body(): lax.all_gather(spectra, 'panel', axis=2, tiled=True)]
    ppermute x0 -> x2, waiting for transfers between devices: none -> 22.1 us  [the longest x1 20.8 us: panel_spectra(): blocks.append(lax.ppermute(spectra, 'panel', pairs))]
    reduce_scatter x1 -> x0, waiting for transfers between devices: 21.8 us -> none  [settle(): lax.psum_scatter(partial_value, 'tm', scatter_dimension=sum_dim, tiled=True)]
    psum x1 -> x0, waiting for transfers between devices: 18.5 us -> none  [settle(): return lax.psum(summed, 'comp')]
    all_to_all x0 -> x1, blocking collectives: none -> 15.5 us  [body(): lax.all_to_all(partial_value.reshape(devices_tm, rows, columns), 'tm', 0,...]
    slice x1, local copies, waits for them, and re-layouts: 10.4 us -> 0.01 us  [synthesize(): longit = angles[1]]
    gather x1, local copies, waits for them, and re-layouts: 6.15 us -> 0.58 us  [body(): jnp.take(by_shift, order, axis=0).reshape(panels * columns, columns)]
    unnamed x14 -> x8, local copies, waits for them, and re-layouts: 5.05 us -> 1.39 us
  transfers between devices with their start and end apart: 5 -> 4, of which waited for: 5 -> 4; matrix products, arithmetic and copies ran while one was open for 3% -> 3% of each run, Pallas kernels for 0% -> 0%
where the time goes in v1:
time: 144 us; the launch traced here: 143 us
  waiting for transfers between devices  71.9 us (50%)
  matrix products  21 us (15%)
  blocking collectives  15.5 us (11%)
  other arithmetic  12.9 us (9%)
  starting transfers between devices  11.7 us (8%)
  local copies, waits for them, and re-layouts  9.72 us (7%)
    all_to_all x1, waiting for transfers between devices, body(): gathered = lax.all_to_all(twisted, 'tm', 0, 0, tiled=True)  46.8 us
    ppermute x1, waiting for transfers between devices, panel_spectra(): blocks.append(lax.ppermute(spectra, 'panel', pairs))  20.8 us
    all_to_all x1, blocking collectives, body(): lax.all_to_all(partial_value.reshape(devices_tm, rows, columns), 'tm', 0,...  15.5 us
    dot_general x10, matrix products, precise_dot(): jnp.dot(left_side, right_side, precision=lax.Precision.HIGHEST, preferred...  13.5 us
    another operation x1, other arithmetic  6.37 us
    all_to_all x1, starting transfers between devices, body(): received = lax.all_to_all(packed, 'tm', 0, 0, tiled=True)  6.32 us
    dot_general x1, matrix products, synthesize(): latitude = jnp.dot(basis_rows, masked, preferred_element_type=jnp.float32)  5.36 us
    all_to_all x1, starting transfers between devices, body(): gathered = lax.all_to_all(twisted, 'tm', 0, 0, tiled=True)  3.79 us
  transfers between devices with their start and end apart: 4, of which 4 were waited for; matrix products, arithmetic and copies ran while one was open for 3% of the time, Pallas kernels for 0%

profile of v1, /device:TPU:0, one launch (start us, length us, event | category | flops | bytes accessed | tf_op | source)
XLA Modules:
  0.0 143.1 jit_solution(8208062323566944856)
XLA Ops:
  0.7 1.3 maximum_bitcast_fusion
  2.0 6.3 %all-to-all-start = ((f32[4,3,256]{2,1,0:T(4,128)}), f32[4,3,256]{2,1,0:T(4,128)S(1)}, u32[]{:S(2)}, u32[]{:S(2)}) async-start(f32[4,3,256]{2,1,0:T(4,128)} %maximum_bitcast_fusion), calls=%async_computation | async-start | bytes 32768 | tf_op jit(solution)/shard_map/all_to_all | solution.py:131
  10.9 3.1 %all-to-all-done = f32[4,3,256]{2,1,0:T(4,128)S(1)} async-done(((f32[4,3,256]{2,1,0:T(4,128)}), f32[4,3,256]{2,1,0:T(4,128)S(1)}, u32[]{:S(2)}, u32[]{:S(2)}) %all-to-all-start) | async-done | bytes 12320 | tf_op jit(solution)/shard_map/all_to_all | solution.py:131
  13.9 6.4 %cosine_convert_fusion = (bf16[1024,320]{1,0:T(8,128)(2,1)S(1)}, bf16[1024,320]{1,0:T(8,128)(2,1)S(1)}) fusion(f32[1024]{0:T(1024)S(1)} %bitcast.98), kind=kLoop, calls=%fused_computation.12 | loop fusion | flops 983040 | bytes 1314816 | tf_op jit(solution)/shard_map/convert
  20.3 5.4 %fusion.6 = f32[1024,256]{1,0:T(8,128)S(1)} fusion(bf16[1024,320]{1,0:T(8,128)(2,1)S(1)} %get-tuple-element.15, bf16[1024,320]{1,0:T(8,128)(2,1)S(1)} %get-tuple-element.14, f32[256]{0:T(256)S(1)} %bitcast.103, f32[1024]{0:T(1024)S(1)} %bitcast.102, f32[256]{0:T(256)S(1)} %bitcast.105, f32[1024]{0:T(1024)S(1)} %bitcast.101, ...), kind=kOutput, calls=%fused_computation.20 | convolution fusion | flops 339804160 | bytes 2701056 | tf_op jit(solution)/shard_map/dot_general | solution.py:23
  26.2 1.9 %convolution_negate_fusion = f32[4,256,256]{2,0,1:T(4,128)S(1)} fusion(f32[256,256,4]{1,2,0:T(4,128)S(1)} %bitcast.84), kind=kOutput, calls=%fused_computation.18 | convolution fusion | flops 12845280 | bytes 2097152 | tf_op jit(solution)/shard_map/dot_general | solution.py:50
  28.1 2.7 %add_bitcast_fusion = (f32[4,1,256,256]{3,0,2,1:T(4,128)S(1)}, f32[4,1,256,256]{3,0,2,1:T(4,128)S(1)}) fusion(f32[4,256,256]{2,0,1:T(4,128)S(1)} %convolution_negate_fusion, f32[4,256]{0,1:T(8,128)S(1)} %copy.30, f32[4,256]{0,1:T(8,128)S(1)} %copy.29, f32[256,256,4]{1,2,0:T(4,128)S(1)} %bitcast.85), kind=kOutput, calls=%fused_computation.37 | convolution fusion | flops 14156000 | bytes 4202496 | tf_op jit(solution)/shard_map/dot_general | solution.py:50
  31.3 1.7 %copy.31 = f32[4,2,256,256]{3,2,1,0:T(8,128)} copy(f32[4,2,256,256]{3,0,2,1:T(4,128)S(1)} %pad_maximum_fusion) | data formatting | bytes 4194304 | tf_op jit(solution)/shard_map/stack | solution.py:145
  33.0 3.8 %all-to-all-start.1 = ((f32[4,2,256,256]{3,2,1,0:T(8,128)}), f32[4,2,256,256]{3,2,1,0:T(8,128)S(1)}, u32[]{:S(2)}, u32[]{:S(2)}) async-start(f32[4,2,256,256]{3,2,1,0:T(8,128)} %copy.31), calls=%async_computation.1 | async-start | bytes 4194304 | tf_op jit(solution)/shard_map/all_to_all | solution.py:146
  36.8 46.8 %all-to-all-done.1 = f32[4,2,256,256]{3,2,1,0:T(8,128)S(1)} async-done(((f32[4,2,256,256]{3,2,1,0:T(8,128)}), f32[4,2,256,256]{3,2,1,0:T(8,128)S(1)}, u32[]{:S(2)}, u32[]{:S(2)}) %all-to-all-start.1) | async-done | bytes 2097184 | tf_op jit(solution)/shard_map/all_to_all | solution.py:146
  83.6 1.2 fusion.121
  85.0 1.2 fusion.32
  86.1 1.4 reshape_squeeze.7
  87.6 1.2 fusion.30
  88.7 1.2 convolution_add_fusion.1
  89.9 1.2 convolution_subtract_fusion.1
  92.1 1.0 fusion.59
  94.8 1.1 fusion.2
  97.1 1.1 fusion.3
  98.8 1.6 %collective-permute-start = (bf16[2,1024,256]{1,2,0:T(8,128)(2,1)S(1)}, bf16[2,1024,256]{1,2,0:T(8,128)(2,1)}, u32[]{:S(2)}, u32[]{:S(2)}) collective-permute-start(bf16[2,1024,256]{1,2,0:T(8,128)(2,1)S(1)} %pad_maximum_fusion.1), channel_id=1, source_target_pairs={{0,1},{1,0},{2,3},{3,2},{4,5},{5,4},{6,7},{7,6},{8,9},{9,8},{10,11... | collective-permute-start | bytes 3145736 | tf_op jit(solution)/shard_map/ppermute | solution.py:106
  102.3 20.8 %collective-permute-done = bf16[2,1024,256]{1,2,0:T(8,128)(2,1)} collective-permute-done((bf16[2,1024,256]{1,2,0:T(8,128)(2,1)S(1)}, bf16[2,1024,256]{1,2,0:T(8,128)(2,1)}, u32[]{:S(2)}, u32[]{:S(2)}) %collective-permute-start) | collective-permute-done | bytes 1048608 | tf_op jit(solution)/shard_map/ppermute | solution.py:106
  123.1 1.7 %fusion.11 = f32[1,256,256]{2,1,0:T(8,128)S(1)} fusion(bf16[2,1024,256]{1,2,0:T(8,128)(2,1)} %collective-permute-done, f32[1024]{0:T(1024)S(1)} %fusion.17, bf16[1,1024,256]{1,2,0:T(8,128)(2,1)S(1)} %copy.37, bf16[1,1024,256]{1,2,0:T(8,128)(2,1)S(1)} %copy-done), kind=kOutput, calls=%fused_computation.25 | convolution fusion | flops 270532608 | bytes 2363392 | tf_op jit(solution)/shard_map/dot_general | solution.py:154
  125.5 15.5 %all_to_all.15 = f32[4,128,256]{2,1,0:T(8,128)S(1)} all-to-all(f32[4,128,256]{2,1,0:T(8,128)S(1)} %broadcast_select_fusion), channel_id=1, replica_groups=mesh['groups'=2,'tm'=4,'comp'=2,'panel'=2] {'tm'}, dimensions={0} | all-to-all | bytes 1048576 | tf_op jit(solution)/shard_map/all_to_all | solution.py:162
  141.1 1.3 collective-permute-done.1
  (46 shorter events, 12.3 us)
Async XLA Ops:
  2.0 11.9 %all-to-all-start = ((f32[4,3,256]{2,1,0:T(4,128)}), f32[4,3,256]{2,1,0:T(4,128)S(1)}, u32[]{:S(2)}, u32[]{:S(2)}) async-start(f32[4,3,256]{2,1,0:T(4,128)} %maximum_bitcast_fusion), calls=%async_computation | async-start | bytes 32768 | tf_op jit(solution)/shard_map/all_to_all | solution.py:131
  33.0 50.6 %all-to-all-start.1 = ((f32[4,2,256,256]{3,2,1,0:T(8,128)}), f32[4,2,256,256]{3,2,1,0:T(8,128)S(1)}, u32[]{:S(2)}, u32[]{:S(2)}) async-start(f32[4,2,256,256]{3,2,1,0:T(8,128)} %copy.31), calls=%async_computation.1 | async-start | bytes 4194304 | tf_op jit(solution)/shard_map/all_to_all | solution.py:146
  97.1 1.5 %copy-start = (bf16[1,1024,256]{1,2,0:T(8,128)(2,1)S(1)}, bf16[1,1024,256]{1,2,0:T(8,128)(2,1)}, u32[]{:S(2)}) copy-start(bf16[1,1024,256]{1,2,0:T(8,128)(2,1)} %copy.36) | copy-start | bytes 1572868
  98.2 2.2 %copy-start.1 = (s32[1,2049]{1,0:T(1,128)S(1)}, s32[1,2049]{1,0:T(1,128)}, u32[]{:S(2)}) copy-start(s32[1,2049]{1,0:T(1,128)} %param.9) | copy-start | bytes 24592
  98.8 24.3 %collective-permute-start = (bf16[2,1024,256]{1,2,0:T(8,128)(2,1)S(1)}, bf16[2,1024,256]{1,2,0:T(8,128)(2,1)}, u32[]{:S(2)}, u32[]{:S(2)}) collective-permute-start(bf16[2,1024,256]{1,2,0:T(8,128)(2,1)S(1)} %pad_maximum_fusion.1), channel_id=1, source_target_pairs={{0,1},{1,0},{2,3},{3,2},{4,5},{5,4},{6,7},{7,6},{8,9},{9,8},{10,11... | collective-permute-start | bytes 3145736 | tf_op jit(solution)/shard_map/ppermute | solution.py:106
  141.0 1.4 collective-permute-start.1

commit v2 on v1

--- a/solution.py
+++ b/solution.py
@@ -6,6 +6,7 @@
 from jax.sharding import PartitionSpec as P
 
 SPLIT = 64
+CHUNKS = 2
 
 
 def synthesize(angles, keep_rows, column_index, coeffs):
@@ -117,6 +118,28 @@
     return value + other
 
 
+def chunk_spectra(flat_orbit, column_index, coeffs, position, samples):
+    devices_tm = lax.axis_size("tm")
+    block_len = flat_orbit.shape[1] // devices_tm
+    columns = coeffs.shape[1]
+    spread = synthesize(flat_orbit[0:2], flat_orbit[2], column_index, coeffs).reshape(
+        devices_tm, block_len, columns
+    )
+    local_epoch = position * block_len + jnp.arange(block_len, dtype=jnp.int32)
+    cos_outer, sin_outer = dft_tables(devices_tm)
+    flat_design = spread.reshape(devices_tm, block_len * columns)
+    real_part = precise_dot(cos_outer, flat_design).reshape(devices_tm, block_len, columns)
+    imag_part = -precise_dot(sin_outer, flat_design).reshape(devices_tm, block_len, columns)
+    real_part, imag_part = rotate(
+        real_part, imag_part, jnp.arange(devices_tm, dtype=jnp.int32), local_epoch, samples
+    )
+    twisted = jnp.stack([real_part, imag_part], axis=1)
+    gathered = lax.all_to_all(twisted, "tm", 0, 0, tiled=True)
+    gathered = gathered.transpose(1, 0, 2, 3).reshape(2, devices_tm * block_len, columns)
+    real_part, imag_part = four_step(gathered[0], gathered[1], samples)
+    return jnp.stack([real_part.astype(jnp.bfloat16), imag_part.astype(jnp.bfloat16)])
+
+
 def body(orbit_angles, gap_mask, column_index, lat_coeffs, psd_table):
     devices_tm = lax.axis_size("tm")
     panels = lax.axis_size("panel")
@@ -130,31 +153,40 @@
     packed = packed.reshape(3, devices_tm, block_len).transpose(1, 0, 2)
     received = lax.all_to_all(packed, "tm", 0, 0, tiled=True)
     flat_orbit = received.transpose(1, 0, 2).reshape(3, devices_tm * block_len)
-    spread = synthesize(flat_orbit[0:2], flat_orbit[2], column_index, coeffs).reshape(
-        devices_tm, block_len, columns
-    )
     position = lax.axis_index("tm")
-    local_epoch = position * block_len + jnp.arange(block_len, dtype=jnp.int32)
-    cos_outer, sin_outer = dft_tables(devices_tm)
-    flat_design = spread.reshape(devices_tm, block_len * columns)
-    real_part = precise_dot(cos_outer, flat_design).reshape(devices_tm, block_len, columns)
-    imag_part = -precise_dot(sin_outer, flat_design).reshape(devices_tm, block_len, columns)
-    real_part, imag_part = rotate(
-        real_part, imag_part, jnp.arange(devices_tm, dtype=jnp.int32), local_epoch, samples
-    )
-    twisted = jnp.stack([real_part, imag_part], axis=1)
-    gathered = lax.all_to_all(twisted, "tm", 0, 0, tiled=True)
-    gathered = gathered.transpose(1, 0, 2, 3).reshape(2, devices_tm * block_len, columns)
-    real_part, imag_part = four_step(gathered[0], gathered[1], samples)
-    spectra = jnp.stack([real_part.astype(jnp.bfloat16), imag_part.astype(jnp.bfloat16)])
     inverse_psd = inverse_weights(psd_table[0], position, devices_tm, epochs, samples)
-    weighted = (spectra.astype(jnp.float32) * inverse_psd[None, :, None]).astype(jnp.bfloat16)
+    chunks = CHUNKS if columns % (CHUNKS * 64) == 0 else 1
+    width = columns // chunks
+    spectra_parts = []
+    moved_parts = []
+    weighted_parts = []
+    for chunk in range(chunks):
+        cols = slice(chunk * width, (chunk + 1) * width)
+        spectra = chunk_spectra(
+            flat_orbit, column_index[:, cols], coeffs[:, cols], position, samples
+        )
+        weighted_parts.append(
+            (spectra.astype(jnp.float32) * inverse_psd[None, :, None]).astype(jnp.bfloat16)
+        )
+        spectra_parts.append(spectra)
+        moved_parts.append(panel_spectra(spectra))
+    weighted = jnp.concatenate(weighted_parts, axis=2)
     contract = (((0, 1), (0, 1)), ((), ()))
-    products = [
-        lax.dot_general(block, weighted, contract, preferred_element_type=jnp.float32)
-        for block in panel_spectra(spectra)
-    ]
-    by_shift = jnp.stack(products)
+    by_shift = jnp.stack(
+        [
+            jnp.concatenate(
+                [
+                    lax.dot_general(
+                        moved_parts[chunk][shift], weighted, contract,
+                        preferred_element_type=jnp.float32,
+                    )
+                    for chunk in range(chunks)
+                ],
+                axis=0,
+            )
+            for shift in range(panels)
+        ]
+    )
     panel = lax.axis_index("panel")
     order = (panel - jnp.arange(panels, dtype=jnp.int32)) % panels
     partial_value = jnp.take(by_shift, order, axis=0).reshape(panels * columns, columns)

time: 144 us -> 145 us (level)
  matrix products: 21 us -> 25.3 us
  waiting for transfers between devices: 71.9 us -> 67.7 us
  starting transfers between devices: 11.7 us -> 15.9 us
  local copies, waits for them, and re-layouts: 9.72 us -> 6.79 us
    dot_general x10 -> x20, matrix products: 13.5 us -> 18.4 us  [precise_dot(): jnp.dot(left_side, right_side, precision=lax.Precision.HIGHEST, preferred...]
    all_to_all x1 -> x2, waiting for transfers between devices: 46.8 us -> 42.7 us  [chunk_spectra(): gathered = lax.all_to_all(twisted, 'tm', 0, 0, tiled=True)]
    all_to_all x1 -> x2, starting transfers between devices: 3.79 us -> 7.34 us  [chunk_spectra(): gathered = lax.all_to_all(twisted, 'tm', 0, 0, tiled=True)]
    another operation x2 -> x6, local copies, waits for them, and re-layouts: 2.23 us -> 3.67 us  [the longest x2 2.1 us: chunk_spectra(): twisted = jnp.stack([real_part, imag_part], axis=1)]
    dot_general x1 -> x2, matrix products: 5.36 us -> 5.54 us  [synthesize(): latitude = jnp.dot(basis_rows, masked, preferred_element_type=jnp.float32)]
    ppermute x1 -> x2, waiting for transfers between devices: 20.8 us -> 20.6 us  [panel_spectra(): blocks.append(lax.ppermute(spectra, 'panel', pairs))]
    another operation x4 -> x6, other arithmetic: 6.95 us -> 6.9 us
  transfers between devices with their start and end apart: 4 -> 6, of which waited for: 4 -> 6; matrix products, arithmetic and copies ran while one was open for 3% -> 7% of each run, Pallas kernels for 0% -> 0%
where the time goes in v2:
time: 145 us
  waiting for transfers between devices  67.7 us (47%)
  matrix products  25.3 us (17%)
  starting transfers between devices  15.9 us (11%)
  blocking collectives  15.4 us (11%)
  other arithmetic  13.2 us (9%)
  local copies, waits for them, and re-layouts  6.79 us (5%)
    all_to_all x2, waiting for transfers between devices, chunk_spectra(): gathered = lax.all_to_all(twisted, 'tm', 0, 0, tiled=True)  42.7 us
    ppermute x2, waiting for transfers between devices, panel_spectra(): blocks.append(lax.ppermute(spectra, 'panel', pairs))  20.6 us
    dot_general x20, matrix products, precise_dot(): jnp.dot(left_side, right_side, precision=lax.Precision.HIGHEST, preferred...  18.4 us
    all_to_all x1, blocking collectives, body(): lax.all_to_all(partial_value.reshape(devices_tm, rows, columns), 'tm', 0,...  15.4 us
    all_to_all x2, starting transfers between devices, chunk_spectra(): gathered = lax.all_to_all(twisted, 'tm', 0, 0, tiled=True)  7.34 us
    another operation x1, other arithmetic  6.37 us
    all_to_all x1, starting transfers between devices, body(): received = lax.all_to_all(packed, 'tm', 0, 0, tiled=True)  6.32 us
    dot_general x2, matrix products, synthesize(): latitude = jnp.dot(basis_rows, masked, preferred_element_type=jnp.float32)  5.54 us
  transfers between devices with their start and end apart: 6, of which 6 were waited for; matrix products, arithmetic and copies ran while one was open for 7% of the time, Pallas kernels for 0%

profile of v2, /device:TPU:0, one launch (start us, length us, event | category | flops | bytes accessed | tf_op | source)
XLA Modules:
  0.0 144.9 jit_solution(7419951226843597445)
XLA Ops:
  0.7 1.3 maximum_bitcast_fusion.2
  2.1 6.3 %all-to-all-start = ((f32[4,3,256]{2,1,0:T(4,128)}), f32[4,3,256]{2,1,0:T(4,128)S(1)}, u32[]{:S(2)}, u32[]{:S(2)}) async-start(f32[4,3,256]{2,1,0:T(4,128)} %maximum_bitcast_fusion.2), calls=%async_computation | async-start | bytes 32768 | tf_op jit(solution)/shard_map/all_to_all | solution.py:154
  10.9 3.1 %all-to-all-done = f32[4,3,256]{2,1,0:T(4,128)S(1)} async-done(((f32[4,3,256]{2,1,0:T(4,128)}), f32[4,3,256]{2,1,0:T(4,128)S(1)}, u32[]{:S(2)}, u32[]{:S(2)}) %all-to-all-start) | async-done | bytes 12320 | tf_op jit(solution)/shard_map/all_to_all | solution.py:154
  14.0 6.4 %cosine_convert_fusion = (bf16[1024,320]{1,0:T(8,128)(2,1)S(1)}, bf16[1024,320]{1,0:T(8,128)(2,1)S(1)}) fusion(f32[1024]{0:T(1024)S(1)} %bitcast.185), kind=kLoop, calls=%fused_computation.18 | loop fusion | flops 983040 | bytes 1314816 | tf_op jit(solution)/shard_map/convert
  20.4 2.4 %fusion.9 = f32[1024,128]{1,0:T(8,128)S(1)} fusion(bf16[1024,320]{1,0:T(8,128)(2,1)S(1)} %get-tuple-element.27, bf16[1024,320]{1,0:T(8,128)(2,1)S(1)} %get-tuple-element.26, f32[128]{0:T(128)S(1)} %get-tuple-element.35, f32[128]{0:T(128)S(1)} %get-tuple-element.30, f32[1024]{0:T(1024)S(1)} %bitcast.190, f32[1024]{0:T(1024)S(1)} %bitcast.188, ...), kind=kOutput, calls=%fused_computation.24 | convolution fusion | flops 171212800 | bytes 2275328 | tf_op jit(solution)/shard_map/dot_general | solution.py:24
  23.0 1.0 convolution_negate_fusion
  24.0 1.0 fusion.33
  25.1 3.2 %fusion.8 = f32[1024,128]{1,0:T(8,128)} fusion(bf16[1024,320]{1,0:T(8,128)(2,1)S(1)} %get-tuple-element.27, bf16[1024,320]{1,0:T(8,128)(2,1)S(1)} %get-tuple-element.26, f32[128]{0:T(128)S(1)} %get-tuple-element.34, f32[1024]{0:T(1024)S(1)} %bitcast.191, f32[128]{0:T(128)S(1)} %get-tuple-element.29, f32[1024]{0:T(1024)S(1)} %bitcast.189, ...), kind=kOutput, calls=%fused_computation.23 | convolution fusion | flops 171212800 | bytes 2275328 | tf_op jit(solution)/shard_map/dot_general | solution.py:24
  28.3 1.3 reshape_reshape.7
  29.5 1.0 convolution_negate_fusion.1
  30.6 1.7 %add_bitcast_fusion.1 = (f32[4,1,256,128]{3,0,2,1:T(4,128)S(1)}, f32[4,1,256,128]{3,0,2,1:T(4,128)S(1)}, f32[4,1,256,128]{3,0,2,1:T(4,128)S(1)}, f32[4,1,256,128]{3,0,2,1:T(4,128)S(1)}) fusion(f32[4,256,128]{2,0,1:T(4,128)S(1)} %convolution_negate_fusion.1, f32[4,256]{0,1:T(8,128)S(1)} %copy.41, f32[4,256]{0,1:T(8,128)S(1)} %copy.40, ...), kind=kOutput, calls=%fused_computation.81 | convolution fusion | flops 7864544 | bytes 4202496 | tf_op jit(solution)/shard_map/dot_general | solution.py:51
  32.5 1.1 copy.47
  33.5 3.6 %all-to-all-start.2 = ((f32[4,2,256,128]{3,2,1,0:T(8,128)}), f32[4,2,256,128]{3,2,1,0:T(8,128)S(1)}, u32[]{:S(2)}, u32[]{:S(2)}) async-start(f32[4,2,256,128]{3,2,1,0:T(8,128)} %copy.47), calls=%async_computation.2 | async-start | bytes 2097152 | tf_op jit(solution)/shard_map/all_to_all | solution.py:137
  37.7 1.0 copy.42
  38.8 23.0 %all-to-all-done.2 = f32[4,2,256,128]{3,2,1,0:T(8,128)S(1)} async-done(((f32[4,2,256,128]{3,2,1,0:T(8,128)}), f32[4,2,256,128]{3,2,1,0:T(8,128)S(1)}, u32[]{:S(2)}, u32[]{:S(2)}) %all-to-all-start.2) | async-done | bytes 1048608 | tf_op jit(solution)/shard_map/all_to_all | solution.py:137
  61.7 3.7 %all-to-all-start.1 = ((f32[4,2,256,128]{3,2,1,0:T(8,128)}), f32[4,2,256,128]{3,2,1,0:T(8,128)S(1)}, u32[]{:S(2)}, u32[]{:S(2)}) async-start(f32[4,2,256,128]{3,2,1,0:T(8,128)} %copy.42), calls=%async_computation.1 | async-start | bytes 2097152 | tf_op jit(solution)/shard_map/all_to_all | solution.py:137
  69.1 1.6 %fusion.13 = f32[8,16,8,128]{3,2,1,0:T(8,128)} fusion(f32[64,2048]{1,0:T(8,128)S(1)} %fusion.63, f32[64,2048]{1,0:T(8,128)S(1)} %reshape_squeeze.14), kind=kOutput, calls=%fused_computation.30 | convolution fusion | flops 100851712 | bytes 1572864 | tf_op jit(solution)/shard_map/dot_general | solution.py:51
  70.7 19.7 %all-to-all-done.1 = f32[4,2,256,128]{3,2,1,0:T(8,128)S(1)} async-done(((f32[4,2,256,128]{3,2,1,0:T(8,128)}), f32[4,2,256,128]{3,2,1,0:T(8,128)S(1)}, u32[]{:S(2)}, u32[]{:S(2)}) %all-to-all-start.1) | async-done | bytes 1048608 | tf_op jit(solution)/shard_map/all_to_all | solution.py:137
  98.9 1.1 fusion.20
  102.0 1.6 %collective-permute-start = (bf16[2,1024,128]{2,1,0:T(8,128)(2,1)S(1)}, bf16[2,1024,128]{2,1,0:T(8,128)(2,1)S(1)}, u32[]{:S(2)}, u32[]{:S(2)}) collective-permute-start(bf16[2,1024,128]{2,1,0:T(8,128)(2,1)S(1)} %constant_dynamic-update-slice_fusion), channel_id=1, source_target_pairs={{0,1},{1,0},{2,3},{3,2},{4,5},{5,4},{6,7},{7,6},{8,9},{9,8},{10,11... | collective-permute-start | bytes 1572872 | tf_op jit(solution)/shard_map/ppermute | solution.py:107
  105.2 11.7 %collective-permute-done = bf16[2,1024,128]{2,1,0:T(8,128)(2,1)S(1)} collective-permute-done((bf16[2,1024,128]{2,1,0:T(8,128)(2,1)S(1)}, bf16[2,1024,128]{2,1,0:T(8,128)(2,1)S(1)}, u32[]{:S(2)}, u32[]{:S(2)}) %collective-permute-start) | collective-permute-done | bytes 524320 | tf_op jit(solution)/shard_map/ppermute | solution.py:107
  117.3 8.9 %collective-permute-done.1 = bf16[2,1024,128]{2,1,0:T(8,128)(2,1)S(1)} collective-permute-done((bf16[2,1024,128]{2,1,0:T(8,128)(2,1)S(1)}, bf16[2,1024,128]{2,1,0:T(8,128)(2,1)S(1)}, u32[]{:S(2)}, u32[]{:S(2)}) %collective-permute-start.1) | collective-permute-done | bytes 524320 | tf_op jit(solution)/shard_map/ppermute | solution.py:107
  127.3 15.4 %all_to_all.20 = f32[4,128,256]{2,1,0:T(8,128)S(1)} all-to-all(f32[4,128,256]{2,1,0:T(8,128)S(1)} %broadcast_select_fusion), channel_id=1, replica_groups=mesh['groups'=2,'tm'=4,'comp'=2,'panel'=2] {'tm'}, dimensions={0} | all-to-all | bytes 1048576 | tf_op jit(solution)/shard_map/all_to_all | solution.py:194
  142.9 1.3 collective-permute-done.2
  (77 shorter events, 22.0 us)
Async XLA Ops:
  0.0 20.4 %copy-start.2 = (bf16[1,640,256]{2,1,0:T(8,128)(2,1)S(1)}, bf16[1,640,256]{2,1,0:T(8,128)(2,1)}, u32[]{:S(2)}) copy-start(bf16[1,640,256]{2,1,0:T(8,128)(2,1)} %param.8) | copy-start | bytes 983044
  2.1 11.9 %all-to-all-start = ((f32[4,3,256]{2,1,0:T(4,128)}), f32[4,3,256]{2,1,0:T(4,128)S(1)}, u32[]{:S(2)}, u32[]{:S(2)}) async-start(f32[4,3,256]{2,1,0:T(4,128)} %maximum_bitcast_fusion.2), calls=%async_computation | async-start | bytes 32768 | tf_op jit(solution)/shard_map/all_to_all | solution.py:154
  23.0 2.1 %copy-start.3 = (bf16[1,640,256]{2,1,0:T(8,128)(2,1)S(1)}, bf16[1,640,256]{2,1,0:T(8,128)(2,1)}, u32[]{:S(2)}) copy-start(bf16[1,640,256]{2,1,0:T(8,128)(2,1)} %param.8) | copy-start | bytes 983044
  33.5 3.7 %copy-start.1 = (s32[1,2049]{1,0:T(1,128)S(1)}, s32[1,2049]{1,0:T(1,128)}, u32[]{:S(2)}) copy-start(s32[1,2049]{1,0:T(1,128)} %param.9) | copy-start | bytes 24592
  33.5 28.2 %all-to-all-start.2 = ((f32[4,2,256,128]{3,2,1,0:T(8,128)}), f32[4,2,256,128]{3,2,1,0:T(8,128)S(1)}, u32[]{:S(2)}, u32[]{:S(2)}) async-start(f32[4,2,256,128]{3,2,1,0:T(8,128)} %copy.47), calls=%async_computation.2 | async-start | bytes 2097152 | tf_op jit(solution)/shard_map/all_to_all | solution.py:137
  61.7 28.7 %all-to-all-start.1 = ((f32[4,2,256,128]{3,2,1,0:T(8,128)}), f32[4,2,256,128]{3,2,1,0:T(8,128)S(1)}, u32[]{:S(2)}, u32[]{:S(2)}) async-start(f32[4,2,256,128]{3,2,1,0:T(8,128)} %copy.42), calls=%async_computation.1 | async-start | bytes 2097152 | tf_op jit(solution)/shard_map/all_to_all | solution.py:137
  92.9 1.0 copy-start
  102.0 14.9 %collective-permute-start = (bf16[2,1024,128]{2,1,0:T(8,128)(2,1)S(1)}, bf16[2,1024,128]{2,1,0:T(8,128)(2,1)S(1)}, u32[]{:S(2)}, u32[]{:S(2)}) collective-permute-start(bf16[2,1024,128]{2,1,0:T(8,128)(2,1)S(1)} %constant_dynamic-update-slice_fusion), channel_id=1, source_target_pairs={{0,1},{1,0},{2,3},{3,2},{4,5},{5,4},{6,7},{7,6},{8,9},{9,8},{10,11... | collective-permute-start | bytes 1572872 | tf_op jit(solution)/shard_map/ppermute | solution.py:107
  103.6 22.6 %collective-permute-start.1 = (bf16[2,1024,128]{2,1,0:T(8,128)(2,1)S(1)}, bf16[2,1024,128]{2,1,0:T(8,128)(2,1)S(1)}, u32[]{:S(2)}, u32[]{:S(2)}) collective-permute-start(bf16[2,1024,128]{2,1,0:T(8,128)(2,1)S(1)} %constant_dynamic-update-slice_fusion.2), channel_id=1, source_target_pairs={{0,1},{1,0},{2,3},{3,2},{4,5},{5,4},{6,7},{7,6},{8,9},{9,8},{10,11... | collective-permute-start | bytes 1572872 | tf_op jit(solution)/shard_map/ppermute | solution.py:107
  142.8 1.4 collective-permute-start.2

commit v3 on v1

--- a/solution.py
+++ b/solution.py
@@ -117,6 +117,47 @@
     return value + other
 
 
+def class_partials(spread, position, samples):
+    devices_tm, block_len, columns = spread.shape
+    index = jnp.arange(devices_tm, dtype=jnp.int32)
+    cos_table, sin_table = phase_tables(index, index, devices_tm)
+    real_part = jnp.sum(cos_table[:, :, None, None] * spread[None], axis=1)
+    imag_part = -jnp.sum(sin_table[:, :, None, None] * spread[None], axis=1)
+    local_epoch = position * block_len + jnp.arange(block_len, dtype=jnp.int32)
+    real_part, imag_part = rotate(real_part, imag_part, index, local_epoch, samples)
+    return jnp.stack([real_part, imag_part], axis=1)
+
+
+def class_spectrum(gathered, samples):
+    devices_tm, _, block_len, columns = gathered.shape
+    length = devices_tm * block_len
+    index = jnp.arange(devices_tm, dtype=jnp.int32)
+    cos_table, sin_table = phase_tables(index, index, devices_tm)
+    real_in = gathered[:, 0]
+    imag_in = gathered[:, 1]
+    cos_b = cos_table[:, :, None, None]
+    sin_b = sin_table[:, :, None, None]
+    real_part = jnp.sum(cos_b * real_in[None] + sin_b * imag_in[None], axis=1)
+    imag_part = jnp.sum(cos_b * imag_in[None] - sin_b * real_in[None], axis=1)
+    real_part, imag_part = rotate(
+        real_part, imag_part, index, jnp.arange(block_len, dtype=jnp.int32), length
+    )
+    cos_inner, sin_inner = dft_tables(block_len)
+    dims = (((1,), (1,)), ((), ()))
+
+    def mat(table, value):
+        return lax.dot_general(
+            table, value, dims, precision=lax.Precision.HIGHEST,
+            preferred_element_type=jnp.float32,
+        )
+
+    new_real = mat(cos_inner, real_part) + mat(sin_inner, imag_part)
+    new_imag = mat(cos_inner, imag_part) - mat(sin_inner, real_part)
+    new_real = (new_real.reshape(length, columns) / samples).astype(jnp.bfloat16)
+    new_imag = (new_imag.reshape(length, columns) / samples).astype(jnp.bfloat16)
+    return jnp.stack([new_real, new_imag])
+
+
 def body(orbit_angles, gap_mask, column_index, lat_coeffs, psd_table):
     devices_tm = lax.axis_size("tm")
     panels = lax.axis_size("panel")
@@ -134,19 +175,9 @@
         devices_tm, block_len, columns
     )
     position = lax.axis_index("tm")
-    local_epoch = position * block_len + jnp.arange(block_len, dtype=jnp.int32)
-    cos_outer, sin_outer = dft_tables(devices_tm)
-    flat_design = spread.reshape(devices_tm, block_len * columns)
-    real_part = precise_dot(cos_outer, flat_design).reshape(devices_tm, block_len, columns)
-    imag_part = -precise_dot(sin_outer, flat_design).reshape(devices_tm, block_len, columns)
-    real_part, imag_part = rotate(
-        real_part, imag_part, jnp.arange(devices_tm, dtype=jnp.int32), local_epoch, samples
-    )
-    twisted = jnp.stack([real_part, imag_part], axis=1)
+    twisted = class_partials(spread, position, samples)
     gathered = lax.all_to_all(twisted, "tm", 0, 0, tiled=True)
-    gathered = gathered.transpose(1, 0, 2, 3).reshape(2, devices_tm * block_len, columns)
-    real_part, imag_part = four_step(gathered[0], gathered[1], samples)
-    spectra = jnp.stack([real_part.astype(jnp.bfloat16), imag_part.astype(jnp.bfloat16)])
+    spectra = class_spectrum(gathered, samples)
     inverse_psd = inverse_weights(psd_table[0], position, devices_tm, epochs, samples)
     weighted = (spectra.astype(jnp.float32) * inverse_psd[None, :, None]).astype(jnp.bfloat16)
     contract = (((0, 1), (0, 1)), ((), ()))

time: 144 us -> 141 us (0.979)
  matrix products: 21 us -> 16.4 us
  other arithmetic: 12.9 us -> 14.6 us
    dot_general x10 -> x4, matrix products: 13.5 us -> 8.88 us  [mat(): lax.dot_general(table, value, dims, precision=lax.Precision.HIGHEST, pref...]
    convert_element_type x4 -> x6, local copies, waits for them, and re-layouts: 1.7 us -> 5.97 us  [the longest x3 5.23 us: class_spectrum(): (new_real.reshape(length, columns) / samples).astype(jnp.bfloat16)]
    another operation x4 -> x1, local copies, waits for them, and re-layouts: 3.83 us -> 1.5 us  [class_partials(): return jnp.stack([real_part, imag_part], axis=1)]
    reduce_sum x0 -> x2, other arithmetic: none -> 1.94 us  [the longest x1 1.23 us: class_spectrum(): imag_part = jnp.sum(cos_b * imag_in[None] - sin_b * real_in[None], axis=1)]
where the time goes in v3:
time: 141 us; the launch traced here: 140 us
  waiting for transfers between devices  72.2 us (51%)
  matrix products  16.4 us (12%)
  blocking collectives  15.5 us (11%)
  other arithmetic  14.6 us (10%)
  starting transfers between devices  11.7 us (8%)
  local copies, waits for them, and re-layouts  9.39 us (7%)
    all_to_all x1, waiting for transfers between devices, body(): gathered = lax.all_to_all(twisted, 'tm', 0, 0, tiled=True)  46.8 us
    ppermute x1, waiting for transfers between devices, panel_spectra(): blocks.append(lax.ppermute(spectra, 'panel', pairs))  20.8 us
    all_to_all x1, blocking collectives, body(): lax.all_to_all(partial_value.reshape(devices_tm, rows, columns), 'tm', 0,...  15.5 us
    dot_general x4, matrix products, mat(): lax.dot_general(table, value, dims, precision=lax.Precision.HIGHEST, pref...  8.88 us
    another operation x1, other arithmetic  6.37 us
    all_to_all x1, starting transfers between devices, body(): received = lax.all_to_all(packed, 'tm', 0, 0, tiled=True)  6.32 us
    dot_general x1, matrix products, synthesize(): latitude = jnp.dot(basis_rows, masked, preferred_element_type=jnp.float32)  5.37 us
    convert_element_type x3, local copies, waits for them, and re-layouts, class_spectrum(): (new_real.reshape(length, columns) / samples).astype(jnp.bfloat16)  5.23 us
  transfers between devices with their start and end apart: 4, of which 4 were waited for; matrix products, arithmetic and copies ran while one was open for 3% of the time, Pallas kernels for 0%

profile of v3, /device:TPU:0, one launch (start us, length us, event | category | flops | bytes accessed | tf_op | source)
XLA Modules:
  0.0 140.0 jit_solution(7246428486843861537)
XLA Ops:
  0.7 1.3 maximum_bitcast_fusion
  2.0 6.3 %all-to-all-start = ((f32[4,3,256]{2,1,0:T(4,128)}), f32[4,3,256]{2,1,0:T(4,128)S(1)}, u32[]{:S(2)}, u32[]{:S(2)}) async-start(f32[4,3,256]{2,1,0:T(4,128)} %maximum_bitcast_fusion), calls=%async_computation | async-start | bytes 32768 | tf_op jit(solution)/shard_map/all_to_all | solution.py:172
  8.3 0.8 fusion.80
  9.8 0.7 compare_reduce_fusion
  10.6 3.3 %all-to-all-done = f32[4,3,256]{2,1,0:T(4,128)S(1)} async-done(((f32[4,3,256]{2,1,0:T(4,128)}), f32[4,3,256]{2,1,0:T(4,128)S(1)}, u32[]{:S(2)}, u32[]{:S(2)}) %all-to-all-start) | async-done | bytes 12320 | tf_op jit(solution)/shard_map/all_to_all | solution.py:172
  13.9 6.4 %cosine_convert_fusion = (bf16[1024,320]{1,0:T(8,128)(2,1)S(1)}, bf16[1024,320]{1,0:T(8,128)(2,1)S(1)}) fusion(f32[1024]{0:T(1024)S(1)} %bitcast.61), kind=kLoop, calls=%fused_computation.8 | loop fusion | flops 983040 | bytes 1314816 | tf_op jit(solution)/shard_map/convert
  20.3 5.4 %fusion.2 = f32[1024,256]{1,0:T(8,128)S(1)} fusion(bf16[1024,320]{1,0:T(8,128)(2,1)S(1)} %get-tuple-element.17, bf16[1024,320]{1,0:T(8,128)(2,1)S(1)} %get-tuple-element.16, f32[256]{0:T(256)S(1)} %bitcast.66, f32[1024]{0:T(1024)S(1)} %bitcast.65, f32[256]{0:T(256)S(1)} %bitcast.68, f32[1024]{0:T(1024)S(1)} %bitcast.64, ...), kind=kOutput, calls=%fused_computation.15 | convolution fusion | flops 339804160 | bytes 2701056 | tf_op jit(solution)/shard_map/dot_general | solution.py:23
  25.7 0.7 multiply_reduce_fusion
  26.9 1.5 %copy.20 = f32[4,2,256,256]{3,2,1,0:T(8,128)} copy(f32[4,2,256,256]{3,2,0,1:T(8,128)S(1)} %pad_maximum_fusion) | data formatting | bytes 4194304 | tf_op jit(solution)/shard_map/stack | solution.py:128
  28.4 3.8 %all-to-all-start.1 = ((f32[4,2,256,256]{3,2,1,0:T(8,128)}), f32[4,2,256,256]{3,2,1,0:T(8,128)S(1)}, u32[]{:S(2)}, u32[]{:S(2)}) async-start(f32[4,2,256,256]{3,2,1,0:T(8,128)} %copy.20), calls=%async_computation.1 | async-start | bytes 4194304 | tf_op jit(solution)/shard_map/all_to_all | solution.py:179
  32.3 46.8 %all-to-all-done.1 = f32[4,2,256,256]{3,2,1,0:T(8,128)S(1)} async-done(((f32[4,2,256,256]{3,2,1,0:T(8,128)}), f32[4,2,256,256]{3,2,1,0:T(8,128)S(1)}, u32[]{:S(2)}, u32[]{:S(2)}) %all-to-all-start.1) | async-done | bytes 2097184 | tf_op jit(solution)/shard_map/all_to_all | solution.py:179
  79.2 1.2 subtract_reduce_fusion
  80.4 2.2 %fusion.18 = f32[256,4,256]{2,0,1:T(8,128)S(1)} fusion(f32[4,256,256]{2,1,0:T(8,128)S(1)} %get-tuple-element.5, f32[4,256,256]{2,1,0:T(8,128)S(1)} %get-tuple-element.6, f32[4,256]{1,0:T(4,128)S(1)} %get-tuple-element.24, f32[4,256]{1,0:T(4,128)S(1)} %get-tuple-element.25), kind=kOutput, calls=%fused_computation.48 | convolution fusion | flops 807010304 | bytes 3153920 | tf_op jit(solution)/shard_map/dot_general | solution.py:149
  82.6 2.2 %fusion.19 = f32[256,4,256]{2,0,1:T(8,128)S(1)} fusion(f32[4,256,256]{2,1,0:T(8,128)S(1)} %get-tuple-element.6, f32[4,256,256]{2,1,0:T(8,128)S(1)} %get-tuple-element.5, f32[4,256]{1,0:T(4,128)S(1)} %get-tuple-element.24, f32[4,256]{1,0:T(4,128)S(1)} %get-tuple-element.25), kind=kOutput, calls=%fused_computation.49 | convolution fusion | flops 807010304 | bytes 3153920 | tf_op jit(solution)/shard_map/dot_general | solution.py:149
  84.8 2.3 %fusion.8 = bf16[256,4,256]{2,0,1:T(8,128)(2,1)S(1)} fusion(f32[256,4,256]{2,0,1:T(8,128)S(1)} %fusion.18, f32[4,256,256]{2,1,0:T(8,128)S(1)} %get-tuple-element.6, f32[4,256,256]{2,1,0:T(8,128)S(1)} %get-tuple-element.5, f32[4,256]{1,0:T(4,128)S(1)} %get-tuple-element.24, f32[4,256]{1,0:T(4,128)S(1)} %get-tuple-element.25), kind=kOutput, calls=%fused_computation.23 | convolution fusion | flops 807796736 | bytes 3678208 | tf_op jit(solution)/shard_map/dot_general | solution.py:149
  87.1 1.2 copy.21
  88.3 2.0 %convert_element_type.116 = bf16[1,1024,256]{2,1,0:T(8,128)(2,1)} reshape(bf16[256,4,256]{2,1,0:T(4,128)(2,1)} %copy.21) | data formatting | bytes 1048576 | tf_op jit(solution)/shard_map/convert_element_type | solution.py:156
  90.2 2.1 %copy.23 = bf16[1,1024,256]{1,2,0:T(8,128)(2,1)} copy(bf16[1,1024,256]{2,1,0:T(8,128)(2,1)} %convert_element_type.116) | data formatting | bytes 1048576 | tf_op jit(solution)/shard_map/convert_element_type | solution.py:156
  92.3 2.2 %fusion.9 = bf16[256,4,256]{2,0,1:T(8,128)(2,1)S(1)} fusion(f32[256,4,256]{2,0,1:T(8,128)S(1)} %fusion.19, f32[4,256,256]{2,1,0:T(8,128)S(1)} %get-tuple-element.5, f32[4,256,256]{2,1,0:T(8,128)S(1)} %get-tuple-element.6, f32[4,256]{1,0:T(4,128)S(1)} %get-tuple-element.24, f32[4,256]{1,0:T(4,128)S(1)} %get-tuple-element.25), kind=kOutput, calls=%fused_computation.24 | convolution fusion | flops 807796736 | bytes 3678208 | tf_op jit(solution)/shard_map/dot_general | solution.py:149
  95.7 1.6 %collective-permute-start = (bf16[2,1024,256]{1,2,0:T(8,128)(2,1)S(1)}, bf16[2,1024,256]{1,2,0:T(8,128)(2,1)}, u32[]{:S(2)}, u32[]{:S(2)}) collective-permute-start(bf16[2,1024,256]{1,2,0:T(8,128)(2,1)S(1)} %pad_maximum_fusion.1), channel_id=1, source_target_pairs={{0,1},{1,0},{2,3},{3,2},{4,5},{5,4},{6,7},{7,6},{8,9},{9,8},{10,11... | collective-permute-start | bytes 3145736 | tf_op jit(solution)/shard_map/ppermute | solution.py:106
  99.2 20.8 %collective-permute-done = bf16[2,1024,256]{1,2,0:T(8,128)(2,1)} collective-permute-done((bf16[2,1024,256]{1,2,0:T(8,128)(2,1)S(1)}, bf16[2,1024,256]{1,2,0:T(8,128)(2,1)}, u32[]{:S(2)}, u32[]{:S(2)}) %collective-permute-start) | collective-permute-done | bytes 1048608 | tf_op jit(solution)/shard_map/ppermute | solution.py:106
  120.0 1.7 %fusion.11 = f32[1,256,256]{2,1,0:T(8,128)S(1)} fusion(bf16[2,1024,256]{1,2,0:T(8,128)(2,1)} %collective-permute-done, f32[1024]{0:T(1024)S(1)} %fusion.17, bf16[1,1024,256]{1,2,0:T(8,128)(2,1)S(1)} %copy.24, bf16[1,1024,256]{1,2,0:T(8,128)(2,1)S(1)} %copy-done), kind=kOutput, calls=%fused_computation.26 | convolution fusion | flops 270532608 | bytes 2363392 | tf_op jit(solution)/shard_map/dot_general | solution.py:185
  122.4 15.5 %all_to_all.15 = f32[4,128,256]{2,1,0:T(8,128)S(1)} all-to-all(f32[4,128,256]{2,1,0:T(8,128)S(1)} %broadcast_select_fusion), channel_id=1, replica_groups=mesh['groups'=2,'tm'=4,'comp'=2,'panel'=2] {'tm'}, dimensions={0} | all-to-all | bytes 1048576 | tf_op jit(solution)/shard_map/all_to_all | solution.py:193
  138.0 1.3 collective-permute-done.1
  (38 shorter events, 6.7 us)
Async XLA Ops:
  2.0 11.9 %all-to-all-start = ((f32[4,3,256]{2,1,0:T(4,128)}), f32[4,3,256]{2,1,0:T(4,128)S(1)}, u32[]{:S(2)}, u32[]{:S(2)}) async-start(f32[4,3,256]{2,1,0:T(4,128)} %maximum_bitcast_fusion), calls=%async_computation | async-start | bytes 32768 | tf_op jit(solution)/shard_map/all_to_all | solution.py:172
  28.4 50.6 %all-to-all-start.1 = ((f32[4,2,256,256]{3,2,1,0:T(8,128)}), f32[4,2,256,256]{3,2,1,0:T(8,128)S(1)}, u32[]{:S(2)}, u32[]{:S(2)}) async-start(f32[4,2,256,256]{3,2,1,0:T(8,128)} %copy.20), calls=%async_computation.1 | async-start | bytes 4194304 | tf_op jit(solution)/shard_map/all_to_all | solution.py:179
  94.5 1.0 copy-start
  95.0 2.3 %copy-start.1 = (s32[1,2049]{1,0:T(1,128)S(1)}, s32[1,2049]{1,0:T(1,128)}, u32[]{:S(2)}) copy-start(s32[1,2049]{1,0:T(1,128)} %param.9) | copy-start | bytes 24592
  95.7 24.3 %collective-permute-start = (bf16[2,1024,256]{1,2,0:T(8,128)(2,1)S(1)}, bf16[2,1024,256]{1,2,0:T(8,128)(2,1)}, u32[]{:S(2)}, u32[]{:S(2)}) collective-permute-start(bf16[2,1024,256]{1,2,0:T(8,128)(2,1)S(1)} %pad_maximum_fusion.1), channel_id=1, source_target_pairs={{0,1},{1,0},{2,3},{3,2},{4,5},{5,4},{6,7},{7,6},{8,9},{9,8},{10,11... | collective-permute-start | bytes 3145736 | tf_op jit(solution)/shard_map/ppermute | solution.py:106
  137.9 1.4 %collective-permute-start.1 = (f32[128,256]{1,0:T(8,128)S(1)}, f32[128,256]{1,0:T(8,128)S(1)}, u32[]{:S(2)}, u32[]{:S(2)}) collective-permute-start(f32[128,256]{1,0:T(8,128)S(1)} %reduce_sum.52), channel_id=1, source_target_pairs={{0,2},{2,0},{1,3},{3,1},{4,6},{6,4},{5,7},{7,5},{8,10},{10,8},{9,1... | collective-permute-start | bytes 393224 | tf_op jit(solution)/shard_map/ppermute | solution.py:116

commit v4 on v3

--- a/solution.py
+++ b/solution.py
@@ -147,7 +147,7 @@
 
     def mat(table, value):
         return lax.dot_general(
-            table, value, dims, precision=lax.Precision.HIGHEST,
+            table, value, dims, precision=lax.Precision.HIGH,
             preferred_element_type=jnp.float32,
         )
 
@@ -189,11 +189,30 @@
     panel = lax.axis_index("panel")
     order = (panel - jnp.arange(panels, dtype=jnp.int32)) % panels
     partial_value = jnp.take(by_shift, order, axis=0).reshape(panels * columns, columns)
-    rows = partial_value.shape[0] // devices_tm
-    pieces = lax.all_to_all(
-        partial_value.reshape(devices_tm, rows, columns), "tm", 0, 0, tiled=True
-    )
-    return comp_sum(jnp.sum(pieces, axis=0))
+    return settle_rows(partial_value)
+
+
+def settle_rows(partial_value):
+    devices_tm = lax.axis_size("tm")
+    comps = lax.axis_size("comp")
+    rows_total, columns = partial_value.shape
+    rows = rows_total // devices_tm
+    if comps != 2 or columns % 256 != 0:
+        pieces = lax.all_to_all(
+            partial_value.reshape(devices_tm, rows, columns), "tm", 0, 0, tiled=True
+        )
+        return comp_sum(jnp.sum(pieces, axis=0))
+    half = columns // 2
+    comp = lax.axis_index("comp")
+    mine = lax.dynamic_slice_in_dim(partial_value, comp * half, half, axis=1)
+    theirs = lax.dynamic_slice_in_dim(partial_value, (1 - comp) * half, half, axis=1)
+    summed = mine + lax.ppermute(theirs, "comp", [(0, 1), (1, 0)])
+    pieces = lax.all_to_all(summed.reshape(devices_tm, rows, half), "tm", 0, 0, tiled=True)
+    block = jnp.sum(pieces, axis=0)
+    other = lax.ppermute(block, "comp", [(0, 1), (1, 0)])
+    first = jnp.where(comp == 0, block, other)
+    second = jnp.where(comp == 0, other, block)
+    return jnp.concatenate([first, second], axis=1)
 
 
 def solution(mesh):

time: 141 us -> 137 us (0.972)
  blocking collectives: 15.5 us -> 11.8 us
  matrix products: 16.4 us -> 14.6 us
  waiting for transfers between devices: 72.2 us -> 73.7 us
    all_to_all x1, blocking collectives: 15.5 us -> 11.8 us  [settle_rows(): lax.all_to_all(summed.reshape(devices_tm, rows, half), 'tm', 0, 0, tiled=...]
    dot_general x4, matrix products: 8.88 us -> 7.05 us  [mat(): lax.dot_general(table, value, dims, precision=lax.Precision.HIGH, preferr...]
    ppermute x1 -> x2, waiting for transfers between devices: 1.33 us -> 2.75 us  [the longest x1 1.52 us: settle_rows(): summed = mine + lax.ppermute(theirs, 'comp', [(0, 1), (1, 0)])]
  transfers between devices with their start and end apart: 4 -> 5, of which waited for: 4 -> 5; matrix products, arithmetic and copies ran while one was open for 3% -> 3% of each run, Pallas kernels for 0% -> 0%
where the time goes in v4:
time: 137 us; the launch traced here: 136 us
  waiting for transfers between devices  73.7 us (54%)
  other arithmetic  14.6 us (11%)
  matrix products  14.6 us (11%)
  starting transfers between devices  11.8 us (9%)
  blocking collectives  11.8 us (9%)
  local copies, waits for them, and re-layouts  9.35 us (7%)
    all_to_all x1, waiting for transfers between devices, body(): gathered = lax.all_to_all(twisted, 'tm', 0, 0, tiled=True)  46.8 us
    ppermute x1, waiting for transfers between devices, panel_spectra(): blocks.append(lax.ppermute(spectra, 'panel', pairs))  20.8 us
    all_to_all x1, blocking collectives, settle_rows(): lax.all_to_all(summed.reshape(devices_tm, rows, half), 'tm', 0, 0, tiled=...  11.8 us
    dot_general x4, matrix products, mat(): lax.dot_general(table, value, dims, precision=lax.Precision.HIGH, preferr...  7.05 us
    another operation x1, other arithmetic  6.37 us
    all_to_all x1, starting transfers between devices, body(): received = lax.all_to_all(packed, 'tm', 0, 0, tiled=True)  6.32 us
    dot_general x1, matrix products, synthesize(): latitude = jnp.dot(basis_rows, masked, preferred_element_type=jnp.float32)  5.37 us
    convert_element_type x3, local copies, waits for them, and re-layouts, class_spectrum(): (new_real.reshape(length, columns) / samples).astype(jnp.bfloat16)  5.23 us
  transfers between devices with their start and end apart: 5, of which 5 were waited for; matrix products, arithmetic and copies ran while one was open for 3% of the time, Pallas kernels for 0%

profile of v4, /device:TPU:0, one launch (start us, length us, event | category | flops | bytes accessed | tf_op | source)
XLA Modules:
  0.0 136.2 jit_solution(8665880657624888067)
XLA Ops:
  0.7 1.3 maximum_bitcast_fusion
  2.0 6.3 %all-to-all-start = ((f32[4,3,256]{2,1,0:T(4,128)}), f32[4,3,256]{2,1,0:T(4,128)S(1)}, u32[]{:S(2)}, u32[]{:S(2)}) async-start(f32[4,3,256]{2,1,0:T(4,128)} %maximum_bitcast_fusion), calls=%async_computation | async-start | bytes 32768 | tf_op jit(solution)/shard_map/all_to_all | solution.py:172
  8.3 0.8 fusion.80
  10.6 3.3 %all-to-all-done = f32[4,3,256]{2,1,0:T(4,128)S(1)} async-done(((f32[4,3,256]{2,1,0:T(4,128)}), f32[4,3,256]{2,1,0:T(4,128)S(1)}, u32[]{:S(2)}, u32[]{:S(2)}) %all-to-all-start) | async-done | bytes 12320 | tf_op jit(solution)/shard_map/all_to_all | solution.py:172
  13.9 6.4 %cosine_convert_fusion = (bf16[1024,320]{1,0:T(8,128)(2,1)S(1)}, bf16[1024,320]{1,0:T(8,128)(2,1)S(1)}) fusion(f32[1024]{0:T(1024)S(1)} %bitcast.63), kind=kLoop, calls=%fused_computation.8 | loop fusion | flops 983040 | bytes 1314816 | tf_op jit(solution)/shard_map/convert
  20.3 5.4 %fusion.2 = f32[1024,256]{1,0:T(8,128)S(1)} fusion(bf16[1024,320]{1,0:T(8,128)(2,1)S(1)} %get-tuple-element.19, bf16[1024,320]{1,0:T(8,128)(2,1)S(1)} %get-tuple-element.18, f32[256]{0:T(256)S(1)} %bitcast.68, f32[1024]{0:T(1024)S(1)} %bitcast.67, f32[256]{0:T(256)S(1)} %bitcast.70, f32[1024]{0:T(1024)S(1)} %bitcast.66, ...), kind=kOutput, calls=%fused_computation.15 | convolution fusion | flops 339804160 | bytes 2701056 | tf_op jit(solution)/shard_map/dot_general | solution.py:23
  25.7 0.7 multiply_reduce_fusion
  26.9 1.5 %copy.20 = f32[4,2,256,256]{3,2,1,0:T(8,128)} copy(f32[4,2,256,256]{3,2,0,1:T(8,128)S(1)} %pad_maximum_fusion) | data formatting | bytes 4194304 | tf_op jit(solution)/shard_map/stack | solution.py:128
  28.4 3.8 %all-to-all-start.1 = ((f32[4,2,256,256]{3,2,1,0:T(8,128)}), f32[4,2,256,256]{3,2,1,0:T(8,128)S(1)}, u32[]{:S(2)}, u32[]{:S(2)}) async-start(f32[4,2,256,256]{3,2,1,0:T(8,128)} %copy.20), calls=%async_computation.1 | async-start | bytes 4194304 | tf_op jit(solution)/shard_map/all_to_all | solution.py:179
  32.3 46.8 %all-to-all-done.1 = f32[4,2,256,256]{3,2,1,0:T(8,128)S(1)} async-done(((f32[4,2,256,256]{3,2,1,0:T(8,128)}), f32[4,2,256,256]{3,2,1,0:T(8,128)S(1)}, u32[]{:S(2)}, u32[]{:S(2)}) %all-to-all-start.1) | async-done | bytes 2097184 | tf_op jit(solution)/shard_map/all_to_all | solution.py:179
  79.2 1.2 subtract_reduce_fusion
  80.4 1.7 %fusion.18 = f32[256,4,256]{2,0,1:T(8,128)S(1)} fusion(f32[4,256,256]{2,1,0:T(8,128)S(1)} %get-tuple-element.5, f32[4,256,256]{2,1,0:T(8,128)S(1)} %get-tuple-element.6, f32[4,256]{1,0:T(4,128)S(1)} %get-tuple-element.26, f32[4,256]{1,0:T(4,128)S(1)} %get-tuple-element.27), kind=kOutput, calls=%fused_computation.49 | convolution fusion | flops 404357120 | bytes 3153920 | tf_op jit(solution)/shard_map/dot_general | solution.py:149
  82.1 1.7 %fusion.19 = f32[256,4,256]{2,0,1:T(8,128)S(1)} fusion(f32[4,256,256]{2,1,0:T(8,128)S(1)} %get-tuple-element.6, f32[4,256,256]{2,1,0:T(8,128)S(1)} %get-tuple-element.5, f32[4,256]{1,0:T(4,128)S(1)} %get-tuple-element.26, f32[4,256]{1,0:T(4,128)S(1)} %get-tuple-element.27), kind=kOutput, calls=%fused_computation.50 | convolution fusion | flops 404357120 | bytes 3153920 | tf_op jit(solution)/shard_map/dot_general | solution.py:149
  83.9 1.8 %fusion.8 = bf16[256,4,256]{2,0,1:T(8,128)(2,1)S(1)} fusion(f32[256,4,256]{2,0,1:T(8,128)S(1)} %fusion.18, f32[4,256,256]{2,1,0:T(8,128)S(1)} %get-tuple-element.6, f32[4,256,256]{2,1,0:T(8,128)S(1)} %get-tuple-element.5, f32[4,256]{1,0:T(4,128)S(1)} %get-tuple-element.26, f32[4,256]{1,0:T(4,128)S(1)} %get-tuple-element.27), kind=kOutput, calls=%fused_computation.23 | convolution fusion | flops 405143552 | bytes 3678208 | tf_op jit(solution)/shard_map/dot_general | solution.py:149
  85.7 1.2 copy.21
  86.9 2.0 %convert_element_type.116 = bf16[1,1024,256]{2,1,0:T(8,128)(2,1)} reshape(bf16[256,4,256]{2,1,0:T(4,128)(2,1)} %copy.21) | data formatting | bytes 1048576 | tf_op jit(solution)/shard_map/convert_element_type | solution.py:156
  88.9 2.1 %copy.23 = bf16[1,1024,256]{1,2,0:T(8,128)(2,1)} copy(bf16[1,1024,256]{2,1,0:T(8,128)(2,1)} %convert_element_type.116) | data formatting | bytes 1048576 | tf_op jit(solution)/shard_map/convert_element_type | solution.py:156
  90.9 1.8 %fusion.9 = bf16[256,4,256]{2,0,1:T(8,128)(2,1)S(1)} fusion(f32[256,4,256]{2,0,1:T(8,128)S(1)} %fusion.19, f32[4,256,256]{2,1,0:T(8,128)S(1)} %get-tuple-element.5, f32[4,256,256]{2,1,0:T(8,128)S(1)} %get-tuple-element.6, f32[4,256]{1,0:T(4,128)S(1)} %get-tuple-element.26, f32[4,256]{1,0:T(4,128)S(1)} %get-tuple-element.27), kind=kOutput, calls=%fused_computation.24 | convolution fusion | flops 405143552 | bytes 3678208 | tf_op jit(solution)/shard_map/dot_general | solution.py:149
  93.9 1.6 %collective-permute-start = (bf16[2,1024,256]{1,2,0:T(8,128)(2,1)S(1)}, bf16[2,1024,256]{1,2,0:T(8,128)(2,1)}, u32[]{:S(2)}, u32[]{:S(2)}) collective-permute-start(bf16[2,1024,256]{1,2,0:T(8,128)(2,1)S(1)} %pad_maximum_fusion.1), channel_id=1, source_target_pairs={{0,1},{1,0},{2,3},{3,2},{4,5},{5,4},{6,7},{7,6},{8,9},{9,8},{10,11... | collective-permute-start | bytes 3145736 | tf_op jit(solution)/shard_map/ppermute | solution.py:106
  97.3 20.8 %collective-permute-done = bf16[2,1024,256]{1,2,0:T(8,128)(2,1)} collective-permute-done((bf16[2,1024,256]{1,2,0:T(8,128)(2,1)S(1)}, bf16[2,1024,256]{1,2,0:T(8,128)(2,1)}, u32[]{:S(2)}, u32[]{:S(2)}) %collective-permute-start) | collective-permute-done | bytes 1048608 | tf_op jit(solution)/shard_map/ppermute | solution.py:106
  118.1 1.7 %fusion.11 = f32[1,256,256]{2,1,0:T(8,128)S(1)} fusion(bf16[2,1024,256]{1,2,0:T(8,128)(2,1)} %collective-permute-done, f32[1024]{0:T(1024)S(1)} %fusion.17, bf16[1,1024,256]{1,2,0:T(8,128)(2,1)S(1)} %copy.24, bf16[1,1024,256]{1,2,0:T(8,128)(2,1)S(1)} %copy-done), kind=kOutput, calls=%fused_computation.26 | convolution fusion | flops 270532608 | bytes 2363392 | tf_op jit(solution)/shard_map/dot_general | solution.py:185
  120.7 1.5 %collective-permute-done.1 = f32[512,128]{1,0:T(8,128)S(1)} collective-permute-done((f32[512,128]{1,0:T(8,128)S(1)}, f32[512,128]{1,0:T(8,128)S(1)}, u32[]{:S(2)}, u32[]{:S(2)}) %collective-permute-start.1) | collective-permute-done | bytes 262176 | tf_op jit(solution)/shard_map/ppermute | solution.py:209
  122.3 11.8 %all_to_all.15 = f32[4,128,128]{2,1,0:T(8,128)S(1)} all-to-all(f32[4,128,128]{2,1,0:T(8,128)S(1)} %bitcast.60), channel_id=1, replica_groups=mesh['groups'=2,'tm'=4,'comp'=2,'panel'=2] {'tm'}, dimensions={0} | all-to-all | bytes 524288 | tf_op jit(solution)/shard_map/all_to_all | solution.py:210
  134.2 1.2 collective-permute-done.2
  (43 shorter events, 7.5 us)
Async XLA Ops:
  2.0 11.9 %all-to-all-start = ((f32[4,3,256]{2,1,0:T(4,128)}), f32[4,3,256]{2,1,0:T(4,128)S(1)}, u32[]{:S(2)}, u32[]{:S(2)}) async-start(f32[4,3,256]{2,1,0:T(4,128)} %maximum_bitcast_fusion), calls=%async_computation | async-start | bytes 32768 | tf_op jit(solution)/shard_map/all_to_all | solution.py:172
  28.4 50.6 %all-to-all-start.1 = ((f32[4,2,256,256]{3,2,1,0:T(8,128)}), f32[4,2,256,256]{3,2,1,0:T(8,128)S(1)}, u32[]{:S(2)}, u32[]{:S(2)}) async-start(f32[4,2,256,256]{3,2,1,0:T(8,128)} %copy.20), calls=%async_computation.1 | async-start | bytes 4194304 | tf_op jit(solution)/shard_map/all_to_all | solution.py:179
  92.7 1.0 copy-start
  93.1 2.3 %copy-start.1 = (s32[1,2049]{1,0:T(1,128)S(1)}, s32[1,2049]{1,0:T(1,128)}, u32[]{:S(2)}) copy-start(s32[1,2049]{1,0:T(1,128)} %param.9) | copy-start | bytes 24592
  93.9 24.3 %collective-permute-start = (bf16[2,1024,256]{1,2,0:T(8,128)(2,1)S(1)}, bf16[2,1024,256]{1,2,0:T(8,128)(2,1)}, u32[]{:S(2)}, u32[]{:S(2)}) collective-permute-start(bf16[2,1024,256]{1,2,0:T(8,128)(2,1)S(1)} %pad_maximum_fusion.1), channel_id=1, source_target_pairs={{0,1},{1,0},{2,3},{3,2},{4,5},{5,4},{6,7},{7,6},{8,9},{9,8},{10,11... | collective-permute-start | bytes 3145736 | tf_op jit(solution)/shard_map/ppermute | solution.py:106
  120.7 1.6 %collective-permute-start.1 = (f32[512,128]{1,0:T(8,128)S(1)}, f32[512,128]{1,0:T(8,128)S(1)}, u32[]{:S(2)}, u32[]{:S(2)}) collective-permute-start(f32[512,128]{1,0:T(8,128)S(1)} %constant_dynamic-slice_fusion), channel_id=1, source_target_pairs={{0,2},{2,0},{1,3},{3,1},{4,6},{6,4},{5,7},{7,5},{8,10},{10,8},{9,1... | collective-permute-start | bytes 786440 | tf_op jit(solution)/shard_map/ppermute | solution.py:209
  134.2 1.3 collective-permute-start.2

commit v5 on v4

--- a/solution.py
+++ b/solution.py
@@ -91,11 +91,18 @@
     return (real_part.astype(jnp.bfloat16), imag_part.astype(jnp.bfloat16))
 
 
-def inverse_weights(psd_row, position, devices_tm, epochs, samples):
+def inverse_weights(psd_row, position, devices_tm, epochs, samples, count):
     half = samples // 2
     mirrored = jnp.concatenate([psd_row[: half + 1], psd_row[1:half][::-1]])
     picked = lax.dynamic_slice_in_dim(mirrored.reshape(epochs, devices_tm), position, 1, axis=1)
-    return 8192.0 / picked[:, 0].astype(jnp.float32)
+    inverse = 8192.0 / picked[:count, 0].astype(jnp.float32)
+    order = jnp.arange(count, dtype=jnp.int32)
+    first = jnp.where(position == 0, 1.0, 2.0)
+    middle = jnp.where(position == 0, 1.0, 0.0)
+    fold = jnp.where(
+        order == 0, first, jnp.where(order < epochs // 2, 2.0, jnp.where(order == epochs // 2, middle, 0.0))
+    )
+    return inverse, fold
 
 
 def panel_spectra(spectra):
@@ -142,7 +149,10 @@
     real_part, imag_part = rotate(
         real_part, imag_part, index, jnp.arange(block_len, dtype=jnp.int32), length
     )
-    cos_inner, sin_inner = dft_tables(block_len)
+    kept = block_len // 2 + 1
+    cos_inner, sin_inner = phase_tables(
+        jnp.arange(kept, dtype=jnp.int32), jnp.arange(block_len, dtype=jnp.int32), block_len
+    )
     dims = (((1,), (1,)), ((), ()))
 
     def mat(table, value):
@@ -153,8 +163,8 @@
 
     new_real = mat(cos_inner, real_part) + mat(sin_inner, imag_part)
     new_imag = mat(cos_inner, imag_part) - mat(sin_inner, real_part)
-    new_real = (new_real.reshape(length, columns) / samples).astype(jnp.bfloat16)
-    new_imag = (new_imag.reshape(length, columns) / samples).astype(jnp.bfloat16)
+    new_real = (new_real.reshape(kept * devices_tm, columns) / samples).astype(jnp.bfloat16)
+    new_imag = (new_imag.reshape(kept * devices_tm, columns) / samples).astype(jnp.bfloat16)
     return jnp.stack([new_real, new_imag])
 
 
@@ -178,8 +188,11 @@
     twisted = class_partials(spread, position, samples)
     gathered = lax.all_to_all(twisted, "tm", 0, 0, tiled=True)
     spectra = class_spectrum(gathered, samples)
-    inverse_psd = inverse_weights(psd_table[0], position, devices_tm, epochs, samples)
+    inverse_psd, fold = inverse_weights(
+        psd_table[0], position, devices_tm, epochs, samples, spectra.shape[1]
+    )
     weighted = (spectra.astype(jnp.float32) * inverse_psd[None, :, None]).astype(jnp.bfloat16)
+    weighted = weighted * fold[None, :, None].astype(jnp.bfloat16)
     contract = (((0, 1), (0, 1)), ((), ()))
     products = [
         lax.dot_general(block, weighted, contract, preferred_element_type=jnp.float32)

time: 137 us -> 116 us (0.85)
  waiting for transfers between devices: 73.7 us -> 62.4 us
  local copies, waits for them, and re-layouts: 9.35 us -> 3.9 us
  matrix products: 14.6 us -> 11 us
    ppermute x1, waiting for transfers between devices: 20.8 us -> 9.96 us  [panel_spectra(): blocks.append(lax.ppermute(spectra, 'panel', pairs))]
    convert_element_type x6 -> x4, local copies, waits for them, and re-layouts: 5.97 us -> 0.34 us  [the longest x2 0.17 us: class_spectrum(): (new_real.reshape(kept * devices_tm, columns) / samples).astype(jnp.bfloa...]
    dot_general x4, matrix products: 7.05 us -> 4.54 us  [mat(): lax.dot_general(table, value, dims, precision=lax.Precision.HIGH, preferr...]
    another operation x2 -> x1, other arithmetic: 6.46 us -> 6.37 us
  transfers between devices with their start and end apart: 5 -> 5, of which waited for: 5 -> 5; matrix products, arithmetic and copies ran while one was open for 3% -> 4% of each run, Pallas kernels for 0% -> 0%
where the time goes in v5:
time: 116 us
  waiting for transfers between devices  62.4 us (54%)
  other arithmetic  14.4 us (12%)
  starting transfers between devices  11.9 us (10%)
  blocking collectives  11.8 us (10%)
  matrix products  11 us (9%)
  local copies, waits for them, and re-layouts  3.9 us (3%)
    all_to_all x1, waiting for transfers between devices, body(): gathered = lax.all_to_all(twisted, 'tm', 0, 0, tiled=True)  46.4 us
    all_to_all x1, blocking collectives, settle_rows(): lax.all_to_all(summed.reshape(devices_tm, rows, half), 'tm', 0, 0, tiled=...  11.8 us
    ppermute x1, waiting for transfers between devices, panel_spectra(): blocks.append(lax.ppermute(spectra, 'panel', pairs))  9.96 us
    another operation x1, other arithmetic  6.37 us
    all_to_all x1, starting transfers between devices, body(): received = lax.all_to_all(packed, 'tm', 0, 0, tiled=True)  6.32 us
    dot_general x1, matrix products, synthesize(): latitude = jnp.dot(basis_rows, masked, preferred_element_type=jnp.float32)  5.37 us
    dot_general x4, matrix products, mat(): lax.dot_general(table, value, dims, precision=lax.Precision.HIGH, preferr...  4.54 us
    all_to_all x1, starting transfers between devices, body(): gathered = lax.all_to_all(twisted, 'tm', 0, 0, tiled=True)  3.92 us
  transfers between devices with their start and end apart: 5, of which 5 were waited for; matrix products, arithmetic and copies ran while one was open for 4% of the time, Pallas kernels for 0%

profile of v5, /device:TPU:0, one launch (start us, length us, event | category | flops | bytes accessed | tf_op | source)
XLA Modules:
  0.0 115.9 jit_solution(13006578265099530786)
XLA Ops:
  0.0 0.7 convert_element_type.118
  0.7 1.3 %maximum_bitcast_fusion = f32[4,3,256]{2,1,0:T(4,128)} fusion(f32[1,4,256]{2,0,1:T(1,128)S(1)} %bitcast.64, f32[2,4,256]{2,0,1:T(2,128)} %bitcast.65), kind=kLoop, calls=%fused_computation.73 | loop fusion | flops 3072 | bytes 24576 | tf_op jit(solution)/shard_map/transpose | solution.py:181
  2.0 6.3 %all-to-all-start = ((f32[4,3,256]{2,1,0:T(4,128)}), f32[4,3,256]{2,1,0:T(4,128)S(1)}, u32[]{:S(2)}, u32[]{:S(2)}) async-start(f32[4,3,256]{2,1,0:T(4,128)} %maximum_bitcast_fusion), calls=%async_computation | async-start | bytes 32768 | tf_op jit(solution)/shard_map/all_to_all | solution.py:182
  8.3 0.8 fusion.83
  9.1 0.7 add_rsqrt_fusion
  9.8 0.7 compare_reduce_fusion
  10.6 3.3 %all-to-all-done = f32[4,3,256]{2,1,0:T(4,128)S(1)} async-done(((f32[4,3,256]{2,1,0:T(4,128)}), f32[4,3,256]{2,1,0:T(4,128)S(1)}, u32[]{:S(2)}, u32[]{:S(2)}) %all-to-all-start) | async-done | bytes 12320 | tf_op jit(solution)/shard_map/all_to_all | solution.py:182
  13.9 6.4 %cosine_convert_fusion = (bf16[1024,320]{1,0:T(8,128)(2,1)S(1)}, bf16[1024,320]{1,0:T(8,128)(2,1)S(1)}) fusion(f32[1024]{0:T(1024)S(1)} %bitcast.63), kind=kLoop, calls=%fused_computation.7 | loop fusion | flops 983040 | bytes 1314816 | tf_op jit(solution)/shard_map/convert
  20.3 5.4 %fusion = f32[1024,256]{1,0:T(8,128)S(1)} fusion(bf16[1024,320]{1,0:T(8,128)(2,1)S(1)} %get-tuple-element.19, bf16[1024,320]{1,0:T(8,128)(2,1)S(1)} %get-tuple-element.18, f32[256]{0:T(256)S(1)} %bitcast.68, f32[1024]{0:T(1024)S(1)} %bitcast.67, f32[256]{0:T(256)S(1)} %bitcast.70, f32[1024]{0:T(1024)S(1)} %bitcast.66, ...), kind=kOutput, calls=%fused_computation.12 | convolution fusion | flops 339804160 | bytes 2701056 | tf_op jit(solution)/shard_map/dot_general | solution.py:23
  25.7 0.7 multiply_reduce_fusion
  26.9 1.5 %copy.12 = f32[4,2,256,256]{3,2,1,0:T(8,128)} copy(f32[4,2,256,256]{3,2,0,1:T(8,128)S(1)} %pad_maximum_fusion) | data formatting | bytes 4194304 | tf_op jit(solution)/shard_map/stack | solution.py:135
  28.4 3.9 %all-to-all-start.1 = ((f32[4,2,256,256]{3,2,1,0:T(8,128)}), f32[4,2,256,256]{3,2,1,0:T(8,128)S(1)}, u32[]{:S(2)}, u32[]{:S(2)}) async-start(f32[4,2,256,256]{3,2,1,0:T(8,128)} %copy.12), calls=%async_computation.1 | async-start | bytes 4194304 | tf_op jit(solution)/shard_map/all_to_all | solution.py:189
  32.8 46.4 %all-to-all-done.1 = f32[4,2,256,256]{3,2,1,0:T(8,128)S(1)} async-done(((f32[4,2,256,256]{3,2,1,0:T(8,128)}), f32[4,2,256,256]{3,2,1,0:T(8,128)S(1)}, u32[]{:S(2)}, u32[]{:S(2)}) %all-to-all-start.1) | async-done | bytes 2097184 | tf_op jit(solution)/shard_map/all_to_all | solution.py:189
  79.3 1.2 %add_reduce_fusion = (f32[4,256,256]{2,1,0:T(8,128)S(1)}, f32[4,256,256]{2,1,0:T(8,128)S(1)}) fusion(f32[4,256,256]{2,1,0:T(8,128)S(1)} %get-tuple-element.12, f32[4,256,256]{2,1,0:T(8,128)S(1)} %get-tuple-element.11, f32[4,4]{1,0:T(4,128)S(1)} %get-tuple-element.24, f32[4,4]{1,0:T(4,128)S(1)} %get-tuple-element.25), kind=kLoop, calls=%fused_computation.2 | loop fusion | flops 7864320 | bytes 4194432 | tf_op jit(solution)/shard_map/reduce_sum | solution.py:147
  80.5 1.1 fusion.18
  81.7 1.1 fusion.17
  82.8 1.1 fusion.6
  84.1 1.1 fusion.7
  86.0 1.6 %collective-permute-start = (bf16[2,516,256]{2,0,1:T(2,128)(2,1)S(1)}, bf16[2,516,256]{2,0,1:T(2,128)(2,1)S(1)}, u32[]{:S(2)}, u32[]{:S(2)}) collective-permute-start(bf16[2,516,256]{2,0,1:T(2,128)(2,1)S(1)} %copy.15), channel_id=1, source_target_pairs={{0,1},{1,0},{2,3},{3,2},{4,5},{5,4},{6,7},{7,6},{8,9},{9,8},{10,11... | collective-permute-start | bytes 1585160 | tf_op jit(solution)/shard_map/ppermute | solution.py:113
  89.0 10.0 %collective-permute-done = bf16[2,516,256]{2,0,1:T(2,128)(2,1)S(1)} collective-permute-done((bf16[2,516,256]{2,0,1:T(2,128)(2,1)S(1)}, bf16[2,516,256]{2,0,1:T(2,128)(2,1)S(1)}, u32[]{:S(2)}, u32[]{:S(2)}) %collective-permute-start) | collective-permute-done | bytes 528416 | tf_op jit(solution)/shard_map/ppermute | solution.py:113
  100.4 1.5 %collective-permute-done.1 = f32[512,128]{1,0:T(8,128)S(1)} collective-permute-done((f32[512,128]{1,0:T(8,128)S(1)}, f32[512,128]{1,0:T(8,128)S(1)}, u32[]{:S(2)}, u32[]{:S(2)}) %collective-permute-start.1) | collective-permute-done | bytes 262176 | tf_op jit(solution)/shard_map/ppermute | solution.py:222
  102.0 11.8 %all_to_all.15 = f32[4,128,128]{2,1,0:T(8,128)S(1)} all-to-all(f32[4,128,128]{2,1,0:T(8,128)S(1)} %bitcast.60), channel_id=1, replica_groups=mesh['groups'=2,'tm'=4,'comp'=2,'panel'=2] {'tm'}, dimensions={0} | all-to-all | bytes 524288 | tf_op jit(solution)/shard_map/all_to_all | solution.py:223
  113.9 1.2 %collective-permute-done.2 = f32[128,128]{1,0:T(8,128)S(1)} collective-permute-done((f32[128,128]{1,0:T(8,128)S(1)}, f32[128,128]{1,0:T(8,128)S(1)}, u32[]{:S(2)}, u32[]{:S(2)}) %collective-permute-start.2) | collective-permute-done | bytes 65568 | tf_op jit(solution)/shard_map/ppermute | solution.py:225
  115.2 0.7 pad_maximum_fusion.2
  (42 shorter events, 4.9 us)
Async XLA Ops:
  2.0 11.9 %all-to-all-start = ((f32[4,3,256]{2,1,0:T(4,128)}), f32[4,3,256]{2,1,0:T(4,128)S(1)}, u32[]{:S(2)}, u32[]{:S(2)}) async-start(f32[4,3,256]{2,1,0:T(4,128)} %maximum_bitcast_fusion), calls=%async_computation | async-start | bytes 32768 | tf_op jit(solution)/shard_map/all_to_all | solution.py:182
  28.4 3.9 %copy-start = (s32[1,2049]{1,0:T(1,128)S(1)}, s32[1,2049]{1,0:T(1,128)}, u32[]{:S(2)}) copy-start(s32[1,2049]{1,0:T(1,128)} %param.9) | copy-start | bytes 24592
  28.4 50.8 %all-to-all-start.1 = ((f32[4,2,256,256]{3,2,1,0:T(8,128)}), f32[4,2,256,256]{3,2,1,0:T(8,128)S(1)}, u32[]{:S(2)}, u32[]{:S(2)}) async-start(f32[4,2,256,256]{3,2,1,0:T(8,128)} %copy.12), calls=%async_computation.1 | async-start | bytes 4194304 | tf_op jit(solution)/shard_map/all_to_all | solution.py:189
  86.0 13.0 %collective-permute-start = (bf16[2,516,256]{2,0,1:T(2,128)(2,1)S(1)}, bf16[2,516,256]{2,0,1:T(2,128)(2,1)S(1)}, u32[]{:S(2)}, u32[]{:S(2)}) collective-permute-start(bf16[2,516,256]{2,0,1:T(2,128)(2,1)S(1)} %copy.15), channel_id=1, source_target_pairs={{0,1},{1,0},{2,3},{3,2},{4,5},{5,4},{6,7},{7,6},{8,9},{9,8},{10,11... | collective-permute-start | bytes 1585160 | tf_op jit(solution)/shard_map/ppermute | solution.py:113
  100.3 1.6 %collective-permute-start.1 = (f32[512,128]{1,0:T(8,128)S(1)}, f32[512,128]{1,0:T(8,128)S(1)}, u32[]{:S(2)}, u32[]{:S(2)}) collective-permute-start(f32[512,128]{1,0:T(8,128)S(1)} %constant_dynamic-slice_fusion), channel_id=1, source_target_pairs={{0,2},{2,0},{1,3},{3,1},{4,6},{6,4},{5,7},{7,5},{8,10},{10,8},{9,1... | collective-permute-start | bytes 786440 | tf_op jit(solution)/shard_map/ppermute | solution.py:222
  113.8 1.3 %collective-permute-start.2 = (f32[128,128]{1,0:T(8,128)S(1)}, f32[128,128]{1,0:T(8,128)S(1)}, u32[]{:S(2)}, u32[]{:S(2)}) collective-permute-start(f32[128,128]{1,0:T(8,128)S(1)} %reduce_sum.52), channel_id=1, source_target_pairs={{0,2},{2,0},{1,3},{3,1},{4,6},{6,4},{5,7},{7,5},{8,10},{10,8},{9,1... | collective-permute-start | bytes 196616 | tf_op jit(solution)/shard_map/ppermute | solution.py:225

commit v6 on v5

--- a/solution.py
+++ b/solution.py
@@ -168,6 +168,26 @@
     return jnp.stack([new_real, new_imag])
 
 
+def swap_blocks(blocks, axis, ordered):
+    count = lax.axis_size(axis)
+    if count > 8:
+        received = lax.all_to_all(blocks, axis, 0, 0, tiled=True)
+        return received if ordered else jnp.sum(received, axis=0)
+    me = lax.axis_index(axis)
+    arrived = [lax.dynamic_index_in_dim(blocks, me, 0, keepdims=False)]
+    for shift in range(1, count):
+        outgoing = lax.dynamic_index_in_dim(blocks, (me + shift) % count, 0, keepdims=False)
+        pairs = [(src, (src + shift) % count) for src in range(count)]
+        arrived.append(lax.ppermute(outgoing, axis, pairs))
+    if not ordered:
+        total = arrived[0]
+        for part in arrived[1:]:
+            total = total + part
+        return total
+    order = (me - jnp.arange(count, dtype=jnp.int32)) % count
+    return jnp.take(jnp.stack(arrived), order, axis=0)
+
+
 def body(orbit_angles, gap_mask, column_index, lat_coeffs, psd_table):
     devices_tm = lax.axis_size("tm")
     panels = lax.axis_size("panel")
@@ -179,7 +199,7 @@
     keep_rows = gap_mask.astype(jnp.float32)
     packed = jnp.concatenate([orbit_angles, keep_rows[None]], axis=0)
     packed = packed.reshape(3, devices_tm, block_len).transpose(1, 0, 2)
-    received = lax.all_to_all(packed, "tm", 0, 0, tiled=True)
+    received = swap_blocks(packed, "tm", True)
     flat_orbit = received.transpose(1, 0, 2).reshape(3, devices_tm * block_len)
     spread = synthesize(flat_orbit[0:2], flat_orbit[2], column_index, coeffs).reshape(
         devices_tm, block_len, columns
@@ -220,8 +240,7 @@
     mine = lax.dynamic_slice_in_dim(partial_value, comp * half, half, axis=1)
     theirs = lax.dynamic_slice_in_dim(partial_value, (1 - comp) * half, half, axis=1)
     summed = mine + lax.ppermute(theirs, "comp", [(0, 1), (1, 0)])
-    pieces = lax.all_to_all(summed.reshape(devices_tm, rows, half), "tm", 0, 0, tiled=True)
-    block = jnp.sum(pieces, axis=0)
+    block = swap_blocks(summed.reshape(devices_tm, rows, half), "tm", False)
     other = lax.ppermute(block, "comp", [(0, 1), (1, 0)])
     first = jnp.where(comp == 0, block, other)
     second = jnp.where(comp == 0, other, block)

time: 116 us -> 111 us (0.957)
  blocking collectives: 11.8 us -> 0 us
  starting transfers between devices: 11.9 us -> 17 us
  waiting for transfers between devices: 62.4 us -> 64 us
  local copies, waits for them, and re-layouts: 3.9 us -> 5.24 us
  other arithmetic: 14.4 us -> 13.2 us
    all_to_all x1 -> x0, blocking collectives: 11.8 us -> none  [settle_rows(): lax.all_to_all(summed.reshape(devices_tm, rows, half), 'tm', 0, 0, tiled=...]
    ppermute x0 -> x6, starting transfers between devices: none -> 10.9 us  [swap_blocks(): arrived.append(lax.ppermute(outgoing, axis, pairs))]
    all_to_all x1 -> x0, starting transfers between devices: 6.32 us -> none  [body(): received = lax.all_to_all(packed, 'tm', 0, 0, tiled=True)]
    ppermute x0 -> x6, waiting for transfers between devices: none -> 4.83 us  [swap_blocks(): arrived.append(lax.ppermute(outgoing, axis, pairs))]
    all_to_all x1 -> x0, waiting for transfers between devices: 3.31 us -> none  [body(): received = lax.all_to_all(packed, 'tm', 0, 0, tiled=True)]
    transpose x1 -> x0, other arithmetic: 1.31 us -> none  [body(): packed = packed.reshape(3, devices_tm, block_len).transpose(1, 0, 2)]
    another operation x1 -> x2, other arithmetic: 6.37 us -> 6.37 us
  transfers between devices with their start and end apart: 5 -> 10, of which waited for: 5 -> 6; matrix products, arithmetic and copies ran while one was open for 4% -> 4% of each run, Pallas kernels for 0% -> 0%
where the time goes in v6:
time: 111 us
  waiting for transfers between devices  64 us (58%)
  starting transfers between devices  17 us (15%)
  other arithmetic  13.2 us (12%)
  matrix products  11 us (10%)
  local copies, waits for them, and re-layouts  5.24 us (5%)
    all_to_all x1, waiting for transfers between devices, body(): gathered = lax.all_to_all(twisted, 'tm', 0, 0, tiled=True)  46.5 us
    ppermute x6, starting transfers between devices, swap_blocks(): arrived.append(lax.ppermute(outgoing, axis, pairs))  10.9 us
    ppermute x1, waiting for transfers between devices, panel_spectra(): blocks.append(lax.ppermute(spectra, 'panel', pairs))  9.95 us
    another operation x1, other arithmetic  6.37 us
    dot_general x1, matrix products, synthesize(): latitude = jnp.dot(basis_rows, masked, preferred_element_type=jnp.float32)  5.38 us
    ppermute x6, waiting for transfers between devices, swap_blocks(): arrived.append(lax.ppermute(outgoing, axis, pairs))  4.83 us
    dot_general x4, matrix products, mat(): lax.dot_general(table, value, dims, precision=lax.Precision.HIGH, preferr...  4.55 us
    all_to_all x1, starting transfers between devices, body(): gathered = lax.all_to_all(twisted, 'tm', 0, 0, tiled=True)  4.41 us
  transfers between devices with their start and end apart: 10, of which 6 were waited for; matrix products, arithmetic and copies ran while one was open for 4% of the time, Pallas kernels for 0%

profile of v6, /device:TPU:0, one launch (start us, length us, event | category | flops | bytes accessed | tf_op | source)
XLA Modules:
  0.0 110.9 jit_solution(84136731079209160)
XLA Ops:
  0.0 0.7 concatenate.18
  1.5 3.1 %collective-permute-start = (f32[3,256]{1,0:T(4,128)S(1)}, f32[3,256]{1,0:T(4,128)S(1)}, u32[]{:S(2)}, u32[]{:S(2)}) collective-permute-start(f32[3,256]{1,0:T(4,128)S(1)} %bitcast.89), channel_id=1, source_target_pairs={{0,4},{4,8},{8,12},{12,0},{1,5},{5,9},{9,13},{13,1},{2,6},{6,10},{... | collective-permute-start | bytes 9224 | tf_op jit(solution)/shard_map/ppermute | solution.py:181
  4.5 2.6 %collective-permute-start.1 = (f32[3,256]{1,0:T(4,128)S(1)}, f32[3,256]{1,0:T(4,128)S(1)}, u32[]{:S(2)}, u32[]{:S(2)}) collective-permute-start(f32[3,256]{1,0:T(4,128)S(1)} %bitcast.90), channel_id=1, source_target_pairs={{0,8},{4,12},{8,0},{12,4},{1,9},{5,13},{9,1},{13,5},{2,10},{6,14},... | collective-permute-start | bytes 9224 | tf_op jit(solution)/shard_map/ppermute | solution.py:181
  7.1 1.3 %collective-permute-start.2 = (f32[3,256]{1,0:T(4,128)S(1)}, f32[3,256]{1,0:T(4,128)S(1)}, u32[]{:S(2)}, u32[]{:S(2)}) collective-permute-start(f32[3,256]{1,0:T(4,128)S(1)} %bitcast.91), channel_id=1, source_target_pairs={{0,12},{4,0},{8,4},{12,8},{1,13},{5,1},{9,5},{13,9},{2,14},{6,2},{... | collective-permute-start | bytes 9224 | tf_op jit(solution)/shard_map/ppermute | solution.py:181
  8.5 0.8 fusion.88
  10.0 0.7 compare_reduce_fusion
  11.6 6.4 %cosine_convert_fusion = (bf16[1024,320]{1,0:T(8,128)(2,1)S(1)}, bf16[1024,320]{1,0:T(8,128)(2,1)S(1)}) fusion(f32[1024]{0:T(1024)S(1)} %bitcast.88), kind=kLoop, calls=%fused_computation.8 | loop fusion | flops 983040 | bytes 1314816 | tf_op jit(solution)/shard_map/convert
  17.9 5.4 %fusion = f32[1024,256]{1,0:T(8,128)S(1)} fusion(bf16[1024,320]{1,0:T(8,128)(2,1)S(1)} %get-tuple-element.26, bf16[1024,320]{1,0:T(8,128)(2,1)S(1)} %get-tuple-element.25, f32[256]{0:T(256)S(1)} %bitcast.97, f32[1024]{0:T(1024)S(1)} %bitcast.93, f32[256]{0:T(256)S(1)} %bitcast.99, f32[1024]{0:T(1024)S(1)} %bitcast.92, ...), kind=kOutput, calls=%fused_computation.13 | convolution fusion | flops 339804160 | bytes 2701056 | tf_op jit(solution)/shard_map/dot_general | solution.py:23
  23.3 0.7 multiply_reduce_fusion
  24.5 1.5 %copy.17 = f32[4,2,256,256]{3,2,1,0:T(8,128)} copy(f32[4,2,256,256]{3,2,0,1:T(8,128)S(1)} %pad_maximum_fusion) | data formatting | bytes 4194304 | tf_op jit(solution)/shard_map/stack | solution.py:135
  26.0 4.4 %all-to-all-start = ((f32[4,2,256,256]{3,2,1,0:T(8,128)}), f32[4,2,256,256]{3,2,1,0:T(8,128)S(1)}, u32[]{:S(2)}, u32[]{:S(2)}) async-start(f32[4,2,256,256]{3,2,1,0:T(8,128)} %copy.17), calls=%async_computation | async-start | bytes 4194304 | tf_op jit(solution)/shard_map/all_to_all | solution.py:209
  30.8 46.5 %all-to-all-done = f32[4,2,256,256]{3,2,1,0:T(8,128)S(1)} async-done(((f32[4,2,256,256]{3,2,1,0:T(8,128)}), f32[4,2,256,256]{3,2,1,0:T(8,128)S(1)}, u32[]{:S(2)}, u32[]{:S(2)}) %all-to-all-start) | async-done | bytes 2097184 | tf_op jit(solution)/shard_map/all_to_all | solution.py:209
  77.5 1.2 %add_reduce_fusion = (f32[4,256,256]{2,1,0:T(8,128)S(1)}, f32[4,256,256]{2,1,0:T(8,128)S(1)}) fusion(f32[4,256,256]{2,1,0:T(8,128)S(1)} %get-tuple-element.12, f32[4,256,256]{2,1,0:T(8,128)S(1)} %get-tuple-element.11, f32[4,4]{1,0:T(4,128)S(1)} %get-tuple-element.33, f32[4,4]{1,0:T(4,128)S(1)} %get-tuple-element.34), kind=kLoop, calls=%fused_computation.3 | loop fusion | flops 7864320 | bytes 4194432 | tf_op jit(solution)/shard_map/reduce_sum | solution.py:147
  78.7 1.1 %fusion.18 = f32[129,4,256]{2,0,1:T(8,128)S(1)} fusion(f32[4,256,256]{2,1,0:T(8,128)S(1)} %get-tuple-element.5, f32[4,256,256]{2,1,0:T(8,128)S(1)} %get-tuple-element.6, f32[4,256]{1,0:T(4,128)S(1)} %get-tuple-element.31, f32[4,256]{1,0:T(4,128)S(1)} %get-tuple-element.32), kind=kOutput, calls=%fused_computation.45 | convolution fusion | flops 204148224 | bytes 2633728 | tf_op jit(solution)/shard_map/dot_general | solution.py:159
  79.9 1.1 %fusion.17 = f32[129,4,256]{2,0,1:T(8,128)S(1)} fusion(f32[4,256,256]{2,1,0:T(8,128)S(1)} %get-tuple-element.6, f32[4,256,256]{2,1,0:T(8,128)S(1)} %get-tuple-element.5, f32[4,256]{1,0:T(4,128)S(1)} %get-tuple-element.31, f32[4,256]{1,0:T(4,128)S(1)} %get-tuple-element.32), kind=kOutput, calls=%fused_computation.44 | convolution fusion | flops 204148224 | bytes 2633728 | tf_op jit(solution)/shard_map/dot_general | solution.py:159
  81.0 1.1 %fusion.6 = bf16[129,4,256]{2,0,1:T(8,128)(2,1)S(1)} fusion(f32[129,4,256]{2,0,1:T(8,128)S(1)} %fusion.18, f32[4,256,256]{2,1,0:T(8,128)S(1)} %get-tuple-element.6, f32[4,256,256]{2,1,0:T(8,128)S(1)} %get-tuple-element.5, f32[4,256]{1,0:T(4,128)S(1)} %get-tuple-element.31, f32[4,256]{1,0:T(4,128)S(1)} %get-tuple-element.32), kind=kOutput, calls=%fused_computation.21 | convolution fusion | flops 204544512 | bytes 2897920 | tf_op jit(solution)/shard_map/dot_general | solution.py:159
  82.3 1.1 %fusion.7 = bf16[129,4,256]{2,0,1:T(8,128)(2,1)S(1)} fusion(f32[129,4,256]{2,0,1:T(8,128)S(1)} %fusion.17, f32[4,256,256]{2,1,0:T(8,128)S(1)} %get-tuple-element.5, f32[4,256,256]{2,1,0:T(8,128)S(1)} %get-tuple-element.6, f32[4,256]{1,0:T(4,128)S(1)} %get-tuple-element.31, f32[4,256]{1,0:T(4,128)S(1)} %get-tuple-element.32), kind=kOutput, calls=%fused_computation.22 | convolution fusion | flops 204544512 | bytes 2897920 | tf_op jit(solution)/shard_map/dot_general | solution.py:159
  84.1 1.6 %collective-permute-start.3 = (bf16[2,516,256]{2,0,1:T(2,128)(2,1)S(1)}, bf16[2,516,256]{2,0,1:T(2,128)(2,1)S(1)}, u32[]{:S(2)}, u32[]{:S(2)}) collective-permute-start(bf16[2,516,256]{2,0,1:T(2,128)(2,1)S(1)} %copy.20), channel_id=1, source_target_pairs={{0,1},{1,0},{2,3},{3,2},{4,5},{5,4},{6,7},{7,6},{8,9},{9,8},{10,11... | collective-permute-start | bytes 1585160 | tf_op jit(solution)/shard_map/ppermute | solution.py:113
  87.2 9.9 %collective-permute-done.3 = bf16[2,516,256]{2,0,1:T(2,128)(2,1)S(1)} collective-permute-done((bf16[2,516,256]{2,0,1:T(2,128)(2,1)S(1)}, bf16[2,516,256]{2,0,1:T(2,128)(2,1)S(1)}, u32[]{:S(2)}, u32[]{:S(2)}) %collective-permute-start.3) | collective-permute-done | bytes 528416 | tf_op jit(solution)/shard_map/ppermute | solution.py:113
  98.6 1.5 %collective-permute-done.4 = f32[512,128]{1,0:T(8,128)S(1)} collective-permute-done((f32[512,128]{1,0:T(8,128)S(1)}, f32[512,128]{1,0:T(8,128)S(1)}, u32[]{:S(2)}, u32[]{:S(2)}) %collective-permute-start.4) | collective-permute-done | bytes 262176 | tf_op jit(solution)/shard_map/ppermute | solution.py:242
  100.6 3.5 %collective-permute-start.7 = (f32[128,128]{1,0:T(8,128)S(1)}, f32[128,128]{1,0:T(8,128)S(1)}, u32[]{:S(2)}, u32[]{:S(2)}) collective-permute-start(f32[128,128]{1,0:T(8,128)S(1)} %get-tuple-element.14), channel_id=1, source_target_pairs={{0,12},{4,0},{8,4},{12,8},{1,13},{5,1},{9,5},{13,9},{2,14},{6,2},{... | collective-permute-start | bytes 196616 | tf_op jit(solution)/shard_map/ppermute | solution.py:181
  104.1 3.0 %collective-permute-done.5 = f32[128,128]{1,0:T(8,128)S(1)} collective-permute-done((f32[128,128]{1,0:T(8,128)S(1)}, f32[128,128]{1,0:T(8,128)S(1)}, u32[]{:S(2)}, u32[]{:S(2)}) %collective-permute-start.5) | collective-permute-done | bytes 65568 | tf_op jit(solution)/shard_map/ppermute | solution.py:181
  107.0 1.9 %collective-permute-done.6 = f32[128,128]{1,0:T(8,128)S(1)} collective-permute-done((f32[128,128]{1,0:T(8,128)S(1)}, f32[128,128]{1,0:T(8,128)S(1)}, u32[]{:S(2)}, u32[]{:S(2)}) %collective-permute-start.6) | collective-permute-done | bytes 65568 | tf_op jit(solution)/shard_map/ppermute | solution.py:181
  109.0 1.2 %collective-permute-done.8 = f32[128,128]{1,0:T(8,128)S(1)} collective-permute-done((f32[128,128]{1,0:T(8,128)S(1)}, f32[128,128]{1,0:T(8,128)S(1)}, u32[]{:S(2)}, u32[]{:S(2)}) %collective-permute-start.8) | collective-permute-done | bytes 65568 | tf_op jit(solution)/shard_map/ppermute | solution.py:244
  (66 shorter events, 8.2 us)
Async XLA Ops:
  1.5 9.4 %collective-permute-start = (f32[3,256]{1,0:T(4,128)S(1)}, f32[3,256]{1,0:T(4,128)S(1)}, u32[]{:S(2)}, u32[]{:S(2)}) collective-permute-start(f32[3,256]{1,0:T(4,128)S(1)} %bitcast.89), channel_id=1, source_target_pairs={{0,4},{4,8},{8,12},{12,0},{1,5},{5,9},{9,13},{13,1},{2,6},{6,10},{... | collective-permute-start | bytes 9224 | tf_op jit(solution)/shard_map/ppermute | solution.py:181
  4.5 6.3 %collective-permute-start.1 = (f32[3,256]{1,0:T(4,128)S(1)}, f32[3,256]{1,0:T(4,128)S(1)}, u32[]{:S(2)}, u32[]{:S(2)}) collective-permute-start(f32[3,256]{1,0:T(4,128)S(1)} %bitcast.90), channel_id=1, source_target_pairs={{0,8},{4,12},{8,0},{12,4},{1,9},{5,13},{9,1},{13,5},{2,10},{6,14},... | collective-permute-start | bytes 9224 | tf_op jit(solution)/shard_map/ppermute | solution.py:181
  7.1 3.7 %collective-permute-start.2 = (f32[3,256]{1,0:T(4,128)S(1)}, f32[3,256]{1,0:T(4,128)S(1)}, u32[]{:S(2)}, u32[]{:S(2)}) collective-permute-start(f32[3,256]{1,0:T(4,128)S(1)} %bitcast.91), channel_id=1, source_target_pairs={{0,12},{4,0},{8,4},{12,8},{1,13},{5,1},{9,5},{13,9},{2,14},{6,2},{... | collective-permute-start | bytes 9224 | tf_op jit(solution)/shard_map/ppermute | solution.py:181
  26.0 4.4 %copy-start = (s32[1,2049]{1,0:T(1,128)S(1)}, s32[1,2049]{1,0:T(1,128)}, u32[]{:S(2)}) copy-start(s32[1,2049]{1,0:T(1,128)} %param.9) | copy-start | bytes 24592
  26.0 51.3 %all-to-all-start = ((f32[4,2,256,256]{3,2,1,0:T(8,128)}), f32[4,2,256,256]{3,2,1,0:T(8,128)S(1)}, u32[]{:S(2)}, u32[]{:S(2)}) async-start(f32[4,2,256,256]{3,2,1,0:T(8,128)} %copy.17), calls=%async_computation | async-start | bytes 4194304 | tf_op jit(solution)/shard_map/all_to_all | solution.py:209
  84.1 13.0 %collective-permute-start.3 = (bf16[2,516,256]{2,0,1:T(2,128)(2,1)S(1)}, bf16[2,516,256]{2,0,1:T(2,128)(2,1)S(1)}, u32[]{:S(2)}, u32[]{:S(2)}) collective-permute-start(bf16[2,516,256]{2,0,1:T(2,128)(2,1)S(1)} %copy.20), channel_id=1, source_target_pairs={{0,1},{1,0},{2,3},{3,2},{4,5},{5,4},{6,7},{7,6},{8,9},{9,8},{10,11... | collective-permute-start | bytes 1585160 | tf_op jit(solution)/shard_map/ppermute | solution.py:113
  98.5 1.6 %collective-permute-start.4 = (f32[512,128]{1,0:T(8,128)S(1)}, f32[512,128]{1,0:T(8,128)S(1)}, u32[]{:S(2)}, u32[]{:S(2)}) collective-permute-start(f32[512,128]{1,0:T(8,128)S(1)} %constant_dynamic-slice_fusion), channel_id=1, source_target_pairs={{0,2},{2,0},{1,3},{3,1},{4,6},{6,4},{5,7},{7,5},{8,10},{10,8},{9,1... | collective-permute-start | bytes 786440 | tf_op jit(solution)/shard_map/ppermute | solution.py:242
  100.2 6.8 %collective-permute-start.5 = (f32[128,128]{1,0:T(8,128)S(1)}, f32[128,128]{1,0:T(8,128)S(1)}, u32[]{:S(2)}, u32[]{:S(2)}) collective-permute-start(f32[128,128]{1,0:T(8,128)S(1)} %get-tuple-element.13), channel_id=1, source_target_pairs={{0,4},{4,8},{8,12},{12,0},{1,5},{5,9},{9,13},{13,1},{2,6},{6,10},{... | collective-permute-start | bytes 196616 | tf_op jit(solution)/shard_map/ppermute | solution.py:181
  100.3 8.6 %collective-permute-start.6 = (f32[128,128]{1,0:T(8,128)S(1)}, f32[128,128]{1,0:T(8,128)S(1)}, u32[]{:S(2)}, u32[]{:S(2)}) collective-permute-start(f32[128,128]{1,0:T(8,128)S(1)} %get-tuple-element.15), channel_id=1, source_target_pairs={{0,8},{4,12},{8,0},{12,4},{1,9},{5,13},{9,1},{13,5},{2,10},{6,14},... | collective-permute-start | bytes 196616 | tf_op jit(solution)/shard_map/ppermute | solution.py:181
  100.6 8.3 %collective-permute-start.7 = (f32[128,128]{1,0:T(8,128)S(1)}, f32[128,128]{1,0:T(8,128)S(1)}, u32[]{:S(2)}, u32[]{:S(2)}) collective-permute-start(f32[128,128]{1,0:T(8,128)S(1)} %get-tuple-element.14), channel_id=1, source_target_pairs={{0,12},{4,0},{8,4},{12,8},{1,13},{5,1},{9,5},{13,9},{2,14},{6,2},{... | collective-permute-start | bytes 196616 | tf_op jit(solution)/shard_map/ppermute | solution.py:181
  108.9 1.3 %collective-permute-start.8 = (f32[128,128]{1,0:T(8,128)S(1)}, f32[128,128]{1,0:T(8,128)S(1)}, u32[]{:S(2)}, u32[]{:S(2)}) collective-permute-start(f32[128,128]{1,0:T(8,128)S(1)} %fusion.44), channel_id=1, source_target_pairs={{0,2},{2,0},{1,3},{3,1},{4,6},{6,4},{5,7},{7,5},{8,10},{10,8},{9,1... | collective-permute-start | bytes 196616 | tf_op jit(solution)/shard_map/ppermute | solution.py:244

commit v7 on v6

--- a/solution.py
+++ b/solution.py
@@ -188,6 +188,68 @@
     return jnp.take(jnp.stack(arrived), order, axis=0)
 
 
+def packed_partials(real_in, imag_in, position, samples):
+    devices_tm, block_len, columns = real_in.shape
+    index = jnp.arange(devices_tm, dtype=jnp.int32)
+    cos_table, sin_table = phase_tables(index, index, devices_tm)
+    cos_b = cos_table[:, :, None, None]
+    sin_b = sin_table[:, :, None, None]
+    real_part = jnp.sum(cos_b * real_in[None] + sin_b * imag_in[None], axis=1)
+    imag_part = jnp.sum(cos_b * imag_in[None] - sin_b * real_in[None], axis=1)
+    local_epoch = position * block_len + jnp.arange(block_len, dtype=jnp.int32)
+    real_part, imag_part = rotate(real_part, imag_part, index, local_epoch, samples)
+    return jnp.stack([real_part, imag_part], axis=1)
+
+
+def packed_transform(gathered):
+    devices_tm, _, block_len, columns = gathered.shape
+    length = devices_tm * block_len
+    index = jnp.arange(devices_tm, dtype=jnp.int32)
+    cos_table, sin_table = phase_tables(index, index, devices_tm)
+    real_in = gathered[:, 0]
+    imag_in = gathered[:, 1]
+    cos_b = cos_table[:, :, None, None]
+    sin_b = sin_table[:, :, None, None]
+    real_part = jnp.sum(cos_b * real_in[None] + sin_b * imag_in[None], axis=1)
+    imag_part = jnp.sum(cos_b * imag_in[None] - sin_b * real_in[None], axis=1)
+    real_part, imag_part = rotate(
+        real_part, imag_part, index, jnp.arange(block_len, dtype=jnp.int32), length
+    )
+    cos_inner, sin_inner = dft_tables(block_len)
+    dims = (((1,), (1,)), ((), ()))
+
+    def mat(table, value):
+        return lax.dot_general(
+            table, value, dims, precision=lax.Precision.HIGH,
+            preferred_element_type=jnp.float32,
+        )
+
+    new_real = mat(cos_inner, real_part) + mat(sin_inner, imag_part)
+    new_imag = mat(cos_inner, imag_part) - mat(sin_inner, real_part)
+    return new_real.reshape(length, columns), new_imag.reshape(length, columns)
+
+
+def unpack_spectra(real_z, imag_z, position, samples):
+    devices_tm = lax.axis_size("tm")
+    length = real_z.shape[0]
+    kept = length // 2 + devices_tm
+    stacked = jnp.stack([real_z, imag_z])
+    backward = stacked[:, ::-1]
+    shifted = jnp.roll(backward, 1, axis=1)
+    outgoing = jnp.where(position == 0, shifted, backward)[:, :kept]
+    pairs = [(src, (devices_tm - src) % devices_tm) for src in range(devices_tm)]
+    mirror = lax.ppermute(outgoing, "tm", pairs)
+    own_real = real_z[:kept]
+    own_imag = imag_z[:kept]
+    first_real = (own_real + mirror[0]) * 0.5
+    first_imag = (own_imag - mirror[1]) * 0.5
+    second_real = (own_imag + mirror[1]) * 0.5
+    second_imag = (mirror[0] - own_real) * 0.5
+    new_real = jnp.concatenate([first_real, second_real], axis=1) / samples
+    new_imag = jnp.concatenate([first_imag, second_imag], axis=1) / samples
+    return jnp.stack([new_real.astype(jnp.bfloat16), new_imag.astype(jnp.bfloat16)])
+
+
 def body(orbit_angles, gap_mask, column_index, lat_coeffs, psd_table):
     devices_tm = lax.axis_size("tm")
     panels = lax.axis_size("panel")
@@ -205,9 +267,11 @@
         devices_tm, block_len, columns
     )
     position = lax.axis_index("tm")
-    twisted = class_partials(spread, position, samples)
+    half_cols = columns // 2
+    twisted = packed_partials(spread[..., :half_cols], spread[..., half_cols:], position, samples)
     gathered = lax.all_to_all(twisted, "tm", 0, 0, tiled=True)
-    spectra = class_spectrum(gathered, samples)
+    real_z, imag_z = packed_transform(gathered)
+    spectra = unpack_spectra(real_z, imag_z, position, samples)
     inverse_psd, fold = inverse_weights(
         psd_table[0], position, devices_tm, epochs, samples, spectra.shape[1]
     )

time: 111 us -> 107 us (0.964)
  waiting for transfers between devices: 64 us -> 44 us
  local copies, waits for them, and re-layouts: 5.24 us -> 13.1 us
  starting transfers between devices: 17 us -> 23.3 us
    all_to_all x1, waiting for transfers between devices: 46.5 us -> 24.3 us  [body(): gathered = lax.all_to_all(twisted, 'tm', 0, 0, tiled=True)]
    ppermute x6, starting transfers between devices: 10.9 us -> 16.6 us  [swap_blocks(): arrived.append(lax.ppermute(outgoing, axis, pairs))]
    rev x0 -> x1, local copies, waits for them, and re-layouts: none -> 5.11 us  [unpack_spectra(): backward = stacked[:, ::-1]]
    slice x0 -> x11, local copies, waits for them, and re-layouts: none -> 2.93 us  [the longest x1 1.06 us: unpack_spectra(): shifted = jnp.roll(backward, 1, axis=1)]
    dot_general x4, matrix products: 4.55 us -> 6.16 us  [mat(): lax.dot_general(table, value, dims, precision=lax.Precision.HIGH, preferr...]
    ppermute x6, waiting for transfers between devices: 4.83 us -> 6.05 us  [swap_blocks(): arrived.append(lax.ppermute(outgoing, axis, pairs))]
    another operation x2 -> x6, other arithmetic: 6.5 us -> 6.63 us
  transfers between devices with their start and end apart: 10 -> 11, of which waited for: 6 -> 7; matrix products, arithmetic and copies ran while one was open for 4% -> 4% of each run, Pallas kernels for 0% -> 0%
where the time goes in v7:
time: 107 us
  waiting for transfers between devices  44 us (41%)
  starting transfers between devices  23.3 us (22%)
  other arithmetic  14.1 us (13%)
  local copies, waits for them, and re-layouts  13.1 us (12%)
  matrix products  11.7 us (11%)
    all_to_all x1, waiting for transfers between devices, body(): gathered = lax.all_to_all(twisted, 'tm', 0, 0, tiled=True)  24.3 us
    ppermute x6, starting transfers between devices, swap_blocks(): arrived.append(lax.ppermute(outgoing, axis, pairs))  16.6 us
    ppermute x1, waiting for transfers between devices, panel_spectra(): blocks.append(lax.ppermute(spectra, 'panel', pairs))  10.9 us
    another operation x1, other arithmetic  6.37 us
    dot_general x4, matrix products, mat(): lax.dot_general(table, value, dims, precision=lax.Precision.HIGH, preferr...  6.16 us
    ppermute x6, waiting for transfers between devices, swap_blocks(): arrived.append(lax.ppermute(outgoing, axis, pairs))  6.05 us
    rev x1, local copies, waits for them, and re-layouts, unpack_spectra(): backward = stacked[:, ::-1]  5.11 us
    dot_general x1, matrix products, synthesize(): latitude = jnp.dot(basis_rows, masked, preferred_element_type=jnp.float32)  4.4 us
  transfers between devices with their start and end apart: 11, of which 7 were waited for; matrix products, arithmetic and copies ran while one was open for 4% of the time, Pallas kernels for 0%

profile of v7, /device:TPU:0, one launch (start us, length us, event | category | flops | bytes accessed | tf_op | source)
XLA Modules:
  0.0 106.7 jit_solution(3690998567645553461)
XLA Ops:
  1.5 3.1 %collective-permute-start = (f32[3,256]{1,0:T(4,128)S(1)}, f32[3,256]{1,0:T(4,128)S(1)}, u32[]{:S(2)}, u32[]{:S(2)}) collective-permute-start(f32[3,256]{1,0:T(4,128)S(1)} %bitcast.96), channel_id=1, source_target_pairs={{0,4},{4,8},{8,12},{12,0},{1,5},{5,9},{9,13},{13,1},{2,6},{6,10},{... | collective-permute-start | bytes 9224 | tf_op jit(solution)/shard_map/ppermute | solution.py:181
  4.6 2.6 %collective-permute-start.1 = (f32[3,256]{1,0:T(4,128)S(1)}, f32[3,256]{1,0:T(4,128)S(1)}, u32[]{:S(2)}, u32[]{:S(2)}) collective-permute-start(f32[3,256]{1,0:T(4,128)S(1)} %bitcast.97), channel_id=1, source_target_pairs={{0,8},{4,12},{8,0},{12,4},{1,9},{5,13},{9,1},{13,5},{2,10},{6,14},... | collective-permute-start | bytes 9224 | tf_op jit(solution)/shard_map/ppermute | solution.py:181
  7.2 1.3 %collective-permute-start.2 = (f32[3,256]{1,0:T(4,128)S(1)}, f32[3,256]{1,0:T(4,128)S(1)}, u32[]{:S(2)}, u32[]{:S(2)}) collective-permute-start(f32[3,256]{1,0:T(4,128)S(1)} %bitcast.98), channel_id=1, source_target_pairs={{0,12},{4,0},{8,4},{12,8},{1,13},{5,1},{9,5},{13,9},{2,14},{6,2},{... | collective-permute-start | bytes 9224 | tf_op jit(solution)/shard_map/ppermute | solution.py:181
  11.6 6.4 %cosine_convert_fusion = (bf16[1024,320]{1,0:T(8,128)(2,1)S(1)}, bf16[1024,320]{1,0:T(8,128)(2,1)S(1)}) fusion(f32[1024]{0:T(1024)S(1)} %bitcast.95), kind=kLoop, calls=%fused_computation.7 | loop fusion | flops 983040 | bytes 1314816 | tf_op jit(solution)/shard_map/convert
  18.0 4.4 %fusion = f32[1024,256]{1,0:T(8,128)S(1)} fusion(bf16[1024,320]{1,0:T(8,128)(2,1)S(1)} %get-tuple-element.34, bf16[1024,320]{1,0:T(8,128)(2,1)S(1)} %get-tuple-element.33, f32[256]{0:T(256)S(1)} %bitcast.104, f32[1024]{0:T(1024)S(1)} %bitcast.100, f32[256]{0:T(256)S(1)} %bitcast.106, f32[1024]{0:T(1024)S(1)} %bitcast.99, ...), kind=kOutput, calls=%fused_computation.17 | convolution fusion | flops 339804160 | bytes 2701056 | tf_op jit(solution)/shard_map/dot_general | solution.py:23
  23.6 1.0 copy.26
  24.6 4.3 %all-to-all-start = ((f32[4,2,256,128]{3,2,1,0:T(8,128)}), f32[4,2,256,128]{3,2,1,0:T(8,128)S(1)}, u32[]{:S(2)}, u32[]{:S(2)}) async-start(f32[4,2,256,128]{3,2,1,0:T(8,128)} %copy.26), calls=%async_computation | async-start | bytes 2097152 | tf_op jit(solution)/shard_map/all_to_all | solution.py:272
  29.0 24.3 %all-to-all-done = f32[4,2,256,128]{3,2,1,0:T(8,128)S(1)} async-done(((f32[4,2,256,128]{3,2,1,0:T(8,128)}), f32[4,2,256,128]{3,2,1,0:T(8,128)S(1)}, u32[]{:S(2)}, u32[]{:S(2)}) %all-to-all-start) | async-done | bytes 1048608 | tf_op jit(solution)/shard_map/all_to_all | solution.py:272
  54.0 1.5 %fusion.28 = f32[256,4,128]{2,0,1:T(8,128)S(1)} fusion(f32[4,256,128]{2,1,0:T(8,128)S(1)} %get-tuple-element.5, f32[4,256,128]{2,1,0:T(8,128)S(1)} %get-tuple-element.6, f32[4,256]{1,0:T(4,128)S(1)} %get-tuple-element.39, f32[4,256]{1,0:T(4,128)S(1)} %get-tuple-element.40), kind=kOutput, calls=%fused_computation.73 | convolution fusion | flops 202637312 | bytes 1581056 | tf_op jit(solution)/shard_map/dot_general | solution.py:222
  55.5 1.5 %fusion.30 = f32[256,4,128]{2,0,1:T(8,128)S(1)} fusion(f32[4,256,128]{2,1,0:T(8,128)S(1)} %get-tuple-element.6, f32[4,256,128]{2,1,0:T(8,128)S(1)} %get-tuple-element.5, f32[4,256]{1,0:T(4,128)S(1)} %get-tuple-element.39, f32[4,256]{1,0:T(4,128)S(1)} %get-tuple-element.40), kind=kOutput, calls=%fused_computation.75 | convolution fusion | flops 202637312 | bytes 1581056 | tf_op jit(solution)/shard_map/dot_general | solution.py:222
  57.1 1.5 %convolution_subtract_fusion = f32[256,4,128]{2,0,1:T(8,128)S(1)} fusion(f32[256,4,128]{2,0,1:T(8,128)S(1)} %fusion.28, f32[4,256,128]{2,1,0:T(8,128)S(1)} %get-tuple-element.6, f32[4,256,128]{2,1,0:T(8,128)S(1)} %get-tuple-element.5, f32[4,256]{1,0:T(4,128)S(1)} %get-tuple-element.39, f32[4,256]{1,0:T(4,128)S(1)} %get-tuple-element.40), kind=kOutput, calls=%fused_computation.21 | convolution fusion | flops 202768384 | bytes 2105344 | tf_op jit(solution)/shard_map/dot_general | solution.py:222
  59.0 1.5 %convolution_add_fusion = f32[256,4,128]{2,0,1:T(8,128)S(1)} fusion(f32[256,4,128]{2,0,1:T(8,128)S(1)} %fusion.30, f32[4,256,128]{2,1,0:T(8,128)S(1)} %get-tuple-element.5, f32[4,256,128]{2,1,0:T(8,128)S(1)} %get-tuple-element.6, f32[4,256]{1,0:T(4,128)S(1)} %get-tuple-element.39, f32[4,256]{1,0:T(4,128)S(1)} %get-tuple-element.40), kind=kOutput, calls=%fused_computation.22 | convolution fusion | flops 202768384 | bytes 2105344 | tf_op jit(solution)/shard_map/dot_general | solution.py:222
  61.1 5.1 %rev.6 = f32[2,1024,128]{2,1,0:T(8,128)} reverse(f32[2,1024,128]{2,1,0:T(8,128)S(1)} %pad_maximum_fusion), dimensions={1} | reverse | bytes 2097152 | tf_op jit(solution)/shard_map/rev | solution.py:237
  66.2 1.1 slice.91
  67.2 1.1 %slice_select_fusion = f32[2,516,128]{2,1,0:T(8,128)S(1)} fusion(f32[2,1024,128]{2,1,0:T(8,128)} %rev.6, f32[2,1023,128]{2,1,0:T(8,128)S(1)} %slice.91, f32[2,1,128]{2,1,0:T(1,128)S(1)} %fusion.64, pred[]{:T(512)S(6)} %eq.48), kind=kLoop, calls=%fused_computation.31 | loop fusion | flops 264192 | bytes 2105345 | tf_op jit(solution)/shard_map/jit(_where)/select_n | solution.py:239
  72.9 1.5 %collective-permute-start.4 = (bf16[2,516,256]{2,0,1:T(2,128)(2,1)S(1)}, bf16[2,516,256]{2,0,1:T(2,128)(2,1)S(1)}, u32[]{:S(2)}, u32[]{:S(2)}) collective-permute-start(bf16[2,516,256]{2,0,1:T(2,128)(2,1)S(1)} %copy.34), channel_id=1, source_target_pairs={{0,1},{1,0},{2,3},{3,2},{4,5},{5,4},{6,7},{7,6},{8,9},{9,8},{10,11... | collective-permute-start | bytes 1585160 | tf_op jit(solution)/shard_map/ppermute | solution.py:113
  75.1 10.9 %collective-permute-done.4 = bf16[2,516,256]{2,0,1:T(2,128)(2,1)S(1)} collective-permute-done((bf16[2,516,256]{2,0,1:T(2,128)(2,1)S(1)}, bf16[2,516,256]{2,0,1:T(2,128)(2,1)S(1)}, u32[]{:S(2)}, u32[]{:S(2)}) %collective-permute-start.4) | collective-permute-done | bytes 528416 | tf_op jit(solution)/shard_map/ppermute | solution.py:113
  87.4 1.5 %collective-permute-done.5 = f32[512,128]{1,0:T(8,128)S(1)} collective-permute-done((f32[512,128]{1,0:T(8,128)S(1)}, f32[512,128]{1,0:T(8,128)S(1)}, u32[]{:S(2)}, u32[]{:S(2)}) %collective-permute-start.5) | collective-permute-done | bytes 262176 | tf_op jit(solution)/shard_map/ppermute | solution.py:306
  89.0 7.3 %collective-permute-start.6 = (f32[128,128]{1,0:T(8,128)S(1)}, f32[128,128]{1,0:T(8,128)S(1)}, u32[]{:S(2)}, u32[]{:S(2)}) collective-permute-start(f32[128,128]{1,0:T(8,128)S(1)} %get-tuple-element.21), channel_id=1, source_target_pairs={{0,4},{4,8},{8,12},{12,0},{1,5},{5,9},{9,13},{13,1},{2,6},{6,10},{... | collective-permute-start | bytes 196616 | tf_op jit(solution)/shard_map/ppermute | solution.py:181
  96.2 1.9 %collective-permute-start.8 = (f32[128,128]{1,0:T(8,128)S(1)}, f32[128,128]{1,0:T(8,128)S(1)}, u32[]{:S(2)}, u32[]{:S(2)}) collective-permute-start(f32[128,128]{1,0:T(8,128)S(1)} %get-tuple-element.22), channel_id=1, source_target_pairs={{0,12},{4,0},{8,4},{12,8},{1,13},{5,1},{9,5},{13,9},{2,14},{6,2},{... | collective-permute-start | bytes 196616 | tf_op jit(solution)/shard_map/ppermute | solution.py:181
  98.6 2.0 %collective-permute-done.6 = f32[128,128]{1,0:T(8,128)S(1)} collective-permute-done((f32[128,128]{1,0:T(8,128)S(1)}, f32[128,128]{1,0:T(8,128)S(1)}, u32[]{:S(2)}, u32[]{:S(2)}) %collective-permute-start.6) | collective-permute-done | bytes 65568 | tf_op jit(solution)/shard_map/ppermute | solution.py:181
  100.6 0.9 collective-permute-done.8
  101.5 3.1 %collective-permute-done.7 = f32[128,128]{1,0:T(8,128)S(1)} collective-permute-done((f32[128,128]{1,0:T(8,128)S(1)}, f32[128,128]{1,0:T(8,128)S(1)}, u32[]{:S(2)}, u32[]{:S(2)}) %collective-permute-start.7) | collective-permute-done | bytes 65568 | tf_op jit(solution)/shard_map/ppermute | solution.py:181
  104.7 1.2 %collective-permute-done.9 = f32[128,128]{1,0:T(8,128)S(1)} collective-permute-done((f32[128,128]{1,0:T(8,128)S(1)}, f32[128,128]{1,0:T(8,128)S(1)}, u32[]{:S(2)}, u32[]{:S(2)}) %collective-permute-start.9) | collective-permute-done | bytes 65568 | tf_op jit(solution)/shard_map/ppermute | solution.py:308
  (89 shorter events, 15.0 us)
Async XLA Ops:
  0.0 18.0 %copy-start.2 = (bf16[1,640,256]{2,1,0:T(8,128)(2,1)S(1)}, bf16[1,640,256]{2,1,0:T(8,128)(2,1)}, u32[]{:S(2)}) copy-start(bf16[1,640,256]{2,1,0:T(8,128)(2,1)} %param.8) | copy-start | bytes 983044
  1.5 9.4 %collective-permute-start = (f32[3,256]{1,0:T(4,128)S(1)}, f32[3,256]{1,0:T(4,128)S(1)}, u32[]{:S(2)}, u32[]{:S(2)}) collective-permute-start(f32[3,256]{1,0:T(4,128)S(1)} %bitcast.96), channel_id=1, source_target_pairs={{0,4},{4,8},{8,12},{12,0},{1,5},{5,9},{9,13},{13,1},{2,6},{6,10},{... | collective-permute-start | bytes 9224 | tf_op jit(solution)/shard_map/ppermute | solution.py:181
  4.6 6.3 %collective-permute-start.1 = (f32[3,256]{1,0:T(4,128)S(1)}, f32[3,256]{1,0:T(4,128)S(1)}, u32[]{:S(2)}, u32[]{:S(2)}) collective-permute-start(f32[3,256]{1,0:T(4,128)S(1)} %bitcast.97), channel_id=1, source_target_pairs={{0,8},{4,12},{8,0},{12,4},{1,9},{5,13},{9,1},{13,5},{2,10},{6,14},... | collective-permute-start | bytes 9224 | tf_op jit(solution)/shard_map/ppermute | solution.py:181
  7.2 3.7 %collective-permute-start.2 = (f32[3,256]{1,0:T(4,128)S(1)}, f32[3,256]{1,0:T(4,128)S(1)}, u32[]{:S(2)}, u32[]{:S(2)}) collective-permute-start(f32[3,256]{1,0:T(4,128)S(1)} %bitcast.98), channel_id=1, source_target_pairs={{0,12},{4,0},{8,4},{12,8},{1,13},{5,1},{9,5},{13,9},{2,14},{6,2},{... | collective-permute-start | bytes 9224 | tf_op jit(solution)/shard_map/ppermute | solution.py:181
  24.6 28.7 %all-to-all-start = ((f32[4,2,256,128]{3,2,1,0:T(8,128)}), f32[4,2,256,128]{3,2,1,0:T(8,128)S(1)}, u32[]{:S(2)}, u32[]{:S(2)}) async-start(f32[4,2,256,128]{3,2,1,0:T(8,128)} %copy.26), calls=%async_computation | async-start | bytes 2097152 | tf_op jit(solution)/shard_map/all_to_all | solution.py:272
  60.5 10.2 %copy-start = (f32[256,4,128]{2,0,1:T(8,128)}, f32[256,4,128]{2,0,1:T(8,128)S(1)}, u32[]{:S(2)}) copy-start(f32[256,4,128]{2,0,1:T(8,128)S(1)} %convolution_add_fusion) | copy-start | bytes 1572868
  68.4 1.0 copy-start.1
  68.6 3.2 %collective-permute-start.3 = (f32[2,516,128]{2,0,1:T(2,128)S(1)}, f32[2,516,128]{2,0,1:T(2,128)S(1)}, u32[]{:S(2)}, u32[]{:S(2)}) collective-permute-start(f32[2,516,128]{2,0,1:T(2,128)S(1)} %copy.30), channel_id=1, source_target_pairs={{0,0},{4,12},{8,8},{12,4},{1,1},{5,13},{9,9},{13,5},{2,2},{6,14},{... | collective-permute-start | bytes 1585160 | tf_op jit(solution)/shard_map/ppermute | solution.py:241
  70.7 1.0 slice-start
  72.9 13.0 %collective-permute-start.4 = (bf16[2,516,256]{2,0,1:T(2,128)(2,1)S(1)}, bf16[2,516,256]{2,0,1:T(2,128)(2,1)S(1)}, u32[]{:S(2)}, u32[]{:S(2)}) collective-permute-start(bf16[2,516,256]{2,0,1:T(2,128)(2,1)S(1)} %copy.34), channel_id=1, source_target_pairs={{0,1},{1,0},{2,3},{3,2},{4,5},{5,4},{6,7},{7,6},{8,9},{9,8},{10,11... | collective-permute-start | bytes 1585160 | tf_op jit(solution)/shard_map/ppermute | solution.py:113
  87.3 1.6 %collective-permute-start.5 = (f32[512,128]{1,0:T(8,128)S(1)}, f32[512,128]{1,0:T(8,128)S(1)}, u32[]{:S(2)}, u32[]{:S(2)}) collective-permute-start(f32[512,128]{1,0:T(8,128)S(1)} %constant_dynamic-slice_fusion), channel_id=1, source_target_pairs={{0,2},{2,0},{1,3},{3,1},{4,6},{6,4},{5,7},{7,5},{8,10},{10,8},{9,1... | collective-permute-start | bytes 786440 | tf_op jit(solution)/shard_map/ppermute | solution.py:306
  89.0 11.6 %collective-permute-start.6 = (f32[128,128]{1,0:T(8,128)S(1)}, f32[128,128]{1,0:T(8,128)S(1)}, u32[]{:S(2)}, u32[]{:S(2)}) collective-permute-start(f32[128,128]{1,0:T(8,128)S(1)} %get-tuple-element.21), channel_id=1, source_target_pairs={{0,4},{4,8},{8,12},{12,0},{1,5},{5,9},{9,13},{13,1},{2,6},{6,10},{... | collective-permute-start | bytes 196616 | tf_op jit(solution)/shard_map/ppermute | solution.py:181
  96.2 5.3 %collective-permute-start.8 = (f32[128,128]{1,0:T(8,128)S(1)}, f32[128,128]{1,0:T(8,128)S(1)}, u32[]{:S(2)}, u32[]{:S(2)}) collective-permute-start(f32[128,128]{1,0:T(8,128)S(1)} %get-tuple-element.22), channel_id=1, source_target_pairs={{0,12},{4,0},{8,4},{12,8},{1,13},{5,1},{9,5},{13,9},{2,14},{6,2},{... | collective-permute-start | bytes 196616 | tf_op jit(solution)/shard_map/ppermute | solution.py:181
  98.1 6.5 %collective-permute-start.7 = (f32[128,128]{1,0:T(8,128)S(1)}, f32[128,128]{1,0:T(8,128)S(1)}, u32[]{:S(2)}, u32[]{:S(2)}) collective-permute-start(f32[128,128]{1,0:T(8,128)S(1)} %get-tuple-element.23), channel_id=1, source_target_pairs={{0,8},{4,12},{8,0},{12,4},{1,9},{5,13},{9,1},{13,5},{2,10},{6,14},... | collective-permute-start | bytes 196616 | tf_op jit(solution)/shard_map/ppermute | solution.py:181
  104.6 1.3 %collective-permute-start.9 = (f32[128,128]{1,0:T(8,128)S(1)}, f32[128,128]{1,0:T(8,128)S(1)}, u32[]{:S(2)}, u32[]{:S(2)}) collective-permute-start(f32[128,128]{1,0:T(8,128)S(1)} %fusion.43), channel_id=1, source_target_pairs={{0,2},{2,0},{1,3},{3,1},{4,6},{6,4},{5,7},{7,5},{8,10},{10,8},{9,1... | collective-permute-start | bytes 196616 | tf_op jit(solution)/shard_map/ppermute | solution.py:308

commit v8 on v7

--- a/solution.py
+++ b/solution.py
@@ -215,7 +215,11 @@
     real_part, imag_part = rotate(
         real_part, imag_part, index, jnp.arange(block_len, dtype=jnp.int32), length
     )
-    cos_inner, sin_inner = dft_tables(block_len)
+    kept = block_len // 2 + 1
+    rows = jnp.arange(kept, dtype=jnp.int32)
+    cols = jnp.arange(block_len, dtype=jnp.int32)
+    cos_own, sin_own = phase_tables(rows, cols, block_len)
+    cos_far, sin_far = phase_tables(block_len - 1 - rows, cols, block_len)
     dims = (((1,), (1,)), ((), ()))
 
     def mat(table, value):
@@ -224,23 +228,24 @@
             preferred_element_type=jnp.float32,
         )
 
-    new_real = mat(cos_inner, real_part) + mat(sin_inner, imag_part)
-    new_imag = mat(cos_inner, imag_part) - mat(sin_inner, real_part)
-    return new_real.reshape(length, columns), new_imag.reshape(length, columns)
-
-
-def unpack_spectra(real_z, imag_z, position, samples):
+    def apply(cos_table, sin_table, real_in, imag_in):
+        new_real = mat(cos_table, real_in) + mat(sin_table, imag_in)
+        new_imag = mat(cos_table, imag_in) - mat(sin_table, real_in)
+        return jnp.stack([new_real, new_imag]).reshape(2, kept * devices_tm, columns)
+
+    own = apply(cos_own, sin_own, real_part, imag_part)
+    far = apply(cos_far, sin_far, real_part[::-1], imag_part[::-1])
+    return own, far
+
+
+def unpack_spectra(own, far, position, samples):
     devices_tm = lax.axis_size("tm")
-    length = real_z.shape[0]
-    kept = length // 2 + devices_tm
-    stacked = jnp.stack([real_z, imag_z])
-    backward = stacked[:, ::-1]
-    shifted = jnp.roll(backward, 1, axis=1)
-    outgoing = jnp.where(position == 0, shifted, backward)[:, :kept]
+    shifted = jnp.concatenate([own[:, :1], far[:, :-1]], axis=1)
+    outgoing = jnp.where(position == 0, shifted, far)
     pairs = [(src, (devices_tm - src) % devices_tm) for src in range(devices_tm)]
     mirror = lax.ppermute(outgoing, "tm", pairs)
-    own_real = real_z[:kept]
-    own_imag = imag_z[:kept]
+    own_real = own[0]
+    own_imag = own[1]
     first_real = (own_real + mirror[0]) * 0.5
     first_imag = (own_imag - mirror[1]) * 0.5
     second_real = (own_imag + mirror[1]) * 0.5
@@ -270,8 +275,8 @@
     half_cols = columns // 2
     twisted = packed_partials(spread[..., :half_cols], spread[..., half_cols:], position, samples)
     gathered = lax.all_to_all(twisted, "tm", 0, 0, tiled=True)
-    real_z, imag_z = packed_transform(gathered)
-    spectra = unpack_spectra(real_z, imag_z, position, samples)
+    own, far = packed_transform(gathered)
+    spectra = unpack_spectra(own, far, position, samples)
     inverse_psd, fold = inverse_weights(
         psd_table[0], position, devices_tm, epochs, samples, spectra.shape[1]
     )

time: 107 us -> 99.8 us (0.933)
  local copies, waits for them, and re-layouts: 13.1 us -> 5.86 us
  starting transfers between devices: 23.3 us -> 24.5 us
    rev x1 -> x0, local copies, waits for them, and re-layouts: 5.11 us -> none  [unpack_spectra(): backward = stacked[:, ::-1]]
    slice x9 -> x0, local copies, waits for them, and re-layouts: 2.45 us -> none  [the longest x1 1.06 us: unpack_spectra(): shifted = jnp.roll(backward, 1, axis=1)]
    ppermute x6, starting transfers between devices: 16.6 us -> 17.9 us  [swap_blocks(): arrived.append(lax.ppermute(outgoing, axis, pairs))]
    dot_general x4 -> x8, matrix products: 6.16 us -> 6.78 us  [mat(): lax.dot_general(table, value, dims, precision=lax.Precision.HIGH, preferr...]
    another operation x4 -> x1, other arithmetic: 6.51 us -> 6.37 us
where the time goes in v8:
time: 99.8 us; the launch traced here: 99.5 us
  waiting for transfers between devices  43.1 us (43%)
  starting transfers between devices  24.5 us (25%)
  other arithmetic  13.2 us (13%)
  matrix products  12.3 us (12%)
  local copies, waits for them, and re-layouts  5.86 us (6%)
    all_to_all x1, waiting for transfers between devices, body(): gathered = lax.all_to_all(twisted, 'tm', 0, 0, tiled=True)  24.3 us
    ppermute x6, starting transfers between devices, swap_blocks(): arrived.append(lax.ppermute(outgoing, axis, pairs))  17.9 us
    ppermute x1, waiting for transfers between devices, panel_spectra(): blocks.append(lax.ppermute(spectra, 'panel', pairs))  10.8 us
    dot_general x8, matrix products, mat(): lax.dot_general(table, value, dims, precision=lax.Precision.HIGH, preferr...  6.78 us
    another operation x1, other arithmetic  6.37 us
    ppermute x6, waiting for transfers between devices, swap_blocks(): arrived.append(lax.ppermute(outgoing, axis, pairs))  5.17 us
    dot_general x1, matrix products, synthesize(): latitude = jnp.dot(basis_rows, masked, preferred_element_type=jnp.float32)  4.4 us
    all_to_all x1, starting transfers between devices, body(): gathered = lax.all_to_all(twisted, 'tm', 0, 0, tiled=True)  4.28 us
  transfers between devices with their start and end apart: 11, of which 7 were waited for; matrix products, arithmetic and copies ran while one was open for 4% of the time, Pallas kernels for 0%

profile of v8, /device:TPU:0, one launch (start us, length us, event | category | flops | bytes accessed | tf_op | source)
XLA Modules:
  0.0 99.5 jit_solution(4499085460040357715)
XLA Ops:
  1.5 3.1 %collective-permute-start = (f32[3,256]{1,0:T(4,128)S(1)}, f32[3,256]{1,0:T(4,128)S(1)}, u32[]{:S(2)}, u32[]{:S(2)}) collective-permute-start(f32[3,256]{1,0:T(4,128)S(1)} %bitcast.108), channel_id=1, source_target_pairs={{0,4},{4,8},{8,12},{12,0},{1,5},{5,9},{9,13},{13,1},{2,6},{6,10},{... | collective-permute-start | bytes 9224 | tf_op jit(solution)/shard_map/ppermute | solution.py:181
  4.6 2.6 %collective-permute-start.1 = (f32[3,256]{1,0:T(4,128)S(1)}, f32[3,256]{1,0:T(4,128)S(1)}, u32[]{:S(2)}, u32[]{:S(2)}) collective-permute-start(f32[3,256]{1,0:T(4,128)S(1)} %bitcast.109), channel_id=1, source_target_pairs={{0,8},{4,12},{8,0},{12,4},{1,9},{5,13},{9,1},{13,5},{2,10},{6,14},... | collective-permute-start | bytes 9224 | tf_op jit(solution)/shard_map/ppermute | solution.py:181
  7.2 1.3 %collective-permute-start.2 = (f32[3,256]{1,0:T(4,128)S(1)}, f32[3,256]{1,0:T(4,128)S(1)}, u32[]{:S(2)}, u32[]{:S(2)}) collective-permute-start(f32[3,256]{1,0:T(4,128)S(1)} %bitcast.110), channel_id=1, source_target_pairs={{0,12},{4,0},{8,4},{12,8},{1,13},{5,1},{9,5},{13,9},{2,14},{6,2},{... | collective-permute-start | bytes 9224 | tf_op jit(solution)/shard_map/ppermute | solution.py:181
  11.6 6.4 %cosine_convert_fusion = (bf16[1024,320]{1,0:T(8,128)(2,1)S(1)}, bf16[1024,320]{1,0:T(8,128)(2,1)S(1)}) fusion(f32[1024]{0:T(1024)S(1)} %bitcast.107), kind=kLoop, calls=%fused_computation.7 | loop fusion | flops 983040 | bytes 1314816 | tf_op jit(solution)/shard_map/convert
  18.0 4.4 %fusion = f32[1024,256]{1,0:T(8,128)S(1)} fusion(bf16[1024,320]{1,0:T(8,128)(2,1)S(1)} %get-tuple-element.36, bf16[1024,320]{1,0:T(8,128)(2,1)S(1)} %get-tuple-element.35, f32[256]{0:T(256)S(1)} %bitcast.116, f32[1024]{0:T(1024)S(1)} %bitcast.112, f32[256]{0:T(256)S(1)} %bitcast.118, f32[1024]{0:T(1024)S(1)} %bitcast.111, ...), kind=kOutput, calls=%fused_computation.12 | convolution fusion | flops 339804160 | bytes 2701056 | tf_op jit(solution)/shard_map/dot_general | solution.py:23
  23.6 1.0 %copy.26 = f32[4,2,256,128]{3,2,1,0:T(8,128)} copy(f32[4,2,256,128]{3,2,0,1:T(8,128)S(1)} %pad_maximum_fusion) | data formatting | bytes 2097152 | tf_op jit(solution)/shard_map/stack | solution.py:201
  24.6 4.3 %all-to-all-start = ((f32[4,2,256,128]{3,2,1,0:T(8,128)}), f32[4,2,256,128]{3,2,1,0:T(8,128)S(1)}, u32[]{:S(2)}, u32[]{:S(2)}) async-start(f32[4,2,256,128]{3,2,1,0:T(8,128)} %copy.26), calls=%async_computation | async-start | bytes 2097152 | tf_op jit(solution)/shard_map/all_to_all | solution.py:277
  28.9 24.3 %all-to-all-done = f32[4,2,256,128]{3,2,1,0:T(8,128)S(1)} async-done(((f32[4,2,256,128]{3,2,1,0:T(8,128)}), f32[4,2,256,128]{3,2,1,0:T(8,128)S(1)}, u32[]{:S(2)}, u32[]{:S(2)}) %all-to-all-start) | async-done | bytes 1048608 | tf_op jit(solution)/shard_map/all_to_all | solution.py:277
  54.3 0.8 fusion.39
  55.1 0.9 fusion.33
  56.0 0.9 fusion.35
  56.9 0.8 fusion.41
  57.7 0.8 convolution_subtract_fusion.1
  58.7 0.9 convolution_subtract_fusion
  59.8 0.9 convolution_add_fusion
  60.9 0.8 convolution_add_fusion.1
  65.4 1.6 %collective-permute-start.4 = (bf16[2,516,256]{2,0,1:T(2,128)(2,1)S(1)}, bf16[2,516,256]{2,0,1:T(2,128)(2,1)S(1)}, u32[]{:S(2)}, u32[]{:S(2)}) collective-permute-start(bf16[2,516,256]{2,0,1:T(2,128)(2,1)S(1)} %copy.34), channel_id=1, source_target_pairs={{0,1},{1,0},{2,3},{3,2},{4,5},{5,4},{6,7},{7,6},{8,9},{9,8},{10,11... | collective-permute-start | bytes 1585160 | tf_op jit(solution)/shard_map/ppermute | solution.py:113
  67.6 10.8 %collective-permute-done.4 = bf16[2,516,256]{2,0,1:T(2,128)(2,1)S(1)} collective-permute-done((bf16[2,516,256]{2,0,1:T(2,128)(2,1)S(1)}, bf16[2,516,256]{2,0,1:T(2,128)(2,1)S(1)}, u32[]{:S(2)}, u32[]{:S(2)}) %collective-permute-start.4) | collective-permute-done | bytes 528416 | tf_op jit(solution)/shard_map/ppermute | solution.py:113
  79.9 1.5 %collective-permute-done.5 = f32[512,128]{1,0:T(8,128)S(1)} collective-permute-done((f32[512,128]{1,0:T(8,128)S(1)}, f32[512,128]{1,0:T(8,128)S(1)}, u32[]{:S(2)}, u32[]{:S(2)}) %collective-permute-start.5) | collective-permute-done | bytes 262176 | tf_op jit(solution)/shard_map/ppermute | solution.py:311
  81.5 8.4 %collective-permute-start.6 = (f32[128,128]{1,0:T(8,128)S(1)}, f32[128,128]{1,0:T(8,128)S(1)}, u32[]{:S(2)}, u32[]{:S(2)}) collective-permute-start(f32[128,128]{1,0:T(8,128)S(1)} %get-tuple-element.23), channel_id=1, source_target_pairs={{0,4},{4,8},{8,12},{12,0},{1,5},{5,9},{9,13},{13,1},{2,6},{6,10},{... | collective-permute-start | bytes 196616 | tf_op jit(solution)/shard_map/ppermute | solution.py:181
  89.9 2.4 %collective-permute-start.7 = (f32[128,128]{1,0:T(8,128)S(1)}, f32[128,128]{1,0:T(8,128)S(1)}, u32[]{:S(2)}, u32[]{:S(2)}) collective-permute-start(f32[128,128]{1,0:T(8,128)S(1)} %get-tuple-element.25), channel_id=1, source_target_pairs={{0,8},{4,12},{8,0},{12,4},{1,9},{5,13},{9,1},{13,5},{2,10},{6,14},... | collective-permute-start | bytes 196616 | tf_op jit(solution)/shard_map/ppermute | solution.py:181
  92.3 2.3 %collective-permute-done.6 = f32[128,128]{1,0:T(8,128)S(1)} collective-permute-done((f32[128,128]{1,0:T(8,128)S(1)}, f32[128,128]{1,0:T(8,128)S(1)}, u32[]{:S(2)}, u32[]{:S(2)}) %collective-permute-start.6) | collective-permute-done | bytes 65568 | tf_op jit(solution)/shard_map/ppermute | solution.py:181
  94.6 2.3 %collective-permute-done.7 = f32[128,128]{1,0:T(8,128)S(1)} collective-permute-done((f32[128,128]{1,0:T(8,128)S(1)}, f32[128,128]{1,0:T(8,128)S(1)}, u32[]{:S(2)}, u32[]{:S(2)}) %collective-permute-start.7) | collective-permute-done | bytes 65568 | tf_op jit(solution)/shard_map/ppermute | solution.py:181
  97.6 1.2 %collective-permute-done.9 = f32[128,128]{1,0:T(8,128)S(1)} collective-permute-done((f32[128,128]{1,0:T(8,128)S(1)}, f32[128,128]{1,0:T(8,128)S(1)}, u32[]{:S(2)}, u32[]{:S(2)}) %collective-permute-start.9) | collective-permute-done | bytes 65568 | tf_op jit(solution)/shard_map/ppermute | solution.py:313
  (89 shorter events, 14.2 us)
Async XLA Ops:
  0.0 18.0 %copy-start.1 = (bf16[1,640,256]{2,1,0:T(8,128)(2,1)S(1)}, bf16[1,640,256]{2,1,0:T(8,128)(2,1)}, u32[]{:S(2)}) copy-start(bf16[1,640,256]{2,1,0:T(8,128)(2,1)} %param.8) | copy-start | bytes 983044
  1.5 9.4 %collective-permute-start = (f32[3,256]{1,0:T(4,128)S(1)}, f32[3,256]{1,0:T(4,128)S(1)}, u32[]{:S(2)}, u32[]{:S(2)}) collective-permute-start(f32[3,256]{1,0:T(4,128)S(1)} %bitcast.108), channel_id=1, source_target_pairs={{0,4},{4,8},{8,12},{12,0},{1,5},{5,9},{9,13},{13,1},{2,6},{6,10},{... | collective-permute-start | bytes 9224 | tf_op jit(solution)/shard_map/ppermute | solution.py:181
  4.6 6.3 %collective-permute-start.1 = (f32[3,256]{1,0:T(4,128)S(1)}, f32[3,256]{1,0:T(4,128)S(1)}, u32[]{:S(2)}, u32[]{:S(2)}) collective-permute-start(f32[3,256]{1,0:T(4,128)S(1)} %bitcast.109), channel_id=1, source_target_pairs={{0,8},{4,12},{8,0},{12,4},{1,9},{5,13},{9,1},{13,5},{2,10},{6,14},... | collective-permute-start | bytes 9224 | tf_op jit(solution)/shard_map/ppermute | solution.py:181
  7.2 3.7 %collective-permute-start.2 = (f32[3,256]{1,0:T(4,128)S(1)}, f32[3,256]{1,0:T(4,128)S(1)}, u32[]{:S(2)}, u32[]{:S(2)}) collective-permute-start(f32[3,256]{1,0:T(4,128)S(1)} %bitcast.110), channel_id=1, source_target_pairs={{0,12},{4,0},{8,4},{12,8},{1,13},{5,1},{9,5},{13,9},{2,14},{6,2},{... | collective-permute-start | bytes 9224 | tf_op jit(solution)/shard_map/ppermute | solution.py:181
  24.6 28.7 %all-to-all-start = ((f32[4,2,256,128]{3,2,1,0:T(8,128)}), f32[4,2,256,128]{3,2,1,0:T(8,128)S(1)}, u32[]{:S(2)}, u32[]{:S(2)}) async-start(f32[4,2,256,128]{3,2,1,0:T(8,128)} %copy.26), calls=%async_computation | async-start | bytes 2097152 | tf_op jit(solution)/shard_map/all_to_all | solution.py:277
  62.0 1.0 %copy-start = (s32[1,2049]{1,0:T(1,128)S(1)}, s32[1,2049]{1,0:T(1,128)}, u32[]{:S(2)}) copy-start(s32[1,2049]{1,0:T(1,128)} %param.9) | copy-start | bytes 24592
  62.3 2.0 %collective-permute-start.3 = (f32[2,516,128]{2,0,1:T(2,128)S(1)}, f32[2,516,128]{2,0,1:T(2,128)S(1)}, u32[]{:S(2)}, u32[]{:S(2)}) collective-permute-start(f32[2,516,128]{2,0,1:T(2,128)S(1)} %copy.31), channel_id=1, source_target_pairs={{0,0},{4,12},{8,8},{12,4},{1,1},{5,13},{9,9},{13,5},{2,2},{6,14},{... | collective-permute-start | bytes 1585160 | tf_op jit(solution)/shard_map/ppermute | solution.py:246
  65.4 13.0 %collective-permute-start.4 = (bf16[2,516,256]{2,0,1:T(2,128)(2,1)S(1)}, bf16[2,516,256]{2,0,1:T(2,128)(2,1)S(1)}, u32[]{:S(2)}, u32[]{:S(2)}) collective-permute-start(bf16[2,516,256]{2,0,1:T(2,128)(2,1)S(1)} %copy.34), channel_id=1, source_target_pairs={{0,1},{1,0},{2,3},{3,2},{4,5},{5,4},{6,7},{7,6},{8,9},{9,8},{10,11... | collective-permute-start | bytes 1585160 | tf_op jit(solution)/shard_map/ppermute | solution.py:113
  79.8 1.6 %collective-permute-start.5 = (f32[512,128]{1,0:T(8,128)S(1)}, f32[512,128]{1,0:T(8,128)S(1)}, u32[]{:S(2)}, u32[]{:S(2)}) collective-permute-start(f32[512,128]{1,0:T(8,128)S(1)} %constant_dynamic-slice_fusion), channel_id=1, source_target_pairs={{0,2},{2,0},{1,3},{3,1},{4,6},{6,4},{5,7},{7,5},{8,10},{10,8},{9,1... | collective-permute-start | bytes 786440 | tf_op jit(solution)/shard_map/ppermute | solution.py:311
  81.5 13.2 %collective-permute-start.6 = (f32[128,128]{1,0:T(8,128)S(1)}, f32[128,128]{1,0:T(8,128)S(1)}, u32[]{:S(2)}, u32[]{:S(2)}) collective-permute-start(f32[128,128]{1,0:T(8,128)S(1)} %get-tuple-element.23), channel_id=1, source_target_pairs={{0,4},{4,8},{8,12},{12,0},{1,5},{5,9},{9,13},{13,1},{2,6},{6,10},{... | collective-permute-start | bytes 196616 | tf_op jit(solution)/shard_map/ppermute | solution.py:181
  89.9 7.1 %collective-permute-start.7 = (f32[128,128]{1,0:T(8,128)S(1)}, f32[128,128]{1,0:T(8,128)S(1)}, u32[]{:S(2)}, u32[]{:S(2)}) collective-permute-start(f32[128,128]{1,0:T(8,128)S(1)} %get-tuple-element.25), channel_id=1, source_target_pairs={{0,8},{4,12},{8,0},{12,4},{1,9},{5,13},{9,1},{13,5},{2,10},{6,14},... | collective-permute-start | bytes 196616 | tf_op jit(solution)/shard_map/ppermute | solution.py:181
  92.2 5.2 %collective-permute-start.8 = (f32[128,128]{1,0:T(8,128)S(1)}, f32[128,128]{1,0:T(8,128)S(1)}, u32[]{:S(2)}, u32[]{:S(2)}) collective-permute-start(f32[128,128]{1,0:T(8,128)S(1)} %get-tuple-element.24), channel_id=1, source_target_pairs={{0,12},{4,0},{8,4},{12,8},{1,13},{5,1},{9,5},{13,9},{2,14},{6,2},{... | collective-permute-start | bytes 196616 | tf_op jit(solution)/shard_map/ppermute | solution.py:181
  97.5 1.3 %collective-permute-start.9 = (f32[128,128]{1,0:T(8,128)S(1)}, f32[128,128]{1,0:T(8,128)S(1)}, u32[]{:S(2)}, u32[]{:S(2)}) collective-permute-start(f32[128,128]{1,0:T(8,128)S(1)} %fusion.62), channel_id=1, source_target_pairs={{0,2},{2,0},{1,3},{3,1},{4,6},{6,4},{5,7},{7,5},{8,10},{10,8},{9,1... | collective-permute-start | bytes 196616 | tf_op jit(solution)/shard_map/ppermute | solution.py:313

commit v9 on v8

--- a/solution.py
+++ b/solution.py
@@ -8,13 +8,45 @@
 SPLIT = 64
 
 
+def rounding_error(value, factor, product):
+    high = lax.reduce_precision(value, exponent_bits=8, mantissa_bits=11)
+    low = value - high
+    return (product - high * factor) - low * factor
+
+
+def colatitude_basis(colatitude, terms):
+    wavenumbers = jnp.arange(terms, dtype=jnp.float32)
+    theta = colatitude[:, None]
+    phases = lax.optimization_barrier(theta * wavenumbers[None, :])
+    if terms % 16 != 0:
+        return jnp.concatenate([jnp.cos(phases), jnp.sin(phases)], axis=1)
+    groups = terms // 16
+    coarse = jnp.arange(groups, dtype=jnp.float32) * 16.0
+    fine = jnp.arange(16, dtype=jnp.float32)
+    phase_a = lax.optimization_barrier(theta * coarse[None, :])
+    phase_b = lax.optimization_barrier(theta * fine[None, :])
+    count = colatitude.shape[0]
+    delta = (
+        rounding_error(theta, wavenumbers[None, :], phases).reshape(count, groups, 16)
+        - rounding_error(theta, coarse[None, :], phase_a)[:, :, None]
+        - rounding_error(theta, fine[None, :], phase_b)[:, None, :]
+    )
+    cos_a = jnp.cos(phase_a)[:, :, None]
+    sin_a = jnp.sin(phase_a)[:, :, None]
+    cos_b = jnp.cos(phase_b)[:, None, :]
+    sin_b = jnp.sin(phase_b)[:, None, :]
+    cos_sum = cos_a * cos_b - sin_a * sin_b
+    sin_sum = sin_a * cos_b + cos_a * sin_b
+    cos_k = (cos_sum - delta * sin_sum).reshape(count, terms)
+    sin_k = (sin_sum + delta * cos_sum).reshape(count, terms)
+    return jnp.concatenate([cos_k, sin_k], axis=1)
+
+
 def synthesize(angles, keep_rows, column_index, coeffs):
     terms_lat = coeffs.shape[0] // 2
     colatitude = angles[0]
     longit = angles[1]
-    wavenumbers = jnp.arange(terms_lat, dtype=jnp.float32)
-    phases = colatitude[:, None] * wavenumbers[None, :]
-    basis_rows = jnp.concatenate([jnp.cos(phases), jnp.sin(phases)], axis=1).astype(jnp.bfloat16)
+    basis_rows = colatitude_basis(colatitude, terms_lat).astype(jnp.bfloat16)
     degree = column_index[0]
     orders = column_index[1]
     levels = jnp.arange(2 * terms_lat, dtype=jnp.int32) % terms_lat
@@ -229,8 +261,11 @@
         )
 
     def apply(cos_table, sin_table, real_in, imag_in):
-        new_real = mat(cos_table, real_in) + mat(sin_table, imag_in)
-        new_imag = mat(cos_table, imag_in) - mat(sin_table, real_in)
+        table = jnp.concatenate([cos_table, sin_table], axis=0)
+        from_real = mat(table, real_in)
+        from_imag = mat(table, imag_in)
+        new_real = from_real[:kept] + from_imag[kept:]
+        new_imag = from_imag[:kept] - from_real[kept:]
         return jnp.stack([new_real, new_imag]).reshape(2, kept * devices_tm, columns)
 
     own = apply(cos_own, sin_own, real_part, imag_part)

time: 99.8 us -> 91.4 us (0.916)
  matrix products: 12.3 us -> 8.23 us
  other arithmetic: 13.2 us -> 9.73 us
  waiting for transfers between devices: 43.1 us -> 41.9 us
    another operation x1, other arithmetic: 6.37 us -> 0.73 us
    dot_general x8 -> x4, matrix products: 6.78 us -> 2.73 us  [mat(): lax.dot_general(table, value, dims, precision=lax.Precision.HIGH, preferr...]
    all_to_all x1, waiting for transfers between devices: 24.3 us -> 23.1 us  [body(): gathered = lax.all_to_all(twisted, 'tm', 0, 0, tiled=True)]
  transfers between devices with their start and end apart: 11 -> 11, of which waited for: 7 -> 7; matrix products, arithmetic and copies ran while one was open for 4% -> 6% of each run, Pallas kernels for 0% -> 0%
where the time goes in v9:
time: 91.4 us; the launch traced here: 91 us
  waiting for transfers between devices  41.9 us (46%)
  starting transfers between devices  24.5 us (27%)
  other arithmetic  9.73 us (11%)
  matrix products  8.23 us (9%)
  local copies, waits for them, and re-layouts  6.05 us (7%)
    all_to_all x1, waiting for transfers between devices, body(): gathered = lax.all_to_all(twisted, 'tm', 0, 0, tiled=True)  23.1 us
    ppermute x6, starting transfers between devices, swap_blocks(): arrived.append(lax.ppermute(outgoing, axis, pairs))  17.9 us
    ppermute x1, waiting for transfers between devices, panel_spectra(): blocks.append(lax.ppermute(spectra, 'panel', pairs))  10.9 us
    ppermute x6, waiting for transfers between devices, swap_blocks(): arrived.append(lax.ppermute(outgoing, axis, pairs))  5.17 us
    dot_general x1, matrix products, synthesize(): latitude = jnp.dot(basis_rows, masked, preferred_element_type=jnp.float32)  4.36 us
    all_to_all x1, starting transfers between devices, body(): gathered = lax.all_to_all(twisted, 'tm', 0, 0, tiled=True)  4.26 us
    dot_general x4, matrix products, mat(): lax.dot_general(table, value, dims, precision=lax.Precision.HIGH, preferr...  2.73 us
  transfers between devices with their start and end apart: 11, of which 7 were waited for; matrix products, arithmetic and copies ran while one was open for 6% of the time, Pallas kernels for 0%

profile of v9, /device:TPU:0, one launch (start us, length us, event | category | flops | bytes accessed | tf_op | source)
XLA Modules:
  0.0 91.0 jit_solution(9719197293812464361)
XLA Ops:
  0.0 0.7 concatenate.50
  0.7 0.7 convert_element_type.117
  1.5 3.1 %collective-permute-start = (f32[3,256]{1,0:T(4,128)S(1)}, f32[3,256]{1,0:T(4,128)S(1)}, u32[]{:S(2)}, u32[]{:S(2)}) collective-permute-start(f32[3,256]{1,0:T(4,128)S(1)} %bitcast.119), channel_id=1, source_target_pairs={{0,4},{4,8},{8,12},{12,0},{1,5},{5,9},{9,13},{13,1},{2,6},{6,10},{... | collective-permute-start | bytes 9224 | tf_op jit(solution)/shard_map/ppermute | solution.py:213
  4.5 2.6 %collective-permute-start.1 = (f32[3,256]{1,0:T(4,128)S(1)}, f32[3,256]{1,0:T(4,128)S(1)}, u32[]{:S(2)}, u32[]{:S(2)}) collective-permute-start(f32[3,256]{1,0:T(4,128)S(1)} %bitcast.120), channel_id=1, source_target_pairs={{0,8},{4,12},{8,0},{12,4},{1,9},{5,13},{9,1},{13,5},{2,10},{6,14},... | collective-permute-start | bytes 9224 | tf_op jit(solution)/shard_map/ppermute | solution.py:213
  7.1 1.3 %collective-permute-start.2 = (f32[3,256]{1,0:T(4,128)S(1)}, f32[3,256]{1,0:T(4,128)S(1)}, u32[]{:S(2)}, u32[]{:S(2)}) collective-permute-start(f32[3,256]{1,0:T(4,128)S(1)} %bitcast.121), channel_id=1, source_target_pairs={{0,12},{4,0},{8,4},{12,8},{1,13},{5,1},{9,5},{13,9},{2,14},{6,2},{... | collective-permute-start | bytes 9224 | tf_op jit(solution)/shard_map/ppermute | solution.py:213
  8.5 0.8 fusion.84
  9.3 0.7 add_rsqrt_fusion
  10.0 0.7 compare_reduce_fusion
  12.9 0.7 fusion.5
  13.8 4.4 %fusion = f32[1024,256]{1,0:T(8,128)S(1)} fusion(bf16[1024,320]{0,1:T(8,128)(2,1)S(1)} %get-tuple-element.10, bf16[1024,320]{0,1:T(8,128)(2,1)S(1)} %get-tuple-element.9, f32[256]{0:T(256)S(1)} %bitcast.127, f32[1024]{0:T(1024)S(1)} %bitcast.123, f32[256]{0:T(256)S(1)} %bitcast.129, f32[1024]{0:T(1024)S(1)} %bitcast.122, ...), kind=kOutput, calls=%fused_computation.9 | convolution fusion | flops 339804160 | bytes 2701056 | tf_op jit(solution)/shard_map/dot_general | solution.py:55
  19.4 1.1 %copy.26 = f32[4,2,256,128]{3,2,1,0:T(8,128)} copy(f32[4,2,256,128]{3,2,0,1:T(8,128)S(1)} %pad_maximum_fusion) | data formatting | bytes 2097152 | tf_op jit(solution)/shard_map/stack | solution.py:233
  20.4 4.3 %all-to-all-start = ((f32[4,2,256,128]{3,2,1,0:T(8,128)}), f32[4,2,256,128]{3,2,1,0:T(8,128)S(1)}, u32[]{:S(2)}, u32[]{:S(2)}) async-start(f32[4,2,256,128]{3,2,1,0:T(8,128)} %copy.26), calls=%async_computation | async-start | bytes 2097152 | tf_op jit(solution)/shard_map/all_to_all | solution.py:312
  25.9 23.1 %all-to-all-done = f32[4,2,256,128]{3,2,1,0:T(8,128)S(1)} async-done(((f32[4,2,256,128]{3,2,1,0:T(8,128)}), f32[4,2,256,128]{3,2,1,0:T(8,128)S(1)}, u32[]{:S(2)}, u32[]{:S(2)}) %all-to-all-start) | async-done | bytes 1048608 | tf_op jit(solution)/shard_map/all_to_all | solution.py:312
  50.5 0.7 fusion.28
  51.9 0.7 fusion.30
  53.8 0.7 collective-permute-start.3
  56.9 1.6 %collective-permute-start.4 = (bf16[2,516,256]{2,0,1:T(2,128)(2,1)S(1)}, bf16[2,516,256]{2,0,1:T(2,128)(2,1)S(1)}, u32[]{:S(2)}, u32[]{:S(2)}) collective-permute-start(bf16[2,516,256]{2,0,1:T(2,128)(2,1)S(1)} %copy.34), channel_id=1, source_target_pairs={{0,1},{1,0},{2,3},{3,2},{4,5},{5,4},{6,7},{7,6},{8,9},{9,8},{10,11... | collective-permute-start | bytes 1585160 | tf_op jit(solution)/shard_map/ppermute | solution.py:145
  59.1 10.9 %collective-permute-done.4 = bf16[2,516,256]{2,0,1:T(2,128)(2,1)S(1)} collective-permute-done((bf16[2,516,256]{2,0,1:T(2,128)(2,1)S(1)}, bf16[2,516,256]{2,0,1:T(2,128)(2,1)S(1)}, u32[]{:S(2)}, u32[]{:S(2)}) %collective-permute-start.4) | collective-permute-done | bytes 528416 | tf_op jit(solution)/shard_map/ppermute | solution.py:145
  71.4 1.5 %collective-permute-done.5 = f32[512,128]{1,0:T(8,128)S(1)} collective-permute-done((f32[512,128]{1,0:T(8,128)S(1)}, f32[512,128]{1,0:T(8,128)S(1)}, u32[]{:S(2)}, u32[]{:S(2)}) %collective-permute-start.5) | collective-permute-done | bytes 262176 | tf_op jit(solution)/shard_map/ppermute | solution.py:346
  73.0 8.4 %collective-permute-start.6 = (f32[128,128]{1,0:T(8,128)S(1)}, f32[128,128]{1,0:T(8,128)S(1)}, u32[]{:S(2)}, u32[]{:S(2)}) collective-permute-start(f32[128,128]{1,0:T(8,128)S(1)} %get-tuple-element.29), channel_id=1, source_target_pairs={{0,4},{4,8},{8,12},{12,0},{1,5},{5,9},{9,13},{13,1},{2,6},{6,10},{... | collective-permute-start | bytes 196616 | tf_op jit(solution)/shard_map/ppermute | solution.py:213
  81.4 2.4 %collective-permute-start.7 = (f32[128,128]{1,0:T(8,128)S(1)}, f32[128,128]{1,0:T(8,128)S(1)}, u32[]{:S(2)}, u32[]{:S(2)}) collective-permute-start(f32[128,128]{1,0:T(8,128)S(1)} %get-tuple-element.31), channel_id=1, source_target_pairs={{0,8},{4,12},{8,0},{12,4},{1,9},{5,13},{9,1},{13,5},{2,10},{6,14},... | collective-permute-start | bytes 196616 | tf_op jit(solution)/shard_map/ppermute | solution.py:213
  83.9 2.3 %collective-permute-done.6 = f32[128,128]{1,0:T(8,128)S(1)} collective-permute-done((f32[128,128]{1,0:T(8,128)S(1)}, f32[128,128]{1,0:T(8,128)S(1)}, u32[]{:S(2)}, u32[]{:S(2)}) %collective-permute-start.6) | collective-permute-done | bytes 65568 | tf_op jit(solution)/shard_map/ppermute | solution.py:213
  86.2 2.3 %collective-permute-done.7 = f32[128,128]{1,0:T(8,128)S(1)} collective-permute-done((f32[128,128]{1,0:T(8,128)S(1)}, f32[128,128]{1,0:T(8,128)S(1)}, u32[]{:S(2)}, u32[]{:S(2)}) %collective-permute-start.7) | collective-permute-done | bytes 65568 | tf_op jit(solution)/shard_map/ppermute | solution.py:213
  89.1 1.2 %collective-permute-done.9 = f32[128,128]{1,0:T(8,128)S(1)} collective-permute-done((f32[128,128]{1,0:T(8,128)S(1)}, f32[128,128]{1,0:T(8,128)S(1)}, u32[]{:S(2)}, u32[]{:S(2)}) %collective-permute-start.9) | collective-permute-done | bytes 65568 | tf_op jit(solution)/shard_map/ppermute | solution.py:348
  (96 shorter events, 13.7 us)
Async XLA Ops:
  1.5 9.4 %collective-permute-start = (f32[3,256]{1,0:T(4,128)S(1)}, f32[3,256]{1,0:T(4,128)S(1)}, u32[]{:S(2)}, u32[]{:S(2)}) collective-permute-start(f32[3,256]{1,0:T(4,128)S(1)} %bitcast.119), channel_id=1, source_target_pairs={{0,4},{4,8},{8,12},{12,0},{1,5},{5,9},{9,13},{13,1},{2,6},{6,10},{... | collective-permute-start | bytes 9224 | tf_op jit(solution)/shard_map/ppermute | solution.py:213
  4.5 6.3 %collective-permute-start.1 = (f32[3,256]{1,0:T(4,128)S(1)}, f32[3,256]{1,0:T(4,128)S(1)}, u32[]{:S(2)}, u32[]{:S(2)}) collective-permute-start(f32[3,256]{1,0:T(4,128)S(1)} %bitcast.120), channel_id=1, source_target_pairs={{0,8},{4,12},{8,0},{12,4},{1,9},{5,13},{9,1},{13,5},{2,10},{6,14},... | collective-permute-start | bytes 9224 | tf_op jit(solution)/shard_map/ppermute | solution.py:213
  7.1 3.7 %collective-permute-start.2 = (f32[3,256]{1,0:T(4,128)S(1)}, f32[3,256]{1,0:T(4,128)S(1)}, u32[]{:S(2)}, u32[]{:S(2)}) collective-permute-start(f32[3,256]{1,0:T(4,128)S(1)} %bitcast.121), channel_id=1, source_target_pairs={{0,12},{4,0},{8,4},{12,8},{1,13},{5,1},{9,5},{13,9},{2,14},{6,2},{... | collective-permute-start | bytes 9224 | tf_op jit(solution)/shard_map/ppermute | solution.py:213
  12.9 1.0 %copy-start.1 = (bf16[1,640,256]{2,1,0:T(8,128)(2,1)S(1)}, bf16[1,640,256]{2,1,0:T(8,128)(2,1)}, u32[]{:S(2)}) copy-start(bf16[1,640,256]{2,1,0:T(8,128)(2,1)} %param.8) | copy-start | bytes 983044
  20.4 28.6 %all-to-all-start = ((f32[4,2,256,128]{3,2,1,0:T(8,128)}), f32[4,2,256,128]{3,2,1,0:T(8,128)S(1)}, u32[]{:S(2)}, u32[]{:S(2)}) async-start(f32[4,2,256,128]{3,2,1,0:T(8,128)} %copy.26), calls=%async_computation | async-start | bytes 2097152 | tf_op jit(solution)/shard_map/all_to_all | solution.py:312
  53.5 1.1 %copy-start = (s32[1,2049]{1,0:T(1,128)S(1)}, s32[1,2049]{1,0:T(1,128)}, u32[]{:S(2)}) copy-start(s32[1,2049]{1,0:T(1,128)} %param.9) | copy-start | bytes 24592
  53.8 2.0 %collective-permute-start.3 = (f32[2,516,128]{2,0,1:T(2,128)S(1)}, f32[2,516,128]{2,0,1:T(2,128)S(1)}, u32[]{:S(2)}, u32[]{:S(2)}) collective-permute-start(f32[2,516,128]{2,0,1:T(2,128)S(1)} %copy.31), channel_id=1, source_target_pairs={{0,0},{4,12},{8,8},{12,4},{1,1},{5,13},{9,9},{13,5},{2,2},{6,14},{... | collective-permute-start | bytes 1585160 | tf_op jit(solution)/shard_map/ppermute | solution.py:281
  56.9 13.0 %collective-permute-start.4 = (bf16[2,516,256]{2,0,1:T(2,128)(2,1)S(1)}, bf16[2,516,256]{2,0,1:T(2,128)(2,1)S(1)}, u32[]{:S(2)}, u32[]{:S(2)}) collective-permute-start(bf16[2,516,256]{2,0,1:T(2,128)(2,1)S(1)} %copy.34), channel_id=1, source_target_pairs={{0,1},{1,0},{2,3},{3,2},{4,5},{5,4},{6,7},{7,6},{8,9},{9,8},{10,11... | collective-permute-start | bytes 1585160 | tf_op jit(solution)/shard_map/ppermute | solution.py:145
  71.3 1.6 %collective-permute-start.5 = (f32[512,128]{1,0:T(8,128)S(1)}, f32[512,128]{1,0:T(8,128)S(1)}, u32[]{:S(2)}, u32[]{:S(2)}) collective-permute-start(f32[512,128]{1,0:T(8,128)S(1)} %constant_dynamic-slice_fusion), channel_id=1, source_target_pairs={{0,2},{2,0},{1,3},{3,1},{4,6},{6,4},{5,7},{7,5},{8,10},{10,8},{9,1... | collective-permute-start | bytes 786440 | tf_op jit(solution)/shard_map/ppermute | solution.py:346
  73.0 13.2 %collective-permute-start.6 = (f32[128,128]{1,0:T(8,128)S(1)}, f32[128,128]{1,0:T(8,128)S(1)}, u32[]{:S(2)}, u32[]{:S(2)}) collective-permute-start(f32[128,128]{1,0:T(8,128)S(1)} %get-tuple-element.29), channel_id=1, source_target_pairs={{0,4},{4,8},{8,12},{12,0},{1,5},{5,9},{9,13},{13,1},{2,6},{6,10},{... | collective-permute-start | bytes 196616 | tf_op jit(solution)/shard_map/ppermute | solution.py:213
  81.4 7.1 %collective-permute-start.7 = (f32[128,128]{1,0:T(8,128)S(1)}, f32[128,128]{1,0:T(8,128)S(1)}, u32[]{:S(2)}, u32[]{:S(2)}) collective-permute-start(f32[128,128]{1,0:T(8,128)S(1)} %get-tuple-element.31), channel_id=1, source_target_pairs={{0,8},{4,12},{8,0},{12,4},{1,9},{5,13},{9,1},{13,5},{2,10},{6,14},... | collective-permute-start | bytes 196616 | tf_op jit(solution)/shard_map/ppermute | solution.py:213
  83.8 5.2 %collective-permute-start.8 = (f32[128,128]{1,0:T(8,128)S(1)}, f32[128,128]{1,0:T(8,128)S(1)}, u32[]{:S(2)}, u32[]{:S(2)}) collective-permute-start(f32[128,128]{1,0:T(8,128)S(1)} %get-tuple-element.30), channel_id=1, source_target_pairs={{0,12},{4,0},{8,4},{12,8},{1,13},{5,1},{9,5},{13,9},{2,14},{6,2},{... | collective-permute-start | bytes 196616 | tf_op jit(solution)/shard_map/ppermute | solution.py:213
  89.0 1.3 %collective-permute-start.9 = (f32[128,128]{1,0:T(8,128)S(1)}, f32[128,128]{1,0:T(8,128)S(1)}, u32[]{:S(2)}, u32[]{:S(2)}) collective-permute-start(f32[128,128]{1,0:T(8,128)S(1)} %fusion.49), channel_id=1, source_target_pairs={{0,2},{2,0},{1,3},{3,1},{4,6},{6,4},{5,7},{7,5},{8,10},{10,8},{9,1... | collective-permute-start | bytes 196616 | tf_op jit(solution)/shard_map/ppermute | solution.py:348

commit v10 on v9

--- a/solution.py
+++ b/solution.py
@@ -233,11 +233,11 @@
     return jnp.stack([real_part, imag_part], axis=1)
 
 
-def packed_transform(gathered):
+def packed_transform(gathered, sources):
     devices_tm, _, block_len, columns = gathered.shape
     length = devices_tm * block_len
     index = jnp.arange(devices_tm, dtype=jnp.int32)
-    cos_table, sin_table = phase_tables(index, index, devices_tm)
+    cos_table, sin_table = phase_tables(index, sources, devices_tm)
     real_in = gathered[:, 0]
     imag_in = gathered[:, 1]
     cos_b = cos_table[:, :, None, None]
@@ -290,6 +290,21 @@
     return jnp.stack([new_real.astype(jnp.bfloat16), new_imag.astype(jnp.bfloat16)])
 
 
+def exchange_classes(twisted, position):
+    devices_tm = lax.axis_size("tm")
+    index = jnp.arange(devices_tm, dtype=jnp.int32)
+    if devices_tm > 8:
+        return lax.all_to_all(twisted, "tm", 0, 0, tiled=True), index
+    arrived = [lax.dynamic_index_in_dim(twisted, position, 0, keepdims=False)]
+    for shift in range(1, devices_tm):
+        outgoing = lax.dynamic_index_in_dim(
+            twisted, (position + shift) % devices_tm, 0, keepdims=False
+        )
+        pairs = [(src, (src + shift) % devices_tm) for src in range(devices_tm)]
+        arrived.append(lax.ppermute(outgoing, "tm", pairs))
+    return jnp.stack(arrived), (position - index) % devices_tm
+
+
 def body(orbit_angles, gap_mask, column_index, lat_coeffs, psd_table):
     devices_tm = lax.axis_size("tm")
     panels = lax.axis_size("panel")
@@ -309,8 +324,8 @@
     position = lax.axis_index("tm")
     half_cols = columns // 2
     twisted = packed_partials(spread[..., :half_cols], spread[..., half_cols:], position, samples)
-    gathered = lax.all_to_all(twisted, "tm", 0, 0, tiled=True)
-    own, far = packed_transform(gathered)
+    gathered, sources = exchange_classes(twisted, position)
+    own, far = packed_transform(gathered, sources)
     spectra = unpack_spectra(own, far, position, samples)
     inverse_psd, fold = inverse_weights(
         psd_table[0], position, devices_tm, epochs, samples, spectra.shape[1]

time: 91.4 us -> 94.6 us (1.035)
  starting transfers between devices: 24.5 us -> 35.1 us
  waiting for transfers between devices: 41.9 us -> 35.4 us
  local copies, waits for them, and re-layouts: 6.05 us -> 5 us
    all_to_all x1 -> x0, waiting for transfers between devices: 23.1 us -> none  [body(): gathered = lax.all_to_all(twisted, 'tm', 0, 0, tiled=True)]
    ppermute x0 -> x3, waiting for transfers between devices: none -> 16 us  [exchange_classes(): arrived.append(lax.ppermute(outgoing, 'tm', pairs))]
    ppermute x6, starting transfers between devices: 17.9 us -> 28.9 us  [swap_blocks(): arrived.append(lax.ppermute(outgoing, axis, pairs))]
    all_to_all x1 -> x0, starting transfers between devices: 4.26 us -> none  [body(): gathered = lax.all_to_all(twisted, 'tm', 0, 0, tiled=True)]
    ppermute x0 -> x3, starting transfers between devices: none -> 3.88 us  [exchange_classes(): arrived.append(lax.ppermute(outgoing, 'tm', pairs))]
    another operation x1 -> x0, local copies, waits for them, and re-layouts: 1.05 us -> none  [packed_partials(): return jnp.stack([real_part, imag_part], axis=1)]
  transfers between devices with their start and end apart: 11 -> 13, of which waited for: 7 -> 7; matrix products, arithmetic and copies ran while one was open for 6% -> 6% of each run, Pallas kernels for 0% -> 0%
where the time goes in v10:
time: 94.6 us; the launch traced here: 94.2 us
  waiting for transfers between devices  35.4 us (37%)
  starting transfers between devices  35.1 us (37%)
  other arithmetic  9.87 us (10%)
  matrix products  8.26 us (9%)
  local copies, waits for them, and re-layouts  5 us (5%)
    ppermute x6, starting transfers between devices, swap_blocks(): arrived.append(lax.ppermute(outgoing, axis, pairs))  28.9 us
    ppermute x3, waiting for transfers between devices, exchange_classes(): arrived.append(lax.ppermute(outgoing, 'tm', pairs))  16 us
    ppermute x1, waiting for transfers between devices, panel_spectra(): blocks.append(lax.ppermute(spectra, 'panel', pairs))  10.6 us
    ppermute x6, waiting for transfers between devices, swap_blocks(): arrived.append(lax.ppermute(outgoing, axis, pairs))  6.07 us
    dot_general x1, matrix products, synthesize(): latitude = jnp.dot(basis_rows, masked, preferred_element_type=jnp.float32)  4.36 us
    ppermute x3, starting transfers between devices, exchange_classes(): arrived.append(lax.ppermute(outgoing, 'tm', pairs))  3.88 us
    dot_general x4, matrix products, mat(): lax.dot_general(table, value, dims, precision=lax.Precision.HIGH, preferr...  2.76 us
  transfers between devices with their start and end apart: 13, of which 7 were waited for; matrix products, arithmetic and copies ran while one was open for 6% of the time, Pallas kernels for 0%

profile of v10, /device:TPU:0, one launch (start us, length us, event | category | flops | bytes accessed | tf_op | source)
XLA Modules:
  0.0 94.2 jit_solution(12706357132508663479)
XLA Ops:
  0.0 0.7 concatenate.50
  1.5 3.1 %collective-permute-start = (f32[3,256]{1,0:T(4,128)S(1)}, f32[3,256]{1,0:T(4,128)S(1)}, u32[]{:S(2)}, u32[]{:S(2)}) collective-permute-start(f32[3,256]{1,0:T(4,128)S(1)} %bitcast.131), channel_id=1, source_target_pairs={{0,4},{4,8},{8,12},{12,0},{1,5},{5,9},{9,13},{13,1},{2,6},{6,10},{... | collective-permute-start | bytes 9224 | tf_op jit(solution)/shard_map/ppermute | solution.py:213
  4.5 2.6 %collective-permute-start.1 = (f32[3,256]{1,0:T(4,128)S(1)}, f32[3,256]{1,0:T(4,128)S(1)}, u32[]{:S(2)}, u32[]{:S(2)}) collective-permute-start(f32[3,256]{1,0:T(4,128)S(1)} %bitcast.132), channel_id=1, source_target_pairs={{0,8},{4,12},{8,0},{12,4},{1,9},{5,13},{9,1},{13,5},{2,10},{6,14},... | collective-permute-start | bytes 9224 | tf_op jit(solution)/shard_map/ppermute | solution.py:213
  7.1 1.3 %collective-permute-start.2 = (f32[3,256]{1,0:T(4,128)S(1)}, f32[3,256]{1,0:T(4,128)S(1)}, u32[]{:S(2)}, u32[]{:S(2)}) collective-permute-start(f32[3,256]{1,0:T(4,128)S(1)} %bitcast.133), channel_id=1, source_target_pairs={{0,12},{4,0},{8,4},{12,8},{1,13},{5,1},{9,5},{13,9},{2,14},{6,2},{... | collective-permute-start | bytes 9224 | tf_op jit(solution)/shard_map/ppermute | solution.py:213
  8.5 0.8 fusion.97
  10.0 0.7 compare_reduce_fusion
  13.6 0.7 fusion.5
  14.5 4.4 %fusion = f32[1024,256]{1,0:T(8,128)S(1)} fusion(bf16[1024,320]{0,1:T(8,128)(2,1)S(1)} %get-tuple-element.10, bf16[1024,320]{0,1:T(8,128)(2,1)S(1)} %get-tuple-element.9, f32[256]{0:T(256)S(1)} %bitcast.139, f32[1024]{0:T(1024)S(1)} %bitcast.135, f32[256]{0:T(256)S(1)} %bitcast.141, f32[1024]{0:T(1024)S(1)} %bitcast.134, ...), kind=kOutput, calls=%fused_computation.17 | convolution fusion | flops 339804160 | bytes 2701056 | tf_op jit(solution)/shard_map/dot_general | solution.py:55
  20.1 0.7 collective-permute-start.3
  20.8 2.2 %collective-permute-start.4 = (f32[2,256,128]{2,1,0:T(8,128)S(1)}, f32[2,256,128]{2,1,0:T(8,128)S(1)}, u32[]{:S(2)}, u32[]{:S(2)}) collective-permute-start(f32[2,256,128]{2,1,0:T(8,128)S(1)} %get-tuple-element.21), channel_id=1, source_target_pairs={{0,8},{4,12},{8,0},{12,4},{1,9},{5,13},{9,1},{13,5},{2,10},{6,14},... | collective-permute-start | bytes 786440 | tf_op jit(solution)/shard_map/ppermute | solution.py:304
  23.0 1.0 %collective-permute-start.5 = (f32[2,256,128]{2,1,0:T(8,128)S(1)}, f32[2,256,128]{2,1,0:T(8,128)S(1)}, u32[]{:S(2)}, u32[]{:S(2)}) collective-permute-start(f32[2,256,128]{2,1,0:T(8,128)S(1)} %get-tuple-element.22), channel_id=1, source_target_pairs={{0,12},{4,0},{8,4},{12,8},{1,13},{5,1},{9,5},{13,9},{2,14},{6,2},{... | collective-permute-start | bytes 786440 | tf_op jit(solution)/shard_map/ppermute | solution.py:304
  24.6 6.7 %collective-permute-done.3 = f32[2,256,128]{2,1,0:T(8,128)S(1)} collective-permute-done((f32[2,256,128]{2,1,0:T(8,128)S(1)}, f32[2,256,128]{2,1,0:T(8,128)S(1)}, u32[]{:S(2)}, u32[]{:S(2)}) %collective-permute-start.3) | collective-permute-done | bytes 262176 | tf_op jit(solution)/shard_map/ppermute | solution.py:304
  31.3 9.3 %collective-permute-done.4 = f32[2,256,128]{2,1,0:T(8,128)S(1)} collective-permute-done((f32[2,256,128]{2,1,0:T(8,128)S(1)}, f32[2,256,128]{2,1,0:T(8,128)S(1)}, u32[]{:S(2)}, u32[]{:S(2)}) %collective-permute-start.4) | collective-permute-done | bytes 262176 | tf_op jit(solution)/shard_map/ppermute | solution.py:304
  42.7 0.7 fusion.36
  43.5 0.7 fusion.37
  45.4 0.7 collective-permute-start.6
  48.5 1.5 %collective-permute-start.7 = (bf16[2,516,256]{2,0,1:T(2,128)(2,1)S(1)}, bf16[2,516,256]{2,0,1:T(2,128)(2,1)S(1)}, u32[]{:S(2)}, u32[]{:S(2)}) collective-permute-start(bf16[2,516,256]{2,0,1:T(2,128)(2,1)S(1)} %copy.33), channel_id=1, source_target_pairs={{0,1},{1,0},{2,3},{3,2},{4,5},{5,4},{6,7},{7,6},{8,9},{9,8},{10,11... | collective-permute-start | bytes 1585160 | tf_op jit(solution)/shard_map/ppermute | solution.py:145
  50.7 10.6 %collective-permute-done.7 = bf16[2,516,256]{2,0,1:T(2,128)(2,1)S(1)} collective-permute-done((bf16[2,516,256]{2,0,1:T(2,128)(2,1)S(1)}, bf16[2,516,256]{2,0,1:T(2,128)(2,1)S(1)}, u32[]{:S(2)}, u32[]{:S(2)}) %collective-permute-start.7) | collective-permute-done | bytes 528416 | tf_op jit(solution)/shard_map/ppermute | solution.py:145
  62.7 1.5 %collective-permute-done.8 = f32[512,128]{1,0:T(8,128)S(1)} collective-permute-done((f32[512,128]{1,0:T(8,128)S(1)}, f32[512,128]{1,0:T(8,128)S(1)}, u32[]{:S(2)}, u32[]{:S(2)}) %collective-permute-start.8) | collective-permute-done | bytes 262176 | tf_op jit(solution)/shard_map/ppermute | solution.py:361
  64.3 5.2 %collective-permute-start.10 = (f32[128,128]{1,0:T(8,128)S(1)}, f32[128,128]{1,0:T(8,128)S(1)}, u32[]{:S(2)}, u32[]{:S(2)}) collective-permute-start(f32[128,128]{1,0:T(8,128)S(1)} %get-tuple-element.35), channel_id=1, source_target_pairs={{0,8},{4,12},{8,0},{12,4},{1,9},{5,13},{9,1},{13,5},{2,10},{6,14},... | collective-permute-start | bytes 196616 | tf_op jit(solution)/shard_map/ppermute | solution.py:213
  69.5 16.6 %collective-permute-start.11 = (f32[128,128]{1,0:T(8,128)S(1)}, f32[128,128]{1,0:T(8,128)S(1)}, u32[]{:S(2)}, u32[]{:S(2)}) collective-permute-start(f32[128,128]{1,0:T(8,128)S(1)} %get-tuple-element.34), channel_id=1, source_target_pairs={{0,12},{4,0},{8,4},{12,8},{1,13},{5,1},{9,5},{13,9},{2,14},{6,2},{... | collective-permute-start | bytes 196616 | tf_op jit(solution)/shard_map/ppermute | solution.py:213
  86.2 2.1 %collective-permute-done.11 = f32[128,128]{1,0:T(8,128)S(1)} collective-permute-done((f32[128,128]{1,0:T(8,128)S(1)}, f32[128,128]{1,0:T(8,128)S(1)}, u32[]{:S(2)}, u32[]{:S(2)}) %collective-permute-start.11) | collective-permute-done | bytes 65568 | tf_op jit(solution)/shard_map/ppermute | solution.py:213
  88.2 4.0 %collective-permute-done.9 = f32[128,128]{1,0:T(8,128)S(1)} collective-permute-done((f32[128,128]{1,0:T(8,128)S(1)}, f32[128,128]{1,0:T(8,128)S(1)}, u32[]{:S(2)}, u32[]{:S(2)}) %collective-permute-start.9) | collective-permute-done | bytes 65568 | tf_op jit(solution)/shard_map/ppermute | solution.py:213
  92.3 1.2 %collective-permute-done.12 = f32[128,128]{1,0:T(8,128)S(1)} collective-permute-done((f32[128,128]{1,0:T(8,128)S(1)}, f32[128,128]{1,0:T(8,128)S(1)}, u32[]{:S(2)}, u32[]{:S(2)}) %collective-permute-start.12) | collective-permute-done | bytes 65568 | tf_op jit(solution)/shard_map/ppermute | solution.py:363
  (102 shorter events, 14.6 us)
Async XLA Ops:
  1.5 10.1 %collective-permute-start = (f32[3,256]{1,0:T(4,128)S(1)}, f32[3,256]{1,0:T(4,128)S(1)}, u32[]{:S(2)}, u32[]{:S(2)}) collective-permute-start(f32[3,256]{1,0:T(4,128)S(1)} %bitcast.131), channel_id=1, source_target_pairs={{0,4},{4,8},{8,12},{12,0},{1,5},{5,9},{9,13},{13,1},{2,6},{6,10},{... | collective-permute-start | bytes 9224 | tf_op jit(solution)/shard_map/ppermute | solution.py:213
  4.5 7.0 %collective-permute-start.1 = (f32[3,256]{1,0:T(4,128)S(1)}, f32[3,256]{1,0:T(4,128)S(1)}, u32[]{:S(2)}, u32[]{:S(2)}) collective-permute-start(f32[3,256]{1,0:T(4,128)S(1)} %bitcast.132), channel_id=1, source_target_pairs={{0,8},{4,12},{8,0},{12,4},{1,9},{5,13},{9,1},{13,5},{2,10},{6,14},... | collective-permute-start | bytes 9224 | tf_op jit(solution)/shard_map/ppermute | solution.py:213
  7.1 4.4 %collective-permute-start.2 = (f32[3,256]{1,0:T(4,128)S(1)}, f32[3,256]{1,0:T(4,128)S(1)}, u32[]{:S(2)}, u32[]{:S(2)}) collective-permute-start(f32[3,256]{1,0:T(4,128)S(1)} %bitcast.133), channel_id=1, source_target_pairs={{0,12},{4,0},{8,4},{12,8},{1,13},{5,1},{9,5},{13,9},{2,14},{6,2},{... | collective-permute-start | bytes 9224 | tf_op jit(solution)/shard_map/ppermute | solution.py:213
  13.6 1.0 %copy-start.1 = (bf16[1,640,256]{2,1,0:T(8,128)(2,1)S(1)}, bf16[1,640,256]{2,1,0:T(8,128)(2,1)}, u32[]{:S(2)}) copy-start(bf16[1,640,256]{2,1,0:T(8,128)(2,1)} %param.8) | copy-start | bytes 983044
  20.1 11.2 %collective-permute-start.3 = (f32[2,256,128]{2,1,0:T(8,128)S(1)}, f32[2,256,128]{2,1,0:T(8,128)S(1)}, u32[]{:S(2)}, u32[]{:S(2)}) collective-permute-start(f32[2,256,128]{2,1,0:T(8,128)S(1)} %get-tuple-element.20), channel_id=1, source_target_pairs={{0,4},{4,8},{8,12},{12,0},{1,5},{5,9},{9,13},{13,1},{2,6},{6,10},{... | collective-permute-start | bytes 786440 | tf_op jit(solution)/shard_map/ppermute | solution.py:304
  20.8 19.8 %collective-permute-start.4 = (f32[2,256,128]{2,1,0:T(8,128)S(1)}, f32[2,256,128]{2,1,0:T(8,128)S(1)}, u32[]{:S(2)}, u32[]{:S(2)}) collective-permute-start(f32[2,256,128]{2,1,0:T(8,128)S(1)} %get-tuple-element.21), channel_id=1, source_target_pairs={{0,8},{4,12},{8,0},{12,4},{1,9},{5,13},{9,1},{13,5},{2,10},{6,14},... | collective-permute-start | bytes 786440 | tf_op jit(solution)/shard_map/ppermute | solution.py:304
  23.0 17.6 %collective-permute-start.5 = (f32[2,256,128]{2,1,0:T(8,128)S(1)}, f32[2,256,128]{2,1,0:T(8,128)S(1)}, u32[]{:S(2)}, u32[]{:S(2)}) collective-permute-start(f32[2,256,128]{2,1,0:T(8,128)S(1)} %get-tuple-element.22), channel_id=1, source_target_pairs={{0,12},{4,0},{8,4},{12,8},{1,13},{5,1},{9,5},{13,9},{2,14},{6,2},{... | collective-permute-start | bytes 786440 | tf_op jit(solution)/shard_map/ppermute | solution.py:304
  45.1 1.1 %copy-start = (s32[1,2049]{1,0:T(1,128)S(1)}, s32[1,2049]{1,0:T(1,128)}, u32[]{:S(2)}) copy-start(s32[1,2049]{1,0:T(1,128)} %param.9) | copy-start | bytes 24592
  45.4 2.0 %collective-permute-start.6 = (f32[2,516,128]{2,0,1:T(2,128)S(1)}, f32[2,516,128]{2,0,1:T(2,128)S(1)}, u32[]{:S(2)}, u32[]{:S(2)}) collective-permute-start(f32[2,516,128]{2,0,1:T(2,128)S(1)} %copy.30), channel_id=1, source_target_pairs={{0,0},{4,12},{8,8},{12,4},{1,1},{5,13},{9,9},{13,5},{2,2},{6,14},{... | collective-permute-start | bytes 1585160 | tf_op jit(solution)/shard_map/ppermute | solution.py:281
  48.5 12.8 %collective-permute-start.7 = (bf16[2,516,256]{2,0,1:T(2,128)(2,1)S(1)}, bf16[2,516,256]{2,0,1:T(2,128)(2,1)S(1)}, u32[]{:S(2)}, u32[]{:S(2)}) collective-permute-start(bf16[2,516,256]{2,0,1:T(2,128)(2,1)S(1)} %copy.33), channel_id=1, source_target_pairs={{0,1},{1,0},{2,3},{3,2},{4,5},{5,4},{6,7},{7,6},{8,9},{9,8},{10,11... | collective-permute-start | bytes 1585160 | tf_op jit(solution)/shard_map/ppermute | solution.py:145
  62.7 1.6 %collective-permute-start.8 = (f32[512,128]{1,0:T(8,128)S(1)}, f32[512,128]{1,0:T(8,128)S(1)}, u32[]{:S(2)}, u32[]{:S(2)}) collective-permute-start(f32[512,128]{1,0:T(8,128)S(1)} %constant_dynamic-slice_fusion), channel_id=1, source_target_pairs={{0,2},{2,0},{1,3},{3,1},{4,6},{6,4},{5,7},{7,5},{8,10},{10,8},{9,1... | collective-permute-start | bytes 786440 | tf_op jit(solution)/shard_map/ppermute | solution.py:361
  64.3 21.8 %collective-permute-start.10 = (f32[128,128]{1,0:T(8,128)S(1)}, f32[128,128]{1,0:T(8,128)S(1)}, u32[]{:S(2)}, u32[]{:S(2)}) collective-permute-start(f32[128,128]{1,0:T(8,128)S(1)} %get-tuple-element.35), channel_id=1, source_target_pairs={{0,8},{4,12},{8,0},{12,4},{1,9},{5,13},{9,1},{13,5},{2,10},{6,14},... | collective-permute-start | bytes 196616 | tf_op jit(solution)/shard_map/ppermute | solution.py:213
  69.5 18.7 %collective-permute-start.11 = (f32[128,128]{1,0:T(8,128)S(1)}, f32[128,128]{1,0:T(8,128)S(1)}, u32[]{:S(2)}, u32[]{:S(2)}) collective-permute-start(f32[128,128]{1,0:T(8,128)S(1)} %get-tuple-element.34), channel_id=1, source_target_pairs={{0,12},{4,0},{8,4},{12,8},{1,13},{5,1},{9,5},{13,9},{2,14},{6,2},{... | collective-permute-start | bytes 196616 | tf_op jit(solution)/shard_map/ppermute | solution.py:213
  86.2 6.1 %collective-permute-start.9 = (f32[128,128]{1,0:T(8,128)S(1)}, f32[128,128]{1,0:T(8,128)S(1)}, u32[]{:S(2)}, u32[]{:S(2)}) collective-permute-start(f32[128,128]{1,0:T(8,128)S(1)} %get-tuple-element.33), channel_id=1, source_target_pairs={{0,4},{4,8},{8,12},{12,0},{1,5},{5,9},{9,13},{13,1},{2,6},{6,10},{... | collective-permute-start | bytes 196616 | tf_op jit(solution)/shard_map/ppermute | solution.py:213
  92.2 1.3 %collective-permute-start.12 = (f32[128,128]{1,0:T(8,128)S(1)}, f32[128,128]{1,0:T(8,128)S(1)}, u32[]{:S(2)}, u32[]{:S(2)}) collective-permute-start(f32[128,128]{1,0:T(8,128)S(1)} %fusion.56), channel_id=1, source_target_pairs={{0,2},{2,0},{1,3},{3,1},{4,6},{6,4},{5,7},{7,5},{8,10},{10,8},{9,1... | collective-permute-start | bytes 196616 | tf_op jit(solution)/shard_map/ppermute | solution.py:363

commit v11 on v9

--- a/solution.py
+++ b/solution.py
@@ -220,16 +220,26 @@
     return jnp.take(jnp.stack(arrived), order, axis=0)
 
 
+def class_order(count):
+    order = [0]
+    for low in range(1, (count + 1) // 2):
+        order += [low, count - low]
+    if count % 2 == 0 and count > 1:
+        order.append(count // 2)
+    return order
+
+
 def packed_partials(real_in, imag_in, position, samples):
     devices_tm, block_len, columns = real_in.shape
     index = jnp.arange(devices_tm, dtype=jnp.int32)
-    cos_table, sin_table = phase_tables(index, index, devices_tm)
+    classes = jnp.asarray(class_order(devices_tm), dtype=jnp.int32)
+    cos_table, sin_table = phase_tables(classes, index, devices_tm)
     cos_b = cos_table[:, :, None, None]
     sin_b = sin_table[:, :, None, None]
     real_part = jnp.sum(cos_b * real_in[None] + sin_b * imag_in[None], axis=1)
     imag_part = jnp.sum(cos_b * imag_in[None] - sin_b * real_in[None], axis=1)
     local_epoch = position * block_len + jnp.arange(block_len, dtype=jnp.int32)
-    real_part, imag_part = rotate(real_part, imag_part, index, local_epoch, samples)
+    real_part, imag_part = rotate(real_part, imag_part, classes, local_epoch, samples)
     return jnp.stack([real_part, imag_part], axis=1)
 
 
@@ -273,11 +283,13 @@
     return own, far
 
 
-def unpack_spectra(own, far, position, samples):
+def unpack_spectra(own, far, klass, samples):
     devices_tm = lax.axis_size("tm")
     shifted = jnp.concatenate([own[:, :1], far[:, :-1]], axis=1)
-    outgoing = jnp.where(position == 0, shifted, far)
-    pairs = [(src, (devices_tm - src) % devices_tm) for src in range(devices_tm)]
+    outgoing = jnp.where(klass == 0, shifted, far)
+    order = class_order(devices_tm)
+    holder = {value: place for place, value in enumerate(order)}
+    pairs = [(src, holder[(devices_tm - order[src]) % devices_tm]) for src in range(devices_tm)]
     mirror = lax.ppermute(outgoing, "tm", pairs)
     own_real = own[0]
     own_imag = own[1]
@@ -311,9 +323,10 @@
     twisted = packed_partials(spread[..., :half_cols], spread[..., half_cols:], position, samples)
     gathered = lax.all_to_all(twisted, "tm", 0, 0, tiled=True)
     own, far = packed_transform(gathered)
-    spectra = unpack_spectra(own, far, position, samples)
+    klass = jnp.asarray(class_order(devices_tm), dtype=jnp.int32)[position]
+    spectra = unpack_spectra(own, far, klass, samples)
     inverse_psd, fold = inverse_weights(
-        psd_table[0], position, devices_tm, epochs, samples, spectra.shape[1]
+        psd_table[0], klass, devices_tm, epochs, samples, spectra.shape[1]
     )
     weighted = (spectra.astype(jnp.float32) * inverse_psd[None, :, None]).astype(jnp.bfloat16)
     weighted = weighted * fold[None, :, None].astype(jnp.bfloat16)

time: 91.4 us -> 93.6 us (1.024)
  waiting for transfers between devices: 41.9 us -> 38 us
  between operations: 0.59 us -> 3.22 us
  other arithmetic: 9.73 us -> 11.2 us
  starting transfers between devices: 24.5 us -> 25.8 us
    ppermute x6, waiting for transfers between devices: 5.17 us -> 2.05 us  [swap_blocks(): arrived.append(lax.ppermute(outgoing, axis, pairs))]
    ppermute x6, starting transfers between devices: 17.9 us -> 19.6 us  [swap_blocks(): arrived.append(lax.ppermute(outgoing, axis, pairs))]
  transfers between devices with their start and end apart: 11 -> 11, of which waited for: 7 -> 5; matrix products, arithmetic and copies ran while one was open for 6% -> 8% of each run, Pallas kernels for 0% -> 0%
where the time goes in v11:
time: 93.6 us; the launch traced here: 93.2 us
  waiting for transfers between devices  38 us (41%)
  starting transfers between devices  25.8 us (28%)
  other arithmetic  11.2 us (12%)
  matrix products  8.23 us (9%)
  local copies, waits for them, and re-layouts  6.66 us (7%)
  between operations  3.22 us (3%)
    all_to_all x1, waiting for transfers between devices, body(): gathered = lax.all_to_all(twisted, 'tm', 0, 0, tiled=True)  22.4 us
    ppermute x6, starting transfers between devices, swap_blocks(): arrived.append(lax.ppermute(outgoing, axis, pairs))  19.6 us
    ppermute x1, waiting for transfers between devices, panel_spectra(): blocks.append(lax.ppermute(spectra, 'panel', pairs))  10.9 us
    dot_general x1, matrix products, synthesize(): latitude = jnp.dot(basis_rows, masked, preferred_element_type=jnp.float32)  4.37 us
    all_to_all x1, starting transfers between devices, body(): gathered = lax.all_to_all(twisted, 'tm', 0, 0, tiled=True)  3.83 us
    dot_general x4, matrix products, mat(): lax.dot_general(table, value, dims, precision=lax.Precision.HIGH, preferr...  2.73 us
    ppermute x6, waiting for transfers between devices, swap_blocks(): arrived.append(lax.ppermute(outgoing, axis, pairs))  2.05 us
  transfers between devices with their start and end apart: 11, of which 5 were waited for; matrix products, arithmetic and copies ran while one was open for 8% of the time, Pallas kernels for 0%

profile of v11, /device:TPU:0, one launch (start us, length us, event | category | flops | bytes accessed | tf_op | source)
XLA Modules:
  0.0 93.2 jit_solution(14716908982877893044)
XLA Ops:
  0.0 0.7 concatenate.50
  0.7 0.7 convert_element_type.119
  1.5 3.1 %collective-permute-start = (f32[3,256]{1,0:T(4,128)S(1)}, f32[3,256]{1,0:T(4,128)S(1)}, u32[]{:S(2)}, u32[]{:S(2)}) collective-permute-start(f32[3,256]{1,0:T(4,128)S(1)} %bitcast.120), channel_id=1, source_target_pairs={{0,4},{4,8},{8,12},{12,0},{1,5},{5,9},{9,13},{13,1},{2,6},{6,10},{... | collective-permute-start | bytes 9224 | tf_op jit(solution)/shard_map/ppermute | solution.py:213
  4.5 2.6 %collective-permute-start.1 = (f32[3,256]{1,0:T(4,128)S(1)}, f32[3,256]{1,0:T(4,128)S(1)}, u32[]{:S(2)}, u32[]{:S(2)}) collective-permute-start(f32[3,256]{1,0:T(4,128)S(1)} %bitcast.121), channel_id=1, source_target_pairs={{0,8},{4,12},{8,0},{12,4},{1,9},{5,13},{9,1},{13,5},{2,10},{6,14},... | collective-permute-start | bytes 9224 | tf_op jit(solution)/shard_map/ppermute | solution.py:213
  7.1 1.3 %collective-permute-start.2 = (f32[3,256]{1,0:T(4,128)S(1)}, f32[3,256]{1,0:T(4,128)S(1)}, u32[]{:S(2)}, u32[]{:S(2)}) collective-permute-start(f32[3,256]{1,0:T(4,128)S(1)} %bitcast.122), channel_id=1, source_target_pairs={{0,12},{4,0},{8,4},{12,8},{1,13},{5,1},{9,5},{13,9},{2,14},{6,2},{... | collective-permute-start | bytes 9224 | tf_op jit(solution)/shard_map/ppermute | solution.py:213
  8.5 0.8 fusion.89
  9.3 0.7 add_rsqrt_fusion
  10.0 0.7 compare_reduce_fusion
  10.7 0.8 fusion.72
  11.5 0.8 fusion.68
  14.3 0.7 fusion.5
  15.3 4.4 %fusion = f32[1024,256]{1,0:T(8,128)S(1)} fusion(bf16[1024,320]{0,1:T(8,128)(2,1)S(1)} %get-tuple-element.10, bf16[1024,320]{0,1:T(8,128)(2,1)S(1)} %get-tuple-element.9, f32[256]{0:T(256)S(1)} %bitcast.128, f32[1024]{0:T(1024)S(1)} %bitcast.124, f32[256]{0:T(256)S(1)} %bitcast.130, f32[1024]{0:T(1024)S(1)} %bitcast.123, ...), kind=kOutput, calls=%fused_computation.9 | convolution fusion | flops 339804160 | bytes 2701056 | tf_op jit(solution)/shard_map/dot_general | solution.py:55
  20.8 1.1 %copy.28 = f32[4,2,256,128]{3,2,1,0:T(8,128)} copy(f32[4,2,256,128]{3,2,0,1:T(8,128)S(1)} %pad_maximum_fusion) | data formatting | bytes 2097152 | tf_op jit(solution)/shard_map/stack | solution.py:243
  21.9 3.8 %all-to-all-start = ((f32[4,2,256,128]{3,2,1,0:T(8,128)}), f32[4,2,256,128]{3,2,1,0:T(8,128)S(1)}, u32[]{:S(2)}, u32[]{:S(2)}) async-start(f32[4,2,256,128]{3,2,1,0:T(8,128)} %copy.28), calls=%async_computation | async-start | bytes 2097152 | tf_op jit(solution)/shard_map/all_to_all | solution.py:324
  28.3 22.4 %all-to-all-done = f32[4,2,256,128]{3,2,1,0:T(8,128)S(1)} async-done(((f32[4,2,256,128]{3,2,1,0:T(8,128)}), f32[4,2,256,128]{3,2,1,0:T(8,128)S(1)}, u32[]{:S(2)}, u32[]{:S(2)}) %all-to-all-start) | async-done | bytes 1048608 | tf_op jit(solution)/shard_map/all_to_all | solution.py:324
  55.4 0.7 collective-permute-start.3
  60.5 1.6 %collective-permute-start.4 = (bf16[2,516,256]{2,0,1:T(2,128)(2,1)S(1)}, bf16[2,516,256]{2,0,1:T(2,128)(2,1)S(1)}, u32[]{:S(2)}, u32[]{:S(2)}) collective-permute-start(bf16[2,516,256]{2,0,1:T(2,128)(2,1)S(1)} %copy.36), channel_id=1, source_target_pairs={{0,1},{1,0},{2,3},{3,2},{4,5},{5,4},{6,7},{7,6},{8,9},{9,8},{10,11... | collective-permute-start | bytes 1585160 | tf_op jit(solution)/shard_map/ppermute | solution.py:145
  62.6 10.9 %collective-permute-done.4 = bf16[2,516,256]{2,0,1:T(2,128)(2,1)S(1)} collective-permute-done((bf16[2,516,256]{2,0,1:T(2,128)(2,1)S(1)}, bf16[2,516,256]{2,0,1:T(2,128)(2,1)S(1)}, u32[]{:S(2)}, u32[]{:S(2)}) %collective-permute-start.4) | collective-permute-done | bytes 528416 | tf_op jit(solution)/shard_map/ppermute | solution.py:145
  75.0 1.5 %collective-permute-done.5 = f32[512,128]{1,0:T(8,128)S(1)} collective-permute-done((f32[512,128]{1,0:T(8,128)S(1)}, f32[512,128]{1,0:T(8,128)S(1)}, u32[]{:S(2)}, u32[]{:S(2)}) %collective-permute-start.5) | collective-permute-done | bytes 262176 | tf_op jit(solution)/shard_map/ppermute | solution.py:359
  76.5 8.2 %collective-permute-start.6 = (f32[128,128]{1,0:T(8,128)S(1)}, f32[128,128]{1,0:T(8,128)S(1)}, u32[]{:S(2)}, u32[]{:S(2)}) collective-permute-start(f32[128,128]{1,0:T(8,128)S(1)} %get-tuple-element.29), channel_id=1, source_target_pairs={{0,4},{4,8},{8,12},{12,0},{1,5},{5,9},{9,13},{13,1},{2,6},{6,10},{... | collective-permute-start | bytes 196616 | tf_op jit(solution)/shard_map/ppermute | solution.py:213
  84.8 1.5 %collective-permute-start.7 = (f32[128,128]{1,0:T(8,128)S(1)}, f32[128,128]{1,0:T(8,128)S(1)}, u32[]{:S(2)}, u32[]{:S(2)}) collective-permute-start(f32[128,128]{1,0:T(8,128)S(1)} %get-tuple-element.31), channel_id=1, source_target_pairs={{0,8},{4,12},{8,0},{12,4},{1,9},{5,13},{9,1},{13,5},{2,10},{6,14},... | collective-permute-start | bytes 196616 | tf_op jit(solution)/shard_map/ppermute | solution.py:213
  86.3 2.8 %collective-permute-start.8 = (f32[128,128]{1,0:T(8,128)S(1)}, f32[128,128]{1,0:T(8,128)S(1)}, u32[]{:S(2)}, u32[]{:S(2)}) collective-permute-start(f32[128,128]{1,0:T(8,128)S(1)} %get-tuple-element.30), channel_id=1, source_target_pairs={{0,12},{4,0},{8,4},{12,8},{1,13},{5,1},{9,5},{13,9},{2,14},{6,2},{... | collective-permute-start | bytes 196616 | tf_op jit(solution)/shard_map/ppermute | solution.py:213
  89.1 2.0 %collective-permute-done.7 = f32[128,128]{1,0:T(8,128)S(1)} collective-permute-done((f32[128,128]{1,0:T(8,128)S(1)}, f32[128,128]{1,0:T(8,128)S(1)}, u32[]{:S(2)}, u32[]{:S(2)}) %collective-permute-start.7) | collective-permute-done | bytes 65568 | tf_op jit(solution)/shard_map/ppermute | solution.py:213
  91.3 1.2 %collective-permute-done.9 = f32[128,128]{1,0:T(8,128)S(1)} collective-permute-done((f32[128,128]{1,0:T(8,128)S(1)}, f32[128,128]{1,0:T(8,128)S(1)}, u32[]{:S(2)}, u32[]{:S(2)}) %collective-permute-start.9) | collective-permute-done | bytes 65568 | tf_op jit(solution)/shard_map/ppermute | solution.py:361
  (100 shorter events, 15.0 us)
Async XLA Ops:
  1.5 10.8 %collective-permute-start = (f32[3,256]{1,0:T(4,128)S(1)}, f32[3,256]{1,0:T(4,128)S(1)}, u32[]{:S(2)}, u32[]{:S(2)}) collective-permute-start(f32[3,256]{1,0:T(4,128)S(1)} %bitcast.120), channel_id=1, source_target_pairs={{0,4},{4,8},{8,12},{12,0},{1,5},{5,9},{9,13},{13,1},{2,6},{6,10},{... | collective-permute-start | bytes 9224 | tf_op jit(solution)/shard_map/ppermute | solution.py:213
  4.5 7.8 %collective-permute-start.1 = (f32[3,256]{1,0:T(4,128)S(1)}, f32[3,256]{1,0:T(4,128)S(1)}, u32[]{:S(2)}, u32[]{:S(2)}) collective-permute-start(f32[3,256]{1,0:T(4,128)S(1)} %bitcast.121), channel_id=1, source_target_pairs={{0,8},{4,12},{8,0},{12,4},{1,9},{5,13},{9,1},{13,5},{2,10},{6,14},... | collective-permute-start | bytes 9224 | tf_op jit(solution)/shard_map/ppermute | solution.py:213
  7.1 5.2 %collective-permute-start.2 = (f32[3,256]{1,0:T(4,128)S(1)}, f32[3,256]{1,0:T(4,128)S(1)}, u32[]{:S(2)}, u32[]{:S(2)}) collective-permute-start(f32[3,256]{1,0:T(4,128)S(1)} %bitcast.122), channel_id=1, source_target_pairs={{0,12},{4,0},{8,4},{12,8},{1,13},{5,1},{9,5},{13,9},{2,14},{6,2},{... | collective-permute-start | bytes 9224 | tf_op jit(solution)/shard_map/ppermute | solution.py:213
  14.3 1.0 %copy-start.2 = (bf16[1,640,256]{2,1,0:T(8,128)(2,1)S(1)}, bf16[1,640,256]{2,1,0:T(8,128)(2,1)}, u32[]{:S(2)}) copy-start(bf16[1,640,256]{2,1,0:T(8,128)(2,1)} %param.10) | copy-start | bytes 983044
  21.9 3.8 %copy-start.1 = (s32[4]{0:T(128)S(1)}, s32[4]{0:T(128)}, u32[]{:S(2)}) copy-start(s32[4]{0:T(128)} %constant.216.clone) | copy-start | bytes 52
  21.9 28.8 %all-to-all-start = ((f32[4,2,256,128]{3,2,1,0:T(8,128)}), f32[4,2,256,128]{3,2,1,0:T(8,128)S(1)}, u32[]{:S(2)}, u32[]{:S(2)}) async-start(f32[4,2,256,128]{3,2,1,0:T(8,128)} %copy.28), calls=%async_computation | async-start | bytes 2097152 | tf_op jit(solution)/shard_map/all_to_all | solution.py:324
  55.0 2.4 %copy-start = (s32[1,2049]{1,0:T(1,128)S(1)}, s32[1,2049]{1,0:T(1,128)}, u32[]{:S(2)}) copy-start(s32[1,2049]{1,0:T(1,128)} %param.11) | copy-start | bytes 24592
  55.4 4.0 %collective-permute-start.3 = (f32[2,516,128]{2,0,1:T(2,128)S(1)}, f32[2,516,128]{2,0,1:T(2,128)S(1)}, u32[]{:S(2)}, u32[]{:S(2)}) collective-permute-start(f32[2,516,128]{2,0,1:T(2,128)S(1)} %copy.33), channel_id=1, source_target_pairs={{0,0},{4,8},{8,4},{12,12},{1,1},{5,9},{9,5},{13,13},{2,2},{6,10},{... | collective-permute-start | bytes 1585160 | tf_op jit(solution)/shard_map/ppermute | solution.py:293
  60.5 13.0 %collective-permute-start.4 = (bf16[2,516,256]{2,0,1:T(2,128)(2,1)S(1)}, bf16[2,516,256]{2,0,1:T(2,128)(2,1)S(1)}, u32[]{:S(2)}, u32[]{:S(2)}) collective-permute-start(bf16[2,516,256]{2,0,1:T(2,128)(2,1)S(1)} %copy.36), channel_id=1, source_target_pairs={{0,1},{1,0},{2,3},{3,2},{4,5},{5,4},{6,7},{7,6},{8,9},{9,8},{10,11... | collective-permute-start | bytes 1585160 | tf_op jit(solution)/shard_map/ppermute | solution.py:145
  74.9 1.6 %collective-permute-start.5 = (f32[512,128]{1,0:T(8,128)S(1)}, f32[512,128]{1,0:T(8,128)S(1)}, u32[]{:S(2)}, u32[]{:S(2)}) collective-permute-start(f32[512,128]{1,0:T(8,128)S(1)} %constant_dynamic-slice_fusion), channel_id=1, source_target_pairs={{0,2},{2,0},{1,3},{3,1},{4,6},{6,4},{5,7},{7,5},{8,10},{10,8},{9,1... | collective-permute-start | bytes 786440 | tf_op jit(solution)/shard_map/ppermute | solution.py:359
  76.5 12.6 %collective-permute-start.6 = (f32[128,128]{1,0:T(8,128)S(1)}, f32[128,128]{1,0:T(8,128)S(1)}, u32[]{:S(2)}, u32[]{:S(2)}) collective-permute-start(f32[128,128]{1,0:T(8,128)S(1)} %get-tuple-element.29), channel_id=1, source_target_pairs={{0,4},{4,8},{8,12},{12,0},{1,5},{5,9},{9,13},{13,1},{2,6},{6,10},{... | collective-permute-start | bytes 196616 | tf_op jit(solution)/shard_map/ppermute | solution.py:213
  84.8 6.4 %collective-permute-start.7 = (f32[128,128]{1,0:T(8,128)S(1)}, f32[128,128]{1,0:T(8,128)S(1)}, u32[]{:S(2)}, u32[]{:S(2)}) collective-permute-start(f32[128,128]{1,0:T(8,128)S(1)} %get-tuple-element.31), channel_id=1, source_target_pairs={{0,8},{4,12},{8,0},{12,4},{1,9},{5,13},{9,1},{13,5},{2,10},{6,14},... | collective-permute-start | bytes 196616 | tf_op jit(solution)/shard_map/ppermute | solution.py:213
  86.3 4.9 %collective-permute-start.8 = (f32[128,128]{1,0:T(8,128)S(1)}, f32[128,128]{1,0:T(8,128)S(1)}, u32[]{:S(2)}, u32[]{:S(2)}) collective-permute-start(f32[128,128]{1,0:T(8,128)S(1)} %get-tuple-element.30), channel_id=1, source_target_pairs={{0,12},{4,0},{8,4},{12,8},{1,13},{5,1},{9,5},{13,9},{2,14},{6,2},{... | collective-permute-start | bytes 196616 | tf_op jit(solution)/shard_map/ppermute | solution.py:213
  91.2 1.3 %collective-permute-start.9 = (f32[128,128]{1,0:T(8,128)S(1)}, f32[128,128]{1,0:T(8,128)S(1)}, u32[]{:S(2)}, u32[]{:S(2)}) collective-permute-start(f32[128,128]{1,0:T(8,128)S(1)} %fusion.49), channel_id=1, source_target_pairs={{0,2},{2,0},{1,3},{3,1},{4,6},{6,4},{5,7},{7,5},{8,10},{10,8},{9,1... | collective-permute-start | bytes 196616 | tf_op jit(solution)/shard_map/ppermute | solution.py:361

commit v12 on v9

--- a/solution.py
+++ b/solution.py
@@ -204,7 +204,9 @@
     count = lax.axis_size(axis)
     if count > 8:
         received = lax.all_to_all(blocks, axis, 0, 0, tiled=True)
-        return received if ordered else jnp.sum(received, axis=0)
+        if ordered:
+            return received, jnp.arange(count, dtype=jnp.int32)
+        return jnp.sum(received, axis=0)
     me = lax.axis_index(axis)
     arrived = [lax.dynamic_index_in_dim(blocks, me, 0, keepdims=False)]
     for shift in range(1, count):
@@ -216,14 +218,13 @@
         for part in arrived[1:]:
             total = total + part
         return total
-    order = (me - jnp.arange(count, dtype=jnp.int32)) % count
-    return jnp.take(jnp.stack(arrived), order, axis=0)
-
-
-def packed_partials(real_in, imag_in, position, samples):
+    return jnp.stack(arrived), (me - jnp.arange(count, dtype=jnp.int32)) % count
+
+
+def packed_partials(real_in, imag_in, position, samples, sources):
     devices_tm, block_len, columns = real_in.shape
     index = jnp.arange(devices_tm, dtype=jnp.int32)
-    cos_table, sin_table = phase_tables(index, index, devices_tm)
+    cos_table, sin_table = phase_tables(index, sources, devices_tm)
     cos_b = cos_table[:, :, None, None]
     sin_b = sin_table[:, :, None, None]
     real_part = jnp.sum(cos_b * real_in[None] + sin_b * imag_in[None], axis=1)
@@ -301,14 +302,16 @@
     keep_rows = gap_mask.astype(jnp.float32)
     packed = jnp.concatenate([orbit_angles, keep_rows[None]], axis=0)
     packed = packed.reshape(3, devices_tm, block_len).transpose(1, 0, 2)
-    received = swap_blocks(packed, "tm", True)
+    received, sources = swap_blocks(packed, "tm", True)
     flat_orbit = received.transpose(1, 0, 2).reshape(3, devices_tm * block_len)
     spread = synthesize(flat_orbit[0:2], flat_orbit[2], column_index, coeffs).reshape(
         devices_tm, block_len, columns
     )
     position = lax.axis_index("tm")
     half_cols = columns // 2
-    twisted = packed_partials(spread[..., :half_cols], spread[..., half_cols:], position, samples)
+    twisted = packed_partials(
+        spread[..., :half_cols], spread[..., half_cols:], position, samples, sources
+    )
     gathered = lax.all_to_all(twisted, "tm", 0, 0, tiled=True)
     own, far = packed_transform(gathered)
     spectra = unpack_spectra(own, far, position, samples)
@@ -334,11 +337,8 @@
     comps = lax.axis_size("comp")
     rows_total, columns = partial_value.shape
     rows = rows_total // devices_tm
-    if comps != 2 or columns % 256 != 0:
-        pieces = lax.all_to_all(
-            partial_value.reshape(devices_tm, rows, columns), "tm", 0, 0, tiled=True
-        )
-        return comp_sum(jnp.sum(pieces, axis=0))
+    if comps != 2 or columns % 256 != 0 or devices_tm <= 8:
+        return comp_sum(swap_blocks(partial_value.reshape(devices_tm, rows, columns), "tm", False))
     half = columns // 2
     comp = lax.axis_index("comp")
     mine = lax.dynamic_slice_in_dim(partial_value, comp * half, half, axis=1)

time: 91.4 us -> 90.3 us (0.988)
    ppermute x2 -> x1, waiting for transfers between devices: 2.75 us -> 1.33 us  [comp_sum(): other = lax.ppermute(value, 'comp', [(0, 1), (1, 0)])]
    ppermute x6, waiting for transfers between devices: 5.17 us -> 6.29 us  [swap_blocks(): arrived.append(lax.ppermute(outgoing, axis, pairs))]
  transfers between devices with their start and end apart: 11 -> 10, of which waited for: 7 -> 6; matrix products, arithmetic and copies ran while one was open for 6% -> 6% of each run, Pallas kernels for 0% -> 0%
where the time goes in v12:
time: 90.3 us; the launch traced here: 89.9 us
  waiting for transfers between devices  41.5 us (46%)
  starting transfers between devices  24.4 us (27%)
  other arithmetic  9.65 us (11%)
  matrix products  8.22 us (9%)
  local copies, waits for them, and re-layouts  5.55 us (6%)
    all_to_all x1, waiting for transfers between devices, body(): gathered = lax.all_to_all(twisted, 'tm', 0, 0, tiled=True)  23.1 us
    ppermute x6, starting transfers between devices, swap_blocks(): arrived.append(lax.ppermute(outgoing, axis, pairs))  17.8 us
    ppermute x1, waiting for transfers between devices, panel_spectra(): blocks.append(lax.ppermute(spectra, 'panel', pairs))  10.9 us
    ppermute x6, waiting for transfers between devices, swap_blocks(): arrived.append(lax.ppermute(outgoing, axis, pairs))  6.29 us
    dot_general x1, matrix products, synthesize(): latitude = jnp.dot(basis_rows, masked, preferred_element_type=jnp.float32)  4.36 us
    all_to_all x1, starting transfers between devices, body(): gathered = lax.all_to_all(twisted, 'tm', 0, 0, tiled=True)  4.28 us
    dot_general x4, matrix products, mat(): lax.dot_general(table, value, dims, precision=lax.Precision.HIGH, preferr...  2.73 us
  transfers between devices with their start and end apart: 10, of which 6 were waited for; matrix products, arithmetic and copies ran while one was open for 6% of the time, Pallas kernels for 0%

profile of v12, /device:TPU:0, one launch (start us, length us, event | category | flops | bytes accessed | tf_op | source)
XLA Modules:
  0.0 89.9 jit_solution(10928111237363328068)
XLA Ops:
  0.0 0.7 concatenate.47
  0.7 0.7 convert_element_type.119
  1.5 3.1 %collective-permute-start = (f32[3,256]{1,0:T(4,128)S(1)}, f32[3,256]{1,0:T(4,128)S(1)}, u32[]{:S(2)}, u32[]{:S(2)}) collective-permute-start(f32[3,256]{1,0:T(4,128)S(1)} %bitcast.117), channel_id=1, source_target_pairs={{0,4},{4,8},{8,12},{12,0},{1,5},{5,9},{9,13},{13,1},{2,6},{6,10},{... | collective-permute-start | bytes 9224 | tf_op jit(solution)/shard_map/ppermute | solution.py:215
  4.5 2.6 %collective-permute-start.1 = (f32[3,256]{1,0:T(4,128)S(1)}, f32[3,256]{1,0:T(4,128)S(1)}, u32[]{:S(2)}, u32[]{:S(2)}) collective-permute-start(f32[3,256]{1,0:T(4,128)S(1)} %bitcast.118), channel_id=1, source_target_pairs={{0,8},{4,12},{8,0},{12,4},{1,9},{5,13},{9,1},{13,5},{2,10},{6,14},... | collective-permute-start | bytes 9224 | tf_op jit(solution)/shard_map/ppermute | solution.py:215
  7.1 1.3 %collective-permute-start.2 = (f32[3,256]{1,0:T(4,128)S(1)}, f32[3,256]{1,0:T(4,128)S(1)}, u32[]{:S(2)}, u32[]{:S(2)}) collective-permute-start(f32[3,256]{1,0:T(4,128)S(1)} %bitcast.119), channel_id=1, source_target_pairs={{0,12},{4,0},{8,4},{12,8},{1,13},{5,1},{9,5},{13,9},{2,14},{6,2},{... | collective-permute-start | bytes 9224 | tf_op jit(solution)/shard_map/ppermute | solution.py:215
  8.5 0.8 fusion.86
  9.3 0.7 add_rsqrt_fusion
  9.9 0.7 compare_reduce_fusion
  12.2 0.7 fusion.5
  13.2 4.4 %fusion = f32[1024,256]{1,0:T(8,128)S(1)} fusion(bf16[1024,320]{0,1:T(8,128)(2,1)S(1)} %get-tuple-element.10, bf16[1024,320]{0,1:T(8,128)(2,1)S(1)} %get-tuple-element.9, f32[256]{0:T(256)S(1)} %bitcast.122, f32[1024]{0:T(1024)S(1)} %bitcast.121, f32[256]{0:T(256)S(1)} %bitcast.124, f32[1024]{0:T(1024)S(1)} %bitcast.120, ...), kind=kOutput, calls=%fused_computation.8 | convolution fusion | flops 339804160 | bytes 2701056 | tf_op jit(solution)/shard_map/dot_general | solution.py:55
  18.7 1.1 %copy.19 = f32[4,2,256,128]{3,2,1,0:T(8,128)} copy(f32[4,2,256,128]{3,2,0,1:T(8,128)S(1)} %pad_maximum_fusion) | data formatting | bytes 2097152 | tf_op jit(solution)/shard_map/stack | solution.py:234
  19.8 4.3 %all-to-all-start = ((f32[4,2,256,128]{3,2,1,0:T(8,128)}), f32[4,2,256,128]{3,2,1,0:T(8,128)S(1)}, u32[]{:S(2)}, u32[]{:S(2)}) async-start(f32[4,2,256,128]{3,2,1,0:T(8,128)} %copy.19), calls=%async_computation | async-start | bytes 2097152 | tf_op jit(solution)/shard_map/all_to_all | solution.py:315
  25.4 23.1 %all-to-all-done = f32[4,2,256,128]{3,2,1,0:T(8,128)S(1)} async-done(((f32[4,2,256,128]{3,2,1,0:T(8,128)}), f32[4,2,256,128]{3,2,1,0:T(8,128)S(1)}, u32[]{:S(2)}, u32[]{:S(2)}) %all-to-all-start) | async-done | bytes 1048608 | tf_op jit(solution)/shard_map/all_to_all | solution.py:315
  49.2 0.7 fusion.27
  51.2 0.7 fusion.30
  53.2 0.7 collective-permute-start.3
  56.4 1.6 %collective-permute-start.4 = (bf16[2,516,256]{2,0,1:T(2,128)(2,1)S(1)}, bf16[2,516,256]{2,0,1:T(2,128)(2,1)S(1)}, u32[]{:S(2)}, u32[]{:S(2)}) collective-permute-start(bf16[2,516,256]{2,0,1:T(2,128)(2,1)S(1)} %copy.27), channel_id=1, source_target_pairs={{0,1},{1,0},{2,3},{3,2},{4,5},{5,4},{6,7},{7,6},{8,9},{9,8},{10,11... | collective-permute-start | bytes 1585160 | tf_op jit(solution)/shard_map/ppermute | solution.py:145
  58.5 10.9 %collective-permute-done.4 = bf16[2,516,256]{2,0,1:T(2,128)(2,1)S(1)} collective-permute-done((bf16[2,516,256]{2,0,1:T(2,128)(2,1)S(1)}, bf16[2,516,256]{2,0,1:T(2,128)(2,1)S(1)}, u32[]{:S(2)}, u32[]{:S(2)}) %collective-permute-start.4) | collective-permute-done | bytes 528416 | tf_op jit(solution)/shard_map/ppermute | solution.py:145
  70.8 8.3 %collective-permute-start.5 = (f32[128,256]{1,0:T(8,128)S(1)}, f32[128,256]{1,0:T(8,128)S(1)}, u32[]{:S(2)}, u32[]{:S(2)}) collective-permute-start(f32[128,256]{1,0:T(8,128)S(1)} %get-tuple-element.27), channel_id=1, source_target_pairs={{0,4},{4,8},{8,12},{12,0},{1,5},{5,9},{9,13},{13,1},{2,6},{6,10},{... | collective-permute-start | bytes 393224 | tf_op jit(solution)/shard_map/ppermute | solution.py:215
  79.1 2.4 %collective-permute-start.6 = (f32[128,256]{1,0:T(8,128)S(1)}, f32[128,256]{1,0:T(8,128)S(1)}, u32[]{:S(2)}, u32[]{:S(2)}) collective-permute-start(f32[128,256]{1,0:T(8,128)S(1)} %get-tuple-element.29), channel_id=1, source_target_pairs={{0,8},{4,12},{8,0},{12,4},{1,9},{5,13},{9,1},{13,5},{2,10},{6,14},... | collective-permute-start | bytes 393224 | tf_op jit(solution)/shard_map/ppermute | solution.py:215
  81.5 2.4 %collective-permute-done.5 = f32[128,256]{1,0:T(8,128)S(1)} collective-permute-done((f32[128,256]{1,0:T(8,128)S(1)}, f32[128,256]{1,0:T(8,128)S(1)}, u32[]{:S(2)}, u32[]{:S(2)}) %collective-permute-start.5) | collective-permute-done | bytes 131104 | tf_op jit(solution)/shard_map/ppermute | solution.py:215
  83.9 2.9 %collective-permute-done.6 = f32[128,256]{1,0:T(8,128)S(1)} collective-permute-done((f32[128,256]{1,0:T(8,128)S(1)}, f32[128,256]{1,0:T(8,128)S(1)}, u32[]{:S(2)}, u32[]{:S(2)}) %collective-permute-start.6) | collective-permute-done | bytes 131104 | tf_op jit(solution)/shard_map/ppermute | solution.py:215
  86.8 1.0 %collective-permute-done.7 = f32[128,256]{1,0:T(8,128)S(1)} collective-permute-done((f32[128,256]{1,0:T(8,128)S(1)}, f32[128,256]{1,0:T(8,128)S(1)}, u32[]{:S(2)}, u32[]{:S(2)}) %collective-permute-start.7) | collective-permute-done | bytes 131104 | tf_op jit(solution)/shard_map/ppermute | solution.py:215
  87.9 1.3 %collective-permute-done.8 = f32[128,256]{1,0:T(8,128)S(1)} collective-permute-done((f32[128,256]{1,0:T(8,128)S(1)}, f32[128,256]{1,0:T(8,128)S(1)}, u32[]{:S(2)}, u32[]{:S(2)}) %collective-permute-start.8) | collective-permute-done | bytes 131104 | tf_op jit(solution)/shard_map/ppermute | solution.py:155
  (93 shorter events, 12.5 us)
Async XLA Ops:
  1.5 9.3 %collective-permute-start = (f32[3,256]{1,0:T(4,128)S(1)}, f32[3,256]{1,0:T(4,128)S(1)}, u32[]{:S(2)}, u32[]{:S(2)}) collective-permute-start(f32[3,256]{1,0:T(4,128)S(1)} %bitcast.117), channel_id=1, source_target_pairs={{0,4},{4,8},{8,12},{12,0},{1,5},{5,9},{9,13},{13,1},{2,6},{6,10},{... | collective-permute-start | bytes 9224 | tf_op jit(solution)/shard_map/ppermute | solution.py:215
  4.5 6.3 %collective-permute-start.1 = (f32[3,256]{1,0:T(4,128)S(1)}, f32[3,256]{1,0:T(4,128)S(1)}, u32[]{:S(2)}, u32[]{:S(2)}) collective-permute-start(f32[3,256]{1,0:T(4,128)S(1)} %bitcast.118), channel_id=1, source_target_pairs={{0,8},{4,12},{8,0},{12,4},{1,9},{5,13},{9,1},{13,5},{2,10},{6,14},... | collective-permute-start | bytes 9224 | tf_op jit(solution)/shard_map/ppermute | solution.py:215
  7.1 3.7 %collective-permute-start.2 = (f32[3,256]{1,0:T(4,128)S(1)}, f32[3,256]{1,0:T(4,128)S(1)}, u32[]{:S(2)}, u32[]{:S(2)}) collective-permute-start(f32[3,256]{1,0:T(4,128)S(1)} %bitcast.119), channel_id=1, source_target_pairs={{0,12},{4,0},{8,4},{12,8},{1,13},{5,1},{9,5},{13,9},{2,14},{6,2},{... | collective-permute-start | bytes 9224 | tf_op jit(solution)/shard_map/ppermute | solution.py:215
  12.2 1.0 %copy-start.1 = (bf16[1,640,256]{2,1,0:T(8,128)(2,1)S(1)}, bf16[1,640,256]{2,1,0:T(8,128)(2,1)}, u32[]{:S(2)}) copy-start(bf16[1,640,256]{2,1,0:T(8,128)(2,1)} %param.8) | copy-start | bytes 983044
  19.8 28.7 %all-to-all-start = ((f32[4,2,256,128]{3,2,1,0:T(8,128)}), f32[4,2,256,128]{3,2,1,0:T(8,128)S(1)}, u32[]{:S(2)}, u32[]{:S(2)}) async-start(f32[4,2,256,128]{3,2,1,0:T(8,128)} %copy.19), calls=%async_computation | async-start | bytes 2097152 | tf_op jit(solution)/shard_map/all_to_all | solution.py:315
  52.8 1.1 %copy-start = (s32[1,2049]{1,0:T(1,128)S(1)}, s32[1,2049]{1,0:T(1,128)}, u32[]{:S(2)}) copy-start(s32[1,2049]{1,0:T(1,128)} %param.9) | copy-start | bytes 24592
  53.2 2.1 %collective-permute-start.3 = (f32[2,516,128]{2,0,1:T(2,128)S(1)}, f32[2,516,128]{2,0,1:T(2,128)S(1)}, u32[]{:S(2)}, u32[]{:S(2)}) collective-permute-start(f32[2,516,128]{2,0,1:T(2,128)S(1)} %copy.24), channel_id=1, source_target_pairs={{0,0},{4,12},{8,8},{12,4},{1,1},{5,13},{9,9},{13,5},{2,2},{6,14},{... | collective-permute-start | bytes 1585160 | tf_op jit(solution)/shard_map/ppermute | solution.py:282
  56.4 13.0 %collective-permute-start.4 = (bf16[2,516,256]{2,0,1:T(2,128)(2,1)S(1)}, bf16[2,516,256]{2,0,1:T(2,128)(2,1)S(1)}, u32[]{:S(2)}, u32[]{:S(2)}) collective-permute-start(bf16[2,516,256]{2,0,1:T(2,128)(2,1)S(1)} %copy.27), channel_id=1, source_target_pairs={{0,1},{1,0},{2,3},{3,2},{4,5},{5,4},{6,7},{7,6},{8,9},{9,8},{10,11... | collective-permute-start | bytes 1585160 | tf_op jit(solution)/shard_map/ppermute | solution.py:145
  70.8 13.2 %collective-permute-start.5 = (f32[128,256]{1,0:T(8,128)S(1)}, f32[128,256]{1,0:T(8,128)S(1)}, u32[]{:S(2)}, u32[]{:S(2)}) collective-permute-start(f32[128,256]{1,0:T(8,128)S(1)} %get-tuple-element.27), channel_id=1, source_target_pairs={{0,4},{4,8},{8,12},{12,0},{1,5},{5,9},{9,13},{13,1},{2,6},{6,10},{... | collective-permute-start | bytes 393224 | tf_op jit(solution)/shard_map/ppermute | solution.py:215
  79.1 7.8 %collective-permute-start.6 = (f32[128,256]{1,0:T(8,128)S(1)}, f32[128,256]{1,0:T(8,128)S(1)}, u32[]{:S(2)}, u32[]{:S(2)}) collective-permute-start(f32[128,256]{1,0:T(8,128)S(1)} %get-tuple-element.29), channel_id=1, source_target_pairs={{0,8},{4,12},{8,0},{12,4},{1,9},{5,13},{9,1},{13,5},{2,10},{6,14},... | collective-permute-start | bytes 393224 | tf_op jit(solution)/shard_map/ppermute | solution.py:215
  81.4 6.4 %collective-permute-start.7 = (f32[128,256]{1,0:T(8,128)S(1)}, f32[128,256]{1,0:T(8,128)S(1)}, u32[]{:S(2)}, u32[]{:S(2)}) collective-permute-start(f32[128,256]{1,0:T(8,128)S(1)} %get-tuple-element.28), channel_id=1, source_target_pairs={{0,12},{4,0},{8,4},{12,8},{1,13},{5,1},{9,5},{13,9},{2,14},{6,2},{... | collective-permute-start | bytes 393224 | tf_op jit(solution)/shard_map/ppermute | solution.py:215
  87.8 1.4 %collective-permute-start.8 = (f32[128,256]{1,0:T(8,128)S(1)}, f32[128,256]{1,0:T(8,128)S(1)}, u32[]{:S(2)}, u32[]{:S(2)}) collective-permute-start(f32[128,256]{1,0:T(8,128)S(1)} %fusion.45), channel_id=1, source_target_pairs={{0,2},{2,0},{1,3},{3,1},{4,6},{6,4},{5,7},{7,5},{8,10},{10,8},{9,1... | collective-permute-start | bytes 393224 | tf_op jit(solution)/shard_map/ppermute | solution.py:155

commit v13 on v12

--- a/solution.py
+++ b/solution.py
@@ -42,20 +42,26 @@
     return jnp.concatenate([cos_k, sin_k], axis=1)
 
 
-def synthesize(angles, keep_rows, column_index, coeffs):
+def column_factors(column_index, coeffs):
     terms_lat = coeffs.shape[0] // 2
-    colatitude = angles[0]
-    longit = angles[1]
-    basis_rows = colatitude_basis(colatitude, terms_lat).astype(jnp.bfloat16)
     degree = column_index[0]
     orders = column_index[1]
     levels = jnp.arange(2 * terms_lat, dtype=jnp.int32) % terms_lat
     allowed = levels[:, None] <= degree[None, :]
     masked = jnp.where(allowed, coeffs, jnp.zeros_like(coeffs))
+    norm_scale = 1.0 / jnp.sqrt(degree.astype(jnp.float32) + 1.0)
+    return masked, norm_scale
+
+
+def synthesize(angles, keep_rows, column_index, masked, norm_scale):
+    terms_lat = masked.shape[0] // 2
+    colatitude = angles[0]
+    longit = angles[1]
+    basis_rows = colatitude_basis(colatitude, terms_lat).astype(jnp.bfloat16)
+    orders = column_index[1]
     latitude = jnp.dot(basis_rows, masked, preferred_element_type=jnp.float32)
     lon_phase = longit[:, None] * jnp.abs(orders).astype(jnp.float32)[None, :]
     lon_wave = jnp.where(orders[None, :] >= 0, jnp.cos(lon_phase), jnp.sin(lon_phase))
-    norm_scale = 1.0 / jnp.sqrt(degree.astype(jnp.float32) + 1.0)
     return latitude * lon_wave * (keep_rows[:, None] * norm_scale[None, :])
 
 
@@ -302,9 +308,11 @@
     keep_rows = gap_mask.astype(jnp.float32)
     packed = jnp.concatenate([orbit_angles, keep_rows[None]], axis=0)
     packed = packed.reshape(3, devices_tm, block_len).transpose(1, 0, 2)
+    masked, norm_scale = column_factors(column_index, coeffs)
+    packed, masked, norm_scale = lax.optimization_barrier((packed, masked, norm_scale))
     received, sources = swap_blocks(packed, "tm", True)
     flat_orbit = received.transpose(1, 0, 2).reshape(3, devices_tm * block_len)
-    spread = synthesize(flat_orbit[0:2], flat_orbit[2], column_index, coeffs).reshape(
+    spread = synthesize(flat_orbit[0:2], flat_orbit[2], column_index, masked, norm_scale).reshape(
         devices_tm, block_len, columns
     )
     position = lax.axis_index("tm")

time: 90.3 us -> 91.5 us (1.013)
  waiting for transfers between devices: 41.5 us -> 42.5 us
    ppermute x6, waiting for transfers between devices: 6.29 us -> 7.64 us  [swap_blocks(): arrived.append(lax.ppermute(outgoing, axis, pairs))]
    select_n x1 -> x2, other arithmetic: 0.01 us -> 1.13 us  [the longest x1 1.12 us: column_factors(): masked = jnp.where(allowed, coeffs, jnp.zeros_like(coeffs))]
  transfers between devices with their start and end apart: 10 -> 10, of which waited for: 6 -> 7; matrix products, arithmetic and copies ran while one was open for 6% -> 4% of each run, Pallas kernels for 0% -> 0%
where the time goes in v13:
time: 91.5 us; the launch traced here: 91.1 us
  waiting for transfers between devices  42.5 us (46%)
  starting transfers between devices  24.5 us (27%)
  other arithmetic  10.1 us (11%)
  matrix products  8.12 us (9%)
  local copies, waits for them, and re-layouts  5.29 us (6%)
    all_to_all x1, waiting for transfers between devices, body(): gathered = lax.all_to_all(twisted, 'tm', 0, 0, tiled=True)  22.7 us
    ppermute x6, starting transfers between devices, swap_blocks(): arrived.append(lax.ppermute(outgoing, axis, pairs))  17.8 us
    ppermute x1, waiting for transfers between devices, panel_spectra(): blocks.append(lax.ppermute(spectra, 'panel', pairs))  10.9 us
    ppermute x6, waiting for transfers between devices, swap_blocks(): arrived.append(lax.ppermute(outgoing, axis, pairs))  7.64 us
    all_to_all x1, starting transfers between devices, body(): gathered = lax.all_to_all(twisted, 'tm', 0, 0, tiled=True)  4.42 us
    dot_general x1, matrix products, synthesize(): latitude = jnp.dot(basis_rows, masked, preferred_element_type=jnp.float32)  4.26 us
    dot_general x4, matrix products, mat(): lax.dot_general(table, value, dims, precision=lax.Precision.HIGH, preferr...  2.73 us
  transfers between devices with their start and end apart: 10, of which 7 were waited for; matrix products, arithmetic and copies ran while one was open for 4% of the time, Pallas kernels for 0%

profile of v13, /device:TPU:0, one launch (start us, length us, event | category | flops | bytes accessed | tf_op | source)
XLA Modules:
  0.0 91.1 jit_solution(674132655827307166)
XLA Ops:
  0.0 0.8 abs_convert_fusion
  0.8 0.7 concatenate.47
  1.5 0.7 convert_element_type.118
  2.2 1.1 %compare_select_fusion = bf16[640,256]{1,0:T(8,128)(2,1)S(1)} fusion(bf16[1,640,256]{2,1,0:T(8,128)(2,1)} %param.8, s32[256]{0:T(256)S(1)} %bitcast.115, s32[640]{0:T(1024)S(1)} %add_select_fusion.4), kind=kLoop, calls=%fused_computation.28 | loop fusion | flops 327680 | bytes 658944 | tf_op jit(solution)/shard_map/jit(_where)/select_n | solution.py:51
  3.4 3.1 %collective-permute-start = (f32[3,256]{1,0:T(4,128)S(1)}, f32[3,256]{1,0:T(4,128)S(1)}, u32[]{:S(2)}, u32[]{:S(2)}) collective-permute-start(f32[3,256]{1,0:T(4,128)S(1)} %bitcast.116), channel_id=1, source_target_pairs={{0,4},{4,8},{8,12},{12,0},{1,5},{5,9},{9,13},{13,1},{2,6},{6,10},{... | collective-permute-start | bytes 9224 | tf_op jit(solution)/shard_map/ppermute | solution.py:221
  6.5 2.6 %collective-permute-start.1 = (f32[3,256]{1,0:T(4,128)S(1)}, f32[3,256]{1,0:T(4,128)S(1)}, u32[]{:S(2)}, u32[]{:S(2)}) collective-permute-start(f32[3,256]{1,0:T(4,128)S(1)} %bitcast.117), channel_id=1, source_target_pairs={{0,8},{4,12},{8,0},{12,4},{1,9},{5,13},{9,1},{13,5},{2,10},{6,14},... | collective-permute-start | bytes 9224 | tf_op jit(solution)/shard_map/ppermute | solution.py:221
  9.1 1.3 %collective-permute-start.2 = (f32[3,256]{1,0:T(4,128)S(1)}, f32[3,256]{1,0:T(4,128)S(1)}, u32[]{:S(2)}, u32[]{:S(2)}) collective-permute-start(f32[3,256]{1,0:T(4,128)S(1)} %bitcast.118), channel_id=1, source_target_pairs={{0,12},{4,0},{8,4},{12,8},{1,13},{5,1},{9,5},{13,9},{2,14},{6,2},{... | collective-permute-start | bytes 9224 | tf_op jit(solution)/shard_map/ppermute | solution.py:221
  10.4 0.7 compare_reduce_fusion
  11.3 1.4 %collective-permute-done.2 = f32[3,256]{1,0:T(4,128)S(1)} collective-permute-done((f32[3,256]{1,0:T(4,128)S(1)}, f32[3,256]{1,0:T(4,128)S(1)}, u32[]{:S(2)}, u32[]{:S(2)}) %collective-permute-start.2) | collective-permute-done | bytes 3104 | tf_op jit(solution)/shard_map/ppermute | solution.py:221
  14.0 0.7 fusion.5
  14.8 4.3 %fusion = f32[1024,256]{1,0:T(8,128)S(1)} fusion(bf16[640,256]{1,0:T(8,128)(2,1)S(1)} %compare_select_fusion, bf16[1024,320]{0,1:T(8,128)(2,1)S(1)} %get-tuple-element.16, bf16[1024,320]{0,1:T(8,128)(2,1)S(1)} %get-tuple-element.15, f32[256]{0:T(256)S(1)} %add_rsqrt_fusion, f32[1024]{0:T(1024)S(1)} %bitcast.120, f32[256]{0:T(256)S(1)} %bitcast.121, ...), kind=kOutput, calls=%fused_computation.8 | convolution fusion | flops 339476480 | bytes 2697472 | tf_op jit(solution)/shard_map/dot_general | solution.py:62
  20.2 1.0 %copy.19 = f32[4,2,256,128]{3,2,1,0:T(8,128)} copy(f32[4,2,256,128]{3,2,0,1:T(8,128)S(1)} %pad_maximum_fusion) | data formatting | bytes 2097152 | tf_op jit(solution)/shard_map/stack | solution.py:240
  21.2 4.4 %all-to-all-start = ((f32[4,2,256,128]{3,2,1,0:T(8,128)}), f32[4,2,256,128]{3,2,1,0:T(8,128)S(1)}, u32[]{:S(2)}, u32[]{:S(2)}) async-start(f32[4,2,256,128]{3,2,1,0:T(8,128)} %copy.19), calls=%async_computation | async-start | bytes 2097152 | tf_op jit(solution)/shard_map/all_to_all | solution.py:323
  27.0 22.7 %all-to-all-done = f32[4,2,256,128]{3,2,1,0:T(8,128)S(1)} async-done(((f32[4,2,256,128]{3,2,1,0:T(8,128)}), f32[4,2,256,128]{3,2,1,0:T(8,128)S(1)}, u32[]{:S(2)}, u32[]{:S(2)}) %all-to-all-start) | async-done | bytes 1048608 | tf_op jit(solution)/shard_map/all_to_all | solution.py:323
  52.5 0.7 fusion.27
  54.4 0.7 collective-permute-start.3
  57.6 1.6 %collective-permute-start.4 = (bf16[2,516,256]{2,0,1:T(2,128)(2,1)S(1)}, bf16[2,516,256]{2,0,1:T(2,128)(2,1)S(1)}, u32[]{:S(2)}, u32[]{:S(2)}) collective-permute-start(bf16[2,516,256]{2,0,1:T(2,128)(2,1)S(1)} %copy.27), channel_id=1, source_target_pairs={{0,1},{1,0},{2,3},{3,2},{4,5},{5,4},{6,7},{7,6},{8,9},{9,8},{10,11... | collective-permute-start | bytes 1585160 | tf_op jit(solution)/shard_map/ppermute | solution.py:151
  59.8 10.9 %collective-permute-done.4 = bf16[2,516,256]{2,0,1:T(2,128)(2,1)S(1)} collective-permute-done((bf16[2,516,256]{2,0,1:T(2,128)(2,1)S(1)}, bf16[2,516,256]{2,0,1:T(2,128)(2,1)S(1)}, u32[]{:S(2)}, u32[]{:S(2)}) %collective-permute-start.4) | collective-permute-done | bytes 528416 | tf_op jit(solution)/shard_map/ppermute | solution.py:151
  72.0 8.3 %collective-permute-start.5 = (f32[128,256]{1,0:T(8,128)S(1)}, f32[128,256]{1,0:T(8,128)S(1)}, u32[]{:S(2)}, u32[]{:S(2)}) collective-permute-start(f32[128,256]{1,0:T(8,128)S(1)} %get-tuple-element.33), channel_id=1, source_target_pairs={{0,4},{4,8},{8,12},{12,0},{1,5},{5,9},{9,13},{13,1},{2,6},{6,10},{... | collective-permute-start | bytes 393224 | tf_op jit(solution)/shard_map/ppermute | solution.py:221
  80.3 2.4 %collective-permute-start.6 = (f32[128,256]{1,0:T(8,128)S(1)}, f32[128,256]{1,0:T(8,128)S(1)}, u32[]{:S(2)}, u32[]{:S(2)}) collective-permute-start(f32[128,256]{1,0:T(8,128)S(1)} %get-tuple-element.35), channel_id=1, source_target_pairs={{0,8},{4,12},{8,0},{12,4},{1,9},{5,13},{9,1},{13,5},{2,10},{6,14},... | collective-permute-start | bytes 393224 | tf_op jit(solution)/shard_map/ppermute | solution.py:221
  82.7 2.4 %collective-permute-done.5 = f32[128,256]{1,0:T(8,128)S(1)} collective-permute-done((f32[128,256]{1,0:T(8,128)S(1)}, f32[128,256]{1,0:T(8,128)S(1)}, u32[]{:S(2)}, u32[]{:S(2)}) %collective-permute-start.5) | collective-permute-done | bytes 131104 | tf_op jit(solution)/shard_map/ppermute | solution.py:221
  85.1 2.9 %collective-permute-done.6 = f32[128,256]{1,0:T(8,128)S(1)} collective-permute-done((f32[128,256]{1,0:T(8,128)S(1)}, f32[128,256]{1,0:T(8,128)S(1)}, u32[]{:S(2)}, u32[]{:S(2)}) %collective-permute-start.6) | collective-permute-done | bytes 131104 | tf_op jit(solution)/shard_map/ppermute | solution.py:221
  88.1 1.0 %collective-permute-done.7 = f32[128,256]{1,0:T(8,128)S(1)} collective-permute-done((f32[128,256]{1,0:T(8,128)S(1)}, f32[128,256]{1,0:T(8,128)S(1)}, u32[]{:S(2)}, u32[]{:S(2)}) %collective-permute-start.7) | collective-permute-done | bytes 131104 | tf_op jit(solution)/shard_map/ppermute | solution.py:221
  89.1 1.3 %collective-permute-done.8 = f32[128,256]{1,0:T(8,128)S(1)} collective-permute-done((f32[128,256]{1,0:T(8,128)S(1)}, f32[128,256]{1,0:T(8,128)S(1)}, u32[]{:S(2)}, u32[]{:S(2)}) %collective-permute-start.8) | collective-permute-done | bytes 131104 | tf_op jit(solution)/shard_map/ppermute | solution.py:161
  (91 shorter events, 13.0 us)
Async XLA Ops:
  3.4 7.9 %collective-permute-start = (f32[3,256]{1,0:T(4,128)S(1)}, f32[3,256]{1,0:T(4,128)S(1)}, u32[]{:S(2)}, u32[]{:S(2)}) collective-permute-start(f32[3,256]{1,0:T(4,128)S(1)} %bitcast.116), channel_id=1, source_target_pairs={{0,4},{4,8},{8,12},{12,0},{1,5},{5,9},{9,13},{13,1},{2,6},{6,10},{... | collective-permute-start | bytes 9224 | tf_op jit(solution)/shard_map/ppermute | solution.py:221
  6.5 4.8 %collective-permute-start.1 = (f32[3,256]{1,0:T(4,128)S(1)}, f32[3,256]{1,0:T(4,128)S(1)}, u32[]{:S(2)}, u32[]{:S(2)}) collective-permute-start(f32[3,256]{1,0:T(4,128)S(1)} %bitcast.117), channel_id=1, source_target_pairs={{0,8},{4,12},{8,0},{12,4},{1,9},{5,13},{9,1},{13,5},{2,10},{6,14},... | collective-permute-start | bytes 9224 | tf_op jit(solution)/shard_map/ppermute | solution.py:221
  9.1 3.6 %collective-permute-start.2 = (f32[3,256]{1,0:T(4,128)S(1)}, f32[3,256]{1,0:T(4,128)S(1)}, u32[]{:S(2)}, u32[]{:S(2)}) collective-permute-start(f32[3,256]{1,0:T(4,128)S(1)} %bitcast.118), channel_id=1, source_target_pairs={{0,12},{4,0},{8,4},{12,8},{1,13},{5,1},{9,5},{13,9},{2,14},{6,2},{... | collective-permute-start | bytes 9224 | tf_op jit(solution)/shard_map/ppermute | solution.py:221
  21.2 28.4 %all-to-all-start = ((f32[4,2,256,128]{3,2,1,0:T(8,128)}), f32[4,2,256,128]{3,2,1,0:T(8,128)S(1)}, u32[]{:S(2)}, u32[]{:S(2)}) async-start(f32[4,2,256,128]{3,2,1,0:T(8,128)} %copy.19), calls=%async_computation | async-start | bytes 2097152 | tf_op jit(solution)/shard_map/all_to_all | solution.py:323
  54.1 1.1 %copy-start = (s32[1,2049]{1,0:T(1,128)S(1)}, s32[1,2049]{1,0:T(1,128)}, u32[]{:S(2)}) copy-start(s32[1,2049]{1,0:T(1,128)} %param.9) | copy-start | bytes 24592
  54.4 2.1 %collective-permute-start.3 = (f32[2,516,128]{2,0,1:T(2,128)S(1)}, f32[2,516,128]{2,0,1:T(2,128)S(1)}, u32[]{:S(2)}, u32[]{:S(2)}) collective-permute-start(f32[2,516,128]{2,0,1:T(2,128)S(1)} %copy.24), channel_id=1, source_target_pairs={{0,0},{4,12},{8,8},{12,4},{1,1},{5,13},{9,9},{13,5},{2,2},{6,14},{... | collective-permute-start | bytes 1585160 | tf_op jit(solution)/shard_map/ppermute | solution.py:288
  57.6 13.0 %collective-permute-start.4 = (bf16[2,516,256]{2,0,1:T(2,128)(2,1)S(1)}, bf16[2,516,256]{2,0,1:T(2,128)(2,1)S(1)}, u32[]{:S(2)}, u32[]{:S(2)}) collective-permute-start(bf16[2,516,256]{2,0,1:T(2,128)(2,1)S(1)} %copy.27), channel_id=1, source_target_pairs={{0,1},{1,0},{2,3},{3,2},{4,5},{5,4},{6,7},{7,6},{8,9},{9,8},{10,11... | collective-permute-start | bytes 1585160 | tf_op jit(solution)/shard_map/ppermute | solution.py:151
  72.0 13.2 %collective-permute-start.5 = (f32[128,256]{1,0:T(8,128)S(1)}, f32[128,256]{1,0:T(8,128)S(1)}, u32[]{:S(2)}, u32[]{:S(2)}) collective-permute-start(f32[128,256]{1,0:T(8,128)S(1)} %get-tuple-element.33), channel_id=1, source_target_pairs={{0,4},{4,8},{8,12},{12,0},{1,5},{5,9},{9,13},{13,1},{2,6},{6,10},{... | collective-permute-start | bytes 393224 | tf_op jit(solution)/shard_map/ppermute | solution.py:221
  80.3 7.8 %collective-permute-start.6 = (f32[128,256]{1,0:T(8,128)S(1)}, f32[128,256]{1,0:T(8,128)S(1)}, u32[]{:S(2)}, u32[]{:S(2)}) collective-permute-start(f32[128,256]{1,0:T(8,128)S(1)} %get-tuple-element.35), channel_id=1, source_target_pairs={{0,8},{4,12},{8,0},{12,4},{1,9},{5,13},{9,1},{13,5},{2,10},{6,14},... | collective-permute-start | bytes 393224 | tf_op jit(solution)/shard_map/ppermute | solution.py:221
  82.7 6.4 %collective-permute-start.7 = (f32[128,256]{1,0:T(8,128)S(1)}, f32[128,256]{1,0:T(8,128)S(1)}, u32[]{:S(2)}, u32[]{:S(2)}) collective-permute-start(f32[128,256]{1,0:T(8,128)S(1)} %get-tuple-element.34), channel_id=1, source_target_pairs={{0,12},{4,0},{8,4},{12,8},{1,13},{5,1},{9,5},{13,9},{2,14},{6,2},{... | collective-permute-start | bytes 393224 | tf_op jit(solution)/shard_map/ppermute | solution.py:221
  89.1 1.4 %collective-permute-start.8 = (f32[128,256]{1,0:T(8,128)S(1)}, f32[128,256]{1,0:T(8,128)S(1)}, u32[]{:S(2)}, u32[]{:S(2)}) collective-permute-start(f32[128,256]{1,0:T(8,128)S(1)} %fusion.41), channel_id=1, source_target_pairs={{0,2},{2,0},{1,3},{3,1},{4,6},{6,4},{5,7},{7,5},{8,10},{10,8},{9,1... | collective-permute-start | bytes 393224 | tf_op jit(solution)/shard_map/ppermute | solution.py:161

commit v14 on v12

--- a/solution.py
+++ b/solution.py
@@ -291,6 +291,26 @@
     return jnp.stack([new_real.astype(jnp.bfloat16), new_imag.astype(jnp.bfloat16)])
 
 
+def packed_direct(spread, position, samples, sources):
+    devices_tm, block_len, columns = spread.shape
+    half_cols = columns // 2
+    index = jnp.arange(devices_tm, dtype=jnp.int32)
+    cos_table, sin_table = phase_tables(index, sources, devices_tm)
+    local_epoch = position * block_len + jnp.arange(block_len, dtype=jnp.int32)
+    cos_turn, sin_turn = phase_tables(index, local_epoch, samples)
+    cos_k = cos_table[:, :, None]
+    sin_k = sin_table[:, :, None]
+    cos_u = cos_turn[:, None, :]
+    sin_u = sin_turn[:, None, :]
+    direct = cos_k * cos_u - sin_k * sin_u
+    cross = sin_k * cos_u + cos_k * sin_u
+    weights = jnp.stack(
+        [jnp.stack([direct, cross], axis=-1), jnp.stack([-cross, direct], axis=-1)], axis=1
+    )
+    parts = spread.reshape(devices_tm, block_len, 2, half_cols)
+    return jnp.sum(weights[..., None] * parts[None, None], axis=(2, 4))
+
+
 def body(orbit_angles, gap_mask, column_index, lat_coeffs, psd_table):
     devices_tm = lax.axis_size("tm")
     panels = lax.axis_size("panel")
@@ -309,9 +329,7 @@
     )
     position = lax.axis_index("tm")
     half_cols = columns // 2
-    twisted = packed_partials(
-        spread[..., :half_cols], spread[..., half_cols:], position, samples, sources
-    )
+    twisted = packed_direct(spread, position, samples, sources)
     gathered = lax.all_to_all(twisted, "tm", 0, 0, tiled=True)
     own, far = packed_transform(gathered)
     spectra = unpack_spectra(own, far, position, samples)

time: 90.3 us -> 93.4 us (1.034)
  other arithmetic: 9.65 us -> 12.2 us
    reduce_sum x1, other arithmetic: 0.65 us -> 3.53 us  [packed_direct(): return jnp.sum(weights[..., None] * parts[None, None], axis=(2, 4))]
    another operation x1, local copies, waits for them, and re-layouts: 1.05 us -> 0.04 us  [packed_direct(): jnp.stack([jnp.stack([direct, cross], axis=-1), jnp.stack([-cross, direct...]
    ppermute x6, starting transfers between devices: 17.8 us -> 18.7 us  [swap_blocks(): arrived.append(lax.ppermute(outgoing, axis, pairs))]
where the time goes in v14:
time: 93.4 us; the launch traced here: 93 us
  waiting for transfers between devices  41.7 us (45%)
  starting transfers between devices  25.2 us (27%)
  other arithmetic  12.2 us (13%)
  matrix products  8.22 us (9%)
  local copies, waits for them, and re-layouts  5.07 us (5%)
    all_to_all x1, waiting for transfers between devices, body(): gathered = lax.all_to_all(twisted, 'tm', 0, 0, tiled=True)  23.2 us
    ppermute x6, starting transfers between devices, swap_blocks(): arrived.append(lax.ppermute(outgoing, axis, pairs))  18.7 us
    ppermute x1, waiting for transfers between devices, panel_spectra(): blocks.append(lax.ppermute(spectra, 'panel', pairs))  10.9 us
    ppermute x6, waiting for transfers between devices, swap_blocks(): arrived.append(lax.ppermute(outgoing, axis, pairs))  6.29 us
    dot_general x1, matrix products, synthesize(): latitude = jnp.dot(basis_rows, masked, preferred_element_type=jnp.float32)  4.35 us
    all_to_all x1, starting transfers between devices, body(): gathered = lax.all_to_all(twisted, 'tm', 0, 0, tiled=True)  4.1 us
    reduce_sum x1, other arithmetic, packed_direct(): return jnp.sum(weights[..., None] * parts[None, None], axis=(2, 4))  3.53 us
    dot_general x4, matrix products, mat(): lax.dot_general(table, value, dims, precision=lax.Precision.HIGH, preferr...  2.73 us
  transfers between devices with their start and end apart: 10, of which 6 were waited for; matrix products, arithmetic and copies ran while one was open for 6% of the time, Pallas kernels for 0%

profile of v14, /device:TPU:0, one launch (start us, length us, event | category | flops | bytes accessed | tf_op | source)
XLA Modules:
  0.0 93.0 jit_solution(10491629427230578754)
XLA Ops:
  0.0 0.7 concatenate.47
  0.7 0.7 convert_element_type.120
  1.5 3.1 %collective-permute-start = (f32[3,256]{1,0:T(4,128)S(1)}, f32[3,256]{1,0:T(4,128)S(1)}, u32[]{:S(2)}, u32[]{:S(2)}) collective-permute-start(f32[3,256]{1,0:T(4,128)S(1)} %bitcast.105), channel_id=1, source_target_pairs={{0,4},{4,8},{8,12},{12,0},{1,5},{5,9},{9,13},{13,1},{2,6},{6,10},{... | collective-permute-start | bytes 9224 | tf_op jit(solution)/shard_map/ppermute | solution.py:215
  4.5 2.6 %collective-permute-start.1 = (f32[3,256]{1,0:T(4,128)S(1)}, f32[3,256]{1,0:T(4,128)S(1)}, u32[]{:S(2)}, u32[]{:S(2)}) collective-permute-start(f32[3,256]{1,0:T(4,128)S(1)} %bitcast.106), channel_id=1, source_target_pairs={{0,8},{4,12},{8,0},{12,4},{1,9},{5,13},{9,1},{13,5},{2,10},{6,14},... | collective-permute-start | bytes 9224 | tf_op jit(solution)/shard_map/ppermute | solution.py:215
  7.1 1.3 %collective-permute-start.2 = (f32[3,256]{1,0:T(4,128)S(1)}, f32[3,256]{1,0:T(4,128)S(1)}, u32[]{:S(2)}, u32[]{:S(2)}) collective-permute-start(f32[3,256]{1,0:T(4,128)S(1)} %bitcast.107), channel_id=1, source_target_pairs={{0,12},{4,0},{8,4},{12,8},{1,13},{5,1},{9,5},{13,9},{2,14},{6,2},{... | collective-permute-start | bytes 9224 | tf_op jit(solution)/shard_map/ppermute | solution.py:215
  8.5 0.8 fusion.84
  9.3 0.7 add_rsqrt_fusion
  9.9 0.7 compare_reduce_fusion
  12.4 0.7 fusion.5
  13.4 4.4 %fusion = f32[1024,256]{1,0:T(8,128)S(1)} fusion(bf16[1024,320]{0,1:T(8,128)(2,1)S(1)} %get-tuple-element.8, bf16[1024,320]{0,1:T(8,128)(2,1)S(1)} %get-tuple-element.7, f32[256]{0:T(256)S(1)} %bitcast.110, f32[1024]{0:T(1024)S(1)} %bitcast.109, f32[256]{0:T(256)S(1)} %bitcast.112, f32[1024]{0:T(1024)S(1)} %bitcast.108, ...), kind=kOutput, calls=%fused_computation.7 | convolution fusion | flops 339804160 | bytes 2701056 | tf_op jit(solution)/shard_map/dot_general | solution.py:55
  18.4 3.5 %multiply_reduce_fusion = f32[4,2,256,128]{3,2,1,0:T(8,128)} fusion(f32[4,256,2,128]{3,1,2,0:T(8,128)S(1)} %copy.25, f32[4,2,4,256,2]{3,4,2,1,0:T(2,128)S(1)} %copy.24), kind=kLoop, calls=%fused_computation.1 | loop fusion | flops 3932160 | bytes 2162688 | tf_op jit(solution)/shard_map/reduce_sum | solution.py:311
  21.9 4.1 %all-to-all-start = ((f32[4,2,256,128]{3,2,1,0:T(8,128)}), f32[4,2,256,128]{3,2,1,0:T(8,128)S(1)}, u32[]{:S(2)}, u32[]{:S(2)}) async-start(f32[4,2,256,128]{3,2,1,0:T(8,128)} %multiply_reduce_fusion), calls=%async_computation | async-start | bytes 2097152 | tf_op jit(solution)/shard_map/all_to_all | solution.py:333
  27.3 23.2 %all-to-all-done = f32[4,2,256,128]{3,2,1,0:T(8,128)S(1)} async-done(((f32[4,2,256,128]{3,2,1,0:T(8,128)}), f32[4,2,256,128]{3,2,1,0:T(8,128)S(1)}, u32[]{:S(2)}, u32[]{:S(2)}) %all-to-all-start) | async-done | bytes 1048608 | tf_op jit(solution)/shard_map/all_to_all | solution.py:333
  51.3 0.7 fusion.25
  52.0 0.7 fusion.26
  53.4 0.7 fusion.28
  55.3 0.7 collective-permute-start.3
  58.5 1.6 %collective-permute-start.4 = (bf16[2,516,256]{2,0,1:T(2,128)(2,1)S(1)}, bf16[2,516,256]{2,0,1:T(2,128)(2,1)S(1)}, u32[]{:S(2)}, u32[]{:S(2)}) collective-permute-start(bf16[2,516,256]{2,0,1:T(2,128)(2,1)S(1)} %copy.33), channel_id=1, source_target_pairs={{0,1},{1,0},{2,3},{3,2},{4,5},{5,4},{6,7},{7,6},{8,9},{9,8},{10,11... | collective-permute-start | bytes 1585160 | tf_op jit(solution)/shard_map/ppermute | solution.py:145
  60.7 10.9 %collective-permute-done.4 = bf16[2,516,256]{2,0,1:T(2,128)(2,1)S(1)} collective-permute-done((bf16[2,516,256]{2,0,1:T(2,128)(2,1)S(1)}, bf16[2,516,256]{2,0,1:T(2,128)(2,1)S(1)}, u32[]{:S(2)}, u32[]{:S(2)}) %collective-permute-start.4) | collective-permute-done | bytes 528416 | tf_op jit(solution)/shard_map/ppermute | solution.py:145
  72.9 9.3 %collective-permute-start.5 = (f32[128,256]{1,0:T(8,128)S(1)}, f32[128,256]{1,0:T(8,128)S(1)}, u32[]{:S(2)}, u32[]{:S(2)}) collective-permute-start(f32[128,256]{1,0:T(8,128)S(1)} %get-tuple-element.21), channel_id=1, source_target_pairs={{0,4},{4,8},{8,12},{12,0},{1,5},{5,9},{9,13},{13,1},{2,6},{6,10},{... | collective-permute-start | bytes 393224 | tf_op jit(solution)/shard_map/ppermute | solution.py:215
  82.2 2.4 %collective-permute-start.6 = (f32[128,256]{1,0:T(8,128)S(1)}, f32[128,256]{1,0:T(8,128)S(1)}, u32[]{:S(2)}, u32[]{:S(2)}) collective-permute-start(f32[128,256]{1,0:T(8,128)S(1)} %get-tuple-element.23), channel_id=1, source_target_pairs={{0,8},{4,12},{8,0},{12,4},{1,9},{5,13},{9,1},{13,5},{2,10},{6,14},... | collective-permute-start | bytes 393224 | tf_op jit(solution)/shard_map/ppermute | solution.py:215
  84.6 2.4 %collective-permute-done.5 = f32[128,256]{1,0:T(8,128)S(1)} collective-permute-done((f32[128,256]{1,0:T(8,128)S(1)}, f32[128,256]{1,0:T(8,128)S(1)}, u32[]{:S(2)}, u32[]{:S(2)}) %collective-permute-start.5) | collective-permute-done | bytes 131104 | tf_op jit(solution)/shard_map/ppermute | solution.py:215
  87.0 3.4 %collective-permute-done.6 = f32[128,256]{1,0:T(8,128)S(1)} collective-permute-done((f32[128,256]{1,0:T(8,128)S(1)}, f32[128,256]{1,0:T(8,128)S(1)}, u32[]{:S(2)}, u32[]{:S(2)}) %collective-permute-start.6) | collective-permute-done | bytes 131104 | tf_op jit(solution)/shard_map/ppermute | solution.py:215
  91.0 1.3 %collective-permute-done.8 = f32[128,256]{1,0:T(8,128)S(1)} collective-permute-done((f32[128,256]{1,0:T(8,128)S(1)}, f32[128,256]{1,0:T(8,128)S(1)}, u32[]{:S(2)}, u32[]{:S(2)}) %collective-permute-start.8) | collective-permute-done | bytes 131104 | tf_op jit(solution)/shard_map/ppermute | solution.py:155
  (95 shorter events, 12.0 us)
Async XLA Ops:
  1.5 9.5 %collective-permute-start = (f32[3,256]{1,0:T(4,128)S(1)}, f32[3,256]{1,0:T(4,128)S(1)}, u32[]{:S(2)}, u32[]{:S(2)}) collective-permute-start(f32[3,256]{1,0:T(4,128)S(1)} %bitcast.105), channel_id=1, source_target_pairs={{0,4},{4,8},{8,12},{12,0},{1,5},{5,9},{9,13},{13,1},{2,6},{6,10},{... | collective-permute-start | bytes 9224 | tf_op jit(solution)/shard_map/ppermute | solution.py:215
  4.5 6.5 %collective-permute-start.1 = (f32[3,256]{1,0:T(4,128)S(1)}, f32[3,256]{1,0:T(4,128)S(1)}, u32[]{:S(2)}, u32[]{:S(2)}) collective-permute-start(f32[3,256]{1,0:T(4,128)S(1)} %bitcast.106), channel_id=1, source_target_pairs={{0,8},{4,12},{8,0},{12,4},{1,9},{5,13},{9,1},{13,5},{2,10},{6,14},... | collective-permute-start | bytes 9224 | tf_op jit(solution)/shard_map/ppermute | solution.py:215
  7.1 3.9 %collective-permute-start.2 = (f32[3,256]{1,0:T(4,128)S(1)}, f32[3,256]{1,0:T(4,128)S(1)}, u32[]{:S(2)}, u32[]{:S(2)}) collective-permute-start(f32[3,256]{1,0:T(4,128)S(1)} %bitcast.107), channel_id=1, source_target_pairs={{0,12},{4,0},{8,4},{12,8},{1,13},{5,1},{9,5},{13,9},{2,14},{6,2},{... | collective-permute-start | bytes 9224 | tf_op jit(solution)/shard_map/ppermute | solution.py:215
  12.4 1.0 %copy-start.1 = (bf16[1,640,256]{2,1,0:T(8,128)(2,1)S(1)}, bf16[1,640,256]{2,1,0:T(8,128)(2,1)}, u32[]{:S(2)}) copy-start(bf16[1,640,256]{2,1,0:T(8,128)(2,1)} %param.8) | copy-start | bytes 983044
  21.9 28.7 %all-to-all-start = ((f32[4,2,256,128]{3,2,1,0:T(8,128)}), f32[4,2,256,128]{3,2,1,0:T(8,128)S(1)}, u32[]{:S(2)}, u32[]{:S(2)}) async-start(f32[4,2,256,128]{3,2,1,0:T(8,128)} %multiply_reduce_fusion), calls=%async_computation | async-start | bytes 2097152 | tf_op jit(solution)/shard_map/all_to_all | solution.py:333
  55.0 1.1 %copy-start = (s32[1,2049]{1,0:T(1,128)S(1)}, s32[1,2049]{1,0:T(1,128)}, u32[]{:S(2)}) copy-start(s32[1,2049]{1,0:T(1,128)} %param.9) | copy-start | bytes 24592
  55.3 2.1 %collective-permute-start.3 = (f32[2,516,128]{2,0,1:T(2,128)S(1)}, f32[2,516,128]{2,0,1:T(2,128)S(1)}, u32[]{:S(2)}, u32[]{:S(2)}) collective-permute-start(f32[2,516,128]{2,0,1:T(2,128)S(1)} %copy.30), channel_id=1, source_target_pairs={{0,0},{4,12},{8,8},{12,4},{1,1},{5,13},{9,9},{13,5},{2,2},{6,14},{... | collective-permute-start | bytes 1585160 | tf_op jit(solution)/shard_map/ppermute | solution.py:282
  58.5 13.0 %collective-permute-start.4 = (bf16[2,516,256]{2,0,1:T(2,128)(2,1)S(1)}, bf16[2,516,256]{2,0,1:T(2,128)(2,1)S(1)}, u32[]{:S(2)}, u32[]{:S(2)}) collective-permute-start(bf16[2,516,256]{2,0,1:T(2,128)(2,1)S(1)} %copy.33), channel_id=1, source_target_pairs={{0,1},{1,0},{2,3},{3,2},{4,5},{5,4},{6,7},{7,6},{8,9},{9,8},{10,11... | collective-permute-start | bytes 1585160 | tf_op jit(solution)/shard_map/ppermute | solution.py:145
  72.9 14.1 %collective-permute-start.5 = (f32[128,256]{1,0:T(8,128)S(1)}, f32[128,256]{1,0:T(8,128)S(1)}, u32[]{:S(2)}, u32[]{:S(2)}) collective-permute-start(f32[128,256]{1,0:T(8,128)S(1)} %get-tuple-element.21), channel_id=1, source_target_pairs={{0,4},{4,8},{8,12},{12,0},{1,5},{5,9},{9,13},{13,1},{2,6},{6,10},{... | collective-permute-start | bytes 393224 | tf_op jit(solution)/shard_map/ppermute | solution.py:215
  82.2 8.2 %collective-permute-start.6 = (f32[128,256]{1,0:T(8,128)S(1)}, f32[128,256]{1,0:T(8,128)S(1)}, u32[]{:S(2)}, u32[]{:S(2)}) collective-permute-start(f32[128,256]{1,0:T(8,128)S(1)} %get-tuple-element.23), channel_id=1, source_target_pairs={{0,8},{4,12},{8,0},{12,4},{1,9},{5,13},{9,1},{13,5},{2,10},{6,14},... | collective-permute-start | bytes 393224 | tf_op jit(solution)/shard_map/ppermute | solution.py:215
  84.5 6.4 %collective-permute-start.7 = (f32[128,256]{1,0:T(8,128)S(1)}, f32[128,256]{1,0:T(8,128)S(1)}, u32[]{:S(2)}, u32[]{:S(2)}) collective-permute-start(f32[128,256]{1,0:T(8,128)S(1)} %get-tuple-element.22), channel_id=1, source_target_pairs={{0,12},{4,0},{8,4},{12,8},{1,13},{5,1},{9,5},{13,9},{2,14},{6,2},{... | collective-permute-start | bytes 393224 | tf_op jit(solution)/shard_map/ppermute | solution.py:215
  90.9 1.4 %collective-permute-start.8 = (f32[128,256]{1,0:T(8,128)S(1)}, f32[128,256]{1,0:T(8,128)S(1)}, u32[]{:S(2)}, u32[]{:S(2)}) collective-permute-start(f32[128,256]{1,0:T(8,128)S(1)} %fusion.43), channel_id=1, source_target_pairs={{0,2},{2,0},{1,3},{3,1},{4,6},{6,4},{5,7},{7,5},{8,10},{10,8},{9,1... | collective-permute-start | bytes 393224 | tf_op jit(solution)/shard_map/ppermute | solution.py:155

commit v15 on v12

--- a/solution.py
+++ b/solution.py
@@ -269,8 +269,15 @@
         new_imag = from_imag[:kept] - from_real[kept:]
         return jnp.stack([new_real, new_imag]).reshape(2, kept * devices_tm, columns)
 
-    own = apply(cos_own, sin_own, real_part, imag_part)
-    far = apply(cos_far, sin_far, real_part[::-1], imag_part[::-1])
+    table = jnp.concatenate([cos_own, sin_own, cos_far, sin_far], axis=0)
+    from_real = mat(table, real_part)
+    from_imag = mat(table, imag_part)
+    own_real = from_real[:kept] + from_imag[kept:2 * kept]
+    own_imag = from_imag[:kept] - from_real[kept:2 * kept]
+    far_real = from_real[2 * kept:3 * kept] + from_imag[3 * kept:]
+    far_imag = from_imag[2 * kept:3 * kept] - from_real[3 * kept:]
+    own = jnp.stack([own_real, own_imag]).reshape(2, kept * devices_tm, columns)
+    far = jnp.stack([far_real, far_imag])[:, :, ::-1].reshape(2, kept * devices_tm, columns)
     return own, far
 
 

time: 90.3 us -> 89.5 us (level)
  matrix products: 8.22 us -> 7.28 us
    dot_general x4 -> x2, matrix products: 2.73 us -> 1.78 us  [mat(): lax.dot_general(table, value, dims, precision=lax.Precision.HIGH, preferr...]
where the time goes in v15:
time: 89.5 us; the launch traced here: 89.2 us
  waiting for transfers between devices  41.5 us (46%)
  starting transfers between devices  24.4 us (27%)
  other arithmetic  10 us (11%)
  matrix products  7.28 us (8%)
  local copies, waits for them, and re-layouts  5.39 us (6%)
    all_to_all x1, waiting for transfers between devices, body(): gathered = lax.all_to_all(twisted, 'tm', 0, 0, tiled=True)  23.1 us
    ppermute x6, starting transfers between devices, swap_blocks(): arrived.append(lax.ppermute(outgoing, axis, pairs))  17.8 us
    ppermute x1, waiting for transfers between devices, panel_spectra(): blocks.append(lax.ppermute(spectra, 'panel', pairs))  10.8 us
    ppermute x6, waiting for transfers between devices, swap_blocks(): arrived.append(lax.ppermute(outgoing, axis, pairs))  6.29 us
    dot_general x1, matrix products, synthesize(): latitude = jnp.dot(basis_rows, masked, preferred_element_type=jnp.float32)  4.36 us
    all_to_all x1, starting transfers between devices, body(): gathered = lax.all_to_all(twisted, 'tm', 0, 0, tiled=True)  4.28 us
  transfers between devices with their start and end apart: 10, of which 6 were waited for; matrix products, arithmetic and copies ran while one was open for 6% of the time, Pallas kernels for 0%

profile of v15, /device:TPU:0, one launch (start us, length us, event | category | flops | bytes accessed | tf_op | source)
XLA Modules:
  0.0 89.2 jit_solution(4054698830000027759)
XLA Ops:
  0.0 0.7 concatenate.43
  0.7 0.7 convert_element_type.120
  1.5 3.1 %collective-permute-start = (f32[3,256]{1,0:T(4,128)S(1)}, f32[3,256]{1,0:T(4,128)S(1)}, u32[]{:S(2)}, u32[]{:S(2)}) collective-permute-start(f32[3,256]{1,0:T(4,128)S(1)} %bitcast.119), channel_id=1, source_target_pairs={{0,4},{4,8},{8,12},{12,0},{1,5},{5,9},{9,13},{13,1},{2,6},{6,10},{... | collective-permute-start | bytes 9224 | tf_op jit(solution)/shard_map/ppermute | solution.py:215
  4.5 2.6 %collective-permute-start.1 = (f32[3,256]{1,0:T(4,128)S(1)}, f32[3,256]{1,0:T(4,128)S(1)}, u32[]{:S(2)}, u32[]{:S(2)}) collective-permute-start(f32[3,256]{1,0:T(4,128)S(1)} %bitcast.120), channel_id=1, source_target_pairs={{0,8},{4,12},{8,0},{12,4},{1,9},{5,13},{9,1},{13,5},{2,10},{6,14},... | collective-permute-start | bytes 9224 | tf_op jit(solution)/shard_map/ppermute | solution.py:215
  7.1 1.3 %collective-permute-start.2 = (f32[3,256]{1,0:T(4,128)S(1)}, f32[3,256]{1,0:T(4,128)S(1)}, u32[]{:S(2)}, u32[]{:S(2)}) collective-permute-start(f32[3,256]{1,0:T(4,128)S(1)} %bitcast.121), channel_id=1, source_target_pairs={{0,12},{4,0},{8,4},{12,8},{1,13},{5,1},{9,5},{13,9},{2,14},{6,2},{... | collective-permute-start | bytes 9224 | tf_op jit(solution)/shard_map/ppermute | solution.py:215
  8.5 0.8 fusion.92
  9.3 0.7 add_rsqrt_fusion
  9.9 0.7 compare_reduce_fusion
  12.2 0.7 fusion.5
  13.2 4.4 %fusion = f32[1024,256]{1,0:T(8,128)S(1)} fusion(bf16[1024,320]{0,1:T(8,128)(2,1)S(1)} %get-tuple-element.10, bf16[1024,320]{0,1:T(8,128)(2,1)S(1)} %get-tuple-element.9, f32[256]{0:T(256)S(1)} %bitcast.125, f32[1024]{0:T(1024)S(1)} %bitcast.123, f32[256]{0:T(256)S(1)} %bitcast.127, f32[1024]{0:T(1024)S(1)} %bitcast.122, ...), kind=kOutput, calls=%fused_computation.8 | convolution fusion | flops 339804160 | bytes 2701056 | tf_op jit(solution)/shard_map/dot_general | solution.py:55
  18.7 1.0 %copy.19 = f32[4,2,256,128]{3,2,1,0:T(8,128)} copy(f32[4,2,256,128]{3,2,0,1:T(8,128)S(1)} %pad_maximum_fusion) | data formatting | bytes 2097152 | tf_op jit(solution)/shard_map/stack | solution.py:234
  19.8 4.3 %all-to-all-start = ((f32[4,2,256,128]{3,2,1,0:T(8,128)}), f32[4,2,256,128]{3,2,1,0:T(8,128)S(1)}, u32[]{:S(2)}, u32[]{:S(2)}) async-start(f32[4,2,256,128]{3,2,1,0:T(8,128)} %copy.19), calls=%async_computation | async-start | bytes 2097152 | tf_op jit(solution)/shard_map/all_to_all | solution.py:322
  25.4 23.1 %all-to-all-done = f32[4,2,256,128]{3,2,1,0:T(8,128)S(1)} async-done(((f32[4,2,256,128]{3,2,1,0:T(8,128)}), f32[4,2,256,128]{3,2,1,0:T(8,128)S(1)}, u32[]{:S(2)}, u32[]{:S(2)}) %all-to-all-start) | async-done | bytes 1048608 | tf_op jit(solution)/shard_map/all_to_all | solution.py:322
  49.2 0.9 fusion.18
  50.1 0.9 fusion.22
  52.4 0.7 collective-permute-start.3
  55.6 1.6 %collective-permute-start.4 = (bf16[2,516,256]{2,0,1:T(2,128)(2,1)S(1)}, bf16[2,516,256]{2,0,1:T(2,128)(2,1)S(1)}, u32[]{:S(2)}, u32[]{:S(2)}) collective-permute-start(bf16[2,516,256]{2,0,1:T(2,128)(2,1)S(1)} %copy.26), channel_id=1, source_target_pairs={{0,1},{1,0},{2,3},{3,2},{4,5},{5,4},{6,7},{7,6},{8,9},{9,8},{10,11... | collective-permute-start | bytes 1585160 | tf_op jit(solution)/shard_map/ppermute | solution.py:145
  57.8 10.8 %collective-permute-done.4 = bf16[2,516,256]{2,0,1:T(2,128)(2,1)S(1)} collective-permute-done((bf16[2,516,256]{2,0,1:T(2,128)(2,1)S(1)}, bf16[2,516,256]{2,0,1:T(2,128)(2,1)S(1)}, u32[]{:S(2)}, u32[]{:S(2)}) %collective-permute-start.4) | collective-permute-done | bytes 528416 | tf_op jit(solution)/shard_map/ppermute | solution.py:145
  70.0 8.3 %collective-permute-start.5 = (f32[128,256]{1,0:T(8,128)S(1)}, f32[128,256]{1,0:T(8,128)S(1)}, u32[]{:S(2)}, u32[]{:S(2)}) collective-permute-start(f32[128,256]{1,0:T(8,128)S(1)} %get-tuple-element.27), channel_id=1, source_target_pairs={{0,4},{4,8},{8,12},{12,0},{1,5},{5,9},{9,13},{13,1},{2,6},{6,10},{... | collective-permute-start | bytes 393224 | tf_op jit(solution)/shard_map/ppermute | solution.py:215
  78.3 2.4 %collective-permute-start.6 = (f32[128,256]{1,0:T(8,128)S(1)}, f32[128,256]{1,0:T(8,128)S(1)}, u32[]{:S(2)}, u32[]{:S(2)}) collective-permute-start(f32[128,256]{1,0:T(8,128)S(1)} %get-tuple-element.29), channel_id=1, source_target_pairs={{0,8},{4,12},{8,0},{12,4},{1,9},{5,13},{9,1},{13,5},{2,10},{6,14},... | collective-permute-start | bytes 393224 | tf_op jit(solution)/shard_map/ppermute | solution.py:215
  80.8 2.4 %collective-permute-done.5 = f32[128,256]{1,0:T(8,128)S(1)} collective-permute-done((f32[128,256]{1,0:T(8,128)S(1)}, f32[128,256]{1,0:T(8,128)S(1)}, u32[]{:S(2)}, u32[]{:S(2)}) %collective-permute-start.5) | collective-permute-done | bytes 131104 | tf_op jit(solution)/shard_map/ppermute | solution.py:215
  83.2 2.9 %collective-permute-done.6 = f32[128,256]{1,0:T(8,128)S(1)} collective-permute-done((f32[128,256]{1,0:T(8,128)S(1)}, f32[128,256]{1,0:T(8,128)S(1)}, u32[]{:S(2)}, u32[]{:S(2)}) %collective-permute-start.6) | collective-permute-done | bytes 131104 | tf_op jit(solution)/shard_map/ppermute | solution.py:215
  86.1 1.0 %collective-permute-done.7 = f32[128,256]{1,0:T(8,128)S(1)} collective-permute-done((f32[128,256]{1,0:T(8,128)S(1)}, f32[128,256]{1,0:T(8,128)S(1)}, u32[]{:S(2)}, u32[]{:S(2)}) %collective-permute-start.7) | collective-permute-done | bytes 131104 | tf_op jit(solution)/shard_map/ppermute | solution.py:215
  87.2 1.3 %collective-permute-done.8 = f32[128,256]{1,0:T(8,128)S(1)} collective-permute-done((f32[128,256]{1,0:T(8,128)S(1)}, f32[128,256]{1,0:T(8,128)S(1)}, u32[]{:S(2)}, u32[]{:S(2)}) %collective-permute-start.8) | collective-permute-done | bytes 131104 | tf_op jit(solution)/shard_map/ppermute | solution.py:155
  (88 shorter events, 11.4 us)
Async XLA Ops:
  1.5 9.3 %collective-permute-start = (f32[3,256]{1,0:T(4,128)S(1)}, f32[3,256]{1,0:T(4,128)S(1)}, u32[]{:S(2)}, u32[]{:S(2)}) collective-permute-start(f32[3,256]{1,0:T(4,128)S(1)} %bitcast.119), channel_id=1, source_target_pairs={{0,4},{4,8},{8,12},{12,0},{1,5},{5,9},{9,13},{13,1},{2,6},{6,10},{... | collective-permute-start | bytes 9224 | tf_op jit(solution)/shard_map/ppermute | solution.py:215
  4.5 6.3 %collective-permute-start.1 = (f32[3,256]{1,0:T(4,128)S(1)}, f32[3,256]{1,0:T(4,128)S(1)}, u32[]{:S(2)}, u32[]{:S(2)}) collective-permute-start(f32[3,256]{1,0:T(4,128)S(1)} %bitcast.120), channel_id=1, source_target_pairs={{0,8},{4,12},{8,0},{12,4},{1,9},{5,13},{9,1},{13,5},{2,10},{6,14},... | collective-permute-start | bytes 9224 | tf_op jit(solution)/shard_map/ppermute | solution.py:215
  7.1 3.7 %collective-permute-start.2 = (f32[3,256]{1,0:T(4,128)S(1)}, f32[3,256]{1,0:T(4,128)S(1)}, u32[]{:S(2)}, u32[]{:S(2)}) collective-permute-start(f32[3,256]{1,0:T(4,128)S(1)} %bitcast.121), channel_id=1, source_target_pairs={{0,12},{4,0},{8,4},{12,8},{1,13},{5,1},{9,5},{13,9},{2,14},{6,2},{... | collective-permute-start | bytes 9224 | tf_op jit(solution)/shard_map/ppermute | solution.py:215
  12.2 1.0 %copy-start.1 = (bf16[1,640,256]{2,1,0:T(8,128)(2,1)S(1)}, bf16[1,640,256]{2,1,0:T(8,128)(2,1)}, u32[]{:S(2)}) copy-start(bf16[1,640,256]{2,1,0:T(8,128)(2,1)} %param.8) | copy-start | bytes 983044
  19.8 28.7 %all-to-all-start = ((f32[4,2,256,128]{3,2,1,0:T(8,128)}), f32[4,2,256,128]{3,2,1,0:T(8,128)S(1)}, u32[]{:S(2)}, u32[]{:S(2)}) async-start(f32[4,2,256,128]{3,2,1,0:T(8,128)} %copy.19), calls=%async_computation | async-start | bytes 2097152 | tf_op jit(solution)/shard_map/all_to_all | solution.py:322
  52.0 1.1 %copy-start = (s32[1,2049]{1,0:T(1,128)S(1)}, s32[1,2049]{1,0:T(1,128)}, u32[]{:S(2)}) copy-start(s32[1,2049]{1,0:T(1,128)} %param.9) | copy-start | bytes 24592
  52.4 2.1 %collective-permute-start.3 = (f32[2,516,128]{2,0,1:T(2,128)S(1)}, f32[2,516,128]{2,0,1:T(2,128)S(1)}, u32[]{:S(2)}, u32[]{:S(2)}) collective-permute-start(f32[2,516,128]{2,0,1:T(2,128)S(1)} %maximum_select_fusion), channel_id=1, source_target_pairs={{0,0},{4,12},{8,8},{12,4},{1,1},{5,13},{9,9},{13,5},{2,2},{6,14},{... | collective-permute-start | bytes 1585160 | tf_op jit(solution)/shard_map/ppermute | solution.py:289
  55.6 13.0 %collective-permute-start.4 = (bf16[2,516,256]{2,0,1:T(2,128)(2,1)S(1)}, bf16[2,516,256]{2,0,1:T(2,128)(2,1)S(1)}, u32[]{:S(2)}, u32[]{:S(2)}) collective-permute-start(bf16[2,516,256]{2,0,1:T(2,128)(2,1)S(1)} %copy.26), channel_id=1, source_target_pairs={{0,1},{1,0},{2,3},{3,2},{4,5},{5,4},{6,7},{7,6},{8,9},{9,8},{10,11... | collective-permute-start | bytes 1585160 | tf_op jit(solution)/shard_map/ppermute | solution.py:145
  70.0 13.2 %collective-permute-start.5 = (f32[128,256]{1,0:T(8,128)S(1)}, f32[128,256]{1,0:T(8,128)S(1)}, u32[]{:S(2)}, u32[]{:S(2)}) collective-permute-start(f32[128,256]{1,0:T(8,128)S(1)} %get-tuple-element.27), channel_id=1, source_target_pairs={{0,4},{4,8},{8,12},{12,0},{1,5},{5,9},{9,13},{13,1},{2,6},{6,10},{... | collective-permute-start | bytes 393224 | tf_op jit(solution)/shard_map/ppermute | solution.py:215
  78.3 7.7 %collective-permute-start.6 = (f32[128,256]{1,0:T(8,128)S(1)}, f32[128,256]{1,0:T(8,128)S(1)}, u32[]{:S(2)}, u32[]{:S(2)}) collective-permute-start(f32[128,256]{1,0:T(8,128)S(1)} %get-tuple-element.29), channel_id=1, source_target_pairs={{0,8},{4,12},{8,0},{12,4},{1,9},{5,13},{9,1},{13,5},{2,10},{6,14},... | collective-permute-start | bytes 393224 | tf_op jit(solution)/shard_map/ppermute | solution.py:215
  80.7 6.4 %collective-permute-start.7 = (f32[128,256]{1,0:T(8,128)S(1)}, f32[128,256]{1,0:T(8,128)S(1)}, u32[]{:S(2)}, u32[]{:S(2)}) collective-permute-start(f32[128,256]{1,0:T(8,128)S(1)} %get-tuple-element.28), channel_id=1, source_target_pairs={{0,12},{4,0},{8,4},{12,8},{1,13},{5,1},{9,5},{13,9},{2,14},{6,2},{... | collective-permute-start | bytes 393224 | tf_op jit(solution)/shard_map/ppermute | solution.py:215
  87.1 1.4 %collective-permute-start.8 = (f32[128,256]{1,0:T(8,128)S(1)}, f32[128,256]{1,0:T(8,128)S(1)}, u32[]{:S(2)}, u32[]{:S(2)}) collective-permute-start(f32[128,256]{1,0:T(8,128)S(1)} %fusion.53), channel_id=1, source_target_pairs={{0,2},{2,0},{1,3},{3,1},{4,6},{6,4},{5,7},{7,5},{8,10},{10,8},{9,1... | collective-permute-start | bytes 393224 | tf_op jit(solution)/shard_map/ppermute | solution.py:155

commit v16 on v15

--- a/solution.py
+++ b/solution.py
@@ -334,6 +334,20 @@
     ]
     by_shift = jnp.stack(products)
     panel = lax.axis_index("panel")
+    rows = panels * columns // devices_tm
+    if devices_tm <= 8 and columns % rows == 0:
+        per_panel = columns // rows
+        grid = by_shift.reshape(panels, per_panel, rows, columns)
+
+        def block(target):
+            start = ((panel - target // per_panel) % panels, target % per_panel, 0, 0)
+            return lax.dynamic_slice(grid, start, (1, 1, rows, columns))[0, 0]
+
+        total = block(position)
+        for shift in range(1, devices_tm):
+            pairs = [(src, (src + shift) % devices_tm) for src in range(devices_tm)]
+            total = total + lax.ppermute(block((position + shift) % devices_tm), "tm", pairs)
+        return comp_sum(total)
     order = (panel - jnp.arange(panels, dtype=jnp.int32)) % panels
     partial_value = jnp.take(by_shift, order, axis=0).reshape(panels * columns, columns)
     return settle_rows(partial_value)

time: 89.5 us -> 88.9 us (level)
  starting transfers between devices: 24.4 us -> 25.8 us
  waiting for transfers between devices: 41.5 us -> 40.2 us
    ppermute x0 -> x3, starting transfers between devices: none -> 12.1 us  [body(): lax.ppermute(block((position + shift) % devices_tm), 'tm', pairs)]
    ppermute x6 -> x3, starting transfers between devices: 17.8 us -> 7.01 us  [swap_blocks(): arrived.append(lax.ppermute(outgoing, axis, pairs))]
    ppermute x6 -> x3, waiting for transfers between devices: 6.29 us -> 0.01 us  [swap_blocks(): arrived.append(lax.ppermute(outgoing, axis, pairs))]
    ppermute x0 -> x3, waiting for transfers between devices: none -> 6.28 us  [body(): lax.ppermute(block((position + shift) % devices_tm), 'tm', pairs)]
    ppermute x1, waiting for transfers between devices: 10.8 us -> 9.55 us  [panel_spectra(): blocks.append(lax.ppermute(spectra, 'panel', pairs))]
where the time goes in v16:
time: 88.9 us; the launch traced here: 88.5 us
  waiting for transfers between devices  40.2 us (45%)
  starting transfers between devices  25.8 us (29%)
  other arithmetic  9.98 us (11%)
  matrix products  7.27 us (8%)
  local copies, waits for them, and re-layouts  4.61 us (5%)
    all_to_all x1, waiting for transfers between devices, body(): gathered = lax.all_to_all(twisted, 'tm', 0, 0, tiled=True)  23.1 us
    ppermute x3, starting transfers between devices, body(): lax.ppermute(block((position + shift) % devices_tm), 'tm', pairs)  12.1 us
    ppermute x1, waiting for transfers between devices, panel_spectra(): blocks.append(lax.ppermute(spectra, 'panel', pairs))  9.55 us
    ppermute x3, starting transfers between devices, swap_blocks(): arrived.append(lax.ppermute(outgoing, axis, pairs))  7.01 us
    ppermute x3, waiting for transfers between devices, body(): lax.ppermute(block((position + shift) % devices_tm), 'tm', pairs)  6.28 us
    dot_general x1, matrix products, synthesize(): latitude = jnp.dot(basis_rows, masked, preferred_element_type=jnp.float32)  4.36 us
    all_to_all x1, starting transfers between devices, body(): gathered = lax.all_to_all(twisted, 'tm', 0, 0, tiled=True)  4.28 us
    dot_general x2, matrix products, mat(): lax.dot_general(table, value, dims, precision=lax.Precision.HIGH, preferr...  1.78 us
  transfers between devices with their start and end apart: 10, of which 6 were waited for; matrix products, arithmetic and copies ran while one was open for 6% of the time, Pallas kernels for 0%

profile of v16, /device:TPU:0, one launch (start us, length us, event | category | flops | bytes accessed | tf_op | source)
XLA Modules:
  0.0 88.5 jit_solution(16373803315244498724)
XLA Ops:
  0.0 0.7 concatenate.44
  0.7 0.7 convert_element_type.120
  1.5 3.1 %collective-permute-start = (f32[3,256]{1,0:T(4,128)S(1)}, f32[3,256]{1,0:T(4,128)S(1)}, u32[]{:S(2)}, u32[]{:S(2)}) collective-permute-start(f32[3,256]{1,0:T(4,128)S(1)} %bitcast.121), channel_id=1, source_target_pairs={{0,4},{4,8},{8,12},{12,0},{1,5},{5,9},{9,13},{13,1},{2,6},{6,10},{... | collective-permute-start | bytes 9224 | tf_op jit(solution)/shard_map/ppermute | solution.py:215
  4.5 2.6 %collective-permute-start.1 = (f32[3,256]{1,0:T(4,128)S(1)}, f32[3,256]{1,0:T(4,128)S(1)}, u32[]{:S(2)}, u32[]{:S(2)}) collective-permute-start(f32[3,256]{1,0:T(4,128)S(1)} %bitcast.122), channel_id=1, source_target_pairs={{0,8},{4,12},{8,0},{12,4},{1,9},{5,13},{9,1},{13,5},{2,10},{6,14},... | collective-permute-start | bytes 9224 | tf_op jit(solution)/shard_map/ppermute | solution.py:215
  7.1 1.3 %collective-permute-start.2 = (f32[3,256]{1,0:T(4,128)S(1)}, f32[3,256]{1,0:T(4,128)S(1)}, u32[]{:S(2)}, u32[]{:S(2)}) collective-permute-start(f32[3,256]{1,0:T(4,128)S(1)} %bitcast.123), channel_id=1, source_target_pairs={{0,12},{4,0},{8,4},{12,8},{1,13},{5,1},{9,5},{13,9},{2,14},{6,2},{... | collective-permute-start | bytes 9224 | tf_op jit(solution)/shard_map/ppermute | solution.py:215
  8.5 0.8 fusion.101
  9.3 0.7 add_rsqrt_fusion
  9.9 0.7 compare_reduce_fusion
  12.2 0.7 fusion.5
  13.2 4.4 %fusion = f32[1024,256]{1,0:T(8,128)S(1)} fusion(bf16[1024,320]{0,1:T(8,128)(2,1)S(1)} %get-tuple-element.10, bf16[1024,320]{0,1:T(8,128)(2,1)S(1)} %get-tuple-element.9, f32[256]{0:T(256)S(1)} %bitcast.127, f32[1024]{0:T(1024)S(1)} %bitcast.125, f32[256]{0:T(256)S(1)} %bitcast.129, f32[1024]{0:T(1024)S(1)} %bitcast.124, ...), kind=kOutput, calls=%fused_computation.7 | convolution fusion | flops 339804160 | bytes 2701056 | tf_op jit(solution)/shard_map/dot_general | solution.py:55
  18.7 1.0 %copy.19 = f32[4,2,256,128]{3,2,1,0:T(8,128)} copy(f32[4,2,256,128]{3,2,0,1:T(8,128)S(1)} %pad_maximum_fusion) | data formatting | bytes 2097152 | tf_op jit(solution)/shard_map/stack | solution.py:234
  19.8 4.3 %all-to-all-start = ((f32[4,2,256,128]{3,2,1,0:T(8,128)}), f32[4,2,256,128]{3,2,1,0:T(8,128)S(1)}, u32[]{:S(2)}, u32[]{:S(2)}) async-start(f32[4,2,256,128]{3,2,1,0:T(8,128)} %copy.19), calls=%async_computation | async-start | bytes 2097152 | tf_op jit(solution)/shard_map/all_to_all | solution.py:322
  25.4 23.1 %all-to-all-done = f32[4,2,256,128]{3,2,1,0:T(8,128)S(1)} async-done(((f32[4,2,256,128]{3,2,1,0:T(8,128)}), f32[4,2,256,128]{3,2,1,0:T(8,128)S(1)}, u32[]{:S(2)}, u32[]{:S(2)}) %all-to-all-start) | async-done | bytes 1048608 | tf_op jit(solution)/shard_map/all_to_all | solution.py:322
  49.2 0.9 %fusion.20 = f32[516,4,128]{2,0,1:T(8,128)S(1)} fusion(f32[4,256,128]{2,1,0:T(8,128)S(1)} %get-tuple-element.6, f32[4,256,128]{2,1,0:T(8,128)S(1)} %get-tuple-element.5, f32[129,256]{1,0:T(8,128)S(1)} %get-tuple-element.50, f32[129,256]{1,0:T(8,128)S(1)} %get-tuple-element.49, f32[129,256]{1,0:T(8,128)S(1)} %get-tuple-element.59, ...), kind=kOutput, calls=%fused_computation.56 | convolution fusion | flops 406588416 | bytes 2641920 | tf_op jit(solution)/shard_map/dot_general | solution.py:259
  50.1 0.9 %fusion.24 = f32[516,4,128]{2,0,1:T(8,128)S(1)} fusion(f32[4,256,128]{2,1,0:T(8,128)S(1)} %get-tuple-element.5, f32[4,256,128]{2,1,0:T(8,128)S(1)} %get-tuple-element.6, f32[129,256]{1,0:T(8,128)S(1)} %get-tuple-element.50, f32[129,256]{1,0:T(8,128)S(1)} %get-tuple-element.49, f32[129,256]{1,0:T(8,128)S(1)} %get-tuple-element.59, ...), kind=kOutput, calls=%fused_computation.60 | convolution fusion | flops 406588416 | bytes 2641920 | tf_op jit(solution)/shard_map/dot_general | solution.py:259
  52.4 0.7 collective-permute-start.3
  54.2 1.6 %collective-permute-start.4 = (bf16[2,516,256]{2,0,1:T(2,128)(2,1)S(1)}, bf16[2,516,256]{2,0,1:T(2,128)(2,1)S(1)}, u32[]{:S(2)}, u32[]{:S(2)}) collective-permute-start(bf16[2,516,256]{2,0,1:T(2,128)(2,1)S(1)} %copy.26), channel_id=1, source_target_pairs={{0,1},{1,0},{2,3},{3,2},{4,5},{5,4},{6,7},{7,6},{8,9},{9,8},{10,11... | collective-permute-start | bytes 1585160 | tf_op jit(solution)/shard_map/ppermute | solution.py:145
  57.7 9.6 %collective-permute-done.4 = bf16[2,516,256]{2,0,1:T(2,128)(2,1)S(1)} collective-permute-done((bf16[2,516,256]{2,0,1:T(2,128)(2,1)S(1)}, bf16[2,516,256]{2,0,1:T(2,128)(2,1)S(1)}, u32[]{:S(2)}, u32[]{:S(2)}) %collective-permute-start.4) | collective-permute-done | bytes 528416 | tf_op jit(solution)/shard_map/ppermute | solution.py:145
  67.9 9.7 %collective-permute-start.5 = (f32[128,256]{1,0:T(8,128)S(1)}, f32[128,256]{1,0:T(8,128)S(1)}, u32[]{:S(2)}, u32[]{:S(2)}) collective-permute-start(f32[128,256]{1,0:T(8,128)S(1)} %get-tuple-element.27), channel_id=1, source_target_pairs={{0,4},{4,8},{8,12},{12,0},{1,5},{5,9},{9,13},{13,1},{2,6},{6,10},{... | collective-permute-start | bytes 393224 | tf_op jit(solution)/shard_map/ppermute | solution.py:349
  77.6 2.4 %collective-permute-start.6 = (f32[128,256]{1,0:T(8,128)S(1)}, f32[128,256]{1,0:T(8,128)S(1)}, u32[]{:S(2)}, u32[]{:S(2)}) collective-permute-start(f32[128,256]{1,0:T(8,128)S(1)} %get-tuple-element.28), channel_id=1, source_target_pairs={{0,8},{4,12},{8,0},{12,4},{1,9},{5,13},{9,1},{13,5},{2,10},{6,14},... | collective-permute-start | bytes 393224 | tf_op jit(solution)/shard_map/ppermute | solution.py:349
  80.1 2.4 %collective-permute-done.5 = f32[128,256]{1,0:T(8,128)S(1)} collective-permute-done((f32[128,256]{1,0:T(8,128)S(1)}, f32[128,256]{1,0:T(8,128)S(1)}, u32[]{:S(2)}, u32[]{:S(2)}) %collective-permute-start.5) | collective-permute-done | bytes 131104 | tf_op jit(solution)/shard_map/ppermute | solution.py:349
  82.5 2.9 %collective-permute-done.6 = f32[128,256]{1,0:T(8,128)S(1)} collective-permute-done((f32[128,256]{1,0:T(8,128)S(1)}, f32[128,256]{1,0:T(8,128)S(1)}, u32[]{:S(2)}, u32[]{:S(2)}) %collective-permute-start.6) | collective-permute-done | bytes 131104 | tf_op jit(solution)/shard_map/ppermute | solution.py:349
  85.4 1.0 %collective-permute-done.7 = f32[128,256]{1,0:T(8,128)S(1)} collective-permute-done((f32[128,256]{1,0:T(8,128)S(1)}, f32[128,256]{1,0:T(8,128)S(1)}, u32[]{:S(2)}, u32[]{:S(2)}) %collective-permute-start.7) | collective-permute-done | bytes 131104 | tf_op jit(solution)/shard_map/ppermute | solution.py:349
  86.5 1.3 %collective-permute-done.8 = f32[128,256]{1,0:T(8,128)S(1)} collective-permute-done((f32[128,256]{1,0:T(8,128)S(1)}, f32[128,256]{1,0:T(8,128)S(1)}, u32[]{:S(2)}, u32[]{:S(2)}) %collective-permute-start.8) | collective-permute-done | bytes 131104 | tf_op jit(solution)/shard_map/ppermute | solution.py:155
  (80 shorter events, 10.6 us)
Async XLA Ops:
  1.5 9.3 %collective-permute-start = (f32[3,256]{1,0:T(4,128)S(1)}, f32[3,256]{1,0:T(4,128)S(1)}, u32[]{:S(2)}, u32[]{:S(2)}) collective-permute-start(f32[3,256]{1,0:T(4,128)S(1)} %bitcast.121), channel_id=1, source_target_pairs={{0,4},{4,8},{8,12},{12,0},{1,5},{5,9},{9,13},{13,1},{2,6},{6,10},{... | collective-permute-start | bytes 9224 | tf_op jit(solution)/shard_map/ppermute | solution.py:215
  4.5 6.3 %collective-permute-start.1 = (f32[3,256]{1,0:T(4,128)S(1)}, f32[3,256]{1,0:T(4,128)S(1)}, u32[]{:S(2)}, u32[]{:S(2)}) collective-permute-start(f32[3,256]{1,0:T(4,128)S(1)} %bitcast.122), channel_id=1, source_target_pairs={{0,8},{4,12},{8,0},{12,4},{1,9},{5,13},{9,1},{13,5},{2,10},{6,14},... | collective-permute-start | bytes 9224 | tf_op jit(solution)/shard_map/ppermute | solution.py:215
  7.1 3.7 %collective-permute-start.2 = (f32[3,256]{1,0:T(4,128)S(1)}, f32[3,256]{1,0:T(4,128)S(1)}, u32[]{:S(2)}, u32[]{:S(2)}) collective-permute-start(f32[3,256]{1,0:T(4,128)S(1)} %bitcast.123), channel_id=1, source_target_pairs={{0,12},{4,0},{8,4},{12,8},{1,13},{5,1},{9,5},{13,9},{2,14},{6,2},{... | collective-permute-start | bytes 9224 | tf_op jit(solution)/shard_map/ppermute | solution.py:215
  12.2 1.0 %copy-start.1 = (bf16[1,640,256]{2,1,0:T(8,128)(2,1)S(1)}, bf16[1,640,256]{2,1,0:T(8,128)(2,1)}, u32[]{:S(2)}) copy-start(bf16[1,640,256]{2,1,0:T(8,128)(2,1)} %param.8) | copy-start | bytes 983044
  19.8 28.7 %all-to-all-start = ((f32[4,2,256,128]{3,2,1,0:T(8,128)}), f32[4,2,256,128]{3,2,1,0:T(8,128)S(1)}, u32[]{:S(2)}, u32[]{:S(2)}) async-start(f32[4,2,256,128]{3,2,1,0:T(8,128)} %copy.19), calls=%async_computation | async-start | bytes 2097152 | tf_op jit(solution)/shard_map/all_to_all | solution.py:322
  52.4 0.7 collective-permute-start.3
  53.8 2.1 %copy-start = (s32[1,2049]{1,0:T(1,128)S(1)}, s32[1,2049]{1,0:T(1,128)}, u32[]{:S(2)}) copy-start(s32[1,2049]{1,0:T(1,128)} %param.9) | copy-start | bytes 24592
  54.2 13.0 %collective-permute-start.4 = (bf16[2,516,256]{2,0,1:T(2,128)(2,1)S(1)}, bf16[2,516,256]{2,0,1:T(2,128)(2,1)S(1)}, u32[]{:S(2)}, u32[]{:S(2)}) collective-permute-start(bf16[2,516,256]{2,0,1:T(2,128)(2,1)S(1)} %copy.26), channel_id=1, source_target_pairs={{0,1},{1,0},{2,3},{3,2},{4,5},{5,4},{6,7},{7,6},{8,9},{9,8},{10,11... | collective-permute-start | bytes 1585160 | tf_op jit(solution)/shard_map/ppermute | solution.py:145
  67.9 14.5 %collective-permute-start.5 = (f32[128,256]{1,0:T(8,128)S(1)}, f32[128,256]{1,0:T(8,128)S(1)}, u32[]{:S(2)}, u32[]{:S(2)}) collective-permute-start(f32[128,256]{1,0:T(8,128)S(1)} %get-tuple-element.27), channel_id=1, source_target_pairs={{0,4},{4,8},{8,12},{12,0},{1,5},{5,9},{9,13},{13,1},{2,6},{6,10},{... | collective-permute-start | bytes 393224 | tf_op jit(solution)/shard_map/ppermute | solution.py:349
  77.6 7.7 %collective-permute-start.6 = (f32[128,256]{1,0:T(8,128)S(1)}, f32[128,256]{1,0:T(8,128)S(1)}, u32[]{:S(2)}, u32[]{:S(2)}) collective-permute-start(f32[128,256]{1,0:T(8,128)S(1)} %get-tuple-element.28), channel_id=1, source_target_pairs={{0,8},{4,12},{8,0},{12,4},{1,9},{5,13},{9,1},{13,5},{2,10},{6,14},... | collective-permute-start | bytes 393224 | tf_op jit(solution)/shard_map/ppermute | solution.py:349
  80.0 6.4 %collective-permute-start.7 = (f32[128,256]{1,0:T(8,128)S(1)}, f32[128,256]{1,0:T(8,128)S(1)}, u32[]{:S(2)}, u32[]{:S(2)}) collective-permute-start(f32[128,256]{1,0:T(8,128)S(1)} %get-tuple-element.29), channel_id=1, source_target_pairs={{0,12},{4,0},{8,4},{12,8},{1,13},{5,1},{9,5},{13,9},{2,14},{6,2},{... | collective-permute-start | bytes 393224 | tf_op jit(solution)/shard_map/ppermute | solution.py:349
  86.4 1.4 %collective-permute-start.8 = (f32[128,256]{1,0:T(8,128)S(1)}, f32[128,256]{1,0:T(8,128)S(1)}, u32[]{:S(2)}, u32[]{:S(2)}) collective-permute-start(f32[128,256]{1,0:T(8,128)S(1)} %fusion.60), channel_id=1, source_target_pairs={{0,2},{2,0},{1,3},{3,1},{4,6},{6,4},{5,7},{7,5},{8,10},{10,8},{9,1... | collective-permute-start | bytes 393224 | tf_op jit(solution)/shard_map/ppermute | solution.py:155

commit v17 on v16

--- a/solution.py
+++ b/solution.py
@@ -55,8 +55,7 @@
     latitude = jnp.dot(basis_rows, masked, preferred_element_type=jnp.float32)
     lon_phase = longit[:, None] * jnp.abs(orders).astype(jnp.float32)[None, :]
     lon_wave = jnp.where(orders[None, :] >= 0, jnp.cos(lon_phase), jnp.sin(lon_phase))
-    norm_scale = 1.0 / jnp.sqrt(degree.astype(jnp.float32) + 1.0)
-    return latitude * lon_wave * (keep_rows[:, None] * norm_scale[None, :])
+    return latitude * lon_wave * keep_rows[:, None]
 
 
 def phase_tables(row_index, col_index, length):
@@ -281,7 +280,7 @@
     return own, far
 
 
-def unpack_spectra(own, far, position, samples):
+def unpack_spectra(own, far, position, samples, norm_scale):
     devices_tm = lax.axis_size("tm")
     shifted = jnp.concatenate([own[:, :1], far[:, :-1]], axis=1)
     outgoing = jnp.where(position == 0, shifted, far)
@@ -293,8 +292,9 @@
     first_imag = (own_imag - mirror[1]) * 0.5
     second_real = (own_imag + mirror[1]) * 0.5
     second_imag = (mirror[0] - own_real) * 0.5
-    new_real = jnp.concatenate([first_real, second_real], axis=1) / samples
-    new_imag = jnp.concatenate([first_imag, second_imag], axis=1) / samples
+    scale = norm_scale[None, :] / samples
+    new_real = jnp.concatenate([first_real, second_real], axis=1) * scale
+    new_imag = jnp.concatenate([first_imag, second_imag], axis=1) * scale
     return jnp.stack([new_real.astype(jnp.bfloat16), new_imag.astype(jnp.bfloat16)])
 
 
@@ -321,7 +321,8 @@
     )
     gathered = lax.all_to_all(twisted, "tm", 0, 0, tiled=True)
     own, far = packed_transform(gathered)
-    spectra = unpack_spectra(own, far, position, samples)
+    norm_scale = 1.0 / jnp.sqrt(column_index[0].astype(jnp.float32) + 1.0)
+    spectra = unpack_spectra(own, far, position, samples, norm_scale)
     inverse_psd, fold = inverse_weights(
         psd_table[0], position, devices_tm, epochs, samples, spectra.shape[1]
     )

time: 88.9 us -> 88.5 us (level)
  transfers between devices with their start and end apart: 10 -> 10, of which waited for: 6 -> 7; matrix products, arithmetic and copies ran while one was open for 6% -> 5% of each run, Pallas kernels for 0% -> 0%
where the time goes in v17:
time: 88.5 us; the launch traced here: 88.2 us
  waiting for transfers between devices  40.5 us (46%)
  starting transfers between devices  25.8 us (29%)
  other arithmetic  9.33 us (11%)
  matrix products  7.29 us (8%)
  local copies, waits for them, and re-layouts  4.62 us (5%)
    all_to_all x1, waiting for transfers between devices, body(): gathered = lax.all_to_all(twisted, 'tm', 0, 0, tiled=True)  22.7 us
    ppermute x3, starting transfers between devices, body(): lax.ppermute(block((position + shift) % devices_tm), 'tm', pairs)  12.1 us
    ppermute x1, waiting for transfers between devices, panel_spectra(): blocks.append(lax.ppermute(spectra, 'panel', pairs))  9.57 us
    ppermute x3, starting transfers between devices, swap_blocks(): arrived.append(lax.ppermute(outgoing, axis, pairs))  7.01 us
    ppermute x3, waiting for transfers between devices, body(): lax.ppermute(block((position + shift) % devices_tm), 'tm', pairs)  6.27 us
    all_to_all x1, starting transfers between devices, body(): gathered = lax.all_to_all(twisted, 'tm', 0, 0, tiled=True)  4.41 us
    dot_general x1, matrix products, synthesize(): latitude = jnp.dot(basis_rows, masked, preferred_element_type=jnp.float32)  4.37 us
    dot_general x2, matrix products, mat(): lax.dot_general(table, value, dims, precision=lax.Precision.HIGH, preferr...  1.78 us
  transfers between devices with their start and end apart: 10, of which 7 were waited for; matrix products, arithmetic and copies ran while one was open for 5% of the time, Pallas kernels for 0%

profile of v17, /device:TPU:0, one launch (start us, length us, event | category | flops | bytes accessed | tf_op | source)
XLA Modules:
  0.0 88.2 jit_solution(3339101193776325957)
XLA Ops:
  0.0 0.7 concatenate.44
  0.7 0.7 convert_element_type.120
  1.5 3.1 %collective-permute-start = (f32[3,256]{1,0:T(4,128)S(1)}, f32[3,256]{1,0:T(4,128)S(1)}, u32[]{:S(2)}, u32[]{:S(2)}) collective-permute-start(f32[3,256]{1,0:T(4,128)S(1)} %bitcast.121), channel_id=1, source_target_pairs={{0,4},{4,8},{8,12},{12,0},{1,5},{5,9},{9,13},{13,1},{2,6},{6,10},{... | collective-permute-start | bytes 9224 | tf_op jit(solution)/shard_map/ppermute | solution.py:214
  4.5 2.6 %collective-permute-start.1 = (f32[3,256]{1,0:T(4,128)S(1)}, f32[3,256]{1,0:T(4,128)S(1)}, u32[]{:S(2)}, u32[]{:S(2)}) collective-permute-start(f32[3,256]{1,0:T(4,128)S(1)} %bitcast.122), channel_id=1, source_target_pairs={{0,8},{4,12},{8,0},{12,4},{1,9},{5,13},{9,1},{13,5},{2,10},{6,14},... | collective-permute-start | bytes 9224 | tf_op jit(solution)/shard_map/ppermute | solution.py:214
  7.1 1.3 %collective-permute-start.2 = (f32[3,256]{1,0:T(4,128)S(1)}, f32[3,256]{1,0:T(4,128)S(1)}, u32[]{:S(2)}, u32[]{:S(2)}) collective-permute-start(f32[3,256]{1,0:T(4,128)S(1)} %bitcast.123), channel_id=1, source_target_pairs={{0,12},{4,0},{8,4},{12,8},{1,13},{5,1},{9,5},{13,9},{2,14},{6,2},{... | collective-permute-start | bytes 9224 | tf_op jit(solution)/shard_map/ppermute | solution.py:214
  8.5 0.8 fusion.101
  9.3 0.7 compare_reduce_fusion
  12.1 0.7 fusion.5
  13.1 4.4 %fusion = f32[1024,256]{1,0:T(8,128)S(1)} fusion(bf16[1024,320]{0,1:T(8,128)(2,1)S(1)} %get-tuple-element.10, bf16[1024,320]{0,1:T(8,128)(2,1)S(1)} %get-tuple-element.9, f32[1024]{0:T(1024)S(1)} %bitcast.125, f32[256]{0:T(256)S(1)} %bitcast.129, f32[1024]{0:T(1024)S(1)} %bitcast.124, pred[256]{0:T(512)(128)(4,1)S(1)} %compare_reduce_fusion, ...), kind=kOutput, calls=%fused_computation.7 | convolution fusion | flops 339542016 | bytes 2700032 | tf_op jit(solution)/shard_map/dot_general | solution.py:55
  18.6 1.1 %copy.19 = f32[4,2,256,128]{3,2,1,0:T(8,128)} copy(f32[4,2,256,128]{3,2,0,1:T(8,128)S(1)} %pad_maximum_fusion) | data formatting | bytes 2097152 | tf_op jit(solution)/shard_map/stack | solution.py:233
  19.7 4.4 %all-to-all-start = ((f32[4,2,256,128]{3,2,1,0:T(8,128)}), f32[4,2,256,128]{3,2,1,0:T(8,128)S(1)}, u32[]{:S(2)}, u32[]{:S(2)}) async-start(f32[4,2,256,128]{3,2,1,0:T(8,128)} %copy.19), calls=%async_computation | async-start | bytes 2097152 | tf_op jit(solution)/shard_map/all_to_all | solution.py:322
  25.4 22.7 %all-to-all-done = f32[4,2,256,128]{3,2,1,0:T(8,128)S(1)} async-done(((f32[4,2,256,128]{3,2,1,0:T(8,128)}), f32[4,2,256,128]{3,2,1,0:T(8,128)S(1)}, u32[]{:S(2)}, u32[]{:S(2)}) %all-to-all-start) | async-done | bytes 1048608 | tf_op jit(solution)/shard_map/all_to_all | solution.py:322
  48.8 0.9 %fusion.20 = f32[516,4,128]{2,0,1:T(8,128)S(1)} fusion(f32[4,256,128]{2,1,0:T(8,128)S(1)} %get-tuple-element.6, f32[4,256,128]{2,1,0:T(8,128)S(1)} %get-tuple-element.5, f32[129,256]{1,0:T(8,128)S(1)} %get-tuple-element.52, f32[129,256]{1,0:T(8,128)S(1)} %get-tuple-element.51, f32[129,256]{1,0:T(8,128)S(1)} %get-tuple-element.61, ...), kind=kOutput, calls=%fused_computation.56 | convolution fusion | flops 406588416 | bytes 2641920 | tf_op jit(solution)/shard_map/dot_general | solution.py:258
  49.7 0.9 %fusion.24 = f32[516,4,128]{2,0,1:T(8,128)S(1)} fusion(f32[4,256,128]{2,1,0:T(8,128)S(1)} %get-tuple-element.5, f32[4,256,128]{2,1,0:T(8,128)S(1)} %get-tuple-element.6, f32[129,256]{1,0:T(8,128)S(1)} %get-tuple-element.52, f32[129,256]{1,0:T(8,128)S(1)} %get-tuple-element.51, f32[129,256]{1,0:T(8,128)S(1)} %get-tuple-element.61, ...), kind=kOutput, calls=%fused_computation.60 | convolution fusion | flops 406588416 | bytes 2641920 | tf_op jit(solution)/shard_map/dot_general | solution.py:258
  52.1 0.7 collective-permute-start.3
  54.0 1.6 %collective-permute-start.4 = (bf16[2,516,256]{2,0,1:T(2,128)(2,1)S(1)}, bf16[2,516,256]{2,0,1:T(2,128)(2,1)S(1)}, u32[]{:S(2)}, u32[]{:S(2)}) collective-permute-start(bf16[2,516,256]{2,0,1:T(2,128)(2,1)S(1)} %copy.26), channel_id=1, source_target_pairs={{0,1},{1,0},{2,3},{3,2},{4,5},{5,4},{6,7},{7,6},{8,9},{9,8},{10,11... | collective-permute-start | bytes 1585160 | tf_op jit(solution)/shard_map/ppermute | solution.py:144
  57.4 9.6 %collective-permute-done.4 = bf16[2,516,256]{2,0,1:T(2,128)(2,1)S(1)} collective-permute-done((bf16[2,516,256]{2,0,1:T(2,128)(2,1)S(1)}, bf16[2,516,256]{2,0,1:T(2,128)(2,1)S(1)}, u32[]{:S(2)}, u32[]{:S(2)}) %collective-permute-start.4) | collective-permute-done | bytes 528416 | tf_op jit(solution)/shard_map/ppermute | solution.py:144
  67.7 9.6 %collective-permute-start.5 = (f32[128,256]{1,0:T(8,128)S(1)}, f32[128,256]{1,0:T(8,128)S(1)}, u32[]{:S(2)}, u32[]{:S(2)}) collective-permute-start(f32[128,256]{1,0:T(8,128)S(1)} %get-tuple-element.27), channel_id=1, source_target_pairs={{0,4},{4,8},{8,12},{12,0},{1,5},{5,9},{9,13},{13,1},{2,6},{6,10},{... | collective-permute-start | bytes 393224 | tf_op jit(solution)/shard_map/ppermute | solution.py:350
  77.3 2.4 %collective-permute-start.6 = (f32[128,256]{1,0:T(8,128)S(1)}, f32[128,256]{1,0:T(8,128)S(1)}, u32[]{:S(2)}, u32[]{:S(2)}) collective-permute-start(f32[128,256]{1,0:T(8,128)S(1)} %get-tuple-element.28), channel_id=1, source_target_pairs={{0,8},{4,12},{8,0},{12,4},{1,9},{5,13},{9,1},{13,5},{2,10},{6,14},... | collective-permute-start | bytes 393224 | tf_op jit(solution)/shard_map/ppermute | solution.py:350
  79.8 2.4 %collective-permute-done.5 = f32[128,256]{1,0:T(8,128)S(1)} collective-permute-done((f32[128,256]{1,0:T(8,128)S(1)}, f32[128,256]{1,0:T(8,128)S(1)}, u32[]{:S(2)}, u32[]{:S(2)}) %collective-permute-start.5) | collective-permute-done | bytes 131104 | tf_op jit(solution)/shard_map/ppermute | solution.py:350
  82.2 2.9 %collective-permute-done.6 = f32[128,256]{1,0:T(8,128)S(1)} collective-permute-done((f32[128,256]{1,0:T(8,128)S(1)}, f32[128,256]{1,0:T(8,128)S(1)}, u32[]{:S(2)}, u32[]{:S(2)}) %collective-permute-start.6) | collective-permute-done | bytes 131104 | tf_op jit(solution)/shard_map/ppermute | solution.py:350
  85.1 1.0 %collective-permute-done.7 = f32[128,256]{1,0:T(8,128)S(1)} collective-permute-done((f32[128,256]{1,0:T(8,128)S(1)}, f32[128,256]{1,0:T(8,128)S(1)}, u32[]{:S(2)}, u32[]{:S(2)}) %collective-permute-start.7) | collective-permute-done | bytes 131104 | tf_op jit(solution)/shard_map/ppermute | solution.py:350
  86.2 1.3 %collective-permute-done.8 = f32[128,256]{1,0:T(8,128)S(1)} collective-permute-done((f32[128,256]{1,0:T(8,128)S(1)}, f32[128,256]{1,0:T(8,128)S(1)}, u32[]{:S(2)}, u32[]{:S(2)}) %collective-permute-start.8) | collective-permute-done | bytes 131104 | tf_op jit(solution)/shard_map/ppermute | solution.py:154
  87.5 0.7 add.307
  (81 shorter events, 10.5 us)
Async XLA Ops:
  1.5 8.7 %collective-permute-start = (f32[3,256]{1,0:T(4,128)S(1)}, f32[3,256]{1,0:T(4,128)S(1)}, u32[]{:S(2)}, u32[]{:S(2)}) collective-permute-start(f32[3,256]{1,0:T(4,128)S(1)} %bitcast.121), channel_id=1, source_target_pairs={{0,4},{4,8},{8,12},{12,0},{1,5},{5,9},{9,13},{13,1},{2,6},{6,10},{... | collective-permute-start | bytes 9224 | tf_op jit(solution)/shard_map/ppermute | solution.py:214
  4.5 5.6 %collective-permute-start.1 = (f32[3,256]{1,0:T(4,128)S(1)}, f32[3,256]{1,0:T(4,128)S(1)}, u32[]{:S(2)}, u32[]{:S(2)}) collective-permute-start(f32[3,256]{1,0:T(4,128)S(1)} %bitcast.122), channel_id=1, source_target_pairs={{0,8},{4,12},{8,0},{12,4},{1,9},{5,13},{9,1},{13,5},{2,10},{6,14},... | collective-permute-start | bytes 9224 | tf_op jit(solution)/shard_map/ppermute | solution.py:214
  7.1 3.6 %collective-permute-start.2 = (f32[3,256]{1,0:T(4,128)S(1)}, f32[3,256]{1,0:T(4,128)S(1)}, u32[]{:S(2)}, u32[]{:S(2)}) collective-permute-start(f32[3,256]{1,0:T(4,128)S(1)} %bitcast.123), channel_id=1, source_target_pairs={{0,12},{4,0},{8,4},{12,8},{1,13},{5,1},{9,5},{13,9},{2,14},{6,2},{... | collective-permute-start | bytes 9224 | tf_op jit(solution)/shard_map/ppermute | solution.py:214
  12.1 1.0 %copy-start.2 = (bf16[1,640,256]{2,1,0:T(8,128)(2,1)S(1)}, bf16[1,640,256]{2,1,0:T(8,128)(2,1)}, u32[]{:S(2)}) copy-start(bf16[1,640,256]{2,1,0:T(8,128)(2,1)} %param.8) | copy-start | bytes 983044
  19.7 28.4 %all-to-all-start = ((f32[4,2,256,128]{3,2,1,0:T(8,128)}), f32[4,2,256,128]{3,2,1,0:T(8,128)S(1)}, u32[]{:S(2)}, u32[]{:S(2)}) async-start(f32[4,2,256,128]{3,2,1,0:T(8,128)} %copy.19), calls=%async_computation | async-start | bytes 2097152 | tf_op jit(solution)/shard_map/all_to_all | solution.py:322
  51.7 1.1 %copy-start.1 = (s32[2,256]{1,0:T(2,128)S(1)}, s32[2,256]{1,0:T(2,128)}, u32[]{:S(2)}) copy-start(s32[2,256]{1,0:T(2,128)} %param.7) | copy-start | bytes 6148
  52.1 0.7 collective-permute-start.3
  53.5 2.1 %copy-start = (s32[1,2049]{1,0:T(1,128)S(1)}, s32[1,2049]{1,0:T(1,128)}, u32[]{:S(2)}) copy-start(s32[1,2049]{1,0:T(1,128)} %param.9) | copy-start | bytes 24592
  54.0 13.0 %collective-permute-start.4 = (bf16[2,516,256]{2,0,1:T(2,128)(2,1)S(1)}, bf16[2,516,256]{2,0,1:T(2,128)(2,1)S(1)}, u32[]{:S(2)}, u32[]{:S(2)}) collective-permute-start(bf16[2,516,256]{2,0,1:T(2,128)(2,1)S(1)} %copy.26), channel_id=1, source_target_pairs={{0,1},{1,0},{2,3},{3,2},{4,5},{5,4},{6,7},{7,6},{8,9},{9,8},{10,11... | collective-permute-start | bytes 1585160 | tf_op jit(solution)/shard_map/ppermute | solution.py:144
  67.7 14.5 %collective-permute-start.5 = (f32[128,256]{1,0:T(8,128)S(1)}, f32[128,256]{1,0:T(8,128)S(1)}, u32[]{:S(2)}, u32[]{:S(2)}) collective-permute-start(f32[128,256]{1,0:T(8,128)S(1)} %get-tuple-element.27), channel_id=1, source_target_pairs={{0,4},{4,8},{8,12},{12,0},{1,5},{5,9},{9,13},{13,1},{2,6},{6,10},{... | collective-permute-start | bytes 393224 | tf_op jit(solution)/shard_map/ppermute | solution.py:350
  77.3 7.7 %collective-permute-start.6 = (f32[128,256]{1,0:T(8,128)S(1)}, f32[128,256]{1,0:T(8,128)S(1)}, u32[]{:S(2)}, u32[]{:S(2)}) collective-permute-start(f32[128,256]{1,0:T(8,128)S(1)} %get-tuple-element.28), channel_id=1, source_target_pairs={{0,8},{4,12},{8,0},{12,4},{1,9},{5,13},{9,1},{13,5},{2,10},{6,14},... | collective-permute-start | bytes 393224 | tf_op jit(solution)/shard_map/ppermute | solution.py:350
  79.7 6.4 %collective-permute-start.7 = (f32[128,256]{1,0:T(8,128)S(1)}, f32[128,256]{1,0:T(8,128)S(1)}, u32[]{:S(2)}, u32[]{:S(2)}) collective-permute-start(f32[128,256]{1,0:T(8,128)S(1)} %get-tuple-element.29), channel_id=1, source_target_pairs={{0,12},{4,0},{8,4},{12,8},{1,13},{5,1},{9,5},{13,9},{2,14},{6,2},{... | collective-permute-start | bytes 393224 | tf_op jit(solution)/shard_map/ppermute | solution.py:350
  86.1 1.4 %collective-permute-start.8 = (f32[128,256]{1,0:T(8,128)S(1)}, f32[128,256]{1,0:T(8,128)S(1)}, u32[]{:S(2)}, u32[]{:S(2)}) collective-permute-start(f32[128,256]{1,0:T(8,128)S(1)} %fusion.60), channel_id=1, source_target_pairs={{0,2},{2,0},{1,3},{3,1},{4,6},{6,4},{5,7},{7,5},{8,10},{10,8},{9,1... | collective-permute-start | bytes 393224 | tf_op jit(solution)/shard_map/ppermute | solution.py:154

commit v18 on v17

--- a/solution.py
+++ b/solution.py
@@ -230,16 +230,17 @@
     imag_part = jnp.sum(cos_b * imag_in[None] - sin_b * real_in[None], axis=1)
     local_epoch = position * block_len + jnp.arange(block_len, dtype=jnp.int32)
     real_part, imag_part = rotate(real_part, imag_part, index, local_epoch, samples)
-    return jnp.stack([real_part, imag_part], axis=1)
+    return jnp.concatenate([real_part, imag_part], axis=-1)
 
 
 def packed_transform(gathered):
-    devices_tm, _, block_len, columns = gathered.shape
+    devices_tm, block_len, doubled = gathered.shape
+    columns = doubled // 2
     length = devices_tm * block_len
     index = jnp.arange(devices_tm, dtype=jnp.int32)
     cos_table, sin_table = phase_tables(index, index, devices_tm)
-    real_in = gathered[:, 0]
-    imag_in = gathered[:, 1]
+    real_in = gathered[..., :columns]
+    imag_in = gathered[..., columns:]
     cos_b = cos_table[:, :, None, None]
     sin_b = sin_table[:, :, None, None]
     real_part = jnp.sum(cos_b * real_in[None] + sin_b * imag_in[None], axis=1)

time: 88.5 us -> 88.5 us (level)
  local copies, waits for them, and re-layouts: 4.62 us -> 3.57 us
  other arithmetic: 9.33 us -> 10.3 us
    concatenate x0 -> x1, other arithmetic: none -> 1.05 us  [packed_partials(): return jnp.concatenate([real_part, imag_part], axis=-1)]
    another operation x1 -> x0, local copies, waits for them, and re-layouts: 1.05 us -> none  [packed_partials(): return jnp.stack([real_part, imag_part], axis=1)]
where the time goes in v18:
time: 88.5 us; the launch traced here: 88.1 us
  waiting for transfers between devices  40.5 us (46%)
  starting transfers between devices  25.9 us (29%)
  other arithmetic  10.3 us (12%)
  matrix products  7.29 us (8%)
  local copies, waits for them, and re-layouts  3.57 us (4%)
    all_to_all x1, waiting for transfers between devices, body(): gathered = lax.all_to_all(twisted, 'tm', 0, 0, tiled=True)  22.7 us
    ppermute x3, starting transfers between devices, body(): lax.ppermute(block((position + shift) % devices_tm), 'tm', pairs)  12.1 us
    ppermute x1, waiting for transfers between devices, panel_spectra(): blocks.append(lax.ppermute(spectra, 'panel', pairs))  9.57 us
    ppermute x3, starting transfers between devices, swap_blocks(): arrived.append(lax.ppermute(outgoing, axis, pairs))  7.01 us
    ppermute x3, waiting for transfers between devices, body(): lax.ppermute(block((position + shift) % devices_tm), 'tm', pairs)  6.28 us
    all_to_all x1, starting transfers between devices, body(): gathered = lax.all_to_all(twisted, 'tm', 0, 0, tiled=True)  4.41 us
    dot_general x1, matrix products, synthesize(): latitude = jnp.dot(basis_rows, masked, preferred_element_type=jnp.float32)  4.37 us
    dot_general x2, matrix products, mat(): lax.dot_general(table, value, dims, precision=lax.Precision.HIGH, preferr...  1.78 us
  transfers between devices with their start and end apart: 10, of which 7 were waited for; matrix products, arithmetic and copies ran while one was open for 5% of the time, Pallas kernels for 0%

profile of v18, /device:TPU:0, one launch (start us, length us, event | category | flops | bytes accessed | tf_op | source)
XLA Modules:
  0.0 88.1 jit_solution(12013035436387611873)
XLA Ops:
  0.0 0.7 concatenate.47
  0.7 0.7 convert_element_type.120
  1.5 3.1 %collective-permute-start = (f32[3,256]{1,0:T(4,128)S(1)}, f32[3,256]{1,0:T(4,128)S(1)}, u32[]{:S(2)}, u32[]{:S(2)}) collective-permute-start(f32[3,256]{1,0:T(4,128)S(1)} %bitcast.103), channel_id=1, source_target_pairs={{0,4},{4,8},{8,12},{12,0},{1,5},{5,9},{9,13},{13,1},{2,6},{6,10},{... | collective-permute-start | bytes 9224 | tf_op jit(solution)/shard_map/ppermute | solution.py:214
  4.5 2.6 %collective-permute-start.1 = (f32[3,256]{1,0:T(4,128)S(1)}, f32[3,256]{1,0:T(4,128)S(1)}, u32[]{:S(2)}, u32[]{:S(2)}) collective-permute-start(f32[3,256]{1,0:T(4,128)S(1)} %bitcast.104), channel_id=1, source_target_pairs={{0,8},{4,12},{8,0},{12,4},{1,9},{5,13},{9,1},{13,5},{2,10},{6,14},... | collective-permute-start | bytes 9224 | tf_op jit(solution)/shard_map/ppermute | solution.py:214
  7.1 1.3 %collective-permute-start.2 = (f32[3,256]{1,0:T(4,128)S(1)}, f32[3,256]{1,0:T(4,128)S(1)}, u32[]{:S(2)}, u32[]{:S(2)}) collective-permute-start(f32[3,256]{1,0:T(4,128)S(1)} %bitcast.105), channel_id=1, source_target_pairs={{0,12},{4,0},{8,4},{12,8},{1,13},{5,1},{9,5},{13,9},{2,14},{6,2},{... | collective-permute-start | bytes 9224 | tf_op jit(solution)/shard_map/ppermute | solution.py:214
  8.5 0.8 fusion.100
  9.3 0.7 compare_reduce_fusion
  12.1 0.7 fusion.5
  13.1 4.4 %fusion = f32[1024,256]{1,0:T(8,128)S(1)} fusion(bf16[1024,320]{0,1:T(8,128)(2,1)S(1)} %get-tuple-element.10, bf16[1024,320]{0,1:T(8,128)(2,1)S(1)} %get-tuple-element.9, f32[1024]{0:T(1024)S(1)} %bitcast.107, f32[256]{0:T(256)S(1)} %bitcast.111, f32[1024]{0:T(1024)S(1)} %bitcast.106, pred[256]{0:T(512)(128)(4,1)S(1)} %compare_reduce_fusion, ...), kind=kOutput, calls=%fused_computation.7 | convolution fusion | flops 339542016 | bytes 2700032 | tf_op jit(solution)/shard_map/dot_general | solution.py:55
  18.5 1.1 %pad_maximum_fusion = f32[4,256,256]{2,1,0:T(8,128)} fusion(f32[4,256,128]{2,1,0:T(8,128)S(1)} %get-tuple-element.16, f32[4,256,128]{2,1,0:T(8,128)S(1)} %get-tuple-element.15), kind=kLoop, calls=%fused_computation.24 | loop fusion | flops 262144 | bytes 2097152 | tf_op jit(solution)/shard_map/concatenate | solution.py:233
  19.6 4.4 %all-to-all-start = ((f32[4,256,256]{2,1,0:T(8,128)}), f32[4,256,256]{2,1,0:T(8,128)S(1)}, u32[]{:S(2)}, u32[]{:S(2)}) async-start(f32[4,256,256]{2,1,0:T(8,128)} %pad_maximum_fusion), calls=%async_computation | async-start | bytes 2097152 | tf_op jit(solution)/shard_map/all_to_all | solution.py:323
  25.3 22.7 %all-to-all-done = f32[4,256,256]{2,1,0:T(8,128)S(1)} async-done(((f32[4,256,256]{2,1,0:T(8,128)}), f32[4,256,256]{2,1,0:T(8,128)S(1)}, u32[]{:S(2)}, u32[]{:S(2)}) %all-to-all-start) | async-done | bytes 1048608 | tf_op jit(solution)/shard_map/all_to_all | solution.py:323
  48.7 0.9 %fusion.18 = f32[516,4,128]{2,0,1:T(8,128)S(1)} fusion(f32[4,256,128]{2,1,0:T(8,128)S(1)} %get-tuple-element.6, f32[4,256,128]{2,1,0:T(8,128)S(1)} %get-tuple-element.5, f32[129,256]{1,0:T(8,128)S(1)} %get-tuple-element.52, f32[129,256]{1,0:T(8,128)S(1)} %get-tuple-element.51, f32[129,256]{1,0:T(8,128)S(1)} %get-tuple-element.61, ...), kind=kOutput, calls=%fused_computation.48 | convolution fusion | flops 406588416 | bytes 2641920 | tf_op jit(solution)/shard_map/dot_general | solution.py:259
  49.6 0.9 %fusion.22 = f32[516,4,128]{2,0,1:T(8,128)S(1)} fusion(f32[4,256,128]{2,1,0:T(8,128)S(1)} %get-tuple-element.5, f32[4,256,128]{2,1,0:T(8,128)S(1)} %get-tuple-element.6, f32[129,256]{1,0:T(8,128)S(1)} %get-tuple-element.52, f32[129,256]{1,0:T(8,128)S(1)} %get-tuple-element.51, f32[129,256]{1,0:T(8,128)S(1)} %get-tuple-element.61, ...), kind=kOutput, calls=%fused_computation.52 | convolution fusion | flops 406588416 | bytes 2641920 | tf_op jit(solution)/shard_map/dot_general | solution.py:259
  52.0 0.7 collective-permute-start.3
  53.9 1.6 %collective-permute-start.4 = (bf16[2,516,256]{2,0,1:T(2,128)(2,1)S(1)}, bf16[2,516,256]{2,0,1:T(2,128)(2,1)S(1)}, u32[]{:S(2)}, u32[]{:S(2)}) collective-permute-start(bf16[2,516,256]{2,0,1:T(2,128)(2,1)S(1)} %copy.25), channel_id=1, source_target_pairs={{0,1},{1,0},{2,3},{3,2},{4,5},{5,4},{6,7},{7,6},{8,9},{9,8},{10,11... | collective-permute-start | bytes 1585160 | tf_op jit(solution)/shard_map/ppermute | solution.py:144
  57.4 9.6 %collective-permute-done.4 = bf16[2,516,256]{2,0,1:T(2,128)(2,1)S(1)} collective-permute-done((bf16[2,516,256]{2,0,1:T(2,128)(2,1)S(1)}, bf16[2,516,256]{2,0,1:T(2,128)(2,1)S(1)}, u32[]{:S(2)}, u32[]{:S(2)}) %collective-permute-start.4) | collective-permute-done | bytes 528416 | tf_op jit(solution)/shard_map/ppermute | solution.py:144
  67.6 9.7 %collective-permute-start.5 = (f32[128,256]{1,0:T(8,128)S(1)}, f32[128,256]{1,0:T(8,128)S(1)}, u32[]{:S(2)}, u32[]{:S(2)}) collective-permute-start(f32[128,256]{1,0:T(8,128)S(1)} %get-tuple-element.27), channel_id=1, source_target_pairs={{0,4},{4,8},{8,12},{12,0},{1,5},{5,9},{9,13},{13,1},{2,6},{6,10},{... | collective-permute-start | bytes 393224 | tf_op jit(solution)/shard_map/ppermute | solution.py:351
  77.3 2.4 %collective-permute-start.6 = (f32[128,256]{1,0:T(8,128)S(1)}, f32[128,256]{1,0:T(8,128)S(1)}, u32[]{:S(2)}, u32[]{:S(2)}) collective-permute-start(f32[128,256]{1,0:T(8,128)S(1)} %get-tuple-element.28), channel_id=1, source_target_pairs={{0,8},{4,12},{8,0},{12,4},{1,9},{5,13},{9,1},{13,5},{2,10},{6,14},... | collective-permute-start | bytes 393224 | tf_op jit(solution)/shard_map/ppermute | solution.py:351
  79.7 2.4 %collective-permute-done.5 = f32[128,256]{1,0:T(8,128)S(1)} collective-permute-done((f32[128,256]{1,0:T(8,128)S(1)}, f32[128,256]{1,0:T(8,128)S(1)}, u32[]{:S(2)}, u32[]{:S(2)}) %collective-permute-start.5) | collective-permute-done | bytes 131104 | tf_op jit(solution)/shard_map/ppermute | solution.py:351
  82.1 2.9 %collective-permute-done.6 = f32[128,256]{1,0:T(8,128)S(1)} collective-permute-done((f32[128,256]{1,0:T(8,128)S(1)}, f32[128,256]{1,0:T(8,128)S(1)}, u32[]{:S(2)}, u32[]{:S(2)}) %collective-permute-start.6) | collective-permute-done | bytes 131104 | tf_op jit(solution)/shard_map/ppermute | solution.py:351
  85.0 1.0 %collective-permute-done.7 = f32[128,256]{1,0:T(8,128)S(1)} collective-permute-done((f32[128,256]{1,0:T(8,128)S(1)}, f32[128,256]{1,0:T(8,128)S(1)}, u32[]{:S(2)}, u32[]{:S(2)}) %collective-permute-start.7) | collective-permute-done | bytes 131104 | tf_op jit(solution)/shard_map/ppermute | solution.py:351
  86.1 1.3 %collective-permute-done.8 = f32[128,256]{1,0:T(8,128)S(1)} collective-permute-done((f32[128,256]{1,0:T(8,128)S(1)}, f32[128,256]{1,0:T(8,128)S(1)}, u32[]{:S(2)}, u32[]{:S(2)}) %collective-permute-start.8) | collective-permute-done | bytes 131104 | tf_op jit(solution)/shard_map/ppermute | solution.py:154
  87.5 0.7 add.300
  (80 shorter events, 10.4 us)
Async XLA Ops:
  1.5 8.7 %collective-permute-start = (f32[3,256]{1,0:T(4,128)S(1)}, f32[3,256]{1,0:T(4,128)S(1)}, u32[]{:S(2)}, u32[]{:S(2)}) collective-permute-start(f32[3,256]{1,0:T(4,128)S(1)} %bitcast.103), channel_id=1, source_target_pairs={{0,4},{4,8},{8,12},{12,0},{1,5},{5,9},{9,13},{13,1},{2,6},{6,10},{... | collective-permute-start | bytes 9224 | tf_op jit(solution)/shard_map/ppermute | solution.py:214
  4.5 5.6 %collective-permute-start.1 = (f32[3,256]{1,0:T(4,128)S(1)}, f32[3,256]{1,0:T(4,128)S(1)}, u32[]{:S(2)}, u32[]{:S(2)}) collective-permute-start(f32[3,256]{1,0:T(4,128)S(1)} %bitcast.104), channel_id=1, source_target_pairs={{0,8},{4,12},{8,0},{12,4},{1,9},{5,13},{9,1},{13,5},{2,10},{6,14},... | collective-permute-start | bytes 9224 | tf_op jit(solution)/shard_map/ppermute | solution.py:214
  7.1 3.6 %collective-permute-start.2 = (f32[3,256]{1,0:T(4,128)S(1)}, f32[3,256]{1,0:T(4,128)S(1)}, u32[]{:S(2)}, u32[]{:S(2)}) collective-permute-start(f32[3,256]{1,0:T(4,128)S(1)} %bitcast.105), channel_id=1, source_target_pairs={{0,12},{4,0},{8,4},{12,8},{1,13},{5,1},{9,5},{13,9},{2,14},{6,2},{... | collective-permute-start | bytes 9224 | tf_op jit(solution)/shard_map/ppermute | solution.py:214
  12.1 1.0 %copy-start.2 = (bf16[1,640,256]{2,1,0:T(8,128)(2,1)S(1)}, bf16[1,640,256]{2,1,0:T(8,128)(2,1)}, u32[]{:S(2)}) copy-start(bf16[1,640,256]{2,1,0:T(8,128)(2,1)} %param.8) | copy-start | bytes 983044
  19.6 28.4 %all-to-all-start = ((f32[4,256,256]{2,1,0:T(8,128)}), f32[4,256,256]{2,1,0:T(8,128)S(1)}, u32[]{:S(2)}, u32[]{:S(2)}) async-start(f32[4,256,256]{2,1,0:T(8,128)} %pad_maximum_fusion), calls=%async_computation | async-start | bytes 2097152 | tf_op jit(solution)/shard_map/all_to_all | solution.py:323
  51.6 1.1 %copy-start.1 = (s32[2,256]{1,0:T(2,128)S(1)}, s32[2,256]{1,0:T(2,128)}, u32[]{:S(2)}) copy-start(s32[2,256]{1,0:T(2,128)} %param.7) | copy-start | bytes 6148
  52.0 0.7 collective-permute-start.3
  53.4 2.1 %copy-start = (s32[1,2049]{1,0:T(1,128)S(1)}, s32[1,2049]{1,0:T(1,128)}, u32[]{:S(2)}) copy-start(s32[1,2049]{1,0:T(1,128)} %param.9) | copy-start | bytes 24592
  53.9 13.0 %collective-permute-start.4 = (bf16[2,516,256]{2,0,1:T(2,128)(2,1)S(1)}, bf16[2,516,256]{2,0,1:T(2,128)(2,1)S(1)}, u32[]{:S(2)}, u32[]{:S(2)}) collective-permute-start(bf16[2,516,256]{2,0,1:T(2,128)(2,1)S(1)} %copy.25), channel_id=1, source_target_pairs={{0,1},{1,0},{2,3},{3,2},{4,5},{5,4},{6,7},{7,6},{8,9},{9,8},{10,11... | collective-permute-start | bytes 1585160 | tf_op jit(solution)/shard_map/ppermute | solution.py:144
  67.6 14.5 %collective-permute-start.5 = (f32[128,256]{1,0:T(8,128)S(1)}, f32[128,256]{1,0:T(8,128)S(1)}, u32[]{:S(2)}, u32[]{:S(2)}) collective-permute-start(f32[128,256]{1,0:T(8,128)S(1)} %get-tuple-element.27), channel_id=1, source_target_pairs={{0,4},{4,8},{8,12},{12,0},{1,5},{5,9},{9,13},{13,1},{2,6},{6,10},{... | collective-permute-start | bytes 393224 | tf_op jit(solution)/shard_map/ppermute | solution.py:351
  77.3 7.7 %collective-permute-start.6 = (f32[128,256]{1,0:T(8,128)S(1)}, f32[128,256]{1,0:T(8,128)S(1)}, u32[]{:S(2)}, u32[]{:S(2)}) collective-permute-start(f32[128,256]{1,0:T(8,128)S(1)} %get-tuple-element.28), channel_id=1, source_target_pairs={{0,8},{4,12},{8,0},{12,4},{1,9},{5,13},{9,1},{13,5},{2,10},{6,14},... | collective-permute-start | bytes 393224 | tf_op jit(solution)/shard_map/ppermute | solution.py:351
  79.6 6.4 %collective-permute-start.7 = (f32[128,256]{1,0:T(8,128)S(1)}, f32[128,256]{1,0:T(8,128)S(1)}, u32[]{:S(2)}, u32[]{:S(2)}) collective-permute-start(f32[128,256]{1,0:T(8,128)S(1)} %get-tuple-element.29), channel_id=1, source_target_pairs={{0,12},{4,0},{8,4},{12,8},{1,13},{5,1},{9,5},{13,9},{2,14},{6,2},{... | collective-permute-start | bytes 393224 | tf_op jit(solution)/shard_map/ppermute | solution.py:351
  86.0 1.4 %collective-permute-start.8 = (f32[128,256]{1,0:T(8,128)S(1)}, f32[128,256]{1,0:T(8,128)S(1)}, u32[]{:S(2)}, u32[]{:S(2)}) collective-permute-start(f32[128,256]{1,0:T(8,128)S(1)} %fusion.58), channel_id=1, source_target_pairs={{0,2},{2,0},{1,3},{3,1},{4,6},{6,4},{5,7},{7,5},{8,10},{10,8},{9,1... | collective-permute-start | bytes 393224 | tf_op jit(solution)/shard_map/ppermute | solution.py:154

commit v19 on v17

--- a/solution.py
+++ b/solution.py
@@ -280,14 +280,14 @@
     return own, far
 
 
-def unpack_spectra(own, far, position, samples, norm_scale):
+def unpack_spectra(own, far, position, samples, norm_scale, start, stop):
     devices_tm = lax.axis_size("tm")
     shifted = jnp.concatenate([own[:, :1], far[:, :-1]], axis=1)
     outgoing = jnp.where(position == 0, shifted, far)
     pairs = [(src, (devices_tm - src) % devices_tm) for src in range(devices_tm)]
-    mirror = lax.ppermute(outgoing, "tm", pairs)
-    own_real = own[0]
-    own_imag = own[1]
+    mirror = lax.ppermute(outgoing[:, start:stop], "tm", pairs)
+    own_real = own[0, start:stop]
+    own_imag = own[1, start:stop]
     first_real = (own_real + mirror[0]) * 0.5
     first_imag = (own_imag - mirror[1]) * 0.5
     second_real = (own_imag + mirror[1]) * 0.5
@@ -322,17 +322,23 @@
     gathered = lax.all_to_all(twisted, "tm", 0, 0, tiled=True)
     own, far = packed_transform(gathered)
     norm_scale = 1.0 / jnp.sqrt(column_index[0].astype(jnp.float32) + 1.0)
-    spectra = unpack_spectra(own, far, position, samples, norm_scale)
+    count = own.shape[1]
     inverse_psd, fold = inverse_weights(
-        psd_table[0], position, devices_tm, epochs, samples, spectra.shape[1]
-    )
-    weighted = (spectra.astype(jnp.float32) * inverse_psd[None, :, None]).astype(jnp.bfloat16)
-    weighted = weighted * fold[None, :, None].astype(jnp.bfloat16)
+        psd_table[0], position, devices_tm, epochs, samples, count
+    )
+    cut = (count // 2) // 16 * 16
     contract = (((0, 1), (0, 1)), ((), ()))
-    products = [
-        lax.dot_general(block, weighted, contract, preferred_element_type=jnp.float32)
-        for block in panel_spectra(spectra)
-    ]
+    products = [0.0] * panels
+    for start, stop in ((0, cut), (cut, count)):
+        spectra = unpack_spectra(own, far, position, samples, norm_scale, start, stop)
+        weighted = (
+            spectra.astype(jnp.float32) * inverse_psd[None, start:stop, None]
+        ).astype(jnp.bfloat16)
+        weighted = weighted * fold[None, start:stop, None].astype(jnp.bfloat16)
+        for shift, block in enumerate(panel_spectra(spectra)):
+            products[shift] = products[shift] + lax.dot_general(
+                block, weighted, contract, preferred_element_type=jnp.float32
+            )
     by_shift = jnp.stack(products)
     panel = lax.axis_index("panel")
     rows = panels * columns // devices_tm

time: 88.5 us -> 91.6 us (1.035)
  waiting for transfers between devices: 40.5 us -> 43 us
    ppermute x1 -> x2, waiting for transfers between devices: 9.57 us -> 12.7 us  [panel_spectra(): blocks.append(lax.ppermute(spectra, 'panel', pairs))]
    all_to_all x1, waiting for transfers between devices: 22.7 us -> 21.4 us  [body(): gathered = lax.all_to_all(twisted, 'tm', 0, 0, tiled=True)]
    ppermute x3, starting transfers between devices: 12.1 us -> 11 us  [body(): lax.ppermute(block((position + shift) % devices_tm), 'tm', pairs)]
    ppermute x1 -> x2, starting transfers between devices: 1.57 us -> 2.16 us  [panel_spectra(): blocks.append(lax.ppermute(spectra, 'panel', pairs))]
  transfers between devices with their start and end apart: 10 -> 12, of which waited for: 7 -> 6; matrix products, arithmetic and copies ran while one was open for 5% -> 6% of each run, Pallas kernels for 0% -> 0%
where the time goes in v19:
time: 91.6 us; the launch traced here: 91.2 us
  waiting for transfers between devices  43 us (47%)
  starting transfers between devices  26.2 us (29%)
  other arithmetic  9.23 us (10%)
  matrix products  7.33 us (8%)
  local copies, waits for them, and re-layouts  4.64 us (5%)
    all_to_all x1, waiting for transfers between devices, body(): gathered = lax.all_to_all(twisted, 'tm', 0, 0, tiled=True)  21.4 us
    ppermute x2, waiting for transfers between devices, panel_spectra(): blocks.append(lax.ppermute(spectra, 'panel', pairs))  12.7 us
    ppermute x3, starting transfers between devices, body(): lax.ppermute(block((position + shift) % devices_tm), 'tm', pairs)  11 us
    ppermute x3, waiting for transfers between devices, body(): lax.ppermute(block((position + shift) % devices_tm), 'tm', pairs)  7.02 us
    ppermute x3, starting transfers between devices, swap_blocks(): arrived.append(lax.ppermute(outgoing, axis, pairs))  7.01 us
    all_to_all x1, starting transfers between devices, body(): gathered = lax.all_to_all(twisted, 'tm', 0, 0, tiled=True)  4.54 us
    dot_general x1, matrix products, synthesize(): latitude = jnp.dot(basis_rows, masked, preferred_element_type=jnp.float32)  4.37 us
    ppermute x2, starting transfers between devices, panel_spectra(): blocks.append(lax.ppermute(spectra, 'panel', pairs))  2.16 us
  transfers between devices with their start and end apart: 12, of which 6 were waited for; matrix products, arithmetic and copies ran while one was open for 6% of the time, Pallas kernels for 0%

profile of v19, /device:TPU:0, one launch (start us, length us, event | category | flops | bytes accessed | tf_op | source)
XLA Modules:
  0.0 91.2 jit_solution(9291970321021768690)
XLA Ops:
  0.0 0.7 concatenate.65
  0.7 0.7 convert_element_type.138
  1.5 3.1 %collective-permute-start = (f32[3,256]{1,0:T(4,128)S(1)}, f32[3,256]{1,0:T(4,128)S(1)}, u32[]{:S(2)}, u32[]{:S(2)}) collective-permute-start(f32[3,256]{1,0:T(4,128)S(1)} %bitcast.133), channel_id=1, source_target_pairs={{0,4},{4,8},{8,12},{12,0},{1,5},{5,9},{9,13},{13,1},{2,6},{6,10},{... | collective-permute-start | bytes 9224 | tf_op jit(solution)/shard_map/ppermute | solution.py:214
  4.5 2.6 %collective-permute-start.1 = (f32[3,256]{1,0:T(4,128)S(1)}, f32[3,256]{1,0:T(4,128)S(1)}, u32[]{:S(2)}, u32[]{:S(2)}) collective-permute-start(f32[3,256]{1,0:T(4,128)S(1)} %bitcast.134), channel_id=1, source_target_pairs={{0,8},{4,12},{8,0},{12,4},{1,9},{5,13},{9,1},{13,5},{2,10},{6,14},... | collective-permute-start | bytes 9224 | tf_op jit(solution)/shard_map/ppermute | solution.py:214
  7.1 1.3 %collective-permute-start.2 = (f32[3,256]{1,0:T(4,128)S(1)}, f32[3,256]{1,0:T(4,128)S(1)}, u32[]{:S(2)}, u32[]{:S(2)}) collective-permute-start(f32[3,256]{1,0:T(4,128)S(1)} %bitcast.135), channel_id=1, source_target_pairs={{0,12},{4,0},{8,4},{12,8},{1,13},{5,1},{9,5},{13,9},{2,14},{6,2},{... | collective-permute-start | bytes 9224 | tf_op jit(solution)/shard_map/ppermute | solution.py:214
  8.5 0.8 fusion.109
  9.3 0.7 compare_reduce_fusion
  12.1 0.7 fusion.5
  13.1 4.4 %fusion = f32[1024,256]{1,0:T(8,128)S(1)} fusion(bf16[1024,320]{0,1:T(8,128)(2,1)S(1)} %get-tuple-element.10, bf16[1024,320]{0,1:T(8,128)(2,1)S(1)} %get-tuple-element.9, f32[1024]{0:T(1024)S(1)} %bitcast.137, f32[256]{0:T(256)S(1)} %bitcast.139, f32[1024]{0:T(1024)S(1)} %bitcast.136, pred[256]{0:T(512)(128)(4,1)S(1)} %compare_reduce_fusion, ...), kind=kOutput, calls=%fused_computation.7 | convolution fusion | flops 339542016 | bytes 2700032 | tf_op jit(solution)/shard_map/dot_general | solution.py:55
  18.6 1.1 %copy.46 = f32[4,2,256,128]{3,2,1,0:T(8,128)} copy(f32[4,2,256,128]{3,2,0,1:T(8,128)S(1)} %pad_maximum_fusion) | data formatting | bytes 2097152 | tf_op jit(solution)/shard_map/stack | solution.py:233
  19.7 4.5 %all-to-all-start = ((f32[4,2,256,128]{3,2,1,0:T(8,128)}), f32[4,2,256,128]{3,2,1,0:T(8,128)S(1)}, u32[]{:S(2)}, u32[]{:S(2)}) async-start(f32[4,2,256,128]{3,2,1,0:T(8,128)} %copy.46), calls=%async_computation | async-start | bytes 2097152 | tf_op jit(solution)/shard_map/all_to_all | solution.py:322
  26.9 21.4 %all-to-all-done = f32[4,2,256,128]{3,2,1,0:T(8,128)S(1)} async-done(((f32[4,2,256,128]{3,2,1,0:T(8,128)}), f32[4,2,256,128]{3,2,1,0:T(8,128)S(1)}, u32[]{:S(2)}, u32[]{:S(2)}) %all-to-all-start) | async-done | bytes 1048608 | tf_op jit(solution)/shard_map/all_to_all | solution.py:322
  49.0 0.9 fusion.18
  49.9 0.9 fusion.14
  52.7 0.7 collective-permute-start.3
  53.7 0.7 collective-permute-start.4
  54.5 1.5 %collective-permute-start.5 = (bf16[2,256,256]{1,2,0:T(8,128)(2,1)S(1)}, bf16[2,256,256]{1,2,0:T(8,128)(2,1)S(1)}, u32[]{:S(2)}, u32[]{:S(2)}) collective-permute-start(bf16[2,256,256]{1,2,0:T(8,128)(2,1)S(1)} %pad_maximum_fusion.3), channel_id=1, source_target_pairs={{0,1},{1,0},{2,3},{3,2},{4,5},{5,4},{6,7},{7,6},{8,9},{9,8},{10,11... | collective-permute-start | bytes 786440 | tf_op jit(solution)/shard_map/ppermute | solution.py:144
  57.6 12.7 %collective-permute-done.6 = bf16[2,260,256]{1,2,0:T(8,128)(2,1)S(1)} collective-permute-done((bf16[2,260,256]{1,2,0:T(8,128)(2,1)S(1)}, bf16[2,260,256]{1,2,0:T(8,128)(2,1)S(1)}, u32[]{:S(2)}, u32[]{:S(2)}) %collective-permute-start.6) | collective-permute-done | bytes 266272 | tf_op jit(solution)/shard_map/ppermute | solution.py:144
  71.0 8.2 %collective-permute-start.7 = (f32[128,256]{1,0:T(8,128)S(1)}, f32[128,256]{1,0:T(8,128)S(1)}, u32[]{:S(2)}, u32[]{:S(2)}) collective-permute-start(f32[128,256]{1,0:T(8,128)S(1)} %get-tuple-element.29), channel_id=1, source_target_pairs={{0,4},{4,8},{8,12},{12,0},{1,5},{5,9},{9,13},{13,1},{2,6},{6,10},{... | collective-permute-start | bytes 393224 | tf_op jit(solution)/shard_map/ppermute | solution.py:356
  79.2 2.8 %collective-permute-start.8 = (f32[128,256]{1,0:T(8,128)S(1)}, f32[128,256]{1,0:T(8,128)S(1)}, u32[]{:S(2)}, u32[]{:S(2)}) collective-permute-start(f32[128,256]{1,0:T(8,128)S(1)} %get-tuple-element.30), channel_id=1, source_target_pairs={{0,8},{4,12},{8,0},{12,4},{1,9},{5,13},{9,1},{13,5},{2,10},{6,14},... | collective-permute-start | bytes 393224 | tf_op jit(solution)/shard_map/ppermute | solution.py:356
  82.1 2.9 %collective-permute-done.7 = f32[128,256]{1,0:T(8,128)S(1)} collective-permute-done((f32[128,256]{1,0:T(8,128)S(1)}, f32[128,256]{1,0:T(8,128)S(1)}, u32[]{:S(2)}, u32[]{:S(2)}) %collective-permute-start.7) | collective-permute-done | bytes 131104 | tf_op jit(solution)/shard_map/ppermute | solution.py:356
  85.0 4.1 %collective-permute-done.8 = f32[128,256]{1,0:T(8,128)S(1)} collective-permute-done((f32[128,256]{1,0:T(8,128)S(1)}, f32[128,256]{1,0:T(8,128)S(1)}, u32[]{:S(2)}, u32[]{:S(2)}) %collective-permute-start.8) | collective-permute-done | bytes 131104 | tf_op jit(solution)/shard_map/ppermute | solution.py:356
  89.2 1.3 %collective-permute-done.10 = f32[128,256]{1,0:T(8,128)S(1)} collective-permute-done((f32[128,256]{1,0:T(8,128)S(1)}, f32[128,256]{1,0:T(8,128)S(1)}, u32[]{:S(2)}, u32[]{:S(2)}) %collective-permute-start.10) | collective-permute-done | bytes 131104 | tf_op jit(solution)/shard_map/ppermute | solution.py:154
  90.5 0.7 add.325
  (94 shorter events, 11.0 us)
Async XLA Ops:
  1.5 8.7 %collective-permute-start = (f32[3,256]{1,0:T(4,128)S(1)}, f32[3,256]{1,0:T(4,128)S(1)}, u32[]{:S(2)}, u32[]{:S(2)}) collective-permute-start(f32[3,256]{1,0:T(4,128)S(1)} %bitcast.133), channel_id=1, source_target_pairs={{0,4},{4,8},{8,12},{12,0},{1,5},{5,9},{9,13},{13,1},{2,6},{6,10},{... | collective-permute-start | bytes 9224 | tf_op jit(solution)/shard_map/ppermute | solution.py:214
  4.5 5.6 %collective-permute-start.1 = (f32[3,256]{1,0:T(4,128)S(1)}, f32[3,256]{1,0:T(4,128)S(1)}, u32[]{:S(2)}, u32[]{:S(2)}) collective-permute-start(f32[3,256]{1,0:T(4,128)S(1)} %bitcast.134), channel_id=1, source_target_pairs={{0,8},{4,12},{8,0},{12,4},{1,9},{5,13},{9,1},{13,5},{2,10},{6,14},... | collective-permute-start | bytes 9224 | tf_op jit(solution)/shard_map/ppermute | solution.py:214
  7.1 3.6 %collective-permute-start.2 = (f32[3,256]{1,0:T(4,128)S(1)}, f32[3,256]{1,0:T(4,128)S(1)}, u32[]{:S(2)}, u32[]{:S(2)}) collective-permute-start(f32[3,256]{1,0:T(4,128)S(1)} %bitcast.135), channel_id=1, source_target_pairs={{0,12},{4,0},{8,4},{12,8},{1,13},{5,1},{9,5},{13,9},{2,14},{6,2},{... | collective-permute-start | bytes 9224 | tf_op jit(solution)/shard_map/ppermute | solution.py:214
  12.1 1.0 %copy-start.2 = (bf16[1,640,256]{2,1,0:T(8,128)(2,1)S(1)}, bf16[1,640,256]{2,1,0:T(8,128)(2,1)}, u32[]{:S(2)}) copy-start(bf16[1,640,256]{2,1,0:T(8,128)(2,1)} %param.8) | copy-start | bytes 983044
  19.7 4.5 %copy-start = (s32[1,2049]{1,0:T(1,128)S(1)}, s32[1,2049]{1,0:T(1,128)}, u32[]{:S(2)}) copy-start(s32[1,2049]{1,0:T(1,128)} %param.9) | copy-start | bytes 24592
  19.7 28.6 %all-to-all-start = ((f32[4,2,256,128]{3,2,1,0:T(8,128)}), f32[4,2,256,128]{3,2,1,0:T(8,128)S(1)}, u32[]{:S(2)}, u32[]{:S(2)}) async-start(f32[4,2,256,128]{3,2,1,0:T(8,128)} %copy.46), calls=%async_computation | async-start | bytes 2097152 | tf_op jit(solution)/shard_map/all_to_all | solution.py:322
  52.4 1.2 %copy-start.1 = (s32[2,256]{1,0:T(2,128)S(1)}, s32[2,256]{1,0:T(2,128)}, u32[]{:S(2)}) copy-start(s32[2,256]{1,0:T(2,128)} %param.7) | copy-start | bytes 6148
  52.7 1.7 %collective-permute-start.3 = (f32[2,256,128]{1,2,0:T(8,128)S(1)}, f32[2,256,128]{1,2,0:T(8,128)S(1)}, u32[]{:S(2)}, u32[]{:S(2)}) collective-permute-start(f32[2,256,128]{1,2,0:T(8,128)S(1)} %slice.189), channel_id=1, source_target_pairs={{0,0},{4,12},{8,8},{12,4},{1,1},{5,13},{9,9},{13,5},{2,2},{6,14},{... | collective-permute-start | bytes 786440 | tf_op jit(solution)/shard_map/ppermute | solution.py:288
  53.7 2.4 %collective-permute-start.4 = (f32[2,260,128]{1,2,0:T(8,128)S(1)}, f32[2,260,128]{1,2,0:T(8,128)S(1)}, u32[]{:S(2)}, u32[]{:S(2)}) collective-permute-start(f32[2,260,128]{1,2,0:T(8,128)S(1)} %slice.195), channel_id=1, source_target_pairs={{0,0},{4,12},{8,8},{12,4},{1,1},{5,13},{9,9},{13,5},{2,2},{6,14},{... | collective-permute-start | bytes 798728 | tf_op jit(solution)/shard_map/ppermute | solution.py:288
  54.5 16.1 %collective-permute-start.5 = (bf16[2,256,256]{1,2,0:T(8,128)(2,1)S(1)}, bf16[2,256,256]{1,2,0:T(8,128)(2,1)S(1)}, u32[]{:S(2)}, u32[]{:S(2)}) collective-permute-start(bf16[2,256,256]{1,2,0:T(8,128)(2,1)S(1)} %pad_maximum_fusion.3), channel_id=1, source_target_pairs={{0,1},{1,0},{2,3},{3,2},{4,5},{5,4},{6,7},{7,6},{8,9},{9,8},{10,11... | collective-permute-start | bytes 786440 | tf_op jit(solution)/shard_map/ppermute | solution.py:144
  56.4 13.9 %collective-permute-start.6 = (bf16[2,260,256]{1,2,0:T(8,128)(2,1)S(1)}, bf16[2,260,256]{1,2,0:T(8,128)(2,1)S(1)}, u32[]{:S(2)}, u32[]{:S(2)}) collective-permute-start(bf16[2,260,256]{1,2,0:T(8,128)(2,1)S(1)} %pad_maximum_fusion.2), channel_id=1, source_target_pairs={{0,1},{1,0},{2,3},{3,2},{4,5},{5,4},{6,7},{7,6},{8,9},{9,8},{10,11... | collective-permute-start | bytes 798728 | tf_op jit(solution)/shard_map/ppermute | solution.py:144
  71.0 13.9 %collective-permute-start.7 = (f32[128,256]{1,0:T(8,128)S(1)}, f32[128,256]{1,0:T(8,128)S(1)}, u32[]{:S(2)}, u32[]{:S(2)}) collective-permute-start(f32[128,256]{1,0:T(8,128)S(1)} %get-tuple-element.29), channel_id=1, source_target_pairs={{0,4},{4,8},{8,12},{12,0},{1,5},{5,9},{9,13},{13,1},{2,6},{6,10},{... | collective-permute-start | bytes 393224 | tf_op jit(solution)/shard_map/ppermute | solution.py:356
  79.2 9.9 %collective-permute-start.8 = (f32[128,256]{1,0:T(8,128)S(1)}, f32[128,256]{1,0:T(8,128)S(1)}, u32[]{:S(2)}, u32[]{:S(2)}) collective-permute-start(f32[128,256]{1,0:T(8,128)S(1)} %get-tuple-element.30), channel_id=1, source_target_pairs={{0,8},{4,12},{8,0},{12,4},{1,9},{5,13},{9,1},{13,5},{2,10},{6,14},... | collective-permute-start | bytes 393224 | tf_op jit(solution)/shard_map/ppermute | solution.py:356
  82.1 7.0 %collective-permute-start.9 = (f32[128,256]{1,0:T(8,128)S(1)}, f32[128,256]{1,0:T(8,128)S(1)}, u32[]{:S(2)}, u32[]{:S(2)}) collective-permute-start(f32[128,256]{1,0:T(8,128)S(1)} %get-tuple-element.31), channel_id=1, source_target_pairs={{0,12},{4,0},{8,4},{12,8},{1,13},{5,1},{9,5},{13,9},{2,14},{6,2},{... | collective-permute-start | bytes 393224 | tf_op jit(solution)/shard_map/ppermute | solution.py:356
  89.1 1.4 %collective-permute-start.10 = (f32[128,256]{1,0:T(8,128)S(1)}, f32[128,256]{1,0:T(8,128)S(1)}, u32[]{:S(2)}, u32[]{:S(2)}) collective-permute-start(f32[128,256]{1,0:T(8,128)S(1)} %fusion.67), channel_id=1, source_target_pairs={{0,2},{2,0},{1,3},{3,1},{4,6},{6,4},{5,7},{7,5},{8,10},{10,8},{9,1... | collective-permute-start | bytes 393224 | tf_op jit(solution)/shard_map/ppermute | solution.py:154

commit v20 on v17

--- a/solution.py
+++ b/solution.py
@@ -54,7 +54,8 @@
     masked = jnp.where(allowed, coeffs, jnp.zeros_like(coeffs))
     latitude = jnp.dot(basis_rows, masked, preferred_element_type=jnp.float32)
     lon_phase = longit[:, None] * jnp.abs(orders).astype(jnp.float32)[None, :]
-    lon_wave = jnp.where(orders[None, :] >= 0, jnp.cos(lon_phase), jnp.sin(lon_phase))
+    quarter = jnp.where(orders >= 0, 0.0, 0.5 * math.pi).astype(jnp.float32)
+    lon_wave = jnp.cos(lon_phase - quarter[None, :])
     return latitude * lon_wave * keep_rows[:, None]
 
 

time: 88.5 us -> 88.2 us (level)
  no operation moved by 1% of the time
where the time goes in v20:
time: 88.2 us; the launch traced here: 87.9 us
  waiting for transfers between devices  40.4 us (46%)
  starting transfers between devices  25.9 us (29%)
  other arithmetic  9.39 us (11%)
  matrix products  6.95 us (8%)
  local copies, waits for them, and re-layouts  4.62 us (5%)
    all_to_all x1, waiting for transfers between devices, body(): gathered = lax.all_to_all(twisted, 'tm', 0, 0, tiled=True)  22.7 us
    ppermute x3, starting transfers between devices, body(): lax.ppermute(block((position + shift) % devices_tm), 'tm', pairs)  12.1 us
    ppermute x1, waiting for transfers between devices, panel_spectra(): blocks.append(lax.ppermute(spectra, 'panel', pairs))  9.56 us
    ppermute x3, starting transfers between devices, swap_blocks(): arrived.append(lax.ppermute(outgoing, axis, pairs))  7.01 us
    ppermute x3, waiting for transfers between devices, body(): lax.ppermute(block((position + shift) % devices_tm), 'tm', pairs)  6.28 us
    all_to_all x1, starting transfers between devices, body(): gathered = lax.all_to_all(twisted, 'tm', 0, 0, tiled=True)  4.42 us
    dot_general x1, matrix products, synthesize(): latitude = jnp.dot(basis_rows, masked, preferred_element_type=jnp.float32)  4.04 us
    dot_general x2, matrix products, mat(): lax.dot_general(table, value, dims, precision=lax.Precision.HIGH, preferr...  1.78 us
  transfers between devices with their start and end apart: 10, of which 7 were waited for; matrix products, arithmetic and copies ran while one was open for 5% of the time, Pallas kernels for 0%

profile of v20, /device:TPU:0, one launch (start us, length us, event | category | flops | bytes accessed | tf_op | source)
XLA Modules:
  0.0 87.9 jit_solution(2934120221714358416)
XLA Ops:
  0.0 0.7 concatenate.44
  0.7 0.7 convert_element_type.120
  1.5 3.1 %collective-permute-start = (f32[3,256]{1,0:T(4,128)S(1)}, f32[3,256]{1,0:T(4,128)S(1)}, u32[]{:S(2)}, u32[]{:S(2)}) collective-permute-start(f32[3,256]{1,0:T(4,128)S(1)} %bitcast.122), channel_id=1, source_target_pairs={{0,4},{4,8},{8,12},{12,0},{1,5},{5,9},{9,13},{13,1},{2,6},{6,10},{... | collective-permute-start | bytes 9224 | tf_op jit(solution)/shard_map/ppermute | solution.py:215
  4.5 2.6 %collective-permute-start.1 = (f32[3,256]{1,0:T(4,128)S(1)}, f32[3,256]{1,0:T(4,128)S(1)}, u32[]{:S(2)}, u32[]{:S(2)}) collective-permute-start(f32[3,256]{1,0:T(4,128)S(1)} %bitcast.123), channel_id=1, source_target_pairs={{0,8},{4,12},{8,0},{12,4},{1,9},{5,13},{9,1},{13,5},{2,10},{6,14},... | collective-permute-start | bytes 9224 | tf_op jit(solution)/shard_map/ppermute | solution.py:215
  7.1 1.3 %collective-permute-start.2 = (f32[3,256]{1,0:T(4,128)S(1)}, f32[3,256]{1,0:T(4,128)S(1)}, u32[]{:S(2)}, u32[]{:S(2)}) collective-permute-start(f32[3,256]{1,0:T(4,128)S(1)} %bitcast.124), channel_id=1, source_target_pairs={{0,12},{4,0},{8,4},{12,8},{1,13},{5,1},{9,5},{13,9},{2,14},{6,2},{... | collective-permute-start | bytes 9224 | tf_op jit(solution)/shard_map/ppermute | solution.py:215
  8.5 0.8 rsqrt_multiply_fusion
  9.2 0.8 fusion.100
  12.1 0.7 fusion.5
  13.1 4.0 %fusion = f32[1024,256]{1,0:T(8,128)S(1)} fusion(bf16[1024,320]{0,1:T(8,128)(2,1)S(1)} %get-tuple-element.10, bf16[1024,320]{0,1:T(8,128)(2,1)S(1)} %get-tuple-element.9, f32[1024]{0:T(1024)S(1)} %bitcast.126, f32[256]{0:T(256)S(1)} %bitcast.129, f32[256]{0:T(256)S(1)} %bitcast.131, f32[1024]{0:T(1024)S(1)} %bitcast.125, ...), kind=kOutput, calls=%fused_computation.5 | convolution fusion | flops 339542016 | bytes 2700800 | tf_op jit(solution)/shard_map/dot_general | solution.py:55
  18.3 1.1 %copy.19 = f32[4,2,256,128]{3,2,1,0:T(8,128)} copy(f32[4,2,256,128]{3,2,0,1:T(8,128)S(1)} %pad_maximum_fusion) | data formatting | bytes 2097152 | tf_op jit(solution)/shard_map/stack | solution.py:234
  19.3 4.4 %all-to-all-start = ((f32[4,2,256,128]{3,2,1,0:T(8,128)}), f32[4,2,256,128]{3,2,1,0:T(8,128)S(1)}, u32[]{:S(2)}, u32[]{:S(2)}) async-start(f32[4,2,256,128]{3,2,1,0:T(8,128)} %copy.19), calls=%async_computation | async-start | bytes 2097152 | tf_op jit(solution)/shard_map/all_to_all | solution.py:323
  25.1 22.7 %all-to-all-done = f32[4,2,256,128]{3,2,1,0:T(8,128)S(1)} async-done(((f32[4,2,256,128]{3,2,1,0:T(8,128)}), f32[4,2,256,128]{3,2,1,0:T(8,128)S(1)}, u32[]{:S(2)}, u32[]{:S(2)}) %all-to-all-start) | async-done | bytes 1048608 | tf_op jit(solution)/shard_map/all_to_all | solution.py:323
  48.5 0.9 %fusion.19 = f32[516,4,128]{2,0,1:T(8,128)S(1)} fusion(f32[4,256,128]{2,1,0:T(8,128)S(1)} %get-tuple-element.6, f32[4,256,128]{2,1,0:T(8,128)S(1)} %get-tuple-element.5, f32[129,256]{1,0:T(8,128)S(1)} %get-tuple-element.54, f32[129,256]{1,0:T(8,128)S(1)} %get-tuple-element.53, f32[129,256]{1,0:T(8,128)S(1)} %get-tuple-element.63, ...), kind=kOutput, calls=%fused_computation.53 | convolution fusion | flops 406588416 | bytes 2641920 | tf_op jit(solution)/shard_map/dot_general | solution.py:259
  49.4 0.9 %fusion.23 = f32[516,4,128]{2,0,1:T(8,128)S(1)} fusion(f32[4,256,128]{2,1,0:T(8,128)S(1)} %get-tuple-element.5, f32[4,256,128]{2,1,0:T(8,128)S(1)} %get-tuple-element.6, f32[129,256]{1,0:T(8,128)S(1)} %get-tuple-element.54, f32[129,256]{1,0:T(8,128)S(1)} %get-tuple-element.53, f32[129,256]{1,0:T(8,128)S(1)} %get-tuple-element.63, ...), kind=kOutput, calls=%fused_computation.57 | convolution fusion | flops 406588416 | bytes 2641920 | tf_op jit(solution)/shard_map/dot_general | solution.py:259
  51.8 0.7 collective-permute-start.3
  53.6 1.6 %collective-permute-start.4 = (bf16[2,516,256]{2,0,1:T(2,128)(2,1)S(1)}, bf16[2,516,256]{2,0,1:T(2,128)(2,1)S(1)}, u32[]{:S(2)}, u32[]{:S(2)}) collective-permute-start(bf16[2,516,256]{2,0,1:T(2,128)(2,1)S(1)} %copy.26), channel_id=1, source_target_pairs={{0,1},{1,0},{2,3},{3,2},{4,5},{5,4},{6,7},{7,6},{8,9},{9,8},{10,11... | collective-permute-start | bytes 1585160 | tf_op jit(solution)/shard_map/ppermute | solution.py:145
  57.1 9.6 %collective-permute-done.4 = bf16[2,516,256]{2,0,1:T(2,128)(2,1)S(1)} collective-permute-done((bf16[2,516,256]{2,0,1:T(2,128)(2,1)S(1)}, bf16[2,516,256]{2,0,1:T(2,128)(2,1)S(1)}, u32[]{:S(2)}, u32[]{:S(2)}) %collective-permute-start.4) | collective-permute-done | bytes 528416 | tf_op jit(solution)/shard_map/ppermute | solution.py:145
  67.3 9.7 %collective-permute-start.5 = (f32[128,256]{1,0:T(8,128)S(1)}, f32[128,256]{1,0:T(8,128)S(1)}, u32[]{:S(2)}, u32[]{:S(2)}) collective-permute-start(f32[128,256]{1,0:T(8,128)S(1)} %get-tuple-element.27), channel_id=1, source_target_pairs={{0,4},{4,8},{8,12},{12,0},{1,5},{5,9},{9,13},{13,1},{2,6},{6,10},{... | collective-permute-start | bytes 393224 | tf_op jit(solution)/shard_map/ppermute | solution.py:351
  77.0 2.4 %collective-permute-start.6 = (f32[128,256]{1,0:T(8,128)S(1)}, f32[128,256]{1,0:T(8,128)S(1)}, u32[]{:S(2)}, u32[]{:S(2)}) collective-permute-start(f32[128,256]{1,0:T(8,128)S(1)} %get-tuple-element.28), channel_id=1, source_target_pairs={{0,8},{4,12},{8,0},{12,4},{1,9},{5,13},{9,1},{13,5},{2,10},{6,14},... | collective-permute-start | bytes 393224 | tf_op jit(solution)/shard_map/ppermute | solution.py:351
  79.5 2.4 %collective-permute-done.5 = f32[128,256]{1,0:T(8,128)S(1)} collective-permute-done((f32[128,256]{1,0:T(8,128)S(1)}, f32[128,256]{1,0:T(8,128)S(1)}, u32[]{:S(2)}, u32[]{:S(2)}) %collective-permute-start.5) | collective-permute-done | bytes 131104 | tf_op jit(solution)/shard_map/ppermute | solution.py:351
  81.9 2.9 %collective-permute-done.6 = f32[128,256]{1,0:T(8,128)S(1)} collective-permute-done((f32[128,256]{1,0:T(8,128)S(1)}, f32[128,256]{1,0:T(8,128)S(1)}, u32[]{:S(2)}, u32[]{:S(2)}) %collective-permute-start.6) | collective-permute-done | bytes 131104 | tf_op jit(solution)/shard_map/ppermute | solution.py:351
  84.8 1.0 %collective-permute-done.7 = f32[128,256]{1,0:T(8,128)S(1)} collective-permute-done((f32[128,256]{1,0:T(8,128)S(1)}, f32[128,256]{1,0:T(8,128)S(1)}, u32[]{:S(2)}, u32[]{:S(2)}) %collective-permute-start.7) | collective-permute-done | bytes 131104 | tf_op jit(solution)/shard_map/ppermute | solution.py:351
  85.9 1.3 %collective-permute-done.8 = f32[128,256]{1,0:T(8,128)S(1)} collective-permute-done((f32[128,256]{1,0:T(8,128)S(1)}, f32[128,256]{1,0:T(8,128)S(1)}, u32[]{:S(2)}, u32[]{:S(2)}) %collective-permute-start.8) | collective-permute-done | bytes 131104 | tf_op jit(solution)/shard_map/ppermute | solution.py:155
  87.2 0.7 add.307
  (78 shorter events, 10.4 us)
Async XLA Ops:
  1.5 8.7 %collective-permute-start = (f32[3,256]{1,0:T(4,128)S(1)}, f32[3,256]{1,0:T(4,128)S(1)}, u32[]{:S(2)}, u32[]{:S(2)}) collective-permute-start(f32[3,256]{1,0:T(4,128)S(1)} %bitcast.122), channel_id=1, source_target_pairs={{0,4},{4,8},{8,12},{12,0},{1,5},{5,9},{9,13},{13,1},{2,6},{6,10},{... | collective-permute-start | bytes 9224 | tf_op jit(solution)/shard_map/ppermute | solution.py:215
  4.5 5.7 %collective-permute-start.1 = (f32[3,256]{1,0:T(4,128)S(1)}, f32[3,256]{1,0:T(4,128)S(1)}, u32[]{:S(2)}, u32[]{:S(2)}) collective-permute-start(f32[3,256]{1,0:T(4,128)S(1)} %bitcast.123), channel_id=1, source_target_pairs={{0,8},{4,12},{8,0},{12,4},{1,9},{5,13},{9,1},{13,5},{2,10},{6,14},... | collective-permute-start | bytes 9224 | tf_op jit(solution)/shard_map/ppermute | solution.py:215
  7.1 3.6 %collective-permute-start.2 = (f32[3,256]{1,0:T(4,128)S(1)}, f32[3,256]{1,0:T(4,128)S(1)}, u32[]{:S(2)}, u32[]{:S(2)}) collective-permute-start(f32[3,256]{1,0:T(4,128)S(1)} %bitcast.124), channel_id=1, source_target_pairs={{0,12},{4,0},{8,4},{12,8},{1,13},{5,1},{9,5},{13,9},{2,14},{6,2},{... | collective-permute-start | bytes 9224 | tf_op jit(solution)/shard_map/ppermute | solution.py:215
  12.1 1.0 %copy-start.1 = (bf16[1,640,256]{2,1,0:T(8,128)(2,1)S(1)}, bf16[1,640,256]{2,1,0:T(8,128)(2,1)}, u32[]{:S(2)}) copy-start(bf16[1,640,256]{2,1,0:T(8,128)(2,1)} %param.8) | copy-start | bytes 983044
  19.3 28.4 %all-to-all-start = ((f32[4,2,256,128]{3,2,1,0:T(8,128)}), f32[4,2,256,128]{3,2,1,0:T(8,128)S(1)}, u32[]{:S(2)}, u32[]{:S(2)}) async-start(f32[4,2,256,128]{3,2,1,0:T(8,128)} %copy.19), calls=%async_computation | async-start | bytes 2097152 | tf_op jit(solution)/shard_map/all_to_all | solution.py:323
  51.8 0.7 collective-permute-start.3
  53.1 2.1 %copy-start = (s32[1,2049]{1,0:T(1,128)S(1)}, s32[1,2049]{1,0:T(1,128)}, u32[]{:S(2)}) copy-start(s32[1,2049]{1,0:T(1,128)} %param.9) | copy-start | bytes 24592
  53.6 13.0 %collective-permute-start.4 = (bf16[2,516,256]{2,0,1:T(2,128)(2,1)S(1)}, bf16[2,516,256]{2,0,1:T(2,128)(2,1)S(1)}, u32[]{:S(2)}, u32[]{:S(2)}) collective-permute-start(bf16[2,516,256]{2,0,1:T(2,128)(2,1)S(1)} %copy.26), channel_id=1, source_target_pairs={{0,1},{1,0},{2,3},{3,2},{4,5},{5,4},{6,7},{7,6},{8,9},{9,8},{10,11... | collective-permute-start | bytes 1585160 | tf_op jit(solution)/shard_map/ppermute | solution.py:145
  67.3 14.5 %collective-permute-start.5 = (f32[128,256]{1,0:T(8,128)S(1)}, f32[128,256]{1,0:T(8,128)S(1)}, u32[]{:S(2)}, u32[]{:S(2)}) collective-permute-start(f32[128,256]{1,0:T(8,128)S(1)} %get-tuple-element.27), channel_id=1, source_target_pairs={{0,4},{4,8},{8,12},{12,0},{1,5},{5,9},{9,13},{13,1},{2,6},{6,10},{... | collective-permute-start | bytes 393224 | tf_op jit(solution)/shard_map/ppermute | solution.py:351
  77.0 7.7 %collective-permute-start.6 = (f32[128,256]{1,0:T(8,128)S(1)}, f32[128,256]{1,0:T(8,128)S(1)}, u32[]{:S(2)}, u32[]{:S(2)}) collective-permute-start(f32[128,256]{1,0:T(8,128)S(1)} %get-tuple-element.28), channel_id=1, source_target_pairs={{0,8},{4,12},{8,0},{12,4},{1,9},{5,13},{9,1},{13,5},{2,10},{6,14},... | collective-permute-start | bytes 393224 | tf_op jit(solution)/shard_map/ppermute | solution.py:351
  79.4 6.4 %collective-permute-start.7 = (f32[128,256]{1,0:T(8,128)S(1)}, f32[128,256]{1,0:T(8,128)S(1)}, u32[]{:S(2)}, u32[]{:S(2)}) collective-permute-start(f32[128,256]{1,0:T(8,128)S(1)} %get-tuple-element.29), channel_id=1, source_target_pairs={{0,12},{4,0},{8,4},{12,8},{1,13},{5,1},{9,5},{13,9},{2,14},{6,2},{... | collective-permute-start | bytes 393224 | tf_op jit(solution)/shard_map/ppermute | solution.py:351
  85.8 1.4 %collective-permute-start.8 = (f32[128,256]{1,0:T(8,128)S(1)}, f32[128,256]{1,0:T(8,128)S(1)}, u32[]{:S(2)}, u32[]{:S(2)}) collective-permute-start(f32[128,256]{1,0:T(8,128)S(1)} %fusion.59), channel_id=1, source_target_pairs={{0,2},{2,0},{1,3},{3,1},{4,6},{6,4},{5,7},{7,5},{8,10},{10,8},{9,1... | collective-permute-start | bytes 393224 | tf_op jit(solution)/shard_map/ppermute | solution.py:155

commit v21 on v18

--- a/solution.py
+++ b/solution.py
@@ -54,7 +54,8 @@
     masked = jnp.where(allowed, coeffs, jnp.zeros_like(coeffs))
     latitude = jnp.dot(basis_rows, masked, preferred_element_type=jnp.float32)
     lon_phase = longit[:, None] * jnp.abs(orders).astype(jnp.float32)[None, :]
-    lon_wave = jnp.where(orders[None, :] >= 0, jnp.cos(lon_phase), jnp.sin(lon_phase))
+    quarter = jnp.where(orders >= 0, 0.0, 0.5 * math.pi).astype(jnp.float32)
+    lon_wave = jnp.cos(lon_phase - quarter[None, :])
     return latitude * lon_wave * keep_rows[:, None]
 
 

time: 88.5 us -> 88.2 us (level)
  no operation moved by 1% of the time
where the time goes in v21:
time: 88.2 us; the launch traced here: 87.8 us
  waiting for transfers between devices  40.4 us (46%)
  starting transfers between devices  25.9 us (29%)
  other arithmetic  10.4 us (12%)
  matrix products  6.97 us (8%)
  local copies, waits for them, and re-layouts  3.56 us (4%)
    all_to_all x1, waiting for transfers between devices, body(): gathered = lax.all_to_all(twisted, 'tm', 0, 0, tiled=True)  22.7 us
    ppermute x3, starting transfers between devices, body(): lax.ppermute(block((position + shift) % devices_tm), 'tm', pairs)  12.2 us
    ppermute x1, waiting for transfers between devices, panel_spectra(): blocks.append(lax.ppermute(spectra, 'panel', pairs))  9.57 us
    ppermute x3, starting transfers between devices, swap_blocks(): arrived.append(lax.ppermute(outgoing, axis, pairs))  7.01 us
    ppermute x3, waiting for transfers between devices, body(): lax.ppermute(block((position + shift) % devices_tm), 'tm', pairs)  6.28 us
    all_to_all x1, starting transfers between devices, body(): gathered = lax.all_to_all(twisted, 'tm', 0, 0, tiled=True)  4.42 us
    dot_general x1, matrix products, synthesize(): latitude = jnp.dot(basis_rows, masked, preferred_element_type=jnp.float32)  4.04 us
    dot_general x2, matrix products, mat(): lax.dot_general(table, value, dims, precision=lax.Precision.HIGH, preferr...  1.8 us
  transfers between devices with their start and end apart: 10, of which 7 were waited for; matrix products, arithmetic and copies ran while one was open for 5% of the time, Pallas kernels for 0%

profile of v21, /device:TPU:0, one launch (start us, length us, event | category | flops | bytes accessed | tf_op | source)
XLA Modules:
  0.0 87.8 jit_solution(5060890392197260079)
XLA Ops:
  0.0 0.7 concatenate.47
  0.7 0.7 convert_element_type.120
  1.5 3.1 %collective-permute-start = (f32[3,256]{1,0:T(4,128)S(1)}, f32[3,256]{1,0:T(4,128)S(1)}, u32[]{:S(2)}, u32[]{:S(2)}) collective-permute-start(f32[3,256]{1,0:T(4,128)S(1)} %bitcast.104), channel_id=1, source_target_pairs={{0,4},{4,8},{8,12},{12,0},{1,5},{5,9},{9,13},{13,1},{2,6},{6,10},{... | collective-permute-start | bytes 9224 | tf_op jit(solution)/shard_map/ppermute | solution.py:215
  4.5 2.6 %collective-permute-start.1 = (f32[3,256]{1,0:T(4,128)S(1)}, f32[3,256]{1,0:T(4,128)S(1)}, u32[]{:S(2)}, u32[]{:S(2)}) collective-permute-start(f32[3,256]{1,0:T(4,128)S(1)} %bitcast.105), channel_id=1, source_target_pairs={{0,8},{4,12},{8,0},{12,4},{1,9},{5,13},{9,1},{13,5},{2,10},{6,14},... | collective-permute-start | bytes 9224 | tf_op jit(solution)/shard_map/ppermute | solution.py:215
  7.1 1.3 %collective-permute-start.2 = (f32[3,256]{1,0:T(4,128)S(1)}, f32[3,256]{1,0:T(4,128)S(1)}, u32[]{:S(2)}, u32[]{:S(2)}) collective-permute-start(f32[3,256]{1,0:T(4,128)S(1)} %bitcast.106), channel_id=1, source_target_pairs={{0,12},{4,0},{8,4},{12,8},{1,13},{5,1},{9,5},{13,9},{2,14},{6,2},{... | collective-permute-start | bytes 9224 | tf_op jit(solution)/shard_map/ppermute | solution.py:215
  8.5 0.8 rsqrt_multiply_fusion
  9.2 0.8 fusion.99
  12.1 0.7 fusion.5
  13.1 4.0 %fusion = f32[1024,256]{1,0:T(8,128)S(1)} fusion(bf16[1024,320]{0,1:T(8,128)(2,1)S(1)} %get-tuple-element.10, bf16[1024,320]{0,1:T(8,128)(2,1)S(1)} %get-tuple-element.9, f32[1024]{0:T(1024)S(1)} %bitcast.108, f32[256]{0:T(256)S(1)} %bitcast.111, f32[256]{0:T(256)S(1)} %bitcast.113, f32[1024]{0:T(1024)S(1)} %bitcast.107, ...), kind=kOutput, calls=%fused_computation.5 | convolution fusion | flops 339542016 | bytes 2700800 | tf_op jit(solution)/shard_map/dot_general | solution.py:55
  18.2 1.1 %pad_maximum_fusion = f32[4,256,256]{2,1,0:T(8,128)} fusion(f32[4,256,128]{2,1,0:T(8,128)S(1)} %get-tuple-element.16, f32[4,256,128]{2,1,0:T(8,128)S(1)} %get-tuple-element.15), kind=kLoop, calls=%fused_computation.21 | loop fusion | flops 262144 | bytes 2097152 | tf_op jit(solution)/shard_map/concatenate | solution.py:234
  19.3 4.4 %all-to-all-start = ((f32[4,256,256]{2,1,0:T(8,128)}), f32[4,256,256]{2,1,0:T(8,128)S(1)}, u32[]{:S(2)}, u32[]{:S(2)}) async-start(f32[4,256,256]{2,1,0:T(8,128)} %pad_maximum_fusion), calls=%async_computation | async-start | bytes 2097152 | tf_op jit(solution)/shard_map/all_to_all | solution.py:324
  25.0 22.7 %all-to-all-done = f32[4,256,256]{2,1,0:T(8,128)S(1)} async-done(((f32[4,256,256]{2,1,0:T(8,128)}), f32[4,256,256]{2,1,0:T(8,128)S(1)}, u32[]{:S(2)}, u32[]{:S(2)}) %all-to-all-start) | async-done | bytes 1048608 | tf_op jit(solution)/shard_map/all_to_all | solution.py:324
  48.4 0.9 %fusion.17 = f32[516,4,128]{2,0,1:T(8,128)S(1)} fusion(f32[4,256,128]{2,1,0:T(8,128)S(1)} %get-tuple-element.6, f32[4,256,128]{2,1,0:T(8,128)S(1)} %get-tuple-element.5, f32[129,256]{1,0:T(8,128)S(1)} %get-tuple-element.54, f32[129,256]{1,0:T(8,128)S(1)} %get-tuple-element.53, f32[129,256]{1,0:T(8,128)S(1)} %get-tuple-element.63, ...), kind=kOutput, calls=%fused_computation.45 | convolution fusion | flops 406588416 | bytes 2641920 | tf_op jit(solution)/shard_map/dot_general | solution.py:260
  49.3 0.9 %fusion.21 = f32[516,4,128]{2,0,1:T(8,128)S(1)} fusion(f32[4,256,128]{2,1,0:T(8,128)S(1)} %get-tuple-element.5, f32[4,256,128]{2,1,0:T(8,128)S(1)} %get-tuple-element.6, f32[129,256]{1,0:T(8,128)S(1)} %get-tuple-element.54, f32[129,256]{1,0:T(8,128)S(1)} %get-tuple-element.53, f32[129,256]{1,0:T(8,128)S(1)} %get-tuple-element.63, ...), kind=kOutput, calls=%fused_computation.49 | convolution fusion | flops 406588416 | bytes 2641920 | tf_op jit(solution)/shard_map/dot_general | solution.py:260
  51.7 0.7 collective-permute-start.3
  53.5 1.5 %collective-permute-start.4 = (bf16[2,516,256]{2,0,1:T(2,128)(2,1)S(1)}, bf16[2,516,256]{2,0,1:T(2,128)(2,1)S(1)}, u32[]{:S(2)}, u32[]{:S(2)}) collective-permute-start(bf16[2,516,256]{2,0,1:T(2,128)(2,1)S(1)} %copy.25), channel_id=1, source_target_pairs={{0,1},{1,0},{2,3},{3,2},{4,5},{5,4},{6,7},{7,6},{8,9},{9,8},{10,11... | collective-permute-start | bytes 1585160 | tf_op jit(solution)/shard_map/ppermute | solution.py:145
  57.0 9.6 %collective-permute-done.4 = bf16[2,516,256]{2,0,1:T(2,128)(2,1)S(1)} collective-permute-done((bf16[2,516,256]{2,0,1:T(2,128)(2,1)S(1)}, bf16[2,516,256]{2,0,1:T(2,128)(2,1)S(1)}, u32[]{:S(2)}, u32[]{:S(2)}) %collective-permute-start.4) | collective-permute-done | bytes 528416 | tf_op jit(solution)/shard_map/ppermute | solution.py:145
  67.2 9.7 %collective-permute-start.5 = (f32[128,256]{1,0:T(8,128)S(1)}, f32[128,256]{1,0:T(8,128)S(1)}, u32[]{:S(2)}, u32[]{:S(2)}) collective-permute-start(f32[128,256]{1,0:T(8,128)S(1)} %get-tuple-element.27), channel_id=1, source_target_pairs={{0,4},{4,8},{8,12},{12,0},{1,5},{5,9},{9,13},{13,1},{2,6},{6,10},{... | collective-permute-start | bytes 393224 | tf_op jit(solution)/shard_map/ppermute | solution.py:352
  77.0 2.3 %collective-permute-start.6 = (f32[128,256]{1,0:T(8,128)S(1)}, f32[128,256]{1,0:T(8,128)S(1)}, u32[]{:S(2)}, u32[]{:S(2)}) collective-permute-start(f32[128,256]{1,0:T(8,128)S(1)} %get-tuple-element.28), channel_id=1, source_target_pairs={{0,8},{4,12},{8,0},{12,4},{1,9},{5,13},{9,1},{13,5},{2,10},{6,14},... | collective-permute-start | bytes 393224 | tf_op jit(solution)/shard_map/ppermute | solution.py:352
  79.4 2.4 %collective-permute-done.5 = f32[128,256]{1,0:T(8,128)S(1)} collective-permute-done((f32[128,256]{1,0:T(8,128)S(1)}, f32[128,256]{1,0:T(8,128)S(1)}, u32[]{:S(2)}, u32[]{:S(2)}) %collective-permute-start.5) | collective-permute-done | bytes 131104 | tf_op jit(solution)/shard_map/ppermute | solution.py:352
  81.8 2.9 %collective-permute-done.6 = f32[128,256]{1,0:T(8,128)S(1)} collective-permute-done((f32[128,256]{1,0:T(8,128)S(1)}, f32[128,256]{1,0:T(8,128)S(1)}, u32[]{:S(2)}, u32[]{:S(2)}) %collective-permute-start.6) | collective-permute-done | bytes 131104 | tf_op jit(solution)/shard_map/ppermute | solution.py:352
  84.7 1.0 %collective-permute-done.7 = f32[128,256]{1,0:T(8,128)S(1)} collective-permute-done((f32[128,256]{1,0:T(8,128)S(1)}, f32[128,256]{1,0:T(8,128)S(1)}, u32[]{:S(2)}, u32[]{:S(2)}) %collective-permute-start.7) | collective-permute-done | bytes 131104 | tf_op jit(solution)/shard_map/ppermute | solution.py:352
  85.8 1.3 %collective-permute-done.8 = f32[128,256]{1,0:T(8,128)S(1)} collective-permute-done((f32[128,256]{1,0:T(8,128)S(1)}, f32[128,256]{1,0:T(8,128)S(1)}, u32[]{:S(2)}, u32[]{:S(2)}) %collective-permute-start.8) | collective-permute-done | bytes 131104 | tf_op jit(solution)/shard_map/ppermute | solution.py:155
  87.1 0.7 add.300
  (77 shorter events, 10.4 us)
Async XLA Ops:
  1.5 8.7 %collective-permute-start = (f32[3,256]{1,0:T(4,128)S(1)}, f32[3,256]{1,0:T(4,128)S(1)}, u32[]{:S(2)}, u32[]{:S(2)}) collective-permute-start(f32[3,256]{1,0:T(4,128)S(1)} %bitcast.104), channel_id=1, source_target_pairs={{0,4},{4,8},{8,12},{12,0},{1,5},{5,9},{9,13},{13,1},{2,6},{6,10},{... | collective-permute-start | bytes 9224 | tf_op jit(solution)/shard_map/ppermute | solution.py:215
  4.5 5.7 %collective-permute-start.1 = (f32[3,256]{1,0:T(4,128)S(1)}, f32[3,256]{1,0:T(4,128)S(1)}, u32[]{:S(2)}, u32[]{:S(2)}) collective-permute-start(f32[3,256]{1,0:T(4,128)S(1)} %bitcast.105), channel_id=1, source_target_pairs={{0,8},{4,12},{8,0},{12,4},{1,9},{5,13},{9,1},{13,5},{2,10},{6,14},... | collective-permute-start | bytes 9224 | tf_op jit(solution)/shard_map/ppermute | solution.py:215
  7.1 3.6 %collective-permute-start.2 = (f32[3,256]{1,0:T(4,128)S(1)}, f32[3,256]{1,0:T(4,128)S(1)}, u32[]{:S(2)}, u32[]{:S(2)}) collective-permute-start(f32[3,256]{1,0:T(4,128)S(1)} %bitcast.106), channel_id=1, source_target_pairs={{0,12},{4,0},{8,4},{12,8},{1,13},{5,1},{9,5},{13,9},{2,14},{6,2},{... | collective-permute-start | bytes 9224 | tf_op jit(solution)/shard_map/ppermute | solution.py:215
  12.1 1.0 %copy-start.1 = (bf16[1,640,256]{2,1,0:T(8,128)(2,1)S(1)}, bf16[1,640,256]{2,1,0:T(8,128)(2,1)}, u32[]{:S(2)}) copy-start(bf16[1,640,256]{2,1,0:T(8,128)(2,1)} %param.8) | copy-start | bytes 983044
  19.3 28.4 %all-to-all-start = ((f32[4,256,256]{2,1,0:T(8,128)}), f32[4,256,256]{2,1,0:T(8,128)S(1)}, u32[]{:S(2)}, u32[]{:S(2)}) async-start(f32[4,256,256]{2,1,0:T(8,128)} %pad_maximum_fusion), calls=%async_computation | async-start | bytes 2097152 | tf_op jit(solution)/shard_map/all_to_all | solution.py:324
  51.7 0.7 collective-permute-start.3
  53.1 2.0 %copy-start = (s32[1,2049]{1,0:T(1,128)S(1)}, s32[1,2049]{1,0:T(1,128)}, u32[]{:S(2)}) copy-start(s32[1,2049]{1,0:T(1,128)} %param.9) | copy-start | bytes 24592
  53.5 13.0 %collective-permute-start.4 = (bf16[2,516,256]{2,0,1:T(2,128)(2,1)S(1)}, bf16[2,516,256]{2,0,1:T(2,128)(2,1)S(1)}, u32[]{:S(2)}, u32[]{:S(2)}) collective-permute-start(bf16[2,516,256]{2,0,1:T(2,128)(2,1)S(1)} %copy.25), channel_id=1, source_target_pairs={{0,1},{1,0},{2,3},{3,2},{4,5},{5,4},{6,7},{7,6},{8,9},{9,8},{10,11... | collective-permute-start | bytes 1585160 | tf_op jit(solution)/shard_map/ppermute | solution.py:145
  67.2 14.6 %collective-permute-start.5 = (f32[128,256]{1,0:T(8,128)S(1)}, f32[128,256]{1,0:T(8,128)S(1)}, u32[]{:S(2)}, u32[]{:S(2)}) collective-permute-start(f32[128,256]{1,0:T(8,128)S(1)} %get-tuple-element.27), channel_id=1, source_target_pairs={{0,4},{4,8},{8,12},{12,0},{1,5},{5,9},{9,13},{13,1},{2,6},{6,10},{... | collective-permute-start | bytes 393224 | tf_op jit(solution)/shard_map/ppermute | solution.py:352
  77.0 7.8 %collective-permute-start.6 = (f32[128,256]{1,0:T(8,128)S(1)}, f32[128,256]{1,0:T(8,128)S(1)}, u32[]{:S(2)}, u32[]{:S(2)}) collective-permute-start(f32[128,256]{1,0:T(8,128)S(1)} %get-tuple-element.28), channel_id=1, source_target_pairs={{0,8},{4,12},{8,0},{12,4},{1,9},{5,13},{9,1},{13,5},{2,10},{6,14},... | collective-permute-start | bytes 393224 | tf_op jit(solution)/shard_map/ppermute | solution.py:352
  79.3 6.4 %collective-permute-start.7 = (f32[128,256]{1,0:T(8,128)S(1)}, f32[128,256]{1,0:T(8,128)S(1)}, u32[]{:S(2)}, u32[]{:S(2)}) collective-permute-start(f32[128,256]{1,0:T(8,128)S(1)} %get-tuple-element.29), channel_id=1, source_target_pairs={{0,12},{4,0},{8,4},{12,8},{1,13},{5,1},{9,5},{13,9},{2,14},{6,2},{... | collective-permute-start | bytes 393224 | tf_op jit(solution)/shard_map/ppermute | solution.py:352
  85.7 1.4 %collective-permute-start.8 = (f32[128,256]{1,0:T(8,128)S(1)}, f32[128,256]{1,0:T(8,128)S(1)}, u32[]{:S(2)}, u32[]{:S(2)}) collective-permute-start(f32[128,256]{1,0:T(8,128)S(1)} %fusion.57), channel_id=1, source_target_pairs={{0,2},{2,0},{1,3},{3,1},{4,6},{6,4},{5,7},{7,5},{8,10},{10,8},{9,1... | collective-permute-start | bytes 393224 | tf_op jit(solution)/shard_map/ppermute | solution.py:155

commit v22 on v17

--- a/solution.py
+++ b/solution.py
@@ -285,7 +285,10 @@
     shifted = jnp.concatenate([own[:, :1], far[:, :-1]], axis=1)
     outgoing = jnp.where(position == 0, shifted, far)
     pairs = [(src, (devices_tm - src) % devices_tm) for src in range(devices_tm)]
-    mirror = lax.ppermute(outgoing, "tm", pairs)
+    half = own.shape[1] - devices_tm
+    mirror = jnp.concatenate(
+        [lax.ppermute(outgoing[:, :half], "tm", pairs), shifted[:, half:]], axis=1
+    )
     own_real = own[0]
     own_imag = own[1]
     first_real = (own_real + mirror[0]) * 0.5

time: 88.5 us -> 87.8 us (level)
  no operation moved by 1% of the time
where the time goes in v22:
time: 87.8 us; the launch traced here: 87.5 us
  waiting for transfers between devices  40.5 us (46%)
  starting transfers between devices  25.8 us (29%)
  other arithmetic  9.04 us (10%)
  matrix products  7.29 us (8%)
  local copies, waits for them, and re-layouts  4.28 us (5%)
    all_to_all x1, waiting for transfers between devices, body(): gathered = lax.all_to_all(twisted, 'tm', 0, 0, tiled=True)  22.7 us
    ppermute x3, starting transfers between devices, body(): lax.ppermute(block((position + shift) % devices_tm), 'tm', pairs)  12 us
    ppermute x1, waiting for transfers between devices, panel_spectra(): blocks.append(lax.ppermute(spectra, 'panel', pairs))  9.55 us
    ppermute x3, starting transfers between devices, swap_blocks(): arrived.append(lax.ppermute(outgoing, axis, pairs))  7.01 us
    ppermute x3, waiting for transfers between devices, body(): lax.ppermute(block((position + shift) % devices_tm), 'tm', pairs)  6.28 us
    all_to_all x1, starting transfers between devices, body(): gathered = lax.all_to_all(twisted, 'tm', 0, 0, tiled=True)  4.41 us
    dot_general x1, matrix products, synthesize(): latitude = jnp.dot(basis_rows, masked, preferred_element_type=jnp.float32)  4.37 us
    dot_general x2, matrix products, mat(): lax.dot_general(table, value, dims, precision=lax.Precision.HIGH, preferr...  1.78 us
  transfers between devices with their start and end apart: 10, of which 7 were waited for; matrix products, arithmetic and copies ran while one was open for 5% of the time, Pallas kernels for 0%

profile of v22, /device:TPU:0, one launch (start us, length us, event | category | flops | bytes accessed | tf_op | source)
XLA Modules:
  0.0 87.5 jit_solution(9985097899365809648)
XLA Ops:
  0.0 0.7 concatenate.47
  0.7 0.7 convert_element_type.120
  1.5 3.1 %collective-permute-start = (f32[3,256]{1,0:T(4,128)S(1)}, f32[3,256]{1,0:T(4,128)S(1)}, u32[]{:S(2)}, u32[]{:S(2)}) collective-permute-start(f32[3,256]{1,0:T(4,128)S(1)} %bitcast.121), channel_id=1, source_target_pairs={{0,4},{4,8},{8,12},{12,0},{1,5},{5,9},{9,13},{13,1},{2,6},{6,10},{... | collective-permute-start | bytes 9224 | tf_op jit(solution)/shard_map/ppermute | solution.py:214
  4.5 2.6 %collective-permute-start.1 = (f32[3,256]{1,0:T(4,128)S(1)}, f32[3,256]{1,0:T(4,128)S(1)}, u32[]{:S(2)}, u32[]{:S(2)}) collective-permute-start(f32[3,256]{1,0:T(4,128)S(1)} %bitcast.122), channel_id=1, source_target_pairs={{0,8},{4,12},{8,0},{12,4},{1,9},{5,13},{9,1},{13,5},{2,10},{6,14},... | collective-permute-start | bytes 9224 | tf_op jit(solution)/shard_map/ppermute | solution.py:214
  7.1 1.3 %collective-permute-start.2 = (f32[3,256]{1,0:T(4,128)S(1)}, f32[3,256]{1,0:T(4,128)S(1)}, u32[]{:S(2)}, u32[]{:S(2)}) collective-permute-start(f32[3,256]{1,0:T(4,128)S(1)} %bitcast.123), channel_id=1, source_target_pairs={{0,12},{4,0},{8,4},{12,8},{1,13},{5,1},{9,5},{13,9},{2,14},{6,2},{... | collective-permute-start | bytes 9224 | tf_op jit(solution)/shard_map/ppermute | solution.py:214
  8.5 0.8 fusion.102
  9.3 0.7 compare_reduce_fusion
  12.1 0.7 fusion.5
  13.1 4.4 %fusion = f32[1024,256]{1,0:T(8,128)S(1)} fusion(bf16[1024,320]{0,1:T(8,128)(2,1)S(1)} %get-tuple-element.10, bf16[1024,320]{0,1:T(8,128)(2,1)S(1)} %get-tuple-element.9, f32[1024]{0:T(1024)S(1)} %bitcast.125, f32[256]{0:T(256)S(1)} %bitcast.128, f32[1024]{0:T(1024)S(1)} %bitcast.124, pred[256]{0:T(512)(128)(4,1)S(1)} %compare_reduce_fusion, ...), kind=kOutput, calls=%fused_computation.7 | convolution fusion | flops 339542016 | bytes 2700032 | tf_op jit(solution)/shard_map/dot_general | solution.py:55
  18.6 1.0 %copy.20 = f32[4,2,256,128]{3,2,1,0:T(8,128)} copy(f32[4,2,256,128]{3,2,0,1:T(8,128)S(1)} %pad_maximum_fusion) | data formatting | bytes 2097152 | tf_op jit(solution)/shard_map/stack | solution.py:233
  19.7 4.4 %all-to-all-start = ((f32[4,2,256,128]{3,2,1,0:T(8,128)}), f32[4,2,256,128]{3,2,1,0:T(8,128)S(1)}, u32[]{:S(2)}, u32[]{:S(2)}) async-start(f32[4,2,256,128]{3,2,1,0:T(8,128)} %copy.20), calls=%async_computation | async-start | bytes 2097152 | tf_op jit(solution)/shard_map/all_to_all | solution.py:325
  25.4 22.7 %all-to-all-done = f32[4,2,256,128]{3,2,1,0:T(8,128)S(1)} async-done(((f32[4,2,256,128]{3,2,1,0:T(8,128)}), f32[4,2,256,128]{3,2,1,0:T(8,128)S(1)}, u32[]{:S(2)}, u32[]{:S(2)}) %all-to-all-start) | async-done | bytes 1048608 | tf_op jit(solution)/shard_map/all_to_all | solution.py:325
  48.8 0.9 %fusion.21 = f32[516,4,128]{2,0,1:T(8,128)S(1)} fusion(f32[4,256,128]{2,1,0:T(8,128)S(1)} %get-tuple-element.6, f32[4,256,128]{2,1,0:T(8,128)S(1)} %get-tuple-element.5, f32[129,256]{1,0:T(8,128)S(1)} %get-tuple-element.52, f32[129,256]{1,0:T(8,128)S(1)} %get-tuple-element.51, f32[129,256]{1,0:T(8,128)S(1)} %get-tuple-element.61, ...), kind=kOutput, calls=%fused_computation.63 | convolution fusion | flops 406588416 | bytes 2641920 | tf_op jit(solution)/shard_map/dot_general | solution.py:258
  49.7 0.9 %fusion.25 = f32[516,4,128]{2,0,1:T(8,128)S(1)} fusion(f32[4,256,128]{2,1,0:T(8,128)S(1)} %get-tuple-element.5, f32[4,256,128]{2,1,0:T(8,128)S(1)} %get-tuple-element.6, f32[129,256]{1,0:T(8,128)S(1)} %get-tuple-element.52, f32[129,256]{1,0:T(8,128)S(1)} %get-tuple-element.51, f32[129,256]{1,0:T(8,128)S(1)} %get-tuple-element.61, ...), kind=kOutput, calls=%fused_computation.67 | convolution fusion | flops 406588416 | bytes 2641920 | tf_op jit(solution)/shard_map/dot_general | solution.py:258
  51.9 0.7 collective-permute-start.3
  53.3 1.6 %collective-permute-start.4 = (bf16[2,516,256]{2,0,1:T(2,128)(2,1)S(1)}, bf16[2,516,256]{2,0,1:T(2,128)(2,1)S(1)}, u32[]{:S(2)}, u32[]{:S(2)}) collective-permute-start(bf16[2,516,256]{2,0,1:T(2,128)(2,1)S(1)} %copy.27), channel_id=1, source_target_pairs={{0,1},{1,0},{2,3},{3,2},{4,5},{5,4},{6,7},{7,6},{8,9},{9,8},{10,11... | collective-permute-start | bytes 1585160 | tf_op jit(solution)/shard_map/ppermute | solution.py:144
  56.8 9.6 %collective-permute-done.4 = bf16[2,516,256]{2,0,1:T(2,128)(2,1)S(1)} collective-permute-done((bf16[2,516,256]{2,0,1:T(2,128)(2,1)S(1)}, bf16[2,516,256]{2,0,1:T(2,128)(2,1)S(1)}, u32[]{:S(2)}, u32[]{:S(2)}) %collective-permute-start.4) | collective-permute-done | bytes 528416 | tf_op jit(solution)/shard_map/ppermute | solution.py:144
  67.0 9.6 %collective-permute-start.5 = (f32[128,256]{1,0:T(8,128)S(1)}, f32[128,256]{1,0:T(8,128)S(1)}, u32[]{:S(2)}, u32[]{:S(2)}) collective-permute-start(f32[128,256]{1,0:T(8,128)S(1)} %get-tuple-element.27), channel_id=1, source_target_pairs={{0,4},{4,8},{8,12},{12,0},{1,5},{5,9},{9,13},{13,1},{2,6},{6,10},{... | collective-permute-start | bytes 393224 | tf_op jit(solution)/shard_map/ppermute | solution.py:353
  76.6 2.4 %collective-permute-start.6 = (f32[128,256]{1,0:T(8,128)S(1)}, f32[128,256]{1,0:T(8,128)S(1)}, u32[]{:S(2)}, u32[]{:S(2)}) collective-permute-start(f32[128,256]{1,0:T(8,128)S(1)} %get-tuple-element.28), channel_id=1, source_target_pairs={{0,8},{4,12},{8,0},{12,4},{1,9},{5,13},{9,1},{13,5},{2,10},{6,14},... | collective-permute-start | bytes 393224 | tf_op jit(solution)/shard_map/ppermute | solution.py:353
  79.1 2.4 %collective-permute-done.5 = f32[128,256]{1,0:T(8,128)S(1)} collective-permute-done((f32[128,256]{1,0:T(8,128)S(1)}, f32[128,256]{1,0:T(8,128)S(1)}, u32[]{:S(2)}, u32[]{:S(2)}) %collective-permute-start.5) | collective-permute-done | bytes 131104 | tf_op jit(solution)/shard_map/ppermute | solution.py:353
  81.5 2.9 %collective-permute-done.6 = f32[128,256]{1,0:T(8,128)S(1)} collective-permute-done((f32[128,256]{1,0:T(8,128)S(1)}, f32[128,256]{1,0:T(8,128)S(1)}, u32[]{:S(2)}, u32[]{:S(2)}) %collective-permute-start.6) | collective-permute-done | bytes 131104 | tf_op jit(solution)/shard_map/ppermute | solution.py:353
  84.4 1.0 %collective-permute-done.7 = f32[128,256]{1,0:T(8,128)S(1)} collective-permute-done((f32[128,256]{1,0:T(8,128)S(1)}, f32[128,256]{1,0:T(8,128)S(1)}, u32[]{:S(2)}, u32[]{:S(2)}) %collective-permute-start.7) | collective-permute-done | bytes 131104 | tf_op jit(solution)/shard_map/ppermute | solution.py:353
  85.5 1.3 %collective-permute-done.8 = f32[128,256]{1,0:T(8,128)S(1)} collective-permute-done((f32[128,256]{1,0:T(8,128)S(1)}, f32[128,256]{1,0:T(8,128)S(1)}, u32[]{:S(2)}, u32[]{:S(2)}) %collective-permute-start.8) | collective-permute-done | bytes 131104 | tf_op jit(solution)/shard_map/ppermute | solution.py:154
  86.8 0.7 add.307
  (82 shorter events, 9.9 us)
Async XLA Ops:
  1.5 8.7 %collective-permute-start = (f32[3,256]{1,0:T(4,128)S(1)}, f32[3,256]{1,0:T(4,128)S(1)}, u32[]{:S(2)}, u32[]{:S(2)}) collective-permute-start(f32[3,256]{1,0:T(4,128)S(1)} %bitcast.121), channel_id=1, source_target_pairs={{0,4},{4,8},{8,12},{12,0},{1,5},{5,9},{9,13},{13,1},{2,6},{6,10},{... | collective-permute-start | bytes 9224 | tf_op jit(solution)/shard_map/ppermute | solution.py:214
  4.5 5.6 %collective-permute-start.1 = (f32[3,256]{1,0:T(4,128)S(1)}, f32[3,256]{1,0:T(4,128)S(1)}, u32[]{:S(2)}, u32[]{:S(2)}) collective-permute-start(f32[3,256]{1,0:T(4,128)S(1)} %bitcast.122), channel_id=1, source_target_pairs={{0,8},{4,12},{8,0},{12,4},{1,9},{5,13},{9,1},{13,5},{2,10},{6,14},... | collective-permute-start | bytes 9224 | tf_op jit(solution)/shard_map/ppermute | solution.py:214
  7.1 3.6 %collective-permute-start.2 = (f32[3,256]{1,0:T(4,128)S(1)}, f32[3,256]{1,0:T(4,128)S(1)}, u32[]{:S(2)}, u32[]{:S(2)}) collective-permute-start(f32[3,256]{1,0:T(4,128)S(1)} %bitcast.123), channel_id=1, source_target_pairs={{0,12},{4,0},{8,4},{12,8},{1,13},{5,1},{9,5},{13,9},{2,14},{6,2},{... | collective-permute-start | bytes 9224 | tf_op jit(solution)/shard_map/ppermute | solution.py:214
  12.1 1.0 %copy-start.2 = (bf16[1,640,256]{2,1,0:T(8,128)(2,1)S(1)}, bf16[1,640,256]{2,1,0:T(8,128)(2,1)}, u32[]{:S(2)}) copy-start(bf16[1,640,256]{2,1,0:T(8,128)(2,1)} %param.8) | copy-start | bytes 983044
  19.7 28.4 %all-to-all-start = ((f32[4,2,256,128]{3,2,1,0:T(8,128)}), f32[4,2,256,128]{3,2,1,0:T(8,128)S(1)}, u32[]{:S(2)}, u32[]{:S(2)}) async-start(f32[4,2,256,128]{3,2,1,0:T(8,128)} %copy.20), calls=%async_computation | async-start | bytes 2097152 | tf_op jit(solution)/shard_map/all_to_all | solution.py:325
  51.7 0.9 %copy-start.1 = (s32[2,256]{1,0:T(2,128)S(1)}, s32[2,256]{1,0:T(2,128)}, u32[]{:S(2)}) copy-start(s32[2,256]{1,0:T(2,128)} %param.7) | copy-start | bytes 6148
  51.9 0.8 collective-permute-start.3
  52.9 2.1 %copy-start = (s32[1,2049]{1,0:T(1,128)S(1)}, s32[1,2049]{1,0:T(1,128)}, u32[]{:S(2)}) copy-start(s32[1,2049]{1,0:T(1,128)} %param.9) | copy-start | bytes 24592
  53.3 13.0 %collective-permute-start.4 = (bf16[2,516,256]{2,0,1:T(2,128)(2,1)S(1)}, bf16[2,516,256]{2,0,1:T(2,128)(2,1)S(1)}, u32[]{:S(2)}, u32[]{:S(2)}) collective-permute-start(bf16[2,516,256]{2,0,1:T(2,128)(2,1)S(1)} %copy.27), channel_id=1, source_target_pairs={{0,1},{1,0},{2,3},{3,2},{4,5},{5,4},{6,7},{7,6},{8,9},{9,8},{10,11... | collective-permute-start | bytes 1585160 | tf_op jit(solution)/shard_map/ppermute | solution.py:144
  67.0 14.4 %collective-permute-start.5 = (f32[128,256]{1,0:T(8,128)S(1)}, f32[128,256]{1,0:T(8,128)S(1)}, u32[]{:S(2)}, u32[]{:S(2)}) collective-permute-start(f32[128,256]{1,0:T(8,128)S(1)} %get-tuple-element.27), channel_id=1, source_target_pairs={{0,4},{4,8},{8,12},{12,0},{1,5},{5,9},{9,13},{13,1},{2,6},{6,10},{... | collective-permute-start | bytes 393224 | tf_op jit(solution)/shard_map/ppermute | solution.py:353
  76.6 7.8 %collective-permute-start.6 = (f32[128,256]{1,0:T(8,128)S(1)}, f32[128,256]{1,0:T(8,128)S(1)}, u32[]{:S(2)}, u32[]{:S(2)}) collective-permute-start(f32[128,256]{1,0:T(8,128)S(1)} %get-tuple-element.28), channel_id=1, source_target_pairs={{0,8},{4,12},{8,0},{12,4},{1,9},{5,13},{9,1},{13,5},{2,10},{6,14},... | collective-permute-start | bytes 393224 | tf_op jit(solution)/shard_map/ppermute | solution.py:353
  79.0 6.4 %collective-permute-start.7 = (f32[128,256]{1,0:T(8,128)S(1)}, f32[128,256]{1,0:T(8,128)S(1)}, u32[]{:S(2)}, u32[]{:S(2)}) collective-permute-start(f32[128,256]{1,0:T(8,128)S(1)} %get-tuple-element.29), channel_id=1, source_target_pairs={{0,12},{4,0},{8,4},{12,8},{1,13},{5,1},{9,5},{13,9},{2,14},{6,2},{... | collective-permute-start | bytes 393224 | tf_op jit(solution)/shard_map/ppermute | solution.py:353
  85.4 1.4 %collective-permute-start.8 = (f32[128,256]{1,0:T(8,128)S(1)}, f32[128,256]{1,0:T(8,128)S(1)}, u32[]{:S(2)}, u32[]{:S(2)}) collective-permute-start(f32[128,256]{1,0:T(8,128)S(1)} %fusion.62), channel_id=1, source_target_pairs={{0,2},{2,0},{1,3},{3,1},{4,6},{6,4},{5,7},{7,5},{8,10},{10,8},{9,1... | collective-permute-start | bytes 393224 | tf_op jit(solution)/shard_map/ppermute | solution.py:154
